TPU v7x, 32 devices: a whole 2x2x4 slice. The times are simulated.
32 devices in a mesh: gx: 4 (over z), gy: 4 (over x, core), gz: 2 (over y).
Axes of the slice: x: 2, y: 2, z: 4, core: 2. Of those that a mesh axis runs over, the one named last changes fastest.
Arguments:
- tokens: bfloat16 [64, 128, 3072], P('gx', ('gy', 'gz')), may hold values from -20 to 20
- grads_out: bfloat16 [64, 128, 3072], P('gx', ('gy', 'gz')), may hold values from -6 to 6
- labels: int32 [64, 128, 16], P('gx', ('gy', 'gz')), may hold values from 0 to 2
- ln_gain: float32 [192], replicated, may hold values from 0.1 to 1.9
- qkv_weight: bfloat16 [192, 576], replicated, may hold values from -0.4375 to 0.4375
- proj_weight: bfloat16 [192, 192], replicated, may hold values from -0.4375 to 0.4375
Outputs:
- grad_tokens: bfloat16 [64, 128, 3072], P('gx', ('gy', 'gz'))
- grad_gain: float32 [192], replicated
- grad_qkv: float32 [110592], replicated
- grad_proj: float32 [36864], replicated
Inputs may be any that keep to these rules, and one draw needn't show every extreme that they name: labels are given on the shifted grid.
All inputs are finite; a program needn't handle non-finite values.
Results may differ from a plain program's by a relative error of at most 0.0087.
Values may be sent and summed in bfloat16 or wider, within the bound.
No kernel may reach another device: no remote copies, remote signals or barrier semaphores. Data moves between devices by JAX's collectives and lax.ppermute only.
A program may use at most 64 MiB of HBM per device.

v0:
```python
import jax
import jax.numpy as jnp
from jax import lax
from jax.sharding import PartitionSpec as P

HEADS = 6
C = 192
WIN = 8
SHIFT = 4
NZ = 16


def passed_along(block, axis, distance):
    devices = range(lax.axis_size(axis))
    route = [((i - distance) % len(devices), i) for i in devices]
    return lax.ppermute(block, axis, route)


def to_windows(values):
    extent_a, extent_b, extent_c = (values.shape[0], values.shape[1], values.shape[2])
    trailing = values.shape[3:]
    shaped = values.reshape(
        (extent_a // WIN, WIN, extent_b // WIN, WIN, extent_c // WIN, WIN) + trailing
    )
    axes_order = (0, 2, 4, 1, 3, 5) + tuple(range(6, 6 + len(trailing)))
    return shaped.transpose(axes_order).reshape((-1, WIN**3) + trailing)


def from_windows(values, extent_a, extent_b, extent_c):
    trailing = values.shape[2:]
    shaped = values.reshape(
        (extent_a // WIN, extent_b // WIN, extent_c // WIN, WIN, WIN, WIN) + trailing
    )
    axes_order = (0, 3, 1, 4, 2, 5) + tuple(range(6, 6 + len(trailing)))
    return shaped.transpose(axes_order).reshape((extent_a, extent_b, extent_c) + trailing)


def window_grads(window_tokens, window_grads_out, mask_keys, ln_gain, qkv_weight, proj_weight):
    channels = window_tokens.shape[1]
    head_size = channels // HEADS
    score_scale = head_size ** (-0.5)
    as_float = window_tokens.astype(jnp.float32)
    row_mean = jnp.mean(as_float, axis=1, keepdims=True)
    centred = as_float - row_mean
    inv_std = lax.rsqrt(jnp.mean(centred * centred, axis=1, keepdims=True) + 1e-05)
    x_hat = centred * inv_std
    normed = (x_hat * ln_gain).astype(jnp.bfloat16)
    qkv_rows = jnp.dot(normed, qkv_weight, preferred_element_type=jnp.float32).astype(jnp.bfloat16)
    queries = qkv_rows[:, :channels].reshape(-1, HEADS, head_size)
    keys_all = qkv_rows[:, channels : 2 * channels].reshape(-1, HEADS, head_size)
    values_all = qkv_rows[:, 2 * channels :].reshape(-1, HEADS, head_size)
    scores = (
        jnp.einsum("ihd,jhd->hij", queries, keys_all, preferred_element_type=jnp.float32)
        * score_scale
    )
    allowed = mask_keys[:, None] == mask_keys[None, :]
    weights = jnp.where(allowed[None], jnp.exp(scores), jnp.float32(0.0))
    softmax_probs = weights / jnp.sum(weights, axis=2, keepdims=True)
    probs_bf = softmax_probs.astype(jnp.bfloat16)
    attended = (
        jnp.einsum("hij,jhd->ihd", probs_bf, values_all, preferred_element_type=jnp.float32)
        .reshape(-1, channels)
        .astype(jnp.bfloat16)
    )
    proj_grad = jnp.einsum(
        "tc,td->cd", attended, window_grads_out, preferred_element_type=jnp.float32
    )
    grad_attended = jnp.einsum(
        "tc,dc->td", window_grads_out, proj_weight, preferred_element_type=jnp.float32
    ).astype(jnp.bfloat16)
    grad_heads = grad_attended.reshape(-1, HEADS, head_size)
    grad_probs = jnp.einsum(
        "ihd,jhd->hij", grad_heads, values_all, preferred_element_type=jnp.float32
    )
    grad_values = jnp.einsum(
        "hij,ihd->jhd", probs_bf, grad_heads, preferred_element_type=jnp.float32
    ).astype(jnp.bfloat16)
    row_total = jnp.sum(softmax_probs * grad_probs, axis=2, keepdims=True)
    grad_scores = (softmax_probs * (grad_probs - row_total) * score_scale).astype(jnp.bfloat16)
    grad_queries = jnp.einsum(
        "hij,jhd->ihd", grad_scores, keys_all, preferred_element_type=jnp.float32
    ).astype(jnp.bfloat16)
    grad_keys = jnp.einsum(
        "hij,ihd->jhd", grad_scores, queries, preferred_element_type=jnp.float32
    ).astype(jnp.bfloat16)
    grad_qkv_rows = jnp.concatenate(
        [
            grad_queries.reshape(-1, channels),
            grad_keys.reshape(-1, channels),
            grad_values.reshape(-1, channels),
        ],
        axis=1,
    )
    qkv_grad = jnp.einsum("tc,td->cd", normed, grad_qkv_rows, preferred_element_type=jnp.float32)
    grad_normed = jnp.einsum(
        "td,cd->tc", grad_qkv_rows, qkv_weight, preferred_element_type=jnp.float32
    )
    gain_grad = jnp.sum(grad_normed * x_hat, axis=0)
    scaled_grad = grad_normed * ln_gain
    grad_shifted = inv_std * (
        scaled_grad
        - jnp.mean(scaled_grad, axis=1, keepdims=True)
        - x_hat * jnp.mean(scaled_grad * x_hat, axis=1, keepdims=True)
    )
    return (grad_shifted.astype(jnp.bfloat16), qkv_grad, proj_grad, gain_grad)


def ahead_first(both_arrays):
    arrived = passed_along((both_arrays[0][:SHIFT], both_arrays[1][:SHIFT]), "gx", -1)
    return (
        jnp.concatenate([both_arrays[0][SHIFT:], arrived[0]], axis=0),
        jnp.concatenate([both_arrays[1][SHIFT:], arrived[1]], axis=0),
    )


def ahead_second(both_arrays):
    arrived = passed_along((both_arrays[0][:, :SHIFT], both_arrays[1][:, :SHIFT]), ("gy", "gz"), -1)
    return (
        jnp.concatenate([both_arrays[0][:, SHIFT:], arrived[0]], axis=1),
        jnp.concatenate([both_arrays[1][:, SHIFT:], arrived[1]], axis=1),
    )


def back_first(gradient):
    arrived = passed_along(gradient[-SHIFT:], "gx", 1)
    return jnp.concatenate([arrived, gradient[:-SHIFT]], axis=0)


def back_second(gradient):
    arrived = passed_along(gradient[:, -SHIFT:], ("gy", "gz"), 1)
    return jnp.concatenate([arrived, gradient[:, :-SHIFT]], axis=1)


def per_device(tokens, grads_out, labels, ln_gain, qkv_weight, proj_weight):
    brick_a, brick_b = (tokens.shape[0], tokens.shape[1])
    brick_c = NZ
    channels = C
    both_arrays = (tokens, grads_out)
    both_arrays = ahead_second(ahead_first(both_arrays))
    shifted_tokens = jnp.roll(
        both_arrays[0].reshape(brick_a, brick_b, brick_c, channels), -SHIFT, axis=2
    )
    shifted_grads = jnp.roll(
        both_arrays[1].reshape(brick_a, brick_b, brick_c, channels), -SHIFT, axis=2
    )
    extent_a = brick_a * lax.axis_size("gx")
    extent_b = brick_b * lax.axis_size(("gy", "gz"))
    first_index = lax.axis_index("gx") * brick_a + jnp.arange(brick_a, dtype=jnp.int32)
    second_index = lax.axis_index(("gy", "gz")) * brick_b + jnp.arange(brick_b, dtype=jnp.int32)
    wrap_first = (first_index >= extent_a - SHIFT).astype(jnp.int32)
    wrap_second = (second_index >= extent_b - SHIFT).astype(jnp.int32)
    wrap_third = (jnp.arange(brick_c, dtype=jnp.int32) >= brick_c - SHIFT).astype(jnp.int32)
    region = (
        wrap_first[:, None, None] * 4 + wrap_second[None, :, None] * 2 + wrap_third[None, None, :]
    )
    mask_key = labels * 8 + region

    def window_step(totals, window_item):
        grad_win, qkv_part, proj_part, gain_part = window_grads(
            window_item[0], window_item[1], window_item[2], ln_gain, qkv_weight, proj_weight
        )
        return ((totals[0] + qkv_part, totals[1] + proj_part, totals[2] + gain_part), grad_win)

    zero_sums = (
        jnp.zeros((channels, 3 * channels), jnp.float32),
        jnp.zeros((channels, channels), jnp.float32),
        jnp.zeros((channels,), jnp.float32),
    )
    sums, grad_windows = lax.scan(
        window_step,
        zero_sums,
        (to_windows(shifted_tokens), to_windows(shifted_grads), to_windows(mask_key)),
    )
    qkv_grad, proj_grad, gain_grad = sums
    qkv_grad, proj_grad, gain_grad = lax.psum((qkv_grad, proj_grad, gain_grad), ("gx", "gy", "gz"))
    grad_branch = jnp.roll(from_windows(grad_windows, brick_a, brick_b, brick_c), SHIFT, axis=2)
    grad_branch = grad_branch.reshape(brick_a, brick_b, brick_c * channels)
    grad_branch = back_first(back_second(grad_branch))
    grad_tokens = (grads_out.astype(jnp.float32) + grad_branch.astype(jnp.float32)).astype(
        jnp.bfloat16
    )
    return (grad_tokens, gain_grad, qkv_grad.reshape(-1), proj_grad.reshape(-1))


def solution(mesh):
    return jax.shard_map(
        per_device,
        mesh=mesh,
        in_specs=(
            P("gx", ("gy", "gz"), None),
            P("gx", ("gy", "gz"), None),
            P("gx", ("gy", "gz"), None),
            P(),
            P(),
            P(),
        ),
        out_specs=(P("gx", ("gy", "gz"), None), P(), P(), P()),
        check_vma=False,
    )
```

profile of v0, /device:TPU:5, one launch (start us, length us, event | category | flops | bytes accessed | tf_op | source)
XLA Modules:
  0.0 584.6 jit_solution(5574990165840329090)
XLA Ops:
  22.5 6.4 %collective-permute-done = bf16[4,16,3072]{2,1,0:T(8,128)(2,1)} collective-permute-done((bf16[4,16,3072]{2,1,0:T(8,128)(2,1)}, bf16[4,16,3072]{2,1,0:T(8,128)(2,1)}, u32[]{:S(2)}, u32[]{:S(2)}) %collective-permute-start) | collective-permute-done | bytes 393248 | tf_op jit(solution)/shard_map/ppermute | solution.py:16
  34.8 3.7 reshape.181
  43.3 3.7 reshape.176
  57.4 358.1 %while.17 = (s32[]{:T(128)}, f32[192,576]{1,0:T(8,128)}, f32[192,192]{1,0:T(8,128)S(1)}, f32[192]{0:T(256)S(1)}, bf16[8,512,192]{1,2,0:T(8,128)(2,1)}, /*index=5...) while((s32[]{:T(128)}, f32[192,576]{1,0:T(8,128)}, ...), condition=%wide.region_8.9_spmd.clone, body=%wide.region_0.8_spmd.clone.sunk | while | flops 1079349888 | bytes 64495856 | solution.py:169
  58.5 4.3 fusion.136
  67.7 10.9 %fusion.140 = bf16[6,32,512]{2,1,0:T(8,128)(2,1)} fusion(bf16[512,6,32]{0,2,1:T(8,128)(2,1)S(1)} %bitcast.169, f32[6,512,512]{1,2,0:T(8,128)} %fusion.138, f32[6,512,512]{1,2,0:T(8,128)} %get-tuple-element.265, f32[6,512]{1,0:T(8,128)S(1)} %get-tuple-element.266, pred[512,512]{0,1:T(8,128)(4,1)S(1)} %broadcast_compare_fusion.2), kind=kOutput, calls=%fused_computation.15.clone.1 | convolution fusion | flops 118066688 | bytes 13250560 | tf_op jit(solution)/shard_map/while/body/eval_jaxpr/hij,jhd->ihd/dot_general | solution.py:80
  78.6 10.3 %fusion.139 = bf16[6,32,512]{2,1,0:T(8,128)(2,1)S(1)} fusion(bf16[512,6,32]{0,2,1:T(8,128)(2,1)S(1)} %bitcast.167, f32[6,512,512]{1,2,0:T(8,128)} %fusion.138, f32[6,512,512]{1,2,0:T(8,128)} %get-tuple-element.265, f32[6,512]{1,0:T(8,128)S(1)} %get-tuple-element.266, pred[512,512]{0,1:T(8,128)(4,1)S(1)} %broadcast_compare_fusion.2), kind=kOutput, calls=%fused_computation.16.clone.1 | convolution fusion | flops 118066688 | bytes 13250560 | tf_op jit(solution)/shard_map/while/body/eval_jaxpr/hij,ihd->jhd/dot_general | solution.py:83
  88.9 4.4 fusion.137
  94.6 4.4 fusion.141
  102.3 4.3 fusion.136
  111.5 10.9 %fusion.140 = bf16[6,32,512]{2,1,0:T(8,128)(2,1)} fusion(bf16[512,6,32]{0,2,1:T(8,128)(2,1)S(1)} %bitcast.169, f32[6,512,512]{1,2,0:T(8,128)} %fusion.138, f32[6,512,512]{1,2,0:T(8,128)} %get-tuple-element.265, f32[6,512]{1,0:T(8,128)S(1)} %get-tuple-element.266, pred[512,512]{0,1:T(8,128)(4,1)S(1)} %broadcast_compare_fusion.2), kind=kOutput, calls=%fused_computation.15.clone.1 | convolution fusion | flops 118066688 | bytes 13250560 | tf_op jit(solution)/shard_map/while/body/eval_jaxpr/hij,jhd->ihd/dot_general | solution.py:80
  122.4 10.3 %fusion.139 = bf16[6,32,512]{2,1,0:T(8,128)(2,1)S(1)} fusion(bf16[512,6,32]{0,2,1:T(8,128)(2,1)S(1)} %bitcast.167, f32[6,512,512]{1,2,0:T(8,128)} %fusion.138, f32[6,512,512]{1,2,0:T(8,128)} %get-tuple-element.265, f32[6,512]{1,0:T(8,128)S(1)} %get-tuple-element.266, pred[512,512]{0,1:T(8,128)(4,1)S(1)} %broadcast_compare_fusion.2), kind=kOutput, calls=%fused_computation.16.clone.1 | convolution fusion | flops 118066688 | bytes 13250560 | tf_op jit(solution)/shard_map/while/body/eval_jaxpr/hij,ihd->jhd/dot_general | solution.py:83
  132.7 4.4 fusion.137
  138.5 4.4 fusion.141
  147.2 4.3 fusion.136
  156.4 10.9 %fusion.140 = bf16[6,32,512]{2,1,0:T(8,128)(2,1)} fusion(bf16[512,6,32]{0,2,1:T(8,128)(2,1)S(1)} %bitcast.169, f32[6,512,512]{1,2,0:T(8,128)} %fusion.138, f32[6,512,512]{1,2,0:T(8,128)} %get-tuple-element.265, f32[6,512]{1,0:T(8,128)S(1)} %get-tuple-element.266, pred[512,512]{0,1:T(8,128)(4,1)S(1)} %broadcast_compare_fusion.2), kind=kOutput, calls=%fused_computation.15.clone.1 | convolution fusion | flops 118066688 | bytes 13250560 | tf_op jit(solution)/shard_map/while/body/eval_jaxpr/hij,jhd->ihd/dot_general | solution.py:80
  167.2 10.3 %fusion.139 = bf16[6,32,512]{2,1,0:T(8,128)(2,1)S(1)} fusion(bf16[512,6,32]{0,2,1:T(8,128)(2,1)S(1)} %bitcast.167, f32[6,512,512]{1,2,0:T(8,128)} %fusion.138, f32[6,512,512]{1,2,0:T(8,128)} %get-tuple-element.265, f32[6,512]{1,0:T(8,128)S(1)} %get-tuple-element.266, pred[512,512]{0,1:T(8,128)(4,1)S(1)} %broadcast_compare_fusion.2), kind=kOutput, calls=%fused_computation.16.clone.1 | convolution fusion | flops 118066688 | bytes 13250560 | tf_op jit(solution)/shard_map/while/body/eval_jaxpr/hij,ihd->jhd/dot_general | solution.py:83
  177.6 4.4 fusion.137
  183.3 4.4 fusion.141
  192.0 4.3 fusion.136
  201.2 10.9 %fusion.140 = bf16[6,32,512]{2,1,0:T(8,128)(2,1)} fusion(bf16[512,6,32]{0,2,1:T(8,128)(2,1)S(1)} %bitcast.169, f32[6,512,512]{1,2,0:T(8,128)} %fusion.138, f32[6,512,512]{1,2,0:T(8,128)} %get-tuple-element.265, f32[6,512]{1,0:T(8,128)S(1)} %get-tuple-element.266, pred[512,512]{0,1:T(8,128)(4,1)S(1)} %broadcast_compare_fusion.2), kind=kOutput, calls=%fused_computation.15.clone.1 | convolution fusion | flops 118066688 | bytes 13250560 | tf_op jit(solution)/shard_map/while/body/eval_jaxpr/hij,jhd->ihd/dot_general | solution.py:80
  212.1 10.3 %fusion.139 = bf16[6,32,512]{2,1,0:T(8,128)(2,1)S(1)} fusion(bf16[512,6,32]{0,2,1:T(8,128)(2,1)S(1)} %bitcast.167, f32[6,512,512]{1,2,0:T(8,128)} %fusion.138, f32[6,512,512]{1,2,0:T(8,128)} %get-tuple-element.265, f32[6,512]{1,0:T(8,128)S(1)} %get-tuple-element.266, pred[512,512]{0,1:T(8,128)(4,1)S(1)} %broadcast_compare_fusion.2), kind=kOutput, calls=%fused_computation.16.clone.1 | convolution fusion | flops 118066688 | bytes 13250560 | tf_op jit(solution)/shard_map/while/body/eval_jaxpr/hij,ihd->jhd/dot_general | solution.py:83
  222.4 4.4 fusion.137
  228.2 4.4 fusion.141
  236.9 4.3 fusion.136
  246.1 10.9 %fusion.140 = bf16[6,32,512]{2,1,0:T(8,128)(2,1)} fusion(bf16[512,6,32]{0,2,1:T(8,128)(2,1)S(1)} %bitcast.169, f32[6,512,512]{1,2,0:T(8,128)} %fusion.138, f32[6,512,512]{1,2,0:T(8,128)} %get-tuple-element.265, f32[6,512]{1,0:T(8,128)S(1)} %get-tuple-element.266, pred[512,512]{0,1:T(8,128)(4,1)S(1)} %broadcast_compare_fusion.2), kind=kOutput, calls=%fused_computation.15.clone.1 | convolution fusion | flops 118066688 | bytes 13250560 | tf_op jit(solution)/shard_map/while/body/eval_jaxpr/hij,jhd->ihd/dot_general | solution.py:80
  257.0 10.3 %fusion.139 = bf16[6,32,512]{2,1,0:T(8,128)(2,1)S(1)} fusion(bf16[512,6,32]{0,2,1:T(8,128)(2,1)S(1)} %bitcast.167, f32[6,512,512]{1,2,0:T(8,128)} %fusion.138, f32[6,512,512]{1,2,0:T(8,128)} %get-tuple-element.265, f32[6,512]{1,0:T(8,128)S(1)} %get-tuple-element.266, pred[512,512]{0,1:T(8,128)(4,1)S(1)} %broadcast_compare_fusion.2), kind=kOutput, calls=%fused_computation.16.clone.1 | convolution fusion | flops 118066688 | bytes 13250560 | tf_op jit(solution)/shard_map/while/body/eval_jaxpr/hij,ihd->jhd/dot_general | solution.py:83
  267.3 4.4 fusion.137
  273.0 4.4 fusion.141
  281.8 4.3 fusion.136
  287.2 3.7 fusion.138
  290.9 10.9 %fusion.140 = bf16[6,32,512]{2,1,0:T(8,128)(2,1)} fusion(bf16[512,6,32]{0,2,1:T(8,128)(2,1)S(1)} %bitcast.169, f32[6,512,512]{1,2,0:T(8,128)} %fusion.138, f32[6,512,512]{1,2,0:T(8,128)} %get-tuple-element.265, f32[6,512]{1,0:T(8,128)S(1)} %get-tuple-element.266, pred[512,512]{0,1:T(8,128)(4,1)S(1)} %broadcast_compare_fusion.2), kind=kOutput, calls=%fused_computation.15.clone.1 | convolution fusion | flops 118066688 | bytes 13250560 | tf_op jit(solution)/shard_map/while/body/eval_jaxpr/hij,jhd->ihd/dot_general | solution.py:80
  301.8 10.3 %fusion.139 = bf16[6,32,512]{2,1,0:T(8,128)(2,1)S(1)} fusion(bf16[512,6,32]{0,2,1:T(8,128)(2,1)S(1)} %bitcast.167, f32[6,512,512]{1,2,0:T(8,128)} %fusion.138, f32[6,512,512]{1,2,0:T(8,128)} %get-tuple-element.265, f32[6,512]{1,0:T(8,128)S(1)} %get-tuple-element.266, pred[512,512]{0,1:T(8,128)(4,1)S(1)} %broadcast_compare_fusion.2), kind=kOutput, calls=%fused_computation.16.clone.1 | convolution fusion | flops 118066688 | bytes 13250560 | tf_op jit(solution)/shard_map/while/body/eval_jaxpr/hij,ihd->jhd/dot_general | solution.py:83
  312.1 4.4 fusion.137
  317.9 4.4 fusion.141
  326.6 4.3 fusion.136
  335.8 10.9 %fusion.140 = bf16[6,32,512]{2,1,0:T(8,128)(2,1)} fusion(bf16[512,6,32]{0,2,1:T(8,128)(2,1)S(1)} %bitcast.169, f32[6,512,512]{1,2,0:T(8,128)} %fusion.138, f32[6,512,512]{1,2,0:T(8,128)} %get-tuple-element.265, f32[6,512]{1,0:T(8,128)S(1)} %get-tuple-element.266, pred[512,512]{0,1:T(8,128)(4,1)S(1)} %broadcast_compare_fusion.2), kind=kOutput, calls=%fused_computation.15.clone.1 | convolution fusion | flops 118066688 | bytes 13250560 | tf_op jit(solution)/shard_map/while/body/eval_jaxpr/hij,jhd->ihd/dot_general | solution.py:80
  346.7 10.3 %fusion.139 = bf16[6,32,512]{2,1,0:T(8,128)(2,1)S(1)} fusion(bf16[512,6,32]{0,2,1:T(8,128)(2,1)S(1)} %bitcast.167, f32[6,512,512]{1,2,0:T(8,128)} %fusion.138, f32[6,512,512]{1,2,0:T(8,128)} %get-tuple-element.265, f32[6,512]{1,0:T(8,128)S(1)} %get-tuple-element.266, pred[512,512]{0,1:T(8,128)(4,1)S(1)} %broadcast_compare_fusion.2), kind=kOutput, calls=%fused_computation.16.clone.1 | convolution fusion | flops 118066688 | bytes 13250560 | tf_op jit(solution)/shard_map/while/body/eval_jaxpr/hij,ihd->jhd/dot_general | solution.py:83
  357.0 4.4 fusion.137
  362.8 4.4 fusion.141
  371.5 4.3 fusion.136
  380.6 10.9 %fusion.140 = bf16[6,32,512]{2,1,0:T(8,128)(2,1)} fusion(bf16[512,6,32]{0,2,1:T(8,128)(2,1)S(1)} %bitcast.169, f32[6,512,512]{1,2,0:T(8,128)} %fusion.138, f32[6,512,512]{1,2,0:T(8,128)} %get-tuple-element.265, f32[6,512]{1,0:T(8,128)S(1)} %get-tuple-element.266, pred[512,512]{0,1:T(8,128)(4,1)S(1)} %broadcast_compare_fusion.2), kind=kOutput, calls=%fused_computation.15.clone.1 | convolution fusion | flops 118066688 | bytes 13250560 | tf_op jit(solution)/shard_map/while/body/eval_jaxpr/hij,jhd->ihd/dot_general | solution.py:80
  391.5 10.3 %fusion.139 = bf16[6,32,512]{2,1,0:T(8,128)(2,1)S(1)} fusion(bf16[512,6,32]{0,2,1:T(8,128)(2,1)S(1)} %bitcast.167, f32[6,512,512]{1,2,0:T(8,128)} %fusion.138, f32[6,512,512]{1,2,0:T(8,128)} %get-tuple-element.265, f32[6,512]{1,0:T(8,128)S(1)} %get-tuple-element.266, pred[512,512]{0,1:T(8,128)(4,1)S(1)} %broadcast_compare_fusion.2), kind=kOutput, calls=%fused_computation.16.clone.1 | convolution fusion | flops 118066688 | bytes 13250560 | tf_op jit(solution)/shard_map/while/body/eval_jaxpr/hij,ihd->jhd/dot_general | solution.py:83
  401.9 4.4 fusion.137
  407.6 4.4 fusion.141
  428.0 5.1 collective-permute-done.4
  437.8 48.9 %psum.21 = f32[192]{0:T(256)} all-reduce(f32[192]{0:T(256)S(1)} %get-tuple-element.65), channel_id=1, replica_groups=mesh['gx'=4,'gy'=4,'gz'=2] {'gx','gy','gz'}, use_global_device_ids=true, to_apply=%region_9.10 | all-reduce | flops 192 | bytes 1536 | tf_op jit(solution)/shard_map/psum | solution.py:175
  489.6 84.8 %all-reduce.3.cloned.1.call-done = (f32[110592]{0:T(1024)}, f32[36864]{0:T(1024)}) async-done(((f32[110592]{0:T(1024)}, f32[36864]{0:T(1024)}), (f32[110592]{0:T(1024)}, f32[36864]{0:T(1024)})) %all-reduce.3.cloned.1.call-update) | async-done | bytes 589840 | tf_op jit(solution)/shard_map/psum | solution.py:175
  (256 shorter events, 138.5 us)
Async XLA Ops:
  7.2 7.3 %copy-start.6 = (bf16[16,16,3072]{2,1,0:T(8,128)(2,1)S(1)}, bf16[16,16,3072]{2,1,0:T(8,128)(2,1)}, u32[]{:S(2)}) copy-start(bf16[16,16,3072]{2,1,0:T(8,128)(2,1)} %param.8) | copy-start | bytes 4718596
  7.2 567.2 %all-reduce.3.cloned.1.call-start = ((), (), s32[]{:S(2)}) async-start(), calls=%async_computation | async-start | bytes 1179648 | tf_op jit(solution)/shard_map/psum | solution.py:175
  9.1 11.4 %collective-permute-start.2 = (bf16[4,16,3072]{2,1,0:T(8,128)(2,1)}, bf16[4,16,3072]{2,1,0:T(8,128)(2,1)}, u32[]{:S(2)}, u32[]{:S(2)}) collective-permute-start(bf16[4,16,3072]{2,1,0:T(8,128)(2,1)} %slice.74), channel_id=1, source_target_pairs={{8,0},{16,8},{24,16},{0,24},{9,1},{17,9},{25,17},{1,25},{10,2},{18... | collective-permute-start | bytes 1179656 | tf_op jit(solution)/shard_map/ppermute | solution.py:16
  14.2 14.8 %collective-permute-start = (bf16[4,16,3072]{2,1,0:T(8,128)(2,1)}, bf16[4,16,3072]{2,1,0:T(8,128)(2,1)}, u32[]{:S(2)}, u32[]{:S(2)}) collective-permute-start(bf16[4,16,3072]{2,1,0:T(8,128)(2,1)} %slice.68), channel_id=1, source_target_pairs={{8,0},{16,8},{24,16},{0,24},{9,1},{17,9},{25,17},{1,25},{10,2},{18... | collective-permute-start | bytes 1179656 | tf_op jit(solution)/shard_map/ppermute | solution.py:16
  14.5 1.1 copy-start.8
  14.5 1.8 slice-start
  16.2 1.3 copy-start.4
  21.9 10.7 %collective-permute-start.3 = (bf16[16,4,3072]{2,0,1:T(8,128)(2,1)S(1)}, bf16[16,4,3072]{2,0,1:T(8,128)(2,1)S(1)}, u32[]{:S(2)}, u32[]{:S(2)}) collective-permute-start(bf16[16,4,3072]{2,0,1:T(8,128)(2,1)S(1)} %pad_maximum_fusion.10), channel_id=1, source_target_pairs={{1,0},{2,1},{3,2},{4,3},{5,4},{6,5},{7,6},{0,7},{9,8},{10,9},{11,1... | collective-permute-start | bytes 1179656 | tf_op jit(solution)/shard_map/ppermute | solution.py:16
  31.1 10.1 %collective-permute-start.1 = (bf16[16,4,3072]{2,0,1:T(8,128)(2,1)}, bf16[16,4,3072]{2,0,1:T(8,128)(2,1)S(1)}, u32[]{:S(2)}, u32[]{:S(2)}) collective-permute-start(bf16[16,4,3072]{2,0,1:T(8,128)(2,1)} %pad_maximum_fusion.11), channel_id=1, source_target_pairs={{1,0},{2,1},{3,2},{4,3},{5,4},{6,5},{7,6},{0,7},{9,8},{10,9},{11,1... | collective-permute-start | bytes 1179656 | tf_op jit(solution)/shard_map/ppermute | solution.py:16
  38.6 2.6 copy-start.3
  47.1 1.6 copy-start
  54.4 3.0 copy-start.2
  54.4 3.0 copy-start.5
  54.4 3.0 copy-start.9
  88.9 4.4 copy-start.10
  93.3 1.3 copy-start.11
  94.6 5.6 copy-start.12
  132.7 4.4 copy-start.10
  137.1 1.3 copy-start.11
  138.4 5.6 copy-start.12
  177.6 4.4 copy-start.10
  182.0 1.3 copy-start.11
  183.3 5.6 copy-start.12
  222.4 4.4 copy-start.10
  226.8 1.3 copy-start.11
  228.2 5.6 copy-start.12
  267.3 4.4 copy-start.10
  271.7 1.3 copy-start.11
  273.0 5.6 copy-start.12
  312.1 4.4 copy-start.10
  316.6 1.3 copy-start.11
  317.9 5.6 copy-start.12
  357.0 4.4 copy-start.10
  361.4 1.3 copy-start.11
  362.7 5.6 copy-start.12
  401.9 4.4 copy-start.10
  406.3 1.3 copy-start.11
  407.6 5.6 copy-start.12
  425.0 61.6 %copy-start.1 = (bf16[16,16,3072]{2,1,0:T(8,128)(2,1)S(1)}, bf16[16,16,3072]{2,1,0:T(8,128)(2,1)}, u32[]{:S(2)}) copy-start(bf16[16,16,3072]{2,1,0:T(8,128)(2,1)} %param.9) | copy-start | bytes 4718596
  425.3 7.9 %collective-permute-start.4 = (bf16[16,4,3072]{2,1,0:T(4,128)(2,1)S(1)}, bf16[16,4,3072]{2,1,0:T(4,128)(2,1)S(1)}, u32[]{:S(2)}, u32[]{:S(2)}) collective-permute-start(bf16[16,4,3072]{2,1,0:T(4,128)(2,1)S(1)} %slice.101), channel_id=1, source_target_pairs={{7,0},{0,1},{1,2},{2,3},{3,4},{4,5},{5,6},{6,7},{15,8},{8,9},{9,10... | collective-permute-start | bytes 1179656 | tf_op jit(solution)/shard_map/ppermute | solution.py:16
  433.2 0.8 copy-start.7
  434.8 51.9 %collective-permute-start.5 = (bf16[4,16,3072]{2,1,0:T(8,128)(2,1)}, bf16[4,16,3072]{2,1,0:T(8,128)(2,1)}, u32[]{:S(2)}, u32[]{:S(2)}) collective-permute-start(bf16[4,16,3072]{2,1,0:T(8,128)(2,1)} %pad_maximum_fusion.9), channel_id=1, source_target_pairs={{24,0},{0,8},{8,16},{16,24},{25,1},{1,9},{9,17},{17,25},{26,2},{2,... | collective-permute-start | bytes 1179656 | tf_op jit(solution)/shard_map/ppermute | solution.py:16
Sparse Core Ops, SparseCore 0:
  437.9 136.4 all-reduce.2
where the time goes:
time: 587 us; the launch traced here: 585 us
  matrix products  347 us (59%)
  waiting for transfers between devices  98.7 us (17%)
  blocking collectives  48.9 us (8%)
  local copies, waits for them, and re-layouts  46.5 us (8%)
  other arithmetic  21.2 us (4%)
  between operations  14.3 us (2%)
  starting transfers between devices  6.98 us (1%)
    dot_general x8, matrix products, window_grads(): jnp.einsum('hij,jhd->ihd', grad_scores, keys_all, preferred_element_type=...  87.2 us
    psum x1, waiting for transfers between devices, per_device(): lax.psum((qkv_grad, proj_grad, gain_grad), ('gx', 'gy', 'gz'))  84.8 us
    dot_general x8, matrix products, window_grads(): jnp.einsum('hij,ihd->jhd', grad_scores, queries, preferred_element_type=j...  82.4 us
    psum x1, blocking collectives, per_device(): lax.psum((qkv_grad, proj_grad, gain_grad), ('gx', 'gy', 'gz'))  48.9 us
    dot_general x8, matrix products, window_grads(): jnp.einsum('hij,jhd->ihd', probs_bf, values_all, preferred_element_type=j...  35.3 us
    dot_general x8, matrix products, window_grads(): jnp.einsum('hij,ihd->jhd', probs_bf, grad_heads, preferred_element_type=j...  35.3 us
    dot_general x8, matrix products, window_grads(): jnp.einsum('ihd,jhd->hij', queries, keys_all, preferred_element_type=jnp....  34.3 us
    dot_general x8, matrix products, window_grads(): jnp.einsum('ihd,jhd->hij', grad_heads, values_all, preferred_element_type...  29.5 us
  transfers between devices with their start and end apart: 7, of which 4 were waited for; matrix products, arithmetic and copies ran while one was open for 4% of the time, Pallas kernels for 0%

commit v1 on v0

v1 whole, which is shorter than its diff:
```python
import jax
import jax.numpy as jnp
from jax import lax
from jax.experimental import pallas as pl
from jax.experimental.pallas import tpu as pltpu
from jax.sharding import PartitionSpec as P

HEADS = 6
C = 192
WIN = 8
SHIFT = 4
NZ = 16
CELLS = WIN**3
HEAD = C // HEADS
SCALE = HEAD ** (-0.5)


def passed_along(block, axis, distance):
    devices = range(lax.axis_size(axis))
    route = [((i - distance) % len(devices), i) for i in devices]
    return lax.ppermute(block, axis, route)


def to_windows_cm(values):
    extent_a, extent_b, extent_c, ch = values.shape
    shaped = values.reshape(extent_a // WIN, WIN, extent_b // WIN, WIN, extent_c // WIN, WIN, ch)
    return shaped.transpose(0, 2, 4, 6, 1, 3, 5).reshape(-1, ch, CELLS)


def from_windows_cm(values, extent_a, extent_b, extent_c):
    ch = values.shape[1]
    shaped = values.reshape(extent_a // WIN, extent_b // WIN, extent_c // WIN, ch, WIN, WIN, WIN)
    return shaped.transpose(0, 4, 1, 5, 2, 6, 3).reshape(extent_a, extent_b, extent_c, ch)


def to_windows_key(values):
    extent_a, extent_b, extent_c = values.shape
    shaped = values.reshape(extent_a // WIN, WIN, extent_b // WIN, WIN, extent_c // WIN, WIN)
    return shaped.transpose(0, 2, 4, 1, 3, 5).reshape(-1, CELLS)


def window_kernel(xt_ref, gt_ref, kcol_ref, krow_ref, gain_ref, wqkvT_ref, wqkv_ref, wp_ref,
                  gs_ref, gqkvT_ref, gproj_ref, ggain_ref, qkv_s, ga_s, drow_s):
    f32 = jnp.float32
    bf16 = jnp.bfloat16
    w = pl.program_id(0)

    @pl.when(w == 0)
    def _():
        gqkvT_ref[...] = jnp.zeros_like(gqkvT_ref)
        gproj_ref[...] = jnp.zeros_like(gproj_ref)
        ggain_ref[...] = jnp.zeros_like(ggain_ref)

    gain = gain_ref[...]
    x = xt_ref[0].astype(f32)
    row_mean = jnp.mean(x, axis=0, keepdims=True)
    centred = x - row_mean
    inv_std = lax.rsqrt(jnp.mean(centred * centred, axis=0, keepdims=True) + 1e-05)
    x_hat = centred * inv_std
    normed = (x_hat * gain).astype(bf16)
    qkv_t = jnp.dot(wqkvT_ref[...], normed, preferred_element_type=f32)
    qkv_s[...] = qkv_t.astype(bf16).astype(f32)
    g = gt_ref[0]
    ga_t = jnp.dot(wp_ref[...], g, preferred_element_type=f32)
    ga_s[...] = ga_t.astype(bf16).astype(f32)
    allowed = kcol_ref[0] == krow_ref[0]
    nt = (((1,), (1,)), ((), ()))

    def head_step(h, carry):
        qo = pl.multiple_of(h * HEAD, HEAD)
        q_t = qkv_s[pl.ds(qo, HEAD), :]
        k_t = qkv_s[pl.ds(qo + C, HEAD), :]
        v_t = qkv_s[pl.ds(qo + 2 * C, HEAD), :]
        ga_th = ga_s[pl.ds(qo, HEAD), :]
        q = q_t.T.astype(bf16)
        scores = jnp.dot(q, k_t.astype(bf16), preferred_element_type=f32) * SCALE
        weights = jnp.where(allowed, jnp.exp(scores), 0.0)
        probs = weights / jnp.sum(weights, axis=1, keepdims=True)
        probs_bf = probs.astype(bf16)
        att_t = lax.dot_general(v_t.astype(bf16), probs_bf, nt, preferred_element_type=f32)
        att_t = att_t.astype(bf16)
        gproj_ref[pl.ds(qo, HEAD), :] += lax.dot_general(att_t, g, nt, preferred_element_type=f32)
        ga = ga_th.T.astype(bf16)
        grad_probs = jnp.dot(ga, v_t.astype(bf16), preferred_element_type=f32)
        dv_t = jnp.dot(ga_th.astype(bf16), probs_bf, preferred_element_type=f32)
        row_total = jnp.sum(probs * grad_probs, axis=1, keepdims=True)
        grad_scores = (probs * (grad_probs - row_total) * SCALE).astype(bf16)
        dq_t = lax.dot_general(k_t.astype(bf16), grad_scores, nt, preferred_element_type=f32)
        dk_t = jnp.dot(q_t.astype(bf16), grad_scores, preferred_element_type=f32)
        drow_s[pl.ds(qo, HEAD), :] = dq_t.astype(bf16).astype(f32)
        drow_s[pl.ds(qo + C, HEAD), :] = dk_t.astype(bf16).astype(f32)
        drow_s[pl.ds(qo + 2 * C, HEAD), :] = dv_t.astype(bf16).astype(f32)
        return carry

    lax.fori_loop(0, HEADS, head_step, 0)
    rows_t = drow_s[...].astype(bf16)
    gqkvT_ref[...] += lax.dot_general(rows_t, normed, nt, preferred_element_type=f32)
    grad_normed = jnp.dot(wqkv_ref[...], rows_t, preferred_element_type=f32)
    ggain_ref[...] += jnp.sum(grad_normed * x_hat, axis=1, keepdims=True)
    scaled = grad_normed * gain
    grad_shifted = inv_std * (
        scaled
        - jnp.mean(scaled, axis=0, keepdims=True)
        - x_hat * jnp.mean(scaled * x_hat, axis=0, keepdims=True)
    )
    gs_ref[0] = grad_shifted.astype(bf16)


def window_grads(xt, gt, kcol, krow, gain_col, wqkv_t, wqkv, wp):
    n_win = xt.shape[0]
    win_spec = pl.BlockSpec((1, C, CELLS), lambda w: (w, 0, 0))
    full = lambda shape: pl.BlockSpec(shape, lambda w: (0,) * len(shape))
    return pl.pallas_call(
        window_kernel,
        grid=(n_win,),
        in_specs=[
            win_spec,
            win_spec,
            pl.BlockSpec((1, CELLS, 1), lambda w: (w, 0, 0)),
            pl.BlockSpec((1, 1, CELLS), lambda w: (w, 0, 0)),
            full((C, 1)),
            full((3 * C, C)),
            full((C, 3 * C)),
            full((C, C)),
        ],
        out_specs=[
            win_spec,
            full((3 * C, C)),
            full((C, C)),
            full((C, 1)),
        ],
        out_shape=[
            jax.ShapeDtypeStruct((n_win, C, CELLS), jnp.bfloat16),
            jax.ShapeDtypeStruct((3 * C, C), jnp.float32),
            jax.ShapeDtypeStruct((C, C), jnp.float32),
            jax.ShapeDtypeStruct((C, 1), jnp.float32),
        ],
        scratch_shapes=[
            pltpu.VMEM((3 * C, CELLS), jnp.float32),
            pltpu.VMEM((C, CELLS), jnp.float32),
            pltpu.VMEM((3 * C, CELLS), jnp.float32),
        ],
        compiler_params=pltpu.CompilerParams(dimension_semantics=("arbitrary",)),
    )(xt, gt, kcol, krow, gain_col, wqkv_t, wqkv, wp)


def ahead_first(both_arrays):
    arrived = passed_along((both_arrays[0][:SHIFT], both_arrays[1][:SHIFT]), "gx", -1)
    return (
        jnp.concatenate([both_arrays[0][SHIFT:], arrived[0]], axis=0),
        jnp.concatenate([both_arrays[1][SHIFT:], arrived[1]], axis=0),
    )


def ahead_second(both_arrays):
    arrived = passed_along((both_arrays[0][:, :SHIFT], both_arrays[1][:, :SHIFT]), ("gy", "gz"), -1)
    return (
        jnp.concatenate([both_arrays[0][:, SHIFT:], arrived[0]], axis=1),
        jnp.concatenate([both_arrays[1][:, SHIFT:], arrived[1]], axis=1),
    )


def back_first(gradient):
    arrived = passed_along(gradient[-SHIFT:], "gx", 1)
    return jnp.concatenate([arrived, gradient[:-SHIFT]], axis=0)


def back_second(gradient):
    arrived = passed_along(gradient[:, -SHIFT:], ("gy", "gz"), 1)
    return jnp.concatenate([arrived, gradient[:, :-SHIFT]], axis=1)


def per_device(tokens, grads_out, labels, ln_gain, qkv_weight, proj_weight):
    brick_a, brick_b = (tokens.shape[0], tokens.shape[1])
    brick_c = NZ
    channels = C
    both_arrays = (tokens, grads_out)
    both_arrays = ahead_second(ahead_first(both_arrays))
    shifted_tokens = jnp.roll(
        both_arrays[0].reshape(brick_a, brick_b, brick_c, channels), -SHIFT, axis=2
    )
    shifted_grads = jnp.roll(
        both_arrays[1].reshape(brick_a, brick_b, brick_c, channels), -SHIFT, axis=2
    )
    extent_a = brick_a * lax.axis_size("gx")
    extent_b = brick_b * lax.axis_size(("gy", "gz"))
    first_index = lax.axis_index("gx") * brick_a + jnp.arange(brick_a, dtype=jnp.int32)
    second_index = lax.axis_index(("gy", "gz")) * brick_b + jnp.arange(brick_b, dtype=jnp.int32)
    wrap_first = (first_index >= extent_a - SHIFT).astype(jnp.int32)
    wrap_second = (second_index >= extent_b - SHIFT).astype(jnp.int32)
    wrap_third = (jnp.arange(brick_c, dtype=jnp.int32) >= brick_c - SHIFT).astype(jnp.int32)
    region = (
        wrap_first[:, None, None] * 4 + wrap_second[None, :, None] * 2 + wrap_third[None, None, :]
    )
    mask_key = to_windows_key(labels * 8 + region)

    grad_windows, qkv_grad_t, proj_grad, gain_grad = window_grads(
        to_windows_cm(shifted_tokens),
        to_windows_cm(shifted_grads),
        mask_key[:, :, None],
        mask_key[:, None, :],
        ln_gain.reshape(channels, 1),
        qkv_weight.T,
        qkv_weight,
        proj_weight,
    )
    qkv_grad_t, proj_grad, gain_grad = lax.psum(
        (qkv_grad_t, proj_grad, gain_grad), ("gx", "gy", "gz")
    )
    qkv_grad = qkv_grad_t.T
    grad_branch = jnp.roll(from_windows_cm(grad_windows, brick_a, brick_b, brick_c), SHIFT, axis=2)
    grad_branch = grad_branch.reshape(brick_a, brick_b, brick_c * channels)
    grad_branch = back_first(back_second(grad_branch))
    grad_tokens = (grads_out.astype(jnp.float32) + grad_branch.astype(jnp.float32)).astype(
        jnp.bfloat16
    )
    return (grad_tokens, gain_grad.reshape(-1), qkv_grad.reshape(-1), proj_grad.reshape(-1))


def solution(mesh):
    return jax.shard_map(
        per_device,
        mesh=mesh,
        in_specs=(
            P("gx", ("gy", "gz"), None),
            P("gx", ("gy", "gz"), None),
            P("gx", ("gy", "gz"), None),
            P(),
            P(),
            P(),
        ),
        out_specs=(P("gx", ("gy", "gz"), None), P(), P(), P()),
        check_vma=False,
    )
```

time: 587 us -> 319 us (0.54)
  matrix products: 347 us -> 0 us
  Pallas kernels: 0 us -> 75.6 us
  other arithmetic: 21.2 us -> 13.8 us
  waiting for transfers between devices: 98.7 us -> 105 us
  starting transfers between devices: 6.98 us -> 13.2 us
    dot_general x88 -> x0, matrix products: 347 us -> none  [the longest x8 87.2 us: window_grads(): jnp.einsum('hij,jhd->ihd', grad_scores, keys_all, preferred_element_type=...]
    pallas_call x0 -> x1, Pallas kernels: none -> 75.6 us  [window_grads(): pl.pallas_call(window_kernel, grid=(n_win,), in_specs=[win_spec, win_spec...]
    dynamic_update_slice x8 -> x0, other arithmetic: 6.53 us -> none  [per_device(): lax.scan(window_step, zero_sums, (to_windows(shifted_tokens), to_windows(...]
    ppermute x6, starting transfers between devices: 6.94 us -> 13.1 us  [passed_along(): return lax.ppermute(block, axis, route)]
    reshape x5 -> x7, local copies, waits for them, and re-layouts: 3.15 us -> 9.32 us  [the longest x2 4.53 us: to_windows_cm(): return shaped.transpose(0, 2, 4, 6, 1, 3, 5).reshape(-1, ch, CELLS)]
  transfers between devices with their start and end apart: 7 -> 7, of which waited for: 4 -> 4; matrix products, arithmetic and copies ran while one was open for 4% -> 9% of each run, Pallas kernels for 0% -> 0%
where the time goes in v1:
time: 319 us; the launch traced here: 318 us
  waiting for transfers between devices  105 us (33%)
  Pallas kernels  75.6 us (24%)
  local copies, waits for them, and re-layouts  51 us (16%)
  blocking collectives  44.7 us (14%)
  between operations  14.3 us (4%)
  other arithmetic  13.8 us (4%)
  starting transfers between devices  13.2 us (4%)
    psum x1, waiting for transfers between devices, per_device(): lax.psum((qkv_grad_t, proj_grad, gain_grad), ('gx', 'gy', 'gz'))  85.9 us
    pallas_call x1, Pallas kernels, window_grads(): pl.pallas_call(window_kernel, grid=(n_win,), in_specs=[win_spec, win_spec...  75.6 us
    psum x1, blocking collectives, per_device(): lax.psum((qkv_grad_t, proj_grad, gain_grad), ('gx', 'gy', 'gz'))  44.7 us
    ppermute x6, waiting for transfers between devices, passed_along(): return lax.ppermute(block, axis, route)  19 us
    ppermute x6, starting transfers between devices, passed_along(): return lax.ppermute(block, axis, route)  13.1 us
    unnamed x17, local copies, waits for them, and re-layouts  6.52 us
  transfers between devices with their start and end apart: 7, of which 4 were waited for; matrix products, arithmetic and copies ran while one was open for 9% of the time, Pallas kernels for 0%

profile of v1, /device:TPU:5, one launch (start us, length us, event | category | flops | bytes accessed | tf_op | source)
XLA Modules:
  0.0 317.6 jit_solution(16222954235095701341)
XLA Ops:
  7.2 1.8 slice.65
  9.0 3.3 %collective-permute-start.2 = (bf16[4,16,3072]{2,1,0:T(8,128)(2,1)}, bf16[4,16,3072]{2,1,0:T(8,128)(2,1)S(1)}, u32[]{:S(2)}, u32[]{:S(2)}) collective-permute-start(bf16[4,16,3072]{2,1,0:T(8,128)(2,1)} %slice.65), channel_id=1, source_target_pairs={{8,0},{16,8},{24,16},{0,24},{9,1},{17,9},{25,17},{1,25},{10,2},{18... | collective-permute-start | bytes 1179656 | tf_op jit(solution)/shard_map/ppermute | solution.py:21
  12.3 1.8 slice.59
  14.3 0.9 copy-done.4
  15.6 0.8 broadcast_in_dim_reshape.7.krow_ref
  16.3 1.9 broadcast_in_dim_reshape.8.kcol_ref
  18.3 0.8 copy.53.gain_ref
  19.0 0.9 copy.49
  19.9 0.7 copy.57
  20.6 0.7 copy.58
  21.3 7.5 %collective-permute-done = bf16[4,16,3072]{2,1,0:T(8,128)(2,1)} collective-permute-done((bf16[4,16,3072]{2,1,0:T(8,128)(2,1)}, bf16[4,16,3072]{2,1,0:T(8,128)(2,1)}, u32[]{:S(2)}, u32[]{:S(2)}) %collective-permute-start) | collective-permute-done | bytes 393248 | tf_op jit(solution)/shard_map/ppermute | solution.py:21
  28.8 1.3 copy.41
  30.2 0.3 collective-permute-start.1
  30.5 0.3 fusion.2
  30.8 0.3 copy.45
  31.1 0.8 pad_maximum_fusion.7
  32.0 2.7 collective-permute-start.3
  34.7 0.3 fusion.1
  35.0 3.5 %collective-permute-done.1 = bf16[16,4,3072]{2,0,1:T(8,128)(2,1)S(1)} collective-permute-done((bf16[16,4,3072]{2,0,1:T(8,128)(2,1)S(1)}, bf16[16,4,3072]{2,0,1:T(8,128)(2,1)S(1)}, u32[]{:S(2)}, u32[]{:S(2)}) %collective-permute-start.1) | collective-permute-done | bytes 393248 | tf_op jit(solution)/shard_map/ppermute | solution.py:21
  38.6 2.0 copy.42
  40.6 3.7 %reshape.101 = bf16[16,16,16,192]{3,2,1,0:T(8,128)(2,1)S(1)} reshape(bf16[16,16,3072]{2,1,0:T(8,128)(2,1)} %copy.42) | data formatting | bytes 3145728 | tf_op jit(solution)/shard_map/reshape | solution.py:180
  44.4 1.0 slice.79
  45.4 2.4 slice.78
  47.7 1.1 pad_maximum_fusion.5
  48.9 2.0 copy.46
  50.9 3.7 %reshape.104 = bf16[16,16,16,192]{3,2,1,0:T(8,128)(2,1)S(1)} reshape(bf16[16,16,3072]{2,1,0:T(8,128)(2,1)} %copy.46) | data formatting | bytes 3145728 | tf_op jit(solution)/shard_map/reshape | solution.py:183
  54.8 2.4 slice.82
  57.2 1.2 pad_maximum_fusion
  58.7 2.3 copy.50.xt_ref
  61.0 2.5 pad_maximum_fusion.1
  63.8 2.3 copy.51.gt_ref
  66.1 75.6 %shard_map.93 = (bf16[8,192,512]{2,1,0:T(8,128)(2,1)}, f32[576,192]{1,0:T(8,128)}, f32[192,192]{1,0:T(8,128)}, f32[192,1]{1,0:T(8,128)}) custom-call(bf16[8,192,512]{2,1,0:T(8,128)(2,1)} %copy.50.xt_ref, bf16[8,192,512]{2,1,0:T(8,128)(2,1)} %copy.51.gt_ref, s32[8,512,1]{2,1,0:T(8,128)} %broadcast_in_dim_reshape.8.kcol_ref, ...), custom_call_target="tpu_custom_call" | custom-call | tf_op jit(solution)/shard_map/pallas_call | solution.py:113
  141.7 3.0 copy.54
  144.9 0.3 slice.84
  145.2 2.4 pad_maximum_fusion.2
  147.5 3.7 %reshape.111 = bf16[16,16,3072]{2,1,0:T(8,128)(2,1)S(1)} reshape(bf16[16,16,16,192]{3,2,1,0:T(8,128)(2,1)} %pad_maximum_fusion.2) | data formatting | bytes 3145728 | tf_op jit(solution)/shard_map/reshape | solution.py:212
  151.4 6.5 %collective-permute-start.4 = (bf16[16,4,3072]{2,1,0:T(4,128)(2,1)S(1)}, bf16[16,4,3072]{2,1,0:T(4,128)(2,1)S(1)}, u32[]{:S(2)}, u32[]{:S(2)}) collective-permute-start(bf16[16,4,3072]{2,1,0:T(4,128)(2,1)S(1)} %slice.86), channel_id=1, source_target_pairs={{7,0},{0,1},{1,2},{2,3},{3,4},{4,5},{5,6},{6,7},{15,8},{8,9},{9,10... | collective-permute-start | bytes 1179656 | tf_op jit(solution)/shard_map/ppermute | solution.py:21
  157.9 8.0 %collective-permute-done.4 = bf16[16,4,3072]{2,1,0:T(4,128)(2,1)S(1)} collective-permute-done((bf16[16,4,3072]{2,1,0:T(4,128)(2,1)S(1)}, bf16[16,4,3072]{2,1,0:T(4,128)(2,1)S(1)}, u32[]{:S(2)}, u32[]{:S(2)}) %collective-permute-start.4) | collective-permute-done | bytes 393248 | tf_op jit(solution)/shard_map/ppermute | solution.py:21
  165.9 0.9 pad_maximum_fusion.6
  167.0 1.8 reshape.114
  168.8 2.1 copy.56
  170.8 2.0 reshape.113
  172.8 1.0 reduce
  173.9 44.7 %psum.21 = f32[192]{0:T(256)} all-reduce(f32[192]{0:T(256)S(1)} %reduce), channel_id=1, replica_groups=mesh['gx'=4,'gy'=4,'gz'=2] {'gx','gy','gz'}, use_global_device_ids=true, to_apply=%region_0.1 | all-reduce | flops 192 | bytes 1536 | tf_op jit(solution)/shard_map/psum | solution.py:207
  218.6 2.9 add_convert_fusion
  221.5 85.9 %all-reduce.3.cloned.1.call-done = (f32[110592]{0:T(1024)}, f32[36864]{0:T(1024)}) async-done(((f32[110592]{0:T(1024)}, f32[36864]{0:T(1024)}), (f32[110592]{0:T(1024)}, f32[36864]{0:T(1024)})) %all-reduce.3.cloned.1.call-update) | async-done | bytes 589840 | tf_op jit(solution)/shard_map/psum | solution.py:207
  307.4 1.8 copy.63
  309.2 1.6 copy.64
  (35 shorter events, 2.2 us)
Async XLA Ops:
  7.2 300.2 %all-reduce.3.cloned.1.call-start = ((), (), s32[]{:S(2)}) async-start(), calls=%async_computation | async-start | bytes 1179648 | tf_op jit(solution)/shard_map/psum | solution.py:207
  9.0 21.8 %collective-permute-start.2 = (bf16[4,16,3072]{2,1,0:T(8,128)(2,1)}, bf16[4,16,3072]{2,1,0:T(8,128)(2,1)S(1)}, u32[]{:S(2)}, u32[]{:S(2)}) collective-permute-start(bf16[4,16,3072]{2,1,0:T(8,128)(2,1)} %slice.65), channel_id=1, source_target_pairs={{8,0},{16,8},{24,16},{0,24},{9,1},{17,9},{25,17},{1,25},{10,2},{18... | collective-permute-start | bytes 1179656 | tf_op jit(solution)/shard_map/ppermute | solution.py:21
  14.1 14.8 %collective-permute-start = (bf16[4,16,3072]{2,1,0:T(8,128)(2,1)}, bf16[4,16,3072]{2,1,0:T(8,128)(2,1)}, u32[]{:S(2)}, u32[]{:S(2)}) collective-permute-start(bf16[4,16,3072]{2,1,0:T(8,128)(2,1)} %slice.59), channel_id=1, source_target_pairs={{8,0},{16,8},{24,16},{0,24},{9,1},{17,9},{25,17},{1,25},{10,2},{18... | collective-permute-start | bytes 1179656 | tf_op jit(solution)/shard_map/ppermute | solution.py:21
  14.3 0.9 copy-start.4
  14.3 3.9 %copy-start.5 = (f32[192]{0:T(256)S(1)}, f32[192]{0:T(256)}, u32[]{:S(2)}) copy-start(f32[192]{0:T(256)} %param.9) | copy-start | bytes 2308
  14.3 4.7 %copy-start.3 = (bf16[192,576]{1,0:T(8,128)(2,1)S(1)}, bf16[192,576]{1,0:T(8,128)(2,1)}, u32[]{:S(2)}) copy-start(bf16[192,576]{1,0:T(8,128)(2,1)} %wqkv_ref.1) | copy-start | bytes 663556
  15.3 4.6 %slice-start.1 = ((bf16[16,16,3072]{2,1,0:T(8,128)(2,1)}), bf16[12,16,3072]{2,1,0:T(8,128)(2,1)S(1)}, s32[]{:S(2)}) async-start(bf16[16,16,3072]{2,1,0:T(8,128)(2,1)} %param.6), calls=%async_computation.2 | async-start | bytes 2359296 | tf_op jit(solution)/shard_map/slice | solution.py:150
  18.3 2.3 slice-start
  30.2 8.3 %collective-permute-start.1 = (bf16[16,4,3072]{2,0,1:T(8,128)(2,1)S(1)}, bf16[16,4,3072]{2,0,1:T(8,128)(2,1)S(1)}, u32[]{:S(2)}, u32[]{:S(2)}) collective-permute-start(bf16[16,4,3072]{2,0,1:T(8,128)(2,1)S(1)} %pad_maximum_fusion.8), channel_id=1, source_target_pairs={{1,0},{2,1},{3,2},{4,3},{5,4},{6,5},{7,6},{0,7},{9,8},{10,9},{11,1... | collective-permute-start | bytes 1179656 | tf_op jit(solution)/shard_map/ppermute | solution.py:21
  32.0 15.8 %collective-permute-start.3 = (bf16[16,4,3072]{2,0,1:T(8,128)(2,1)}, bf16[16,4,3072]{2,0,1:T(8,128)(2,1)}, u32[]{:S(2)}, u32[]{:S(2)}) collective-permute-start(bf16[16,4,3072]{2,0,1:T(8,128)(2,1)} %pad_maximum_fusion.7), channel_id=1, source_target_pairs={{1,0},{2,1},{3,2},{4,3},{5,4},{6,5},{7,6},{0,7},{9,8},{10,9},{11,1... | collective-permute-start | bytes 1179656 | tf_op jit(solution)/shard_map/ppermute | solution.py:21
  54.8 2.4 copy-start
  54.8 2.4 copy-start.2
  151.4 14.4 %collective-permute-start.4 = (bf16[16,4,3072]{2,1,0:T(4,128)(2,1)S(1)}, bf16[16,4,3072]{2,1,0:T(4,128)(2,1)S(1)}, u32[]{:S(2)}, u32[]{:S(2)}) collective-permute-start(bf16[16,4,3072]{2,1,0:T(4,128)(2,1)S(1)} %slice.86), channel_id=1, source_target_pairs={{7,0},{0,1},{1,2},{2,3},{3,4},{4,5},{5,6},{6,7},{15,8},{8,9},{9,10... | collective-permute-start | bytes 1179656 | tf_op jit(solution)/shard_map/ppermute | solution.py:21
  166.8 51.9 %copy-start.1 = (bf16[16,16,3072]{2,1,0:T(8,128)(2,1)S(1)}, bf16[16,16,3072]{2,1,0:T(8,128)(2,1)}, u32[]{:S(2)}) copy-start(bf16[16,16,3072]{2,1,0:T(8,128)(2,1)} %param.7) | copy-start | bytes 4718596
  166.8 51.9 %collective-permute-start.5 = (bf16[4,16,3072]{2,1,0:T(8,128)(2,1)}, bf16[4,16,3072]{2,1,0:T(8,128)(2,1)}, u32[]{:S(2)}, u32[]{:S(2)}) collective-permute-start(bf16[4,16,3072]{2,1,0:T(8,128)(2,1)} %pad_maximum_fusion.6), channel_id=1, source_target_pairs={{24,0},{0,8},{8,16},{16,24},{25,1},{1,9},{9,17},{17,25},{26,2},{2,... | collective-permute-start | bytes 1179656 | tf_op jit(solution)/shard_map/ppermute | solution.py:21
Sparse Core Ops, SparseCore 0:
  174.0 133.3 all-reduce.2

commit v2 on v1

--- a/solution.py
+++ b/solution.py
@@ -144,6 +144,49 @@
     )(xt, gt, kcol, krow, gain_col, wqkv_t, wqkv, wp)
 
 
+SUM_AXES = ("gy", "gx", "gz")
+
+
+def swapped(block, axis, distance):
+    return lax.ppermute(block, axis, [(i, i ^ distance) for i in range(lax.axis_size(axis))])
+
+
+def summed_everywhere(parts):
+    sizes = [lax.axis_size(axis) for axis in SUM_AXES]
+    if any(size & (size - 1) for size in sizes):
+        return lax.psum(parts, SUM_AXES)
+    flat = jnp.concatenate([part.reshape(-1) for part in parts])
+    total = flat.shape[0]
+    devices = 1
+    for size in sizes:
+        devices *= size
+    padded = -(-total // devices) * devices
+    values = jnp.pad(flat, (0, padded - total))
+    steps = []
+    for axis, size in zip(SUM_AXES, sizes):
+        distance = 1
+        while distance < size:
+            bit = (lax.axis_index(axis) // distance) % 2
+            half = values.shape[0] // 2
+            keep = lax.dynamic_slice_in_dim(values, bit * half, half)
+            send = lax.dynamic_slice_in_dim(values, (1 - bit) * half, half)
+            values = keep + swapped(send, axis, distance)
+            steps.append((axis, distance))
+            distance *= 2
+    for axis, distance in reversed(steps):
+        bit = (lax.axis_index(axis) // distance) % 2
+        other = swapped(values, axis, distance)
+        values = jnp.where(
+            bit == 0, jnp.concatenate([values, other]), jnp.concatenate([other, values])
+        )
+    out = []
+    start = 0
+    for part in parts:
+        out.append(values[start : start + part.size].reshape(part.shape))
+        start += part.size
+    return tuple(out)
+
+
 def ahead_first(both_arrays):
     arrived = passed_along((both_arrays[0][:SHIFT], both_arrays[1][:SHIFT]), "gx", -1)
     return (
@@ -204,9 +247,7 @@
         qkv_weight,
         proj_weight,
     )
-    qkv_grad_t, proj_grad, gain_grad = lax.psum(
-        (qkv_grad_t, proj_grad, gain_grad), ("gx", "gy", "gz")
-    )
+    qkv_grad_t, proj_grad, gain_grad = summed_everywhere((qkv_grad_t, proj_grad, gain_grad))
     qkv_grad = qkv_grad_t.T
     grad_branch = jnp.roll(from_windows_cm(grad_windows, brick_a, brick_b, brick_c), SHIFT, axis=2)
     grad_branch = grad_branch.reshape(brick_a, brick_b, brick_c * channels)

time: 319 us -> 210 us (0.66)
  the two profiles are of different devices: /device:TPU:5 before, /device:TPU:1 now
where the time goes in v2:
time: 210 us; the launch traced here: 209 us
  Pallas kernels  75.6 us (36%)
  local copies, waits for them, and re-layouts  49.7 us (24%)
  waiting for transfers between devices  48.1 us (23%)
  starting transfers between devices  21.2 us (10%)
  other arithmetic  13.3 us (6%)
    pallas_call x1, Pallas kernels, window_grads(): pl.pallas_call(window_kernel, grid=(n_win,), in_specs=[win_spec, win_spec...  75.6 us
    ppermute x6, waiting for transfers between devices, passed_along(): return lax.ppermute(block, axis, route)  34.4 us
    ppermute x10, waiting for transfers between devices, swapped(): lax.ppermute(block, axis, [(i, i ^ distance) for i in range(lax.axis_size...  13.7 us
    ppermute x6, starting transfers between devices, passed_along(): return lax.ppermute(block, axis, route)  11 us
    ppermute x10, starting transfers between devices, swapped(): lax.ppermute(block, axis, [(i, i ^ distance) for i in range(lax.axis_size...  10.2 us
    reshape x2, local copies, waits for them, and re-layouts, to_windows_cm(): return shaped.transpose(0, 2, 4, 6, 1, 3, 5).reshape(-1, ch, CELLS)  4.51 us
  transfers between devices with their start and end apart: 16, of which 10 were waited for; matrix products, arithmetic and copies ran while one was open for 17% of the time, Pallas kernels for 0%

profile of v2, /device:TPU:1, one launch (start us, length us, event | category | flops | bytes accessed | tf_op | source)
XLA Modules:
  0.0 209.0 jit_solution(10573024756169595419)
XLA Ops:
  0.6 1.9 slice.72
  2.5 4.2 %collective-permute-start = (bf16[4,16,3072]{2,1,0:T(8,128)(2,1)}, bf16[4,16,3072]{2,1,0:T(8,128)(2,1)}, u32[]{:S(2)}, u32[]{:S(2)}) collective-permute-start(bf16[4,16,3072]{2,1,0:T(8,128)(2,1)} %slice.72), channel_id=1, source_target_pairs={{8,0},{16,8},{24,16},{0,24},{9,1},{17,9},{25,17},{1,25},{10,2},{18... | collective-permute-start | bytes 1179656 | tf_op jit(solution)/shard_map/ppermute | solution.py:21
  6.7 1.8 slice.78
  8.7 1.1 slice.77
  10.2 1.9 broadcast_in_dim_reshape.8.kcol_ref
  13.6 2.0 copy.58
  17.2 1.3 copy.41
  18.6 2.4 %collective-permute-start.1 = (bf16[16,4,3072]{2,0,1:T(8,128)(2,1)S(1)}, bf16[16,4,3072]{2,0,1:T(8,128)(2,1)S(1)}, u32[]{:S(2)}, u32[]{:S(2)}) collective-permute-start(bf16[16,4,3072]{2,0,1:T(8,128)(2,1)S(1)} %pad_maximum_fusion.9), channel_id=1, source_target_pairs={{1,0},{2,1},{3,2},{4,3},{5,4},{6,5},{7,6},{0,7},{9,8},{10,9},{11,1... | collective-permute-start | bytes 1179656 | tf_op jit(solution)/shard_map/ppermute | solution.py:21
  21.4 1.8 collective-permute-done.2
  23.2 1.3 copy.45
  25.4 2.7 %collective-permute-start.3 = (bf16[16,4,3072]{2,0,1:T(8,128)(2,1)}, bf16[16,4,3072]{2,0,1:T(8,128)(2,1)}, u32[]{:S(2)}, u32[]{:S(2)}) collective-permute-start(bf16[16,4,3072]{2,0,1:T(8,128)(2,1)} %pad_maximum_fusion.8), channel_id=1, source_target_pairs={{1,0},{2,1},{3,2},{4,3},{5,4},{6,5},{7,6},{0,7},{9,8},{10,9},{11,1... | collective-permute-start | bytes 1179656 | tf_op jit(solution)/shard_map/ppermute | solution.py:21
  28.3 5.9 %collective-permute-done.1 = bf16[16,4,3072]{2,0,1:T(8,128)(2,1)S(1)} collective-permute-done((bf16[16,4,3072]{2,0,1:T(8,128)(2,1)S(1)}, bf16[16,4,3072]{2,0,1:T(8,128)(2,1)S(1)}, u32[]{:S(2)}, u32[]{:S(2)}) %collective-permute-start.1) | collective-permute-done | bytes 393248 | tf_op jit(solution)/shard_map/ppermute | solution.py:21
  34.3 2.0 copy.42
  36.4 3.7 %reshape.111 = bf16[16,16,16,192]{3,2,1,0:T(8,128)(2,1)S(1)} reshape(bf16[16,16,3072]{2,1,0:T(8,128)(2,1)} %copy.42) | data formatting | bytes 3145728 | tf_op jit(solution)/shard_map/reshape | solution.py:223
  40.1 1.0 slice.96
  41.1 2.4 %slice.95 = bf16[16,16,12,192]{3,2,1,0:T(8,128)(2,1)} slice(bf16[16,16,16,192]{3,2,1,0:T(8,128)(2,1)S(1)} %reshape.111), slice={[0:16], [0:16], [4:16], [0:192]} | slice | bytes 2359296 | tf_op jit(solution)/shard_map/jit(_roll_static)/slice | solution.py:222
  43.4 1.1 pad_maximum_fusion.5
  44.6 2.0 copy.46
  46.6 3.7 %reshape.114 = bf16[16,16,16,192]{3,2,1,0:T(8,128)(2,1)S(1)} reshape(bf16[16,16,3072]{2,1,0:T(8,128)(2,1)} %copy.46) | data formatting | bytes 3145728 | tf_op jit(solution)/shard_map/reshape | solution.py:226
  50.5 2.4 %slice.99 = bf16[16,16,12,192]{3,2,1,0:T(8,128)(2,1)} slice(bf16[16,16,16,192]{3,2,1,0:T(8,128)(2,1)S(1)} %reshape.114), slice={[0:16], [0:16], [4:16], [0:192]} | slice | bytes 2359296 | tf_op jit(solution)/shard_map/jit(_roll_static)/slice | solution.py:225
  52.9 1.2 pad_maximum_fusion
  54.4 2.3 %copy.50.xt_ref = bf16[8,192,512]{2,1,0:T(8,128)(2,1)} copy(bf16[8,192,512]{1,2,0:T(8,128)(2,1)S(1)} %bitcast.30) | data formatting | bytes 3145728 | tf_op jit(solution)/shard_map/reshape | solution.py:27
  56.7 2.5 %pad_maximum_fusion.1 = bf16[16,16,16,192]{3,2,1,0:T(8,128)(2,1)S(1)} fusion(bf16[16,16,4,192]{3,2,1,0:T(4,128)(2,1)S(1)} %slice.100, bf16[16,16,12,192]{3,2,1,0:T(8,128)(2,1)} %slice.99), kind=kLoop, calls=%fused_computation.2 | loop fusion | flops 3145728 | bytes 3145728 | tf_op jit(solution)/shard_map/jit(_roll_static)/concatenate | solution.py:225
  59.5 2.3 %copy.51.gt_ref = bf16[8,192,512]{2,1,0:T(8,128)(2,1)} copy(bf16[8,192,512]{1,2,0:T(8,128)(2,1)S(1)} %bitcast.31) | data formatting | bytes 3145728 | tf_op jit(solution)/shard_map/reshape | solution.py:27
  61.7 75.6 %shard_map.93 = (bf16[8,192,512]{2,1,0:T(8,128)(2,1)}, f32[576,192]{1,0:T(8,128)}, f32[192,192]{1,0:T(8,128)}, f32[192,1]{1,0:T(8,128)}) custom-call(bf16[8,192,512]{2,1,0:T(8,128)(2,1)} %copy.50.xt_ref, bf16[8,192,512]{2,1,0:T(8,128)(2,1)} %copy.51.gt_ref, s32[8,512,1]{2,1,0:T(8,128)} %broadcast_in_dim_reshape.8.kcol_ref, ...), custom_call_target="tpu_custom_call" | custom-call | tf_op jit(solution)/shard_map/pallas_call | solution.py:113
  137.4 1.0 reshape.123
  138.4 1.4 reshape.122
  139.8 1.0 reduce
  141.1 1.5 collective-permute-done.6
  142.9 1.3 collective-permute-start.7
  144.2 4.2 %collective-permute-done.7 = f32[36912]{0:T(1024)S(1)} collective-permute-done((f32[36912]{0:T(1024)S(1)}, f32[36912]{0:T(1024)S(1)}, u32[]{:S(2)}, u32[]{:S(2)}) %collective-permute-start.7) | collective-permute-done | bytes 147680 | tf_op jit(solution)/shard_map/ppermute | solution.py:151
  148.6 1.4 collective-permute-start.8
  150.0 1.9 collective-permute-done.8
  152.2 3.7 %collective-permute-done.9 = f32[9228]{0:T(1024)S(1)} collective-permute-done((f32[9228]{0:T(1024)S(1)}, f32[9228]{0:T(1024)S(1)}, u32[]{:S(2)}, u32[]{:S(2)}) %collective-permute-start.9) | collective-permute-done | bytes 36944 | tf_op jit(solution)/shard_map/ppermute | solution.py:151
  156.1 2.0 collective-permute-start.10
  158.0 1.2 collective-permute-done.10
  159.3 1.8 collective-permute-start.11
  161.1 1.2 collective-permute-done.11
  162.3 1.6 collective-permute-start.12
  163.9 2.7 %copy.54 = bf16[8,192,512]{1,2,0:T(8,128)(2,1)S(1)} copy(bf16[8,192,512]{2,1,0:T(8,128)(2,1)} %get-tuple-element.8) | data formatting | bytes 3145728 | tf_op jit(solution)/shard_map/pallas_call | solution.py:113
  167.3 1.8 collective-permute-start.13
  169.1 2.4 %pad_maximum_fusion.2 = bf16[16,16,16,192]{3,2,1,0:T(8,128)(2,1)} fusion(bf16[16,16,12,192]{3,2,1,0:T(8,128)(2,1)S(1)} %bitcast.29, bf16[16,16,4,192]{3,2,1,0:T(4,128)(2,1)S(1)} %slice.101), kind=kLoop, calls=%fused_computation.3 | loop fusion | flops 3145728 | bytes 3145728 | tf_op jit(solution)/shard_map/jit(_roll_static)/concatenate | solution.py:252
  171.4 3.7 %reshape.121 = bf16[16,16,3072]{2,1,0:T(8,128)(2,1)S(1)} reshape(bf16[16,16,16,192]{3,2,1,0:T(8,128)(2,1)} %pad_maximum_fusion.2) | data formatting | bytes 3145728 | tf_op jit(solution)/shard_map/reshape | solution.py:253
  175.3 1.5 collective-permute-start.4
  177.2 15.3 %collective-permute-done.4 = bf16[16,4,3072]{2,1,0:T(4,128)(2,1)S(1)} collective-permute-done((bf16[16,4,3072]{2,1,0:T(4,128)(2,1)S(1)}, bf16[16,4,3072]{2,1,0:T(4,128)(2,1)S(1)}, u32[]{:S(2)}, u32[]{:S(2)}) %collective-permute-start.4) | collective-permute-done | bytes 393248 | tf_op jit(solution)/shard_map/ppermute | solution.py:21
  193.0 11.4 %collective-permute-done.5 = bf16[4,16,3072]{2,1,0:T(8,128)(2,1)S(1)} collective-permute-done((bf16[4,16,3072]{2,1,0:T(8,128)(2,1)S(1)}, bf16[4,16,3072]{2,1,0:T(8,128)(2,1)S(1)}, u32[]{:S(2)}, u32[]{:S(2)}) %collective-permute-start.5) | collective-permute-done | bytes 393248 | tf_op jit(solution)/shard_map/ppermute | solution.py:21
  204.3 1.8 add_convert_fusion
  208.1 1.0 reshape.125
  (71 shorter events, 10.8 us)
Async XLA Ops:
  0.6 8.1 %copy-start.1 = (bf16[16,16,3072]{2,1,0:T(8,128)(2,1)S(1)}, bf16[16,16,3072]{2,1,0:T(8,128)(2,1)}, u32[]{:S(2)}) copy-start(bf16[16,16,3072]{2,1,0:T(8,128)(2,1)} %param.7) | copy-start | bytes 4718596
  2.5 14.7 %collective-permute-start = (bf16[4,16,3072]{2,1,0:T(8,128)(2,1)}, bf16[4,16,3072]{2,1,0:T(8,128)(2,1)}, u32[]{:S(2)}, u32[]{:S(2)}) collective-permute-start(bf16[4,16,3072]{2,1,0:T(8,128)(2,1)} %slice.72), channel_id=1, source_target_pairs={{8,0},{16,8},{24,16},{0,24},{9,1},{17,9},{25,17},{1,25},{10,2},{18... | collective-permute-start | bytes 1179656 | tf_op jit(solution)/shard_map/ppermute | solution.py:21
  8.4 14.8 %collective-permute-start.2 = (bf16[4,16,3072]{2,1,0:T(8,128)(2,1)}, bf16[4,16,3072]{2,1,0:T(8,128)(2,1)}, u32[]{:S(2)}, u32[]{:S(2)}) collective-permute-start(bf16[4,16,3072]{2,1,0:T(8,128)(2,1)} %slice.78), channel_id=1, source_target_pairs={{8,0},{16,8},{24,16},{0,24},{9,1},{17,9},{25,17},{1,25},{10,2},{18... | collective-permute-start | bytes 1179656 | tf_op jit(solution)/shard_map/ppermute | solution.py:21
  8.7 1.1 copy-start.5
  9.8 3.0 %slice-start = ((bf16[16,16,3072]{2,1,0:T(8,128)(2,1)}), bf16[12,16,3072]{2,1,0:T(8,128)(2,1)S(1)}, s32[]{:S(2)}) async-start(bf16[16,16,3072]{2,1,0:T(8,128)(2,1)} %param.6), calls=%async_computation | async-start | bytes 2359296 | tf_op jit(solution)/shard_map/slice | solution.py:193
  12.9 2.7 %copy-start.6 = (f32[192]{0:T(256)S(1)}, f32[192]{0:T(256)}, u32[]{:S(2)}) copy-start(f32[192]{0:T(256)} %param.9) | copy-start | bytes 2308
  13.5 2.8 %copy-start.4 = (bf16[192,576]{1,0:T(8,128)(2,1)S(1)}, bf16[192,576]{1,0:T(8,128)(2,1)}, u32[]{:S(2)}) copy-start(bf16[192,576]{1,0:T(8,128)(2,1)} %wqkv_ref.1) | copy-start | bytes 663556
  18.6 15.6 %collective-permute-start.1 = (bf16[16,4,3072]{2,0,1:T(8,128)(2,1)S(1)}, bf16[16,4,3072]{2,0,1:T(8,128)(2,1)S(1)}, u32[]{:S(2)}, u32[]{:S(2)}) collective-permute-start(bf16[16,4,3072]{2,0,1:T(8,128)(2,1)S(1)} %pad_maximum_fusion.9), channel_id=1, source_target_pairs={{1,0},{2,1},{3,2},{4,3},{5,4},{6,5},{7,6},{0,7},{9,8},{10,9},{11,1... | collective-permute-start | bytes 1179656 | tf_op jit(solution)/shard_map/ppermute | solution.py:21
  25.4 18.1 %collective-permute-start.3 = (bf16[16,4,3072]{2,0,1:T(8,128)(2,1)}, bf16[16,4,3072]{2,0,1:T(8,128)(2,1)}, u32[]{:S(2)}, u32[]{:S(2)}) collective-permute-start(bf16[16,4,3072]{2,0,1:T(8,128)(2,1)} %pad_maximum_fusion.8), channel_id=1, source_target_pairs={{1,0},{2,1},{3,2},{4,3},{5,4},{6,5},{7,6},{0,7},{9,8},{10,9},{11,1... | collective-permute-start | bytes 1179656 | tf_op jit(solution)/shard_map/ppermute | solution.py:21
  50.5 2.4 %copy-start = (bf16[16,16,12,192]{3,2,1,0:T(8,128)(2,1)S(1)}, bf16[16,16,12,192]{3,2,1,0:T(8,128)(2,1)}, u32[]{:S(2)}) copy-start(bf16[16,16,12,192]{3,2,1,0:T(8,128)(2,1)} %slice.95) | copy-start | bytes 3538948
  50.5 2.4 %copy-start.3 = (bf16[16,16,4,192]{3,2,1,0:T(4,128)(2,1)S(1)}, bf16[16,16,4,192]{3,2,1,0:T(4,128)(2,1)}, u32[]{:S(2)}) copy-start(bf16[16,16,4,192]{3,2,1,0:T(4,128)(2,1)} %slice.96) | copy-start | bytes 1179652
  141.0 1.7 collective-permute-start.6
  142.9 5.5 %collective-permute-start.7 = (f32[36912]{0:T(1024)S(1)}, f32[36912]{0:T(1024)S(1)}, u32[]{:S(2)}, u32[]{:S(2)}) collective-permute-start(f32[36912]{0:T(1024)S(1)} %dynamic_slice.33), channel_id=1, source_target_pairs={{0,4},{2,6},{4,0},{6,2},{1,5},{3,7},{5,1},{7,3},{8,12},{10,14},{12... | collective-permute-start | bytes 442952 | tf_op jit(solution)/shard_map/ppermute | solution.py:151
  148.6 3.3 %collective-permute-start.8 = (f32[18456]{0:T(1024)S(1)}, f32[18456]{0:T(1024)S(1)}, u32[]{:S(2)}, u32[]{:S(2)}) collective-permute-start(f32[18456]{0:T(1024)S(1)} %dynamic_slice.35), channel_id=1, source_target_pairs={{0,8},{8,0},{16,24},{24,16},{1,9},{9,1},{17,25},{25,17},{2,10},{10... | collective-permute-start | bytes 221480 | tf_op jit(solution)/shard_map/ppermute | solution.py:151
  152.1 3.8 %collective-permute-start.9 = (f32[9228]{0:T(1024)S(1)}, f32[9228]{0:T(1024)S(1)}, u32[]{:S(2)}, u32[]{:S(2)}) collective-permute-start(f32[9228]{0:T(1024)S(1)} %dynamic_slice.37), channel_id=1, source_target_pairs={{0,16},{8,24},{16,0},{24,8},{1,17},{9,25},{17,1},{25,9},{2,18},{10... | collective-permute-start | bytes 110744 | tf_op jit(solution)/shard_map/ppermute | solution.py:151
  156.1 3.2 %collective-permute-start.10 = (f32[4614]{0:T(1024)S(1)}, f32[4614]{0:T(1024)S(1)}, u32[]{:S(2)}, u32[]{:S(2)}) collective-permute-start(f32[4614]{0:T(1024)S(1)} %dynamic_slice.39), channel_id=1, source_target_pairs={{0,1},{1,0},{2,3},{3,2},{4,5},{5,4},{6,7},{7,6},{8,9},{9,8},{10,11... | collective-permute-start | bytes 55376 | tf_op jit(solution)/shard_map/ppermute | solution.py:151
  159.3 2.9 %collective-permute-start.11 = (f32[4614]{0:T(1024)S(1)}, f32[4614]{0:T(1024)S(1)}, u32[]{:S(2)}, u32[]{:S(2)}) collective-permute-start(f32[4614]{0:T(1024)S(1)} %dynamic-slice_add_fusion.4), channel_id=1, source_target_pairs={{0,1},{1,0},{2,3},{3,2},{4,5},{5,4},{6,7},{7,6},{8,9},{9,8},{10,11... | collective-permute-start | bytes 55376 | tf_op jit(solution)/shard_map/ppermute | solution.py:151
  162.3 4.9 %collective-permute-start.12 = (f32[9228]{0:T(1024)S(1)}, f32[9228]{0:T(1024)S(1)}, u32[]{:S(2)}, u32[]{:S(2)}) collective-permute-start(f32[9228]{0:T(1024)S(1)} %maximum_select_fusion.4), channel_id=1, source_target_pairs={{0,16},{8,24},{16,0},{24,8},{1,17},{9,25},{17,1},{25,9},{2,18},{10... | collective-permute-start | bytes 110744 | tf_op jit(solution)/shard_map/ppermute | solution.py:151
  167.3 9.6 %collective-permute-start.13 = (f32[18456]{0:T(1024)S(1)}, f32[18456]{0:T(1024)S(1)}, u32[]{:S(2)}, u32[]{:S(2)}) collective-permute-start(f32[18456]{0:T(1024)S(1)} %maximum_select_fusion.3), channel_id=1, source_target_pairs={{0,8},{8,0},{16,24},{24,16},{1,9},{9,1},{17,25},{25,17},{2,10},{10... | collective-permute-start | bytes 221480 | tf_op jit(solution)/shard_map/ppermute | solution.py:151
  175.1 29.2 %copy-start.2 = (bf16[16,16,3072]{2,1,0:T(8,128)(2,1)S(1)}, bf16[16,16,3072]{2,1,0:T(8,128)(2,1)}, u32[]{:S(2)}) copy-start(bf16[16,16,3072]{2,1,0:T(8,128)(2,1)} %param.7) | copy-start | bytes 4718596
  175.3 17.1 %collective-permute-start.4 = (bf16[16,4,3072]{2,1,0:T(4,128)(2,1)S(1)}, bf16[16,4,3072]{2,1,0:T(4,128)(2,1)S(1)}, u32[]{:S(2)}, u32[]{:S(2)}) collective-permute-start(bf16[16,4,3072]{2,1,0:T(4,128)(2,1)S(1)} %slice.103), channel_id=1, source_target_pairs={{7,0},{0,1},{1,2},{2,3},{3,4},{4,5},{5,6},{6,7},{15,8},{8,9},{9,10... | collective-permute-start | bytes 1179656 | tf_op jit(solution)/shard_map/ppermute | solution.py:21
  177.0 15.7 %collective-permute-start.14 = (f32[36912]{0:T(1024)S(1)}, f32[36912]{0:T(1024)S(1)}, u32[]{:S(2)}, u32[]{:S(2)}) collective-permute-start(f32[36912]{0:T(1024)S(1)} %maximum_select_fusion.2), channel_id=1, source_target_pairs={{0,4},{2,6},{4,0},{6,2},{1,5},{3,7},{5,1},{7,3},{8,12},{10,14},{12... | collective-permute-start | bytes 442952 | tf_op jit(solution)/shard_map/ppermute | solution.py:151
  192.7 11.7 %collective-permute-start.5 = (bf16[4,16,3072]{2,1,0:T(8,128)(2,1)S(1)}, bf16[4,16,3072]{2,1,0:T(8,128)(2,1)S(1)}, u32[]{:S(2)}, u32[]{:S(2)}) collective-permute-start(bf16[4,16,3072]{2,1,0:T(8,128)(2,1)S(1)} %pad_maximum_fusion.7), channel_id=1, source_target_pairs={{24,0},{0,8},{8,16},{16,24},{25,1},{1,9},{9,17},{17,25},{26,2},{2,... | collective-permute-start | bytes 1179656 | tf_op jit(solution)/shard_map/ppermute | solution.py:21
  192.9 13.3 %collective-permute-start.15 = (f32[73824]{0:T(1024)S(1)}, f32[73824]{0:T(1024)S(1)}, u32[]{:S(2)}, u32[]{:S(2)}) collective-permute-start(f32[73824]{0:T(1024)S(1)} %maximum_select_fusion.1), channel_id=1, source_target_pairs={{0,2},{2,0},{4,6},{6,4},{1,3},{3,1},{5,7},{7,5},{8,10},{10,8},{12,... | collective-permute-start | bytes 885896 | tf_op jit(solution)/shard_map/ppermute | solution.py:151

commit v3 on v2

--- a/solution.py
+++ b/solution.py
@@ -187,44 +187,46 @@
     return tuple(out)
 
 
-def ahead_first(both_arrays):
-    arrived = passed_along((both_arrays[0][:SHIFT], both_arrays[1][:SHIFT]), "gx", -1)
-    return (
-        jnp.concatenate([both_arrays[0][SHIFT:], arrived[0]], axis=0),
-        jnp.concatenate([both_arrays[1][SHIFT:], arrived[1]], axis=0),
-    )
-
-
-def ahead_second(both_arrays):
-    arrived = passed_along((both_arrays[0][:, :SHIFT], both_arrays[1][:, :SHIFT]), ("gy", "gz"), -1)
-    return (
-        jnp.concatenate([both_arrays[0][:, SHIFT:], arrived[0]], axis=1),
-        jnp.concatenate([both_arrays[1][:, SHIFT:], arrived[1]], axis=1),
-    )
-
-
-def back_first(gradient):
-    arrived = passed_along(gradient[-SHIFT:], "gx", 1)
-    return jnp.concatenate([arrived, gradient[:-SHIFT]], axis=0)
-
-
-def back_second(gradient):
-    arrived = passed_along(gradient[:, -SHIFT:], ("gy", "gz"), 1)
-    return jnp.concatenate([arrived, gradient[:, :-SHIFT]], axis=1)
+def halo_route(distance_a, distance_b):
+    size_a = lax.axis_size("gx")
+    size_b = lax.axis_size(("gy", "gz"))
+    route = []
+    for ia in range(size_a):
+        for ib in range(size_b):
+            target = ((ia + distance_a) % size_a) * size_b + (ib + distance_b) % size_b
+            route.append((ia * size_b + ib, target))
+    return route
+
+
+def moved(block, distance_a, distance_b):
+    return lax.ppermute(block, ("gx", "gy", "gz"), halo_route(distance_a, distance_b))
+
+
+def shifted_block(both):
+    from_a = moved(both[:, :SHIFT, SHIFT:], -1, 0)
+    from_b = moved(both[:, SHIFT:, :SHIFT], 0, -1)
+    from_ab = moved(both[:, :SHIFT, :SHIFT], -1, -1)
+    upper = jnp.concatenate([both[:, SHIFT:, SHIFT:], from_b], axis=2)
+    lower = jnp.concatenate([from_a, from_ab], axis=2)
+    return jnp.concatenate([upper, lower], axis=1)
+
+
+def unshifted_sum(grads_out, grad_shifted):
+    to_a = moved(grad_shifted[-SHIFT:, :-SHIFT], 1, 0)
+    to_b = moved(grad_shifted[:-SHIFT, -SHIFT:], 0, 1)
+    to_ab = moved(grad_shifted[-SHIFT:, -SHIFT:], 1, 1)
+    upper = jnp.concatenate([to_ab, to_a], axis=1)
+    lower = jnp.concatenate([to_b, grad_shifted[:-SHIFT, :-SHIFT]], axis=1)
+    branch = jnp.concatenate([upper, lower], axis=0)
+    return (grads_out.astype(jnp.float32) + branch.astype(jnp.float32)).astype(jnp.bfloat16)
 
 
 def per_device(tokens, grads_out, labels, ln_gain, qkv_weight, proj_weight):
     brick_a, brick_b = (tokens.shape[0], tokens.shape[1])
     brick_c = NZ
     channels = C
-    both_arrays = (tokens, grads_out)
-    both_arrays = ahead_second(ahead_first(both_arrays))
-    shifted_tokens = jnp.roll(
-        both_arrays[0].reshape(brick_a, brick_b, brick_c, channels), -SHIFT, axis=2
-    )
-    shifted_grads = jnp.roll(
-        both_arrays[1].reshape(brick_a, brick_b, brick_c, channels), -SHIFT, axis=2
-    )
+    both = shifted_block(jnp.stack([tokens, grads_out]))
+    both = jnp.roll(both.reshape(2, brick_a, brick_b, brick_c, channels), -SHIFT, axis=3)
     extent_a = brick_a * lax.axis_size("gx")
     extent_b = brick_b * lax.axis_size(("gy", "gz"))
     first_index = lax.axis_index("gx") * brick_a + jnp.arange(brick_a, dtype=jnp.int32)
@@ -238,8 +240,8 @@
     mask_key = to_windows_key(labels * 8 + region)
 
     grad_windows, qkv_grad_t, proj_grad, gain_grad = window_grads(
-        to_windows_cm(shifted_tokens),
-        to_windows_cm(shifted_grads),
+        to_windows_cm(both[0]),
+        to_windows_cm(both[1]),
         mask_key[:, :, None],
         mask_key[:, None, :],
         ln_gain.reshape(channels, 1),
@@ -251,10 +253,7 @@
     qkv_grad = qkv_grad_t.T
     grad_branch = jnp.roll(from_windows_cm(grad_windows, brick_a, brick_b, brick_c), SHIFT, axis=2)
     grad_branch = grad_branch.reshape(brick_a, brick_b, brick_c * channels)
-    grad_branch = back_first(back_second(grad_branch))
-    grad_tokens = (grads_out.astype(jnp.float32) + grad_branch.astype(jnp.float32)).astype(
-        jnp.bfloat16
-    )
+    grad_tokens = unshifted_sum(grads_out, grad_branch)
     return (grad_tokens, gain_grad.reshape(-1), qkv_grad.reshape(-1), proj_grad.reshape(-1))
 
 

time: 210 us -> 208 us (level)
  waiting for transfers between devices: 48.1 us -> 36.1 us
  other arithmetic: 13.3 us -> 20.5 us
  starting transfers between devices: 21.2 us -> 24.9 us
    ppermute x6, waiting for transfers between devices: 34.4 us -> 17.9 us  [moved(): lax.ppermute(block, ('gx', 'gy', 'gz'), halo_route(distance_a, distance_b))]
    ppermute x6, starting transfers between devices: 11 us -> 16.8 us  [moved(): lax.ppermute(block, ('gx', 'gy', 'gz'), halo_route(distance_a, distance_b))]
    another operation x0 -> x4, other arithmetic: none -> 4.86 us  [per_device(): both = shifted_block(jnp.stack([tokens, grads_out]))]
    ppermute x10, waiting for transfers between devices: 13.7 us -> 18.2 us  [swapped(): lax.ppermute(block, axis, [(i, i ^ distance) for i in range(lax.axis_size...]
    transpose x2, local copies, waits for them, and re-layouts: 0.53 us -> 4.75 us  [to_windows_cm(): return shaped.transpose(0, 2, 4, 6, 1, 3, 5).reshape(-1, ch, CELLS)]
    concatenate x2 -> x0, local copies, waits for them, and re-layouts: 4.01 us -> none  [the longest x1 2.01 us: ahead_second(): jnp.concatenate([both_arrays[0][:, SHIFT:], arrived[0]], axis=1)]
    reshape x2, local copies, waits for them, and re-layouts: 4.51 us -> 7.69 us  [to_windows_cm(): return shaped.transpose(0, 2, 4, 6, 1, 3, 5).reshape(-1, ch, CELLS)]
    slice x10 -> x7, local copies, waits for them, and re-layouts: 10.9 us -> 8.04 us  [the longest x2 6.45 us: per_device(): jnp.roll(both.reshape(2, brick_a, brick_b, brick_c, channels), -SHIFT, ax...]
  transfers between devices with their start and end apart: 16 -> 16, of which waited for: 10 -> 12; matrix products, arithmetic and copies ran while one was open for 17% -> 11% of each run, Pallas kernels for 0% -> 0%
where the time goes in v3:
time: 208 us
  Pallas kernels  75.6 us (36%)
  local copies, waits for them, and re-layouts  49.4 us (24%)
  waiting for transfers between devices  36.1 us (17%)
  starting transfers between devices  24.9 us (12%)
  other arithmetic  20.5 us (10%)
    pallas_call x1, Pallas kernels, window_grads(): pl.pallas_call(window_kernel, grid=(n_win,), in_specs=[win_spec, win_spec...  75.6 us
    ppermute x10, waiting for transfers between devices, swapped(): lax.ppermute(block, axis, [(i, i ^ distance) for i in range(lax.axis_size...  18.2 us
    ppermute x6, waiting for transfers between devices, moved(): lax.ppermute(block, ('gx', 'gy', 'gz'), halo_route(distance_a, distance_b))  17.9 us
    ppermute x6, starting transfers between devices, moved(): lax.ppermute(block, ('gx', 'gy', 'gz'), halo_route(distance_a, distance_b))  16.8 us
    ppermute x10, starting transfers between devices, swapped(): lax.ppermute(block, axis, [(i, i ^ distance) for i in range(lax.axis_size...  8.1 us
    reshape x1, local copies, waits for them, and re-layouts, per_device(): both.reshape(2, brick_a, brick_b, brick_c, channels)  8.01 us
    reshape x2, local copies, waits for them, and re-layouts, to_windows_cm(): return shaped.transpose(0, 2, 4, 6, 1, 3, 5).reshape(-1, ch, CELLS)  7.69 us
    slice x2, local copies, waits for them, and re-layouts, per_device(): jnp.roll(both.reshape(2, brick_a, brick_b, brick_c, channels), -SHIFT, ax...  6.45 us
  transfers between devices with their start and end apart: 16, of which 12 were waited for; matrix products, arithmetic and copies ran while one was open for 11% of the time, Pallas kernels for 0%

profile of v3, /device:TPU:1, one launch (start us, length us, event | category | flops | bytes accessed | tf_op | source)
XLA Modules:
  0.0 207.6 jit_solution(9404337535540410480)
XLA Ops:
  0.7 1.5 fusion.2
  2.2 1.3 copy.37
  3.5 4.2 %collective-permute-start.1 = (bf16[2,4,12,3072]{3,1,2,0:T(4,128)(2,1)}, bf16[2,4,12,3072]{3,1,2,0:T(4,128)(2,1)}, u32[]{:S(2)}, u32[]{:S(2)}) collective-permute-start(bf16[2,4,12,3072]{3,1,2,0:T(4,128)(2,1)} %copy.37), channel_id=1, source_target_pairs={{0,24},{1,25},{2,26},{3,27},{4,28},{5,29},{6,30},{7,31},{8,0},{9,1... | collective-permute-start | bytes 1769480 | tf_op jit(solution)/shard_map/ppermute | solution.py:202
  7.6 1.0 fusion.3
  8.6 2.1 %collective-permute-start = (bf16[2,12,4,3072]{3,2,1,0:T(4,128)(2,1)}, bf16[2,12,4,3072]{3,2,1,0:T(4,128)(2,1)}, u32[]{:S(2)}, u32[]{:S(2)}) collective-permute-start(bf16[2,12,4,3072]{3,2,1,0:T(4,128)(2,1)} %fusion.3), channel_id=1, source_target_pairs={{0,7},{1,0},{2,1},{3,2},{4,3},{5,4},{6,5},{7,6},{8,15},{9,8},{10,9... | collective-permute-start | bytes 1769480 | tf_op jit(solution)/shard_map/ppermute | solution.py:202
  11.3 2.2 %fusion = bf16[2,12,12,3072]{3,2,1,0:T(8,128)(2,1)} fusion(bf16[1,16,16,3072]{3,2,1,0:T(8,128)(2,1)S(1)} %bitcast.36, bf16[1,16,16,3072]{3,2,1,0:T(8,128)(2,1)S(1)} %bitcast.32), kind=kLoop, calls=%fused_computation.10 | loop fusion | flops 884736 | bytes 4915200 | tf_op jit(solution)/shard_map/stack | solution.py:228
  13.9 2.0 broadcast_in_dim_reshape.8.kcol_ref
  16.7 0.9 copy.42
  18.3 1.6 collective-permute-done.1
  19.9 1.3 copy.38
  21.2 2.8 %collective-permute-done.2 = bf16[2,4,4,3072]{3,2,1,0:T(4,128)(2,1)S(1)} collective-permute-done((bf16[2,4,4,3072]{3,2,1,0:T(4,128)(2,1)S(1)}, bf16[2,4,4,3072]{3,2,1,0:T(4,128)(2,1)S(1)}, u32[]{:S(2)}, u32[]{:S(2)}) %collective-permute-start.2) | collective-permute-done | bytes 196640 | tf_op jit(solution)/shard_map/ppermute | solution.py:202
  24.0 4.4 %collective-permute-done = bf16[2,12,4,3072]{3,2,1,0:T(4,128)(2,1)} collective-permute-done((bf16[2,12,4,3072]{3,2,1,0:T(4,128)(2,1)}, bf16[2,12,4,3072]{3,2,1,0:T(4,128)(2,1)}, u32[]{:S(2)}, u32[]{:S(2)}) %collective-permute-start) | collective-permute-done | bytes 589856 | tf_op jit(solution)/shard_map/ppermute | solution.py:202
  28.4 3.8 %maximum_maximum_fusion = bf16[2,16,16,3072]{3,2,1,0:T(8,128)(2,1)} fusion(bf16[2,4,4,3072]{3,2,1,0:T(4,128)(2,1)S(1)} %collective-permute-done.2, bf16[2,4,12,3072]{3,2,1,0:T(8,128)(2,1)S(1)} %copy.38, bf16[2,12,4,3072]{3,2,1,0:T(4,128)(2,1)} %collective-permute-done, bf16[2,12,12,3072]{3,2,1,0:T(8,128)(2,1)} %fusion), kind=kLoop, calls=%fused_computation.8 | loop fusion | flops 12582912 | bytes 6291456 | tf_op jit(solution)/shard_map/concatenate | solution.py:211
  32.2 8.0 %reshape.102 = bf16[2,16,16,16,192]{4,3,2,1,0:T(8,128)(2,1)} reshape(bf16[2,16,16,3072]{3,2,1,0:T(8,128)(2,1)} %maximum_maximum_fusion) | data formatting | bytes 6291456 | tf_op jit(solution)/shard_map/reshape | solution.py:229
  40.2 4.4 %slice.83 = bf16[2,16,16,12,192]{4,3,2,1,0:T(8,128)(2,1)S(1)} slice(bf16[2,16,16,16,192]{4,3,2,1,0:T(8,128)(2,1)} %reshape.102), slice={[0:2], [0:16], [0:16], [4:16], [0:192]} | slice | bytes 4718592 | tf_op jit(solution)/shard_map/jit(_roll_static)/slice | solution.py:229
  44.6 2.0 slice.84
  46.6 3.4 %pad_maximum_fusion = (bf16[1,16,16,16,192]{4,3,2,1,0:T(8,128)(2,1)}, bf16[1,16,16,16,192]{4,3,2,1,0:T(8,128)(2,1)S(1)}) fusion(bf16[2,16,16,4,192]{4,3,2,1,0:T(4,128)(2,1)S(1)} %slice.84, bf16[2,16,16,12,192]{4,3,2,1,0:T(8,128)(2,1)S(1)} %slice.83), kind=kLoop, calls=%fused_computation.12 | loop fusion | flops 6291456 | bytes 6291456 | tf_op jit(solution)/shard_map/jit(_roll_static)/concatenate | solution.py:229
  50.1 1.6 copy.39
  51.6 3.8 %copy.43.xt_ref = bf16[8,192,512]{2,1,0:T(8,128)(2,1)} copy(bf16[8,192,512]{1,2,0:T(8,128)(2,1)} %bitcast.39) | data formatting | bytes 3145728 | tf_op jit(solution)/shard_map/reshape | solution.py:27
  55.5 3.2 %copy.40 = bf16[2,2,2,192,8,8,8]{3,6,5,4,2,1,0:T(8,128)(2,1)} copy(bf16[2,2,2,192,8,8,8]{3,6,2,5,1,4,0:T(8,128)(2,1)} %bitcast.42) | data formatting | bytes 3145728 | tf_op jit(solution)/shard_map/transpose | solution.py:27
  58.7 3.8 %copy.44.gt_ref = bf16[8,192,512]{2,1,0:T(8,128)(2,1)} copy(bf16[8,192,512]{1,2,0:T(8,128)(2,1)} %bitcast.40) | data formatting | bytes 3145728 | tf_op jit(solution)/shard_map/reshape | solution.py:27
  62.5 75.6 %shard_map.93 = (bf16[8,192,512]{2,1,0:T(8,128)(2,1)}, f32[576,192]{1,0:T(8,128)}, f32[192,192]{1,0:T(8,128)}, f32[192,1]{1,0:T(8,128)}) custom-call(bf16[8,192,512]{2,1,0:T(8,128)(2,1)} %copy.43.xt_ref, bf16[8,192,512]{2,1,0:T(8,128)(2,1)} %copy.44.gt_ref, s32[8,512,1]{2,1,0:T(8,128)} %broadcast_in_dim_reshape.8.kcol_ref, ...), custom_call_target="tpu_custom_call" | custom-call | tf_op jit(solution)/shard_map/pallas_call | solution.py:113
  138.1 1.4 reshape.110
  139.5 1.0 reshape.111
  140.6 1.0 reduce
  142.4 1.2 collective-permute-done.6
  144.5 1.2 collective-permute-start.7
  145.7 4.2 %collective-permute-done.7 = f32[36912]{0:T(1024)} collective-permute-done((f32[36912]{0:T(1024)}, f32[36912]{0:T(1024)}, u32[]{:S(2)}, u32[]{:S(2)}) %collective-permute-start.7) | collective-permute-done | bytes 147680 | tf_op jit(solution)/shard_map/ppermute | solution.py:151
  150.0 1.0 dynamic-slice_add_fusion.1
  151.9 3.2 %collective-permute-done.8 = f32[18456]{0:T(1024)S(1)} collective-permute-done((f32[18456]{0:T(1024)S(1)}, f32[18456]{0:T(1024)S(1)}, u32[]{:S(2)}, u32[]{:S(2)}) %collective-permute-start.8) | collective-permute-done | bytes 73856 | tf_op jit(solution)/shard_map/ppermute | solution.py:151
  155.1 1.0 dynamic-slice_add_fusion.2
  156.6 3.5 %collective-permute-done.9 = f32[9228]{0:T(1024)S(1)} collective-permute-done((f32[9228]{0:T(1024)S(1)}, f32[9228]{0:T(1024)S(1)}, u32[]{:S(2)}, u32[]{:S(2)}) %collective-permute-start.9) | collective-permute-done | bytes 36944 | tf_op jit(solution)/shard_map/ppermute | solution.py:151
  160.3 2.1 %collective-permute-start.10 = (f32[4614]{0:T(1024)S(1)}, f32[4614]{0:T(1024)S(1)}, u32[]{:S(2)}, u32[]{:S(2)}) collective-permute-start(f32[4614]{0:T(1024)S(1)} %dynamic_slice.39), channel_id=1, source_target_pairs={{0,1},{1,0},{2,3},{3,2},{4,5},{5,4},{6,7},{7,6},{8,9},{9,8},{10,11... | collective-permute-start | bytes 55376 | tf_op jit(solution)/shard_map/ppermute | solution.py:151
  162.4 1.2 collective-permute-done.10
  163.6 1.6 collective-permute-start.11
  165.2 1.2 collective-permute-done.11
  166.6 3.7 %collective-permute-done.12 = f32[9228]{0:T(1024)S(1)} collective-permute-done((f32[9228]{0:T(1024)S(1)}, f32[9228]{0:T(1024)S(1)}, u32[]{:S(2)}, u32[]{:S(2)}) %collective-permute-start.12) | collective-permute-done | bytes 36944 | tf_op jit(solution)/shard_map/ppermute | solution.py:151
  170.5 2.4 %copy.47 = bf16[8,192,512]{1,2,0:T(8,128)(2,1)} copy(bf16[8,192,512]{2,1,0:T(8,128)(2,1)S(1)} %copy-done.2) | data formatting | bytes 3145728 | tf_op jit(solution)/shard_map/pallas_call | solution.py:113
  172.9 1.8 copy.48
  175.1 1.3 collective-permute-start.14
  176.4 2.3 %pad_maximum_fusion.1 = bf16[16,16,16,192]{3,2,1,0:T(8,128)(2,1)} fusion(bf16[16,16,12,192]{3,2,1,0:T(8,128)(2,1)S(1)} %bitcast.38, bf16[16,16,4,192]{3,2,1,0:T(4,128)(2,1)S(1)} %slice.87), kind=kLoop, calls=%fused_computation.13 | loop fusion | flops 3145728 | bytes 3145728 | tf_op jit(solution)/shard_map/jit(_roll_static)/concatenate | solution.py:254
  178.8 3.7 %reshape.109 = bf16[16,16,3072]{2,1,0:T(8,128)(2,1)S(1)} reshape(bf16[16,16,16,192]{3,2,1,0:T(8,128)(2,1)} %pad_maximum_fusion.1) | data formatting | bytes 3145728 | tf_op jit(solution)/shard_map/reshape | solution.py:255
  182.8 1.5 collective-permute-start.4
  184.2 1.5 collective-permute-start.5
  185.7 7.2 %collective-permute-start.3 = (bf16[4,4,3072]{2,1,0:T(4,128)(2,1)S(1)}, bf16[4,4,3072]{2,1,0:T(4,128)(2,1)S(1)}, u32[]{:S(2)}, u32[]{:S(2)}) collective-permute-start(bf16[4,4,3072]{2,1,0:T(4,128)(2,1)S(1)} %slice.89), channel_id=1, source_target_pairs={{0,9},{1,10},{2,11},{3,12},{4,13},{5,14},{6,15},{7,8},{8,17},{9,18... | collective-permute-start | bytes 294920 | tf_op jit(solution)/shard_map/ppermute | solution.py:202
  193.7 8.7 %collective-permute-done.3 = bf16[4,4,3072]{2,1,0:T(4,128)(2,1)S(1)} collective-permute-done((bf16[4,4,3072]{2,1,0:T(4,128)(2,1)S(1)}, bf16[4,4,3072]{2,1,0:T(4,128)(2,1)S(1)}, u32[]{:S(2)}, u32[]{:S(2)}) %collective-permute-start.3) | collective-permute-done | bytes 98336 | tf_op jit(solution)/shard_map/ppermute | solution.py:202
  202.8 2.0 add_convert_fusion
  206.6 1.0 reshape.113
  (59 shorter events, 9.9 us)
Async XLA Ops:
  0.6 7.0 %copy-start = (bf16[16,16,3072]{2,1,0:T(8,128)(2,1)S(1)}, bf16[16,16,3072]{2,1,0:T(8,128)(2,1)}, u32[]{:S(2)}) copy-start(bf16[16,16,3072]{2,1,0:T(8,128)(2,1)} %param.7) | copy-start | bytes 4718596
  0.6 7.0 %copy-start.1 = (bf16[16,16,3072]{2,1,0:T(8,128)(2,1)S(1)}, bf16[16,16,3072]{2,1,0:T(8,128)(2,1)}, u32[]{:S(2)}) copy-start(bf16[16,16,3072]{2,1,0:T(8,128)(2,1)} %param.6) | copy-start | bytes 4718596
  3.5 16.5 %collective-permute-start.1 = (bf16[2,4,12,3072]{3,1,2,0:T(4,128)(2,1)}, bf16[2,4,12,3072]{3,1,2,0:T(4,128)(2,1)}, u32[]{:S(2)}, u32[]{:S(2)}) collective-permute-start(bf16[2,4,12,3072]{3,1,2,0:T(4,128)(2,1)} %copy.37), channel_id=1, source_target_pairs={{0,24},{1,25},{2,26},{3,27},{4,28},{5,29},{6,30},{7,31},{8,0},{9,1... | collective-permute-start | bytes 1769480 | tf_op jit(solution)/shard_map/ppermute | solution.py:202
  8.6 19.8 %collective-permute-start = (bf16[2,12,4,3072]{3,2,1,0:T(4,128)(2,1)}, bf16[2,12,4,3072]{3,2,1,0:T(4,128)(2,1)}, u32[]{:S(2)}, u32[]{:S(2)}) collective-permute-start(bf16[2,12,4,3072]{3,2,1,0:T(4,128)(2,1)} %fusion.3), channel_id=1, source_target_pairs={{0,7},{1,0},{2,1},{3,2},{4,3},{5,4},{6,5},{7,6},{8,15},{9,8},{10,9... | collective-permute-start | bytes 1769480 | tf_op jit(solution)/shard_map/ppermute | solution.py:202
  10.8 13.2 %collective-permute-start.2 = (bf16[2,4,4,3072]{3,2,1,0:T(4,128)(2,1)S(1)}, bf16[2,4,4,3072]{3,2,1,0:T(4,128)(2,1)S(1)}, u32[]{:S(2)}, u32[]{:S(2)}) collective-permute-start(bf16[2,4,4,3072]{3,2,1,0:T(4,128)(2,1)S(1)} %pad_maximum_fusion.3), channel_id=1, source_target_pairs={{0,31},{1,24},{2,25},{3,26},{4,27},{5,28},{6,29},{7,30},{8,7},{9,0... | collective-permute-start | bytes 589832 | tf_op jit(solution)/shard_map/ppermute | solution.py:202
  11.3 2.3 %copy-start.5 = (s32[16,16,16]{2,1,0:T(8,128)S(1)}, s32[16,16,16]{2,1,0:T(8,128)}, u32[]{:S(2)}) copy-start(s32[16,16,16]{2,1,0:T(8,128)} %param.8) | copy-start | bytes 49156
  13.6 3.1 %copy-start.3 = (bf16[192,576]{1,0:T(8,128)(2,1)S(1)}, bf16[192,576]{1,0:T(8,128)(2,1)}, u32[]{:S(2)}) copy-start(bf16[192,576]{1,0:T(8,128)(2,1)} %wqkv_ref.1) | copy-start | bytes 663556
  13.6 4.0 %copy-start.6 = (f32[192]{0:T(256)S(1)}, f32[192]{0:T(256)}, u32[]{:S(2)}) copy-start(f32[192]{0:T(256)} %param.9) | copy-start | bytes 2308
  141.8 1.8 collective-permute-start.6
  143.7 26.7 %copy-start.2 = (bf16[8,192,512]{2,1,0:T(8,128)(2,1)S(1)}, bf16[8,192,512]{2,1,0:T(8,128)(2,1)}, u32[]{:S(2)}) copy-start(bf16[8,192,512]{2,1,0:T(8,128)(2,1)} %get-tuple-element.8) | copy-start | bytes 4718596
  144.5 5.5 %collective-permute-start.7 = (f32[36912]{0:T(1024)}, f32[36912]{0:T(1024)}, u32[]{:S(2)}, u32[]{:S(2)}) collective-permute-start(f32[36912]{0:T(1024)} %dynamic_slice.33), channel_id=1, source_target_pairs={{0,4},{2,6},{4,0},{6,2},{1,5},{3,7},{5,1},{7,3},{8,12},{10,14},{12... | collective-permute-start | bytes 442952 | tf_op jit(solution)/shard_map/ppermute | solution.py:151
  151.0 0.7 copy-start.4
  151.8 3.3 %collective-permute-start.8 = (f32[18456]{0:T(1024)S(1)}, f32[18456]{0:T(1024)S(1)}, u32[]{:S(2)}, u32[]{:S(2)}) collective-permute-start(f32[18456]{0:T(1024)S(1)} %dynamic_slice.35), channel_id=1, source_target_pairs={{0,8},{8,0},{16,24},{24,16},{1,9},{9,1},{17,25},{25,17},{2,10},{10... | collective-permute-start | bytes 221480 | tf_op jit(solution)/shard_map/ppermute | solution.py:151
  156.2 3.9 %collective-permute-start.9 = (f32[9228]{0:T(1024)S(1)}, f32[9228]{0:T(1024)S(1)}, u32[]{:S(2)}, u32[]{:S(2)}) collective-permute-start(f32[9228]{0:T(1024)S(1)} %dynamic_slice.37), channel_id=1, source_target_pairs={{0,16},{8,24},{16,0},{24,8},{1,17},{9,25},{17,1},{25,9},{2,18},{10... | collective-permute-start | bytes 110744 | tf_op jit(solution)/shard_map/ppermute | solution.py:151
  160.3 3.3 %collective-permute-start.10 = (f32[4614]{0:T(1024)S(1)}, f32[4614]{0:T(1024)S(1)}, u32[]{:S(2)}, u32[]{:S(2)}) collective-permute-start(f32[4614]{0:T(1024)S(1)} %dynamic_slice.39), channel_id=1, source_target_pairs={{0,1},{1,0},{2,3},{3,2},{4,5},{5,4},{6,7},{7,6},{8,9},{9,8},{10,11... | collective-permute-start | bytes 55376 | tf_op jit(solution)/shard_map/ppermute | solution.py:151
  163.6 2.8 %collective-permute-start.11 = (f32[4614]{0:T(1024)S(1)}, f32[4614]{0:T(1024)S(1)}, u32[]{:S(2)}, u32[]{:S(2)}) collective-permute-start(f32[4614]{0:T(1024)S(1)} %dynamic-slice_add_fusion.4), channel_id=1, source_target_pairs={{0,1},{1,0},{2,3},{3,2},{4,5},{5,4},{6,7},{7,6},{8,9},{9,8},{10,11... | collective-permute-start | bytes 55376 | tf_op jit(solution)/shard_map/ppermute | solution.py:151
  166.5 3.8 %collective-permute-start.12 = (f32[9228]{0:T(1024)S(1)}, f32[9228]{0:T(1024)S(1)}, u32[]{:S(2)}, u32[]{:S(2)}) collective-permute-start(f32[9228]{0:T(1024)S(1)} %maximum_select_fusion.4), channel_id=1, source_target_pairs={{0,16},{8,24},{16,0},{24,8},{1,17},{9,25},{17,1},{25,9},{2,18},{10... | collective-permute-start | bytes 110744 | tf_op jit(solution)/shard_map/ppermute | solution.py:151
  170.4 4.6 %collective-permute-start.13 = (f32[18456]{0:T(1024)S(1)}, f32[18456]{0:T(1024)S(1)}, u32[]{:S(2)}, u32[]{:S(2)}) collective-permute-start(f32[18456]{0:T(1024)S(1)} %maximum_select_fusion.3), channel_id=1, source_target_pairs={{0,8},{8,0},{16,24},{24,16},{1,9},{9,1},{17,25},{25,17},{2,10},{10... | collective-permute-start | bytes 221480 | tf_op jit(solution)/shard_map/ppermute | solution.py:151
  175.1 17.7 %collective-permute-start.14 = (f32[36912]{0:T(1024)S(1)}, f32[36912]{0:T(1024)S(1)}, u32[]{:S(2)}, u32[]{:S(2)}) collective-permute-start(f32[36912]{0:T(1024)S(1)} %maximum_select_fusion.2), channel_id=1, source_target_pairs={{0,4},{2,6},{4,0},{6,2},{1,5},{3,7},{5,1},{7,3},{8,12},{10,14},{12... | collective-permute-start | bytes 442952 | tf_op jit(solution)/shard_map/ppermute | solution.py:151
  182.8 19.6 %collective-permute-start.4 = (bf16[4,12,3072]{2,1,0:T(8,128)(2,1)S(1)}, bf16[4,12,3072]{2,1,0:T(8,128)(2,1)S(1)}, u32[]{:S(2)}, u32[]{:S(2)}) collective-permute-start(bf16[4,12,3072]{2,1,0:T(8,128)(2,1)S(1)} %slice.90), channel_id=1, source_target_pairs={{0,8},{1,9},{2,10},{3,11},{4,12},{5,13},{6,14},{7,15},{8,16},{9,17... | collective-permute-start | bytes 884744 | tf_op jit(solution)/shard_map/ppermute | solution.py:202
  184.2 18.5 %collective-permute-start.5 = (bf16[12,4,3072]{2,1,0:T(4,128)(2,1)S(1)}, bf16[12,4,3072]{2,1,0:T(4,128)(2,1)S(1)}, u32[]{:S(2)}, u32[]{:S(2)}) collective-permute-start(bf16[12,4,3072]{2,1,0:T(4,128)(2,1)S(1)} %slice.91), channel_id=1, source_target_pairs={{0,1},{1,2},{2,3},{3,4},{4,5},{5,6},{6,7},{7,0},{8,9},{9,10},{10,1... | collective-permute-start | bytes 884744 | tf_op jit(solution)/shard_map/ppermute | solution.py:202
  185.7 16.7 %collective-permute-start.3 = (bf16[4,4,3072]{2,1,0:T(4,128)(2,1)S(1)}, bf16[4,4,3072]{2,1,0:T(4,128)(2,1)S(1)}, u32[]{:S(2)}, u32[]{:S(2)}) collective-permute-start(bf16[4,4,3072]{2,1,0:T(4,128)(2,1)S(1)} %slice.89), channel_id=1, source_target_pairs={{0,9},{1,10},{2,11},{3,12},{4,13},{5,14},{6,15},{7,8},{8,17},{9,18... | collective-permute-start | bytes 294920 | tf_op jit(solution)/shard_map/ppermute | solution.py:202
  193.0 11.7 %collective-permute-start.15 = (f32[73824]{0:T(1024)S(1)}, f32[73824]{0:T(1024)S(1)}, u32[]{:S(2)}, u32[]{:S(2)}) collective-permute-start(f32[73824]{0:T(1024)S(1)} %maximum_select_fusion.1), channel_id=1, source_target_pairs={{0,2},{2,0},{4,6},{6,4},{1,3},{3,1},{5,7},{7,5},{8,10},{10,8},{12,... | collective-permute-start | bytes 885896 | tf_op jit(solution)/shard_map/ppermute | solution.py:151

commit v4 on v3

v4 whole, which is shorter than its diff:
```python
import jax
import jax.numpy as jnp
from jax import lax
from jax.experimental import pallas as pl
from jax.experimental.pallas import tpu as pltpu
from jax.sharding import PartitionSpec as P

HEADS = 6
C = 192
WIN = 8
SHIFT = 4
NZ = 16
CELLS = WIN**3
HEAD = C // HEADS
SCALE = HEAD ** (-0.5)


def passed_along(block, axis, distance):
    devices = range(lax.axis_size(axis))
    route = [((i - distance) % len(devices), i) for i in devices]
    return lax.ppermute(block, axis, route)


def to_windows_cm(values):
    extent_a, extent_b, extent_c, ch = values.shape
    shaped = values.reshape(extent_a // WIN, WIN, extent_b // WIN, WIN, extent_c // WIN, WIN, ch)
    return shaped.transpose(0, 2, 4, 6, 1, 3, 5).reshape(-1, ch, CELLS)


def from_windows_cm(values, extent_a, extent_b, extent_c):
    ch = values.shape[1]
    shaped = values.reshape(extent_a // WIN, extent_b // WIN, extent_c // WIN, ch, WIN, WIN, WIN)
    return shaped.transpose(0, 4, 1, 5, 2, 6, 3).reshape(extent_a, extent_b, extent_c, ch)


def to_windows_key(values):
    extent_a, extent_b, extent_c = values.shape
    shaped = values.reshape(extent_a // WIN, WIN, extent_b // WIN, WIN, extent_c // WIN, WIN)
    return shaped.transpose(0, 2, 4, 5, 1, 3).reshape(-1, CELLS)


def window_kernel(both_ref, kcol_ref, krow_ref, gain_ref, wqkvT_ref, wqkv_ref, wp_ref,
                  gs_ref, gqkvT_ref, gproj_ref, ggain_ref, qkv_s, ga_s, drow_s):
    f32 = jnp.float32
    bf16 = jnp.bfloat16
    gqkvT_ref[...] = jnp.zeros_like(gqkvT_ref)
    gproj_ref[...] = jnp.zeros_like(gproj_ref)
    ggain_ref[...] = jnp.zeros_like(ggain_ref)
    gain = gain_ref[...]
    nt = (((1,), (1,)), ((), ()))
    pair = 2 * C
    n_pairs = NZ // 2

    def gathered(which, i, j, l):
        pieces = []
        for q in range(WIN // 2):
            p = (WIN // 2 * l + SHIFT // 2 + q) % n_pairs
            block = both_ref[which, pl.ds(i * WIN, WIN), :, pl.ds(p * pair, pair)].astype(f32)
            block = jnp.where(j == 0, block[:, :WIN], block[:, WIN:]).reshape(WIN * WIN, pair)
            pieces.append(block[:, :C])
            pieces.append(block[:, C:])
        return jnp.concatenate(pieces, axis=0).T

    def scattered(values_t, i, j, l):
        rows = values_t.T
        for q in range(WIN // 2):
            p = (WIN // 2 * l + SHIFT // 2 + q) % n_pairs
            even = rows[2 * q * WIN * WIN:(2 * q + 1) * WIN * WIN]
            odd = rows[(2 * q + 1) * WIN * WIN:(2 * q + 2) * WIN * WIN]
            block = jnp.concatenate([even, odd], axis=1).reshape(WIN, WIN, pair)
            gs_ref[pl.ds(i * WIN, WIN), pl.ds(pl.multiple_of(j * WIN, WIN), WIN), pl.ds(p * pair, pair)] = block

    def window(ij, l):
        i = ij // 2
        j = ij % 2
        w = ij * 2 + l
        x = gathered(0, i, j, l)
        row_mean = jnp.mean(x, axis=0, keepdims=True)
        centred = x - row_mean
        inv_std = lax.rsqrt(jnp.mean(centred * centred, axis=0, keepdims=True) + 1e-05)
        x_hat = centred * inv_std
        normed = (x_hat * gain).astype(bf16)
        qkv_t = jnp.dot(wqkvT_ref[...], normed, preferred_element_type=f32)
        qkv_s[...] = qkv_t.astype(bf16).astype(f32)
        g = gathered(1, i, j, l).astype(bf16)
        ga_t = jnp.dot(wp_ref[...], g, preferred_element_type=f32)
        ga_s[...] = ga_t.astype(bf16).astype(f32)
        allowed = kcol_ref[w] == krow_ref[w]

        def head_step(h, carry):
            qo = pl.multiple_of(h * HEAD, HEAD)
            q_t = qkv_s[pl.ds(qo, HEAD), :]
            k_t = qkv_s[pl.ds(qo + C, HEAD), :]
            v_t = qkv_s[pl.ds(qo + 2 * C, HEAD), :]
            ga_th = ga_s[pl.ds(qo, HEAD), :]
            q = q_t.T.astype(bf16)
            scores = jnp.dot(q, k_t.astype(bf16), preferred_element_type=f32) * SCALE
            weights = jnp.where(allowed, jnp.exp(scores), 0.0)
            probs = weights / jnp.sum(weights, axis=1, keepdims=True)
            probs_bf = probs.astype(bf16)
            att_t = lax.dot_general(v_t.astype(bf16), probs_bf, nt, preferred_element_type=f32)
            att_t = att_t.astype(bf16)
            gproj_ref[pl.ds(qo, HEAD), :] += lax.dot_general(
                att_t, g, nt, preferred_element_type=f32
            )
            ga = ga_th.T.astype(bf16)
            grad_probs = jnp.dot(ga, v_t.astype(bf16), preferred_element_type=f32)
            dv_t = jnp.dot(ga_th.astype(bf16), probs_bf, preferred_element_type=f32)
            row_total = jnp.sum(probs * grad_probs, axis=1, keepdims=True)
            grad_scores = (probs * (grad_probs - row_total) * SCALE).astype(bf16)
            dq_t = lax.dot_general(k_t.astype(bf16), grad_scores, nt, preferred_element_type=f32)
            dk_t = jnp.dot(q_t.astype(bf16), grad_scores, preferred_element_type=f32)
            drow_s[pl.ds(qo, HEAD), :] = dq_t.astype(bf16).astype(f32)
            drow_s[pl.ds(qo + C, HEAD), :] = dk_t.astype(bf16).astype(f32)
            drow_s[pl.ds(qo + 2 * C, HEAD), :] = dv_t.astype(bf16).astype(f32)
            return carry

        lax.fori_loop(0, HEADS, head_step, 0)
        rows_t = drow_s[...].astype(bf16)
        gqkvT_ref[...] += lax.dot_general(rows_t, normed, nt, preferred_element_type=f32)
        grad_normed = jnp.dot(wqkv_ref[...], rows_t, preferred_element_type=f32)
        ggain_ref[...] += jnp.sum(grad_normed * x_hat, axis=1, keepdims=True)
        scaled = grad_normed * gain
        grad_shifted = inv_std * (
            scaled
            - jnp.mean(scaled, axis=0, keepdims=True)
            - x_hat * jnp.mean(scaled * x_hat, axis=0, keepdims=True)
        )
        scattered(grad_shifted.astype(bf16).astype(f32), i, j, l)

    def block_step(ij, carry):
        for l in range(2):
            window(ij, l)
        return carry

    lax.fori_loop(0, 4, block_step, 0)


def window_grads(both, kcol, krow, gain_col, wqkv_t, wqkv, wp):
    extent_a, extent_b, width = both.shape[1:]
    return pl.pallas_call(
        window_kernel,
        out_shape=[
            jax.ShapeDtypeStruct((extent_a, extent_b, width), jnp.float32),
            jax.ShapeDtypeStruct((3 * C, C), jnp.float32),
            jax.ShapeDtypeStruct((C, C), jnp.float32),
            jax.ShapeDtypeStruct((C, 1), jnp.float32),
        ],
        scratch_shapes=[
            pltpu.VMEM((3 * C, CELLS), jnp.float32),
            pltpu.VMEM((C, CELLS), jnp.float32),
            pltpu.VMEM((3 * C, CELLS), jnp.float32),
        ],
    )(both, kcol, krow, gain_col, wqkv_t, wqkv, wp)


SUM_AXES = ("gy", "gx", "gz")


def swapped(block, axis, distance):
    return lax.ppermute(block, axis, [(i, i ^ distance) for i in range(lax.axis_size(axis))])


def summed_everywhere(parts):
    sizes = [lax.axis_size(axis) for axis in SUM_AXES]
    if any(size & (size - 1) for size in sizes):
        return lax.psum(parts, SUM_AXES)
    flat = jnp.concatenate([part.reshape(-1) for part in parts])
    total = flat.shape[0]
    devices = 1
    for size in sizes:
        devices *= size
    padded = -(-total // devices) * devices
    values = jnp.pad(flat, (0, padded - total))
    steps = []
    for axis, size in zip(SUM_AXES, sizes):
        distance = 1
        while distance < size:
            bit = (lax.axis_index(axis) // distance) % 2
            half = values.shape[0] // 2
            keep = lax.dynamic_slice_in_dim(values, bit * half, half)
            send = lax.dynamic_slice_in_dim(values, (1 - bit) * half, half)
            values = keep + swapped(send, axis, distance)
            steps.append((axis, distance))
            distance *= 2
    for axis, distance in reversed(steps):
        bit = (lax.axis_index(axis) // distance) % 2
        other = swapped(values, axis, distance)
        values = jnp.where(
            bit == 0, jnp.concatenate([values, other]), jnp.concatenate([other, values])
        )
    out = []
    start = 0
    for part in parts:
        out.append(values[start : start + part.size].reshape(part.shape))
        start += part.size
    return tuple(out)


def halo_route(distance_a, distance_b):
    size_a = lax.axis_size("gx")
    size_b = lax.axis_size(("gy", "gz"))
    route = []
    for ia in range(size_a):
        for ib in range(size_b):
            target = ((ia + distance_a) % size_a) * size_b + (ib + distance_b) % size_b
            route.append((ia * size_b + ib, target))
    return route


def moved(block, distance_a, distance_b):
    return lax.ppermute(block, ("gx", "gy", "gz"), halo_route(distance_a, distance_b))


def shifted_block(both):
    from_a = moved(both[:, :SHIFT, SHIFT:], -1, 0)
    from_b = moved(both[:, SHIFT:, :SHIFT], 0, -1)
    from_ab = moved(both[:, :SHIFT, :SHIFT], -1, -1)
    upper = jnp.concatenate([both[:, SHIFT:, SHIFT:], from_b], axis=2)
    lower = jnp.concatenate([from_a, from_ab], axis=2)
    return jnp.concatenate([upper, lower], axis=1)


def unshifted_sum(grads_out, grad_shifted):
    narrow = grad_shifted.astype(jnp.bfloat16)
    to_a = moved(narrow[-SHIFT:, :-SHIFT], 1, 0).astype(jnp.float32)
    to_b = moved(narrow[:-SHIFT, -SHIFT:], 0, 1).astype(jnp.float32)
    to_ab = moved(narrow[-SHIFT:, -SHIFT:], 1, 1).astype(jnp.float32)
    upper = jnp.concatenate([to_ab, to_a], axis=1)
    lower = jnp.concatenate([to_b, grad_shifted[:-SHIFT, :-SHIFT]], axis=1)
    branch = jnp.concatenate([upper, lower], axis=0)
    return (grads_out.astype(jnp.float32) + branch.astype(jnp.float32)).astype(jnp.bfloat16)


def per_device(tokens, grads_out, labels, ln_gain, qkv_weight, proj_weight):
    brick_a, brick_b = (tokens.shape[0], tokens.shape[1])
    brick_c = NZ
    channels = C
    both = shifted_block(jnp.stack([tokens, grads_out]))
    extent_a = brick_a * lax.axis_size("gx")
    extent_b = brick_b * lax.axis_size(("gy", "gz"))
    first_index = lax.axis_index("gx") * brick_a + jnp.arange(brick_a, dtype=jnp.int32)
    second_index = lax.axis_index(("gy", "gz")) * brick_b + jnp.arange(brick_b, dtype=jnp.int32)
    wrap_first = (first_index >= extent_a - SHIFT).astype(jnp.int32)
    wrap_second = (second_index >= extent_b - SHIFT).astype(jnp.int32)
    wrap_third = (jnp.arange(brick_c, dtype=jnp.int32) >= brick_c - SHIFT).astype(jnp.int32)
    region = (
        wrap_first[:, None, None] * 4 + wrap_second[None, :, None] * 2 + wrap_third[None, None, :]
    )
    mask_key = to_windows_key(labels * 8 + region)

    grad_branch, qkv_grad_t, proj_grad, gain_grad = window_grads(
        both,
        mask_key[:, :, None],
        mask_key[:, None, :],
        ln_gain.reshape(channels, 1),
        qkv_weight.T,
        qkv_weight,
        proj_weight,
    )
    qkv_grad_t, proj_grad, gain_grad = summed_everywhere((qkv_grad_t, proj_grad, gain_grad))
    qkv_grad = qkv_grad_t.T
    grad_tokens = unshifted_sum(grads_out, grad_branch)
    return (grad_tokens, gain_grad.reshape(-1), qkv_grad.reshape(-1), proj_grad.reshape(-1))


def solution(mesh):
    return jax.shard_map(
        per_device,
        mesh=mesh,
        in_specs=(
            P("gx", ("gy", "gz"), None),
            P("gx", ("gy", "gz"), None),
            P("gx", ("gy", "gz"), None),
            P(),
            P(),
            P(),
        ),
        out_specs=(P("gx", ("gy", "gz"), None), P(), P(), P()),
        check_vma=False,
    )
```

time: 208 us -> 169 us (0.81)
  the two profiles are of different devices: /device:TPU:1 before, /device:TPU:5 now
where the time goes in v4:
time: 169 us; the launch traced here: 168 us
  Pallas kernels  79.2 us (47%)
  waiting for transfers between devices  35.1 us (21%)
  starting transfers between devices  23.5 us (14%)
  other arithmetic  15.2 us (9%)
  local copies, waits for them, and re-layouts  13.5 us (8%)
    pallas_call x1, Pallas kernels, window_grads(): pl.pallas_call(window_kernel, out_shape=[jax.ShapeDtypeStruct((extent_a,...  79.2 us
    ppermute x10, waiting for transfers between devices, swapped(): lax.ppermute(block, axis, [(i, i ^ distance) for i in range(lax.axis_size...  22.2 us
    ppermute x6, starting transfers between devices, moved(): lax.ppermute(block, ('gx', 'gy', 'gz'), halo_route(distance_a, distance_b))  16.4 us
    ppermute x6, waiting for transfers between devices, moved(): lax.ppermute(block, ('gx', 'gy', 'gz'), halo_route(distance_a, distance_b))  12.9 us
    ppermute x10, starting transfers between devices, swapped(): lax.ppermute(block, axis, [(i, i ^ distance) for i in range(lax.axis_size...  7.18 us
    another operation x4, other arithmetic, per_device(): both = shifted_block(jnp.stack([tokens, grads_out]))  4.89 us
    concatenate x1, other arithmetic, shifted_block(): return jnp.concatenate([upper, lower], axis=1)  3.72 us
  transfers between devices with their start and end apart: 16, of which 13 were waited for; matrix products, arithmetic and copies ran while one was open for 8% of the time, Pallas kernels for 0%

profile of v4, /device:TPU:5, one launch (start us, length us, event | category | flops | bytes accessed | tf_op | source)
XLA Modules:
  0.0 167.6 jit_solution(10810737609976745837)
XLA Ops:
  0.7 1.5 fusion.2
  2.2 1.3 copy.17
  3.5 3.3 %collective-permute-start.1 = (bf16[2,4,12,3072]{3,1,2,0:T(4,128)(2,1)}, bf16[2,4,12,3072]{3,1,2,0:T(4,128)(2,1)}, u32[]{:S(2)}, u32[]{:S(2)}) collective-permute-start(bf16[2,4,12,3072]{3,1,2,0:T(4,128)(2,1)} %copy.17), channel_id=1, source_target_pairs={{0,24},{1,25},{2,26},{3,27},{4,28},{5,29},{6,30},{7,31},{8,0},{9,1... | collective-permute-start | bytes 1769480 | tf_op jit(solution)/shard_map/ppermute | solution.py:212
  6.8 1.1 fusion.3
  7.8 0.2 collective-permute-start
  8.1 2.0 %collective-permute-start.2 = (bf16[2,4,4,3072]{3,2,1,0:T(4,128)(2,1)S(1)}, bf16[2,4,4,3072]{3,2,1,0:T(4,128)(2,1)S(1)}, u32[]{:S(2)}, u32[]{:S(2)}) collective-permute-start(bf16[2,4,4,3072]{3,2,1,0:T(4,128)(2,1)S(1)} %pad_maximum_fusion.1), channel_id=1, source_target_pairs={{0,31},{1,24},{2,25},{3,26},{4,27},{5,28},{6,29},{7,30},{8,7},{9,0... | collective-permute-start | bytes 589832 | tf_op jit(solution)/shard_map/ppermute | solution.py:212
  10.2 2.3 %fusion.1 = bf16[2,12,12,3072]{3,2,1,0:T(8,128)(2,1)} fusion(bf16[1,16,16,3072]{3,2,1,0:T(8,128)(2,1)S(1)} %bitcast.17, bf16[1,16,16,3072]{3,2,1,0:T(8,128)(2,1)S(1)} %bitcast.13), kind=kLoop, calls=%fused_computation.9 | loop fusion | flops 884736 | bytes 4915200 | tf_op jit(solution)/shard_map/stack | solution.py:239
  12.6 0.2 reshape.84
  12.8 0.2 copy.19
  13.0 2.0 %broadcast_in_dim_reshape.8.kcol_ref = s32[8,512,1]{2,1,0:T(8,128)} reshape(s32[2,2,2,8,8,8]{5,4,3,2,1,0:T(8,128)S(1)} %bitcast.18) | data formatting | bytes 32768 | tf_op jit(solution)/shard_map/broadcast_in_dim;reshape | solution.py:254
  14.9 0.8 broadcast_in_dim_reshape.7.krow_ref
  15.7 0.9 copy.20
  16.6 0.8 copy.22.gain_ref
  17.3 1.7 %collective-permute-done.1 = bf16[2,4,12,3072]{3,1,2,0:T(4,128)(2,1)} collective-permute-done((bf16[2,4,12,3072]{3,1,2,0:T(4,128)(2,1)}, bf16[2,4,12,3072]{3,1,2,0:T(4,128)(2,1)}, u32[]{:S(2)}, u32[]{:S(2)}) %collective-permute-start.1) | collective-permute-done | bytes 589856 | tf_op jit(solution)/shard_map/ppermute | solution.py:212
  19.1 1.3 copy.18
  20.3 3.5 %collective-permute-done.2 = bf16[2,4,4,3072]{3,2,1,0:T(4,128)(2,1)S(1)} collective-permute-done((bf16[2,4,4,3072]{3,2,1,0:T(4,128)(2,1)S(1)}, bf16[2,4,4,3072]{3,2,1,0:T(4,128)(2,1)S(1)}, u32[]{:S(2)}, u32[]{:S(2)}) %collective-permute-start.2) | collective-permute-done | bytes 196640 | tf_op jit(solution)/shard_map/ppermute | solution.py:212
  23.9 0.4 collective-permute-done
  24.3 3.7 %maximum_maximum_fusion.both_ref = bf16[2,16,16,3072]{3,2,1,0:T(8,128)(2,1)} fusion(bf16[2,4,4,3072]{3,2,1,0:T(4,128)(2,1)S(1)} %collective-permute-done.2, bf16[2,4,12,3072]{3,2,1,0:T(8,128)(2,1)S(1)} %copy.18, bf16[2,12,4,3072]{3,2,1,0:T(4,128)(2,1)} %collective-permute-done, bf16[2,12,12,3072]{3,2,1,0:T(8,128)(2,1)} %fusion.1), kind=kLoop, calls=%fused_computation.6 | loop fusion | flops 12582912 | bytes 6291456 | tf_op jit(solution)/shard_map/concatenate | solution.py:221
  28.0 79.2 %shard_map.93 = (f32[16,16,3072]{2,1,0:T(8,128)}, f32[576,192]{1,0:T(8,128)}, f32[192,192]{1,0:T(8,128)}, f32[192,1]{1,0:T(8,128)}) custom-call(bf16[2,16,16,3072]{3,2,1,0:T(8,128)(2,1)} %maximum_maximum_fusion.both_ref, s32[8,512,1]{2,1,0:T(8,128)} %broadcast_in_dim_reshape.8.kcol_ref, s32[8,1,512]{2,1,0:T(1,128)} %broadcast_in_dim_reshape.7.krow_ref, ...), custom_call_target="tpu_custom_call" | custom-call | tf_op jit(solution)/shard_map/pallas_call | solution.py:141
  107.1 1.4 reshape.86
  108.5 1.0 reshape.87
  109.6 1.0 reduce
  110.6 0.2 dynamic_slice.31
  110.8 4.7 %collective-permute-start.6 = (f32[73824]{0:T(1024)S(1)}, f32[73824]{0:T(1024)S(1)}, u32[]{:S(2)}, u32[]{:S(2)}) collective-permute-start(f32[73824]{0:T(1024)S(1)} %dynamic_slice.31), channel_id=1, source_target_pairs={{0,2},{2,0},{4,6},{6,4},{1,3},{3,1},{5,7},{7,5},{8,10},{10,8},{12,... | collective-permute-start | bytes 885896 | tf_op jit(solution)/shard_map/ppermute | solution.py:161
  115.5 1.2 collective-permute-done.6
  117.0 1.3 collective-permute-start.7
  118.3 3.9 %collective-permute-done.7 = f32[36912]{0:T(1024)S(1)} collective-permute-done((f32[36912]{0:T(1024)S(1)}, f32[36912]{0:T(1024)S(1)}, u32[]{:S(2)}, u32[]{:S(2)}) %collective-permute-start.7) | collective-permute-done | bytes 147680 | tf_op jit(solution)/shard_map/ppermute | solution.py:161
  122.6 3.2 %collective-permute-done.8 = f32[18456]{0:T(1024)S(1)} collective-permute-done((f32[18456]{0:T(1024)S(1)}, f32[18456]{0:T(1024)S(1)}, u32[]{:S(2)}, u32[]{:S(2)}) %collective-permute-start.8) | collective-permute-done | bytes 73856 | tf_op jit(solution)/shard_map/ppermute | solution.py:161
  126.0 3.9 %collective-permute-done.9 = f32[9228]{0:T(1024)S(1)} collective-permute-done((f32[9228]{0:T(1024)S(1)}, f32[9228]{0:T(1024)S(1)}, u32[]{:S(2)}, u32[]{:S(2)}) %collective-permute-start.9) | collective-permute-done | bytes 36944 | tf_op jit(solution)/shard_map/ppermute | solution.py:161
  130.1 2.7 %collective-permute-done.10 = f32[4614]{0:T(1024)S(1)} collective-permute-done((f32[4614]{0:T(1024)S(1)}, f32[4614]{0:T(1024)S(1)}, u32[]{:S(2)}, u32[]{:S(2)}) %collective-permute-start.10) | collective-permute-done | bytes 18488 | tf_op jit(solution)/shard_map/ppermute | solution.py:161
  132.9 2.6 %collective-permute-done.11 = f32[4614]{0:T(1024)S(1)} collective-permute-done((f32[4614]{0:T(1024)S(1)}, f32[4614]{0:T(1024)S(1)}, u32[]{:S(2)}, u32[]{:S(2)}) %collective-permute-start.11) | collective-permute-done | bytes 18488 | tf_op jit(solution)/shard_map/ppermute | solution.py:161
  135.7 3.7 %collective-permute-done.12 = f32[9228]{0:T(1024)S(1)} collective-permute-done((f32[9228]{0:T(1024)S(1)}, f32[9228]{0:T(1024)S(1)}, u32[]{:S(2)}, u32[]{:S(2)}) %collective-permute-start.12) | collective-permute-done | bytes 36944 | tf_op jit(solution)/shard_map/ppermute | solution.py:161
  139.6 2.3 %convert_element_type.27 = bf16[16,16,3072]{2,1,0:T(8,128)(2,1)S(1)} convert(f32[16,16,3072]{2,1,0:T(8,128)} %get-tuple-element.8) | non-fusion elementwise | flops 786432 | bytes 4718592 | tf_op jit(solution)/shard_map/convert_element_type | solution.py:225
  142.0 0.2 slice.57
  142.2 0.3 copy-done.2
  142.5 0.2 slice.44
  142.6 1.5 collective-permute-start.4
  144.1 7.8 %collective-permute-start.3 = (bf16[4,4,3072]{2,1,0:T(4,128)(2,1)S(1)}, bf16[4,4,3072]{2,1,0:T(4,128)(2,1)S(1)}, u32[]{:S(2)}, u32[]{:S(2)}) collective-permute-start(bf16[4,4,3072]{2,1,0:T(4,128)(2,1)S(1)} %slice.55), channel_id=1, source_target_pairs={{0,9},{1,10},{2,11},{3,12},{4,13},{5,14},{6,15},{7,8},{8,17},{9,18... | collective-permute-start | bytes 294920 | tf_op jit(solution)/shard_map/ppermute | solution.py:212
  151.9 1.5 collective-permute-start.5
  153.5 0.8 collective-permute-start.14
  154.6 7.1 %collective-permute-done.5 = bf16[12,4,3072]{2,1,0:T(4,128)(2,1)S(1)} collective-permute-done((bf16[12,4,3072]{2,1,0:T(4,128)(2,1)S(1)}, bf16[12,4,3072]{2,1,0:T(4,128)(2,1)S(1)}, u32[]{:S(2)}, u32[]{:S(2)}) %collective-permute-start.5) | collective-permute-done | bytes 294944 | tf_op jit(solution)/shard_map/ppermute | solution.py:212
  161.8 0.9 collective-permute-done.14
  162.9 1.8 %fusion = bf16[16,16,3072]{2,1,0:T(8,128)(2,1)} fusion(f32[12,12,3072]{2,1,0:T(8,128)S(1)} %slice.44, f32[12,4,3072]{2,1,0:T(4,128)S(1)} %convert_element_type.28, f32[4,16,3072]{2,1,0:T(8,128)S(1)} %maximum_convert_fusion, bf16[16,16,3072]{2,1,0:T(8,128)(2,1)S(1)} %copy-done), kind=kLoop, calls=%fused_computation.8 | loop fusion | flops 3932160 | bytes 6291456 | tf_op jit(solution)/shard_map/convert_element_type | solution.py:232
  164.7 0.2 maximum_select_fusion
  165.0 0.7 slice.60
  165.7 0.6 slice.58
  166.4 0.2 copy.23
  166.6 1.0 reshape.89
  (47 shorter events, 2.5 us)
Async XLA Ops:
  0.6 6.1 %copy-start.1 = (bf16[16,16,3072]{2,1,0:T(8,128)(2,1)S(1)}, bf16[16,16,3072]{2,1,0:T(8,128)(2,1)}, u32[]{:S(2)}) copy-start(bf16[16,16,3072]{2,1,0:T(8,128)(2,1)} %param.6) | copy-start | bytes 4718596
  0.6 6.1 %copy-start = (bf16[16,16,3072]{2,1,0:T(8,128)(2,1)S(1)}, bf16[16,16,3072]{2,1,0:T(8,128)(2,1)}, u32[]{:S(2)}) copy-start(bf16[16,16,3072]{2,1,0:T(8,128)(2,1)} %param.7) | copy-start | bytes 4718596
  3.5 15.6 %collective-permute-start.1 = (bf16[2,4,12,3072]{3,1,2,0:T(4,128)(2,1)}, bf16[2,4,12,3072]{3,1,2,0:T(4,128)(2,1)}, u32[]{:S(2)}, u32[]{:S(2)}) collective-permute-start(bf16[2,4,12,3072]{3,1,2,0:T(4,128)(2,1)} %copy.17), channel_id=1, source_target_pairs={{0,24},{1,25},{2,26},{3,27},{4,28},{5,29},{6,30},{7,31},{8,0},{9,1... | collective-permute-start | bytes 1769480 | tf_op jit(solution)/shard_map/ppermute | solution.py:212
  7.8 16.4 %collective-permute-start = (bf16[2,12,4,3072]{3,2,1,0:T(4,128)(2,1)}, bf16[2,12,4,3072]{3,2,1,0:T(4,128)(2,1)}, u32[]{:S(2)}, u32[]{:S(2)}) collective-permute-start(bf16[2,12,4,3072]{3,2,1,0:T(4,128)(2,1)} %fusion.3), channel_id=1, source_target_pairs={{0,7},{1,0},{2,1},{3,2},{4,3},{5,4},{6,5},{7,6},{8,15},{9,8},{10,9... | collective-permute-start | bytes 1769480 | tf_op jit(solution)/shard_map/ppermute | solution.py:212
  8.1 15.7 %collective-permute-start.2 = (bf16[2,4,4,3072]{3,2,1,0:T(4,128)(2,1)S(1)}, bf16[2,4,4,3072]{3,2,1,0:T(4,128)(2,1)S(1)}, u32[]{:S(2)}, u32[]{:S(2)}) collective-permute-start(bf16[2,4,4,3072]{3,2,1,0:T(4,128)(2,1)S(1)} %pad_maximum_fusion.1), channel_id=1, source_target_pairs={{0,31},{1,24},{2,25},{3,26},{4,27},{5,28},{6,29},{7,30},{8,7},{9,0... | collective-permute-start | bytes 589832 | tf_op jit(solution)/shard_map/ppermute | solution.py:212
  10.2 2.3 %copy-start.4 = (s32[16,16,16]{2,1,0:T(8,128)S(1)}, s32[16,16,16]{2,1,0:T(8,128)}, u32[]{:S(2)}) copy-start(s32[16,16,16]{2,1,0:T(8,128)} %param.8) | copy-start | bytes 49156
  12.5 3.2 %copy-start.3 = (bf16[192,576]{1,0:T(8,128)(2,1)S(1)}, bf16[192,576]{1,0:T(8,128)(2,1)}, u32[]{:S(2)}) copy-start(bf16[192,576]{1,0:T(8,128)(2,1)} %wqkv_ref.1) | copy-start | bytes 663556
  12.5 4.1 %copy-start.5 = (f32[192]{0:T(256)S(1)}, f32[192]{0:T(256)}, u32[]{:S(2)}) copy-start(f32[192]{0:T(256)} %param.9) | copy-start | bytes 2308
  110.8 6.0 %collective-permute-start.6 = (f32[73824]{0:T(1024)S(1)}, f32[73824]{0:T(1024)S(1)}, u32[]{:S(2)}, u32[]{:S(2)}) collective-permute-start(f32[73824]{0:T(1024)S(1)} %dynamic_slice.31), channel_id=1, source_target_pairs={{0,2},{2,0},{4,6},{6,4},{1,3},{3,1},{5,7},{7,5},{8,10},{10,8},{12,... | collective-permute-start | bytes 885896 | tf_op jit(solution)/shard_map/ppermute | solution.py:161
  117.0 5.2 %collective-permute-start.7 = (f32[36912]{0:T(1024)S(1)}, f32[36912]{0:T(1024)S(1)}, u32[]{:S(2)}, u32[]{:S(2)}) collective-permute-start(f32[36912]{0:T(1024)S(1)} %dynamic_slice.33), channel_id=1, source_target_pairs={{0,4},{2,6},{4,0},{6,2},{1,5},{3,7},{5,1},{7,3},{8,12},{10,14},{12... | collective-permute-start | bytes 442952 | tf_op jit(solution)/shard_map/ppermute | solution.py:161
  122.4 3.3 %collective-permute-start.8 = (f32[18456]{0:T(1024)S(1)}, f32[18456]{0:T(1024)S(1)}, u32[]{:S(2)}, u32[]{:S(2)}) collective-permute-start(f32[18456]{0:T(1024)S(1)} %dynamic_slice.35), channel_id=1, source_target_pairs={{0,8},{8,0},{16,24},{24,16},{1,9},{9,1},{17,25},{25,17},{2,10},{10... | collective-permute-start | bytes 221480 | tf_op jit(solution)/shard_map/ppermute | solution.py:161
  125.9 3.9 %collective-permute-start.9 = (f32[9228]{0:T(1024)S(1)}, f32[9228]{0:T(1024)S(1)}, u32[]{:S(2)}, u32[]{:S(2)}) collective-permute-start(f32[9228]{0:T(1024)S(1)} %dynamic_slice.37), channel_id=1, source_target_pairs={{0,16},{8,24},{16,0},{24,8},{1,17},{9,25},{17,1},{25,9},{2,18},{10... | collective-permute-start | bytes 110744 | tf_op jit(solution)/shard_map/ppermute | solution.py:161
  130.1 2.8 %collective-permute-start.10 = (f32[4614]{0:T(1024)S(1)}, f32[4614]{0:T(1024)S(1)}, u32[]{:S(2)}, u32[]{:S(2)}) collective-permute-start(f32[4614]{0:T(1024)S(1)} %dynamic_slice.39), channel_id=1, source_target_pairs={{0,1},{1,0},{2,3},{3,2},{4,5},{5,4},{6,7},{7,6},{8,9},{9,8},{10,11... | collective-permute-start | bytes 55376 | tf_op jit(solution)/shard_map/ppermute | solution.py:161
  132.9 2.6 %collective-permute-start.11 = (f32[4614]{0:T(1024)S(1)}, f32[4614]{0:T(1024)S(1)}, u32[]{:S(2)}, u32[]{:S(2)}) collective-permute-start(f32[4614]{0:T(1024)S(1)} %dynamic-slice_add_fusion.4), channel_id=1, source_target_pairs={{0,1},{1,0},{2,3},{3,2},{4,5},{5,4},{6,7},{7,6},{8,9},{9,8},{10,11... | collective-permute-start | bytes 55376 | tf_op jit(solution)/shard_map/ppermute | solution.py:161
  135.6 3.8 %collective-permute-start.12 = (f32[9228]{0:T(1024)S(1)}, f32[9228]{0:T(1024)S(1)}, u32[]{:S(2)}, u32[]{:S(2)}) collective-permute-start(f32[9228]{0:T(1024)S(1)} %maximum_select_fusion.4), channel_id=1, source_target_pairs={{0,16},{8,24},{16,0},{24,8},{1,17},{9,25},{17,1},{25,9},{2,18},{10... | collective-permute-start | bytes 110744 | tf_op jit(solution)/shard_map/ppermute | solution.py:161
  139.5 13.9 %collective-permute-start.13 = (f32[18456]{0:T(1024)S(1)}, f32[18456]{0:T(1024)S(1)}, u32[]{:S(2)}, u32[]{:S(2)}) collective-permute-start(f32[18456]{0:T(1024)S(1)} %maximum_select_fusion.3), channel_id=1, source_target_pairs={{0,8},{8,0},{16,24},{24,16},{1,9},{9,1},{17,25},{25,17},{2,10},{10... | collective-permute-start | bytes 221480 | tf_op jit(solution)/shard_map/ppermute | solution.py:161
  139.6 2.8 %copy-start.2 = (f32[16,16,3072]{2,1,0:T(8,128)S(1)}, f32[16,16,3072]{2,1,0:T(8,128)}, u32[]{:S(2)}) copy-start(f32[16,16,3072]{2,1,0:T(8,128)} %get-tuple-element.8) | copy-start | bytes 9437188
  142.6 11.8 %collective-permute-start.4 = (bf16[4,12,3072]{2,1,0:T(8,128)(2,1)S(1)}, bf16[4,12,3072]{2,1,0:T(8,128)(2,1)S(1)}, u32[]{:S(2)}, u32[]{:S(2)}) collective-permute-start(bf16[4,12,3072]{2,1,0:T(8,128)(2,1)S(1)} %slice.56), channel_id=1, source_target_pairs={{0,8},{1,9},{2,10},{3,11},{4,12},{5,13},{6,14},{7,15},{8,16},{9,17... | collective-permute-start | bytes 884744 | tf_op jit(solution)/shard_map/ppermute | solution.py:212
  144.1 10.4 %collective-permute-start.3 = (bf16[4,4,3072]{2,1,0:T(4,128)(2,1)S(1)}, bf16[4,4,3072]{2,1,0:T(4,128)(2,1)S(1)}, u32[]{:S(2)}, u32[]{:S(2)}) collective-permute-start(bf16[4,4,3072]{2,1,0:T(4,128)(2,1)S(1)} %slice.55), channel_id=1, source_target_pairs={{0,9},{1,10},{2,11},{3,12},{4,13},{5,14},{6,15},{7,8},{8,17},{9,18... | collective-permute-start | bytes 294920 | tf_op jit(solution)/shard_map/ppermute | solution.py:212
  151.9 9.8 %collective-permute-start.5 = (bf16[12,4,3072]{2,1,0:T(4,128)(2,1)S(1)}, bf16[12,4,3072]{2,1,0:T(4,128)(2,1)S(1)}, u32[]{:S(2)}, u32[]{:S(2)}) collective-permute-start(bf16[12,4,3072]{2,1,0:T(4,128)(2,1)S(1)} %slice.57), channel_id=1, source_target_pairs={{0,1},{1,2},{2,3},{3,4},{4,5},{5,6},{6,7},{7,0},{8,9},{9,10},{10,1... | collective-permute-start | bytes 884744 | tf_op jit(solution)/shard_map/ppermute | solution.py:212
  153.5 9.2 %collective-permute-start.14 = (f32[36912]{0:T(1024)S(1)}, f32[36912]{0:T(1024)S(1)}, u32[]{:S(2)}, u32[]{:S(2)}) collective-permute-start(f32[36912]{0:T(1024)S(1)} %maximum_select_fusion.2), channel_id=1, source_target_pairs={{0,4},{2,6},{4,0},{6,2},{1,5},{3,7},{5,1},{7,3},{8,12},{10,14},{12... | collective-permute-start | bytes 442952 | tf_op jit(solution)/shard_map/ppermute | solution.py:161
  162.8 1.9 %collective-permute-start.15 = (f32[73824]{0:T(1024)S(1)}, f32[73824]{0:T(1024)S(1)}, u32[]{:S(2)}, u32[]{:S(2)}) collective-permute-start(f32[73824]{0:T(1024)S(1)} %maximum_select_fusion.1), channel_id=1, source_target_pairs={{0,2},{2,0},{4,6},{6,4},{1,3},{3,1},{5,7},{7,5},{8,10},{10,8},{12,... | collective-permute-start | bytes 885896 | tf_op jit(solution)/shard_map/ppermute | solution.py:161

commit v5 on v4

--- a/solution.py
+++ b/solution.py
@@ -221,11 +221,16 @@
     return jnp.concatenate([upper, lower], axis=1)
 
 
-def unshifted_sum(grads_out, grad_shifted):
+def sent_back(grad_shifted):
     narrow = grad_shifted.astype(jnp.bfloat16)
-    to_a = moved(narrow[-SHIFT:, :-SHIFT], 1, 0).astype(jnp.float32)
-    to_b = moved(narrow[:-SHIFT, -SHIFT:], 0, 1).astype(jnp.float32)
-    to_ab = moved(narrow[-SHIFT:, -SHIFT:], 1, 1).astype(jnp.float32)
+    to_a = moved(narrow[-SHIFT:, :-SHIFT], 1, 0)
+    to_b = moved(narrow[:-SHIFT, -SHIFT:], 0, 1)
+    to_ab = moved(narrow[-SHIFT:, -SHIFT:], 1, 1)
+    return to_a, to_b, to_ab
+
+
+def unshifted_sum(grads_out, grad_shifted, arrived):
+    to_a, to_b, to_ab = (piece.astype(jnp.float32) for piece in arrived)
     upper = jnp.concatenate([to_ab, to_a], axis=1)
     lower = jnp.concatenate([to_b, grad_shifted[:-SHIFT, :-SHIFT]], axis=1)
     branch = jnp.concatenate([upper, lower], axis=0)
@@ -258,9 +263,13 @@
         qkv_weight,
         proj_weight,
     )
+    arrived = sent_back(grad_branch)
+    arrived, qkv_grad_t, proj_grad, gain_grad = lax.optimization_barrier(
+        (arrived, qkv_grad_t, proj_grad, gain_grad)
+    )
     qkv_grad_t, proj_grad, gain_grad = summed_everywhere((qkv_grad_t, proj_grad, gain_grad))
     qkv_grad = qkv_grad_t.T
-    grad_tokens = unshifted_sum(grads_out, grad_branch)
+    grad_tokens = unshifted_sum(grads_out, grad_branch, arrived)
     return (grad_tokens, gain_grad.reshape(-1), qkv_grad.reshape(-1), proj_grad.reshape(-1))
 
 

time: 169 us -> 178 us (1.053)
  waiting for transfers between devices: 35.1 us -> 41.2 us
  starting transfers between devices: 23.5 us -> 25.8 us
    ppermute x10, starting transfers between devices: 7.18 us -> 13.3 us  [swapped(): lax.ppermute(block, axis, [(i, i ^ distance) for i in range(lax.axis_size...]
    ppermute x6, starting transfers between devices: 16.4 us -> 12.5 us  [moved(): lax.ppermute(block, ('gx', 'gy', 'gz'), halo_route(distance_a, distance_b))]
    ppermute x6, waiting for transfers between devices: 12.9 us -> 16 us  [moved(): lax.ppermute(block, ('gx', 'gy', 'gz'), halo_route(distance_a, distance_b))]
    ppermute x10, waiting for transfers between devices: 22.2 us -> 25.2 us  [swapped(): lax.ppermute(block, axis, [(i, i ^ distance) for i in range(lax.axis_size...]
where the time goes in v5:
time: 178 us; the launch traced here: 177 us
  Pallas kernels  79.1 us (44%)
  waiting for transfers between devices  41.2 us (23%)
  starting transfers between devices  25.8 us (14%)
  other arithmetic  15.1 us (8%)
  local copies, waits for them, and re-layouts  14.7 us (8%)
    pallas_call x1, Pallas kernels, window_grads(): pl.pallas_call(window_kernel, out_shape=[jax.ShapeDtypeStruct((extent_a,...  79.1 us
    ppermute x10, waiting for transfers between devices, swapped(): lax.ppermute(block, axis, [(i, i ^ distance) for i in range(lax.axis_size...  25.2 us
    ppermute x6, waiting for transfers between devices, moved(): lax.ppermute(block, ('gx', 'gy', 'gz'), halo_route(distance_a, distance_b))  16 us
    ppermute x10, starting transfers between devices, swapped(): lax.ppermute(block, axis, [(i, i ^ distance) for i in range(lax.axis_size...  13.3 us
    ppermute x6, starting transfers between devices, moved(): lax.ppermute(block, ('gx', 'gy', 'gz'), halo_route(distance_a, distance_b))  12.5 us
    another operation x4, other arithmetic, per_device(): both = shifted_block(jnp.stack([tokens, grads_out]))  4.88 us
    concatenate x1, other arithmetic, shifted_block(): return jnp.concatenate([upper, lower], axis=1)  3.72 us
  transfers between devices with their start and end apart: 16, of which 13 were waited for; matrix products, arithmetic and copies ran while one was open for 8% of the time, Pallas kernels for 0%

profile of v5, /device:TPU:5, one launch (start us, length us, event | category | flops | bytes accessed | tf_op | source)
XLA Modules:
  0.0 177.0 jit_solution(2760526880184130283)
XLA Ops:
  0.7 1.5 fusion.2
  2.2 1.3 copy.17
  3.5 3.3 %collective-permute-start.1 = (bf16[2,4,12,3072]{3,1,2,0:T(4,128)(2,1)}, bf16[2,4,12,3072]{3,1,2,0:T(4,128)(2,1)}, u32[]{:S(2)}, u32[]{:S(2)}) collective-permute-start(bf16[2,4,12,3072]{3,1,2,0:T(4,128)(2,1)} %copy.17), channel_id=1, source_target_pairs={{0,24},{1,25},{2,26},{3,27},{4,28},{5,29},{6,30},{7,31},{8,0},{9,1... | collective-permute-start | bytes 1769480 | tf_op jit(solution)/shard_map/ppermute | solution.py:212
  6.8 1.1 fusion.3
  7.8 0.2 collective-permute-start
  8.1 2.0 %collective-permute-start.2 = (bf16[2,4,4,3072]{3,2,1,0:T(4,128)(2,1)S(1)}, bf16[2,4,4,3072]{3,2,1,0:T(4,128)(2,1)S(1)}, u32[]{:S(2)}, u32[]{:S(2)}) collective-permute-start(bf16[2,4,4,3072]{3,2,1,0:T(4,128)(2,1)S(1)} %pad_maximum_fusion.1), channel_id=1, source_target_pairs={{0,31},{1,24},{2,25},{3,26},{4,27},{5,28},{6,29},{7,30},{8,7},{9,0... | collective-permute-start | bytes 589832 | tf_op jit(solution)/shard_map/ppermute | solution.py:212
  10.2 2.2 %fusion.1 = bf16[2,12,12,3072]{3,2,1,0:T(8,128)(2,1)} fusion(bf16[1,16,16,3072]{3,2,1,0:T(8,128)(2,1)S(1)} %bitcast.17, bf16[1,16,16,3072]{3,2,1,0:T(8,128)(2,1)S(1)} %bitcast.13), kind=kLoop, calls=%fused_computation.9 | loop fusion | flops 884736 | bytes 4915200 | tf_op jit(solution)/shard_map/stack | solution.py:244
  12.6 0.2 reshape.84
  12.8 0.2 copy.19
  12.9 2.0 %broadcast_in_dim_reshape.8.kcol_ref = s32[8,512,1]{2,1,0:T(8,128)} reshape(s32[2,2,2,8,8,8]{5,4,3,2,1,0:T(8,128)S(1)} %bitcast.18) | data formatting | bytes 32768 | tf_op jit(solution)/shard_map/broadcast_in_dim;reshape | solution.py:259
  14.9 0.8 broadcast_in_dim_reshape.7.krow_ref
  15.7 0.9 copy.20
  16.6 0.8 copy.22.gain_ref
  17.3 1.8 collective-permute-done.1
  19.1 1.3 copy.18
  20.3 3.5 %collective-permute-done.2 = bf16[2,4,4,3072]{3,2,1,0:T(4,128)(2,1)S(1)} collective-permute-done((bf16[2,4,4,3072]{3,2,1,0:T(4,128)(2,1)S(1)}, bf16[2,4,4,3072]{3,2,1,0:T(4,128)(2,1)S(1)}, u32[]{:S(2)}, u32[]{:S(2)}) %collective-permute-start.2) | collective-permute-done | bytes 196640 | tf_op jit(solution)/shard_map/ppermute | solution.py:212
  23.9 0.4 collective-permute-done
  24.3 3.7 %maximum_maximum_fusion.both_ref = bf16[2,16,16,3072]{3,2,1,0:T(8,128)(2,1)} fusion(bf16[2,4,4,3072]{3,2,1,0:T(4,128)(2,1)S(1)} %collective-permute-done.2, bf16[2,4,12,3072]{3,2,1,0:T(8,128)(2,1)S(1)} %copy.18, bf16[2,12,4,3072]{3,2,1,0:T(4,128)(2,1)} %collective-permute-done, bf16[2,12,12,3072]{3,2,1,0:T(8,128)(2,1)} %fusion.1), kind=kLoop, calls=%fused_computation.6 | loop fusion | flops 12582912 | bytes 6291456 | tf_op jit(solution)/shard_map/concatenate | solution.py:221
  28.0 79.1 %shard_map.93 = (f32[16,16,3072]{2,1,0:T(8,128)}, f32[576,192]{1,0:T(8,128)}, f32[192,192]{1,0:T(8,128)}, f32[192,1]{1,0:T(8,128)}) custom-call(bf16[2,16,16,3072]{3,2,1,0:T(8,128)(2,1)} %maximum_maximum_fusion.both_ref, s32[8,512,1]{2,1,0:T(8,128)} %broadcast_in_dim_reshape.8.kcol_ref, s32[8,1,512]{2,1,0:T(1,128)} %broadcast_in_dim_reshape.7.krow_ref, ...), custom_call_target="tpu_custom_call" | custom-call | tf_op jit(solution)/shard_map/pallas_call | solution.py:141
  107.1 2.2 %convert_element_type.27 = bf16[16,16,3072]{2,1,0:T(8,128)(2,1)S(1)} convert(f32[16,16,3072]{2,1,0:T(8,128)} %get-tuple-element.14) | non-fusion elementwise | flops 786432 | bytes 4718592 | tf_op jit(solution)/shard_map/convert_element_type | solution.py:225
  109.4 0.9 slice.56
  110.2 0.9 collective-permute-start.3
  111.1 4.0 %collective-permute-start.4 = (bf16[12,4,3072]{2,1,0:T(4,128)(2,1)}, bf16[12,4,3072]{2,1,0:T(4,128)(2,1)S(1)}, u32[]{:S(2)}, u32[]{:S(2)}) collective-permute-start(bf16[12,4,3072]{2,1,0:T(4,128)(2,1)} %slice.56), channel_id=1, source_target_pairs={{0,1},{1,2},{2,3},{3,4},{4,5},{5,6},{6,7},{7,0},{8,9},{9,10},{10,1... | collective-permute-start | bytes 884744 | tf_op jit(solution)/shard_map/ppermute | solution.py:212
  115.2 2.0 %collective-permute-start.5 = (bf16[4,4,3072]{2,1,0:T(4,128)(2,1)S(1)}, bf16[4,4,3072]{2,1,0:T(4,128)(2,1)S(1)}, u32[]{:S(2)}, u32[]{:S(2)}) collective-permute-start(bf16[4,4,3072]{2,1,0:T(4,128)(2,1)S(1)} %slice.57), channel_id=1, source_target_pairs={{0,9},{1,10},{2,11},{3,12},{4,13},{5,14},{6,15},{7,8},{8,17},{9,18... | collective-permute-start | bytes 294920 | tf_op jit(solution)/shard_map/ppermute | solution.py:212
  117.2 10.4 %collective-permute-done.5 = bf16[4,4,3072]{2,1,0:T(4,128)(2,1)S(1)} collective-permute-done((bf16[4,4,3072]{2,1,0:T(4,128)(2,1)S(1)}, bf16[4,4,3072]{2,1,0:T(4,128)(2,1)S(1)}, u32[]{:S(2)}, u32[]{:S(2)}) %collective-permute-start.5) | collective-permute-done | bytes 98336 | tf_op jit(solution)/shard_map/ppermute | solution.py:212
  127.6 0.3 reshape.86
  127.9 1.0 reshape.87
  128.9 1.0 reduce
  130.2 1.4 collective-permute-start.6
  131.6 1.2 collective-permute-done.6
  133.1 1.3 collective-permute-start.7
  134.4 3.9 %collective-permute-done.7 = f32[36912]{0:T(1024)S(1)} collective-permute-done((f32[36912]{0:T(1024)S(1)}, f32[36912]{0:T(1024)S(1)}, u32[]{:S(2)}, u32[]{:S(2)}) %collective-permute-start.7) | collective-permute-done | bytes 147680 | tf_op jit(solution)/shard_map/ppermute | solution.py:161
  138.6 3.2 %collective-permute-done.8 = f32[18456]{0:T(1024)S(1)} collective-permute-done((f32[18456]{0:T(1024)S(1)}, f32[18456]{0:T(1024)S(1)}, u32[]{:S(2)}, u32[]{:S(2)}) %collective-permute-start.8) | collective-permute-done | bytes 73856 | tf_op jit(solution)/shard_map/ppermute | solution.py:161
  142.1 3.9 %collective-permute-done.9 = f32[9228]{0:T(1024)S(1)} collective-permute-done((f32[9228]{0:T(1024)S(1)}, f32[9228]{0:T(1024)S(1)}, u32[]{:S(2)}, u32[]{:S(2)}) %collective-permute-start.9) | collective-permute-done | bytes 36944 | tf_op jit(solution)/shard_map/ppermute | solution.py:161
  146.2 2.7 %collective-permute-done.10 = f32[4614]{0:T(1024)S(1)} collective-permute-done((f32[4614]{0:T(1024)S(1)}, f32[4614]{0:T(1024)S(1)}, u32[]{:S(2)}, u32[]{:S(2)}) %collective-permute-start.10) | collective-permute-done | bytes 18488 | tf_op jit(solution)/shard_map/ppermute | solution.py:161
  149.0 2.6 %collective-permute-done.11 = f32[4614]{0:T(1024)S(1)} collective-permute-done((f32[4614]{0:T(1024)S(1)}, f32[4614]{0:T(1024)S(1)}, u32[]{:S(2)}, u32[]{:S(2)}) %collective-permute-start.11) | collective-permute-done | bytes 18488 | tf_op jit(solution)/shard_map/ppermute | solution.py:161
  151.8 3.7 %collective-permute-done.12 = f32[9228]{0:T(1024)S(1)} collective-permute-done((f32[9228]{0:T(1024)S(1)}, f32[9228]{0:T(1024)S(1)}, u32[]{:S(2)}, u32[]{:S(2)}) %collective-permute-start.12) | collective-permute-done | bytes 36944 | tf_op jit(solution)/shard_map/ppermute | solution.py:161
  155.7 1.9 %slice.44 = f32[12,12,3072]{2,1,0:T(8,128)S(1)} slice(f32[16,16,3072]{2,1,0:T(8,128)} %get-tuple-element.14), slice={[0:12], [0:12], [0:3072]} | slice | bytes 3538944 | tf_op jit(solution)/shard_map/slice | solution.py:235
  157.7 1.3 collective-permute-done.13
  159.0 1.3 collective-permute-start.14
  160.5 2.6 %collective-permute-done.14 = f32[36912]{0:T(1024)S(1)} collective-permute-done((f32[36912]{0:T(1024)S(1)}, f32[36912]{0:T(1024)S(1)}, u32[]{:S(2)}, u32[]{:S(2)}) %collective-permute-start.14) | collective-permute-done | bytes 147680 | tf_op jit(solution)/shard_map/ppermute | solution.py:161
  163.3 9.0 %collective-permute-start.15 = (f32[73824]{0:T(1024)S(1)}, f32[73824]{0:T(1024)S(1)}, u32[]{:S(2)}, u32[]{:S(2)}) collective-permute-start(f32[73824]{0:T(1024)S(1)} %maximum_select_fusion.1), channel_id=1, source_target_pairs={{0,2},{2,0},{4,6},{6,4},{1,3},{3,1},{5,7},{7,5},{8,10},{10,8},{12,... | collective-permute-start | bytes 885896 | tf_op jit(solution)/shard_map/ppermute | solution.py:161
  172.3 1.8 %fusion = bf16[16,16,3072]{2,1,0:T(8,128)(2,1)} fusion(f32[12,12,3072]{2,1,0:T(8,128)S(1)} %slice.44, f32[12,4,3072]{2,1,0:T(4,128)S(1)} %convert_element_type.28, f32[4,16,3072]{2,1,0:T(8,128)S(1)} %maximum_convert_fusion, bf16[16,16,3072]{2,1,0:T(8,128)(2,1)S(1)} %copy-done), kind=kLoop, calls=%fused_computation.8 | loop fusion | flops 3932160 | bytes 6291456 | tf_op jit(solution)/shard_map/convert_element_type | solution.py:237
  174.1 0.2 maximum_select_fusion
  174.4 0.7 slice.60
  175.1 0.6 slice.58
  175.8 0.2 copy.23
  176.0 1.0 reshape.89
  (51 shorter events, 2.5 us)
Async XLA Ops:
  0.6 6.1 %copy-start.1 = (bf16[16,16,3072]{2,1,0:T(8,128)(2,1)S(1)}, bf16[16,16,3072]{2,1,0:T(8,128)(2,1)}, u32[]{:S(2)}) copy-start(bf16[16,16,3072]{2,1,0:T(8,128)(2,1)} %param.6) | copy-start | bytes 4718596
  0.6 6.1 %copy-start = (bf16[16,16,3072]{2,1,0:T(8,128)(2,1)S(1)}, bf16[16,16,3072]{2,1,0:T(8,128)(2,1)}, u32[]{:S(2)}) copy-start(bf16[16,16,3072]{2,1,0:T(8,128)(2,1)} %param.7) | copy-start | bytes 4718596
  3.5 15.6 %collective-permute-start.1 = (bf16[2,4,12,3072]{3,1,2,0:T(4,128)(2,1)}, bf16[2,4,12,3072]{3,1,2,0:T(4,128)(2,1)}, u32[]{:S(2)}, u32[]{:S(2)}) collective-permute-start(bf16[2,4,12,3072]{3,1,2,0:T(4,128)(2,1)} %copy.17), channel_id=1, source_target_pairs={{0,24},{1,25},{2,26},{3,27},{4,28},{5,29},{6,30},{7,31},{8,0},{9,1... | collective-permute-start | bytes 1769480 | tf_op jit(solution)/shard_map/ppermute | solution.py:212
  7.8 16.4 %collective-permute-start = (bf16[2,12,4,3072]{3,2,1,0:T(4,128)(2,1)}, bf16[2,12,4,3072]{3,2,1,0:T(4,128)(2,1)}, u32[]{:S(2)}, u32[]{:S(2)}) collective-permute-start(bf16[2,12,4,3072]{3,2,1,0:T(4,128)(2,1)} %fusion.3), channel_id=1, source_target_pairs={{0,7},{1,0},{2,1},{3,2},{4,3},{5,4},{6,5},{7,6},{8,15},{9,8},{10,9... | collective-permute-start | bytes 1769480 | tf_op jit(solution)/shard_map/ppermute | solution.py:212
  8.1 15.7 %collective-permute-start.2 = (bf16[2,4,4,3072]{3,2,1,0:T(4,128)(2,1)S(1)}, bf16[2,4,4,3072]{3,2,1,0:T(4,128)(2,1)S(1)}, u32[]{:S(2)}, u32[]{:S(2)}) collective-permute-start(bf16[2,4,4,3072]{3,2,1,0:T(4,128)(2,1)S(1)} %pad_maximum_fusion.1), channel_id=1, source_target_pairs={{0,31},{1,24},{2,25},{3,26},{4,27},{5,28},{6,29},{7,30},{8,7},{9,0... | collective-permute-start | bytes 589832 | tf_op jit(solution)/shard_map/ppermute | solution.py:212
  10.2 2.3 %copy-start.6 = (s32[16,16,16]{2,1,0:T(8,128)S(1)}, s32[16,16,16]{2,1,0:T(8,128)}, u32[]{:S(2)}) copy-start(s32[16,16,16]{2,1,0:T(8,128)} %param.8) | copy-start | bytes 49156
  12.5 3.2 %copy-start.2 = (bf16[192,576]{1,0:T(8,128)(2,1)S(1)}, bf16[192,576]{1,0:T(8,128)(2,1)}, u32[]{:S(2)}) copy-start(bf16[192,576]{1,0:T(8,128)(2,1)} %wqkv_ref.1) | copy-start | bytes 663556
  12.5 4.1 %copy-start.7 = (f32[192]{0:T(256)S(1)}, f32[192]{0:T(256)}, u32[]{:S(2)}) copy-start(f32[192]{0:T(256)} %param.9) | copy-start | bytes 2308
  107.1 20.4 %copy-start.3 = (f32[576,192]{1,0:T(8,128)S(1)}, f32[576,192]{1,0:T(8,128)}, u32[]{:S(2)}) copy-start(f32[576,192]{1,0:T(8,128)} %get-tuple-element.21) | copy-start | bytes 1327108
  110.2 17.3 %collective-permute-start.3 = (bf16[4,12,3072]{2,1,0:T(8,128)(2,1)S(1)}, bf16[4,12,3072]{2,1,0:T(8,128)(2,1)S(1)}, u32[]{:S(2)}, u32[]{:S(2)}) collective-permute-start(bf16[4,12,3072]{2,1,0:T(8,128)(2,1)S(1)} %slice.55), channel_id=1, source_target_pairs={{0,8},{1,9},{2,10},{3,11},{4,12},{5,13},{6,14},{7,15},{8,16},{9,17... | collective-permute-start | bytes 884744 | tf_op jit(solution)/shard_map/ppermute | solution.py:212
  111.1 16.5 %collective-permute-start.4 = (bf16[12,4,3072]{2,1,0:T(4,128)(2,1)}, bf16[12,4,3072]{2,1,0:T(4,128)(2,1)S(1)}, u32[]{:S(2)}, u32[]{:S(2)}) collective-permute-start(bf16[12,4,3072]{2,1,0:T(4,128)(2,1)} %slice.56), channel_id=1, source_target_pairs={{0,1},{1,2},{2,3},{3,4},{4,5},{5,6},{6,7},{7,0},{8,9},{9,10},{10,1... | collective-permute-start | bytes 884744 | tf_op jit(solution)/shard_map/ppermute | solution.py:212
  115.2 12.4 %collective-permute-start.5 = (bf16[4,4,3072]{2,1,0:T(4,128)(2,1)S(1)}, bf16[4,4,3072]{2,1,0:T(4,128)(2,1)S(1)}, u32[]{:S(2)}, u32[]{:S(2)}) collective-permute-start(bf16[4,4,3072]{2,1,0:T(4,128)(2,1)S(1)} %slice.57), channel_id=1, source_target_pairs={{0,9},{1,10},{2,11},{3,12},{4,13},{5,14},{6,15},{7,8},{8,17},{9,18... | collective-permute-start | bytes 294920 | tf_op jit(solution)/shard_map/ppermute | solution.py:212
  127.6 2.4 %copy-start.4 = (bf16[12,4,3072]{2,1,0:T(4,128)(2,1)}, bf16[12,4,3072]{2,1,0:T(4,128)(2,1)S(1)}, u32[]{:S(2)}) copy-start(bf16[12,4,3072]{2,1,0:T(4,128)(2,1)S(1)} %collective-permute-done.4) | copy-start | bytes 884740
  130.2 2.6 %collective-permute-start.6 = (f32[73824]{0:T(1024)S(1)}, f32[73824]{0:T(1024)S(1)}, u32[]{:S(2)}, u32[]{:S(2)}) collective-permute-start(f32[73824]{0:T(1024)S(1)} %dynamic_slice.31), channel_id=1, source_target_pairs={{0,2},{2,0},{4,6},{6,4},{1,3},{3,1},{5,7},{7,5},{8,10},{10,8},{12,... | collective-permute-start | bytes 885896 | tf_op jit(solution)/shard_map/ppermute | solution.py:161
  133.1 5.2 %collective-permute-start.7 = (f32[36912]{0:T(1024)S(1)}, f32[36912]{0:T(1024)S(1)}, u32[]{:S(2)}, u32[]{:S(2)}) collective-permute-start(f32[36912]{0:T(1024)S(1)} %dynamic_slice.33), channel_id=1, source_target_pairs={{0,4},{2,6},{4,0},{6,2},{1,5},{3,7},{5,1},{7,3},{8,12},{10,14},{12... | collective-permute-start | bytes 442952 | tf_op jit(solution)/shard_map/ppermute | solution.py:161
  138.5 3.3 %collective-permute-start.8 = (f32[18456]{0:T(1024)S(1)}, f32[18456]{0:T(1024)S(1)}, u32[]{:S(2)}, u32[]{:S(2)}) collective-permute-start(f32[18456]{0:T(1024)S(1)} %dynamic_slice.35), channel_id=1, source_target_pairs={{0,8},{8,0},{16,24},{24,16},{1,9},{9,1},{17,25},{25,17},{2,10},{10... | collective-permute-start | bytes 221480 | tf_op jit(solution)/shard_map/ppermute | solution.py:161
  142.0 3.9 %collective-permute-start.9 = (f32[9228]{0:T(1024)S(1)}, f32[9228]{0:T(1024)S(1)}, u32[]{:S(2)}, u32[]{:S(2)}) collective-permute-start(f32[9228]{0:T(1024)S(1)} %dynamic_slice.37), channel_id=1, source_target_pairs={{0,16},{8,24},{16,0},{24,8},{1,17},{9,25},{17,1},{25,9},{2,18},{10... | collective-permute-start | bytes 110744 | tf_op jit(solution)/shard_map/ppermute | solution.py:161
  146.1 2.8 %collective-permute-start.10 = (f32[4614]{0:T(1024)S(1)}, f32[4614]{0:T(1024)S(1)}, u32[]{:S(2)}, u32[]{:S(2)}) collective-permute-start(f32[4614]{0:T(1024)S(1)} %dynamic_slice.39), channel_id=1, source_target_pairs={{0,1},{1,0},{2,3},{3,2},{4,5},{5,4},{6,7},{7,6},{8,9},{9,8},{10,11... | collective-permute-start | bytes 55376 | tf_op jit(solution)/shard_map/ppermute | solution.py:161
  149.0 2.6 %collective-permute-start.11 = (f32[4614]{0:T(1024)S(1)}, f32[4614]{0:T(1024)S(1)}, u32[]{:S(2)}, u32[]{:S(2)}) collective-permute-start(f32[4614]{0:T(1024)S(1)} %dynamic-slice_add_fusion.4), channel_id=1, source_target_pairs={{0,1},{1,0},{2,3},{3,2},{4,5},{5,4},{6,7},{7,6},{8,9},{9,8},{10,11... | collective-permute-start | bytes 55376 | tf_op jit(solution)/shard_map/ppermute | solution.py:161
  151.7 3.8 %collective-permute-start.12 = (f32[9228]{0:T(1024)S(1)}, f32[9228]{0:T(1024)S(1)}, u32[]{:S(2)}, u32[]{:S(2)}) collective-permute-start(f32[9228]{0:T(1024)S(1)} %maximum_select_fusion.4), channel_id=1, source_target_pairs={{0,16},{8,24},{16,0},{24,8},{1,17},{9,25},{17,1},{25,9},{2,18},{10... | collective-permute-start | bytes 110744 | tf_op jit(solution)/shard_map/ppermute | solution.py:161
  155.6 3.3 %collective-permute-start.13 = (f32[18456]{0:T(1024)S(1)}, f32[18456]{0:T(1024)S(1)}, u32[]{:S(2)}, u32[]{:S(2)}) collective-permute-start(f32[18456]{0:T(1024)S(1)} %maximum_select_fusion.3), channel_id=1, source_target_pairs={{0,8},{8,0},{16,24},{24,16},{1,9},{9,1},{17,25},{25,17},{2,10},{10... | collective-permute-start | bytes 221480 | tf_op jit(solution)/shard_map/ppermute | solution.py:161
  155.7 4.7 %copy-start.5 = (bf16[12,4,3072]{2,1,0:T(4,128)(2,1)S(1)}, bf16[12,4,3072]{2,1,0:T(4,128)(2,1)}, u32[]{:S(2)}) copy-start(bf16[12,4,3072]{2,1,0:T(4,128)(2,1)} %copy-done.4) | copy-start | bytes 884740
  159.0 4.1 %collective-permute-start.14 = (f32[36912]{0:T(1024)S(1)}, f32[36912]{0:T(1024)S(1)}, u32[]{:S(2)}, u32[]{:S(2)}) collective-permute-start(f32[36912]{0:T(1024)S(1)} %maximum_select_fusion.2), channel_id=1, source_target_pairs={{0,4},{2,6},{4,0},{6,2},{1,5},{3,7},{5,1},{7,3},{8,12},{10,14},{12... | collective-permute-start | bytes 442952 | tf_op jit(solution)/shard_map/ppermute | solution.py:161
  163.3 10.8 %collective-permute-start.15 = (f32[73824]{0:T(1024)S(1)}, f32[73824]{0:T(1024)S(1)}, u32[]{:S(2)}, u32[]{:S(2)}) collective-permute-start(f32[73824]{0:T(1024)S(1)} %maximum_select_fusion.1), channel_id=1, source_target_pairs={{0,2},{2,0},{4,6},{6,4},{1,3},{3,1},{5,7},{7,5},{8,10},{10,8},{12,... | collective-permute-start | bytes 885896 | tf_op jit(solution)/shard_map/ppermute | solution.py:161

commit v6 on v4

--- a/solution.py
+++ b/solution.py
@@ -39,107 +39,142 @@
     return shaped.transpose(0, 2, 4, 5, 1, 3).reshape(-1, CELLS)
 
 
-def window_kernel(both_ref, kcol_ref, krow_ref, gain_ref, wqkvT_ref, wqkv_ref, wp_ref,
-                  gs_ref, gqkvT_ref, gproj_ref, ggain_ref, qkv_s, ga_s, drow_s):
-    f32 = jnp.float32
-    bf16 = jnp.bfloat16
-    gqkvT_ref[...] = jnp.zeros_like(gqkvT_ref)
-    gproj_ref[...] = jnp.zeros_like(gproj_ref)
-    ggain_ref[...] = jnp.zeros_like(ggain_ref)
-    gain = gain_ref[...]
-    nt = (((1,), (1,)), ((), ()))
-    pair = 2 * C
-    n_pairs = NZ // 2
-
-    def gathered(which, i, j, l):
-        pieces = []
-        for q in range(WIN // 2):
-            p = (WIN // 2 * l + SHIFT // 2 + q) % n_pairs
-            block = both_ref[which, pl.ds(i * WIN, WIN), :, pl.ds(p * pair, pair)].astype(f32)
-            block = jnp.where(j == 0, block[:, :WIN], block[:, WIN:]).reshape(WIN * WIN, pair)
-            pieces.append(block[:, :C])
-            pieces.append(block[:, C:])
-        return jnp.concatenate(pieces, axis=0).T
-
-    def scattered(values_t, i, j, l):
-        rows = values_t.T
-        for q in range(WIN // 2):
-            p = (WIN // 2 * l + SHIFT // 2 + q) % n_pairs
-            even = rows[2 * q * WIN * WIN:(2 * q + 1) * WIN * WIN]
-            odd = rows[(2 * q + 1) * WIN * WIN:(2 * q + 2) * WIN * WIN]
-            block = jnp.concatenate([even, odd], axis=1).reshape(WIN, WIN, pair)
-            gs_ref[pl.ds(i * WIN, WIN), pl.ds(pl.multiple_of(j * WIN, WIN), WIN), pl.ds(p * pair, pair)] = block
-
-    def window(ij, l):
-        i = ij // 2
-        j = ij % 2
-        w = ij * 2 + l
-        x = gathered(0, i, j, l)
-        row_mean = jnp.mean(x, axis=0, keepdims=True)
-        centred = x - row_mean
-        inv_std = lax.rsqrt(jnp.mean(centred * centred, axis=0, keepdims=True) + 1e-05)
-        x_hat = centred * inv_std
-        normed = (x_hat * gain).astype(bf16)
-        qkv_t = jnp.dot(wqkvT_ref[...], normed, preferred_element_type=f32)
-        qkv_s[...] = qkv_t.astype(bf16).astype(f32)
-        g = gathered(1, i, j, l).astype(bf16)
-        ga_t = jnp.dot(wp_ref[...], g, preferred_element_type=f32)
-        ga_s[...] = ga_t.astype(bf16).astype(f32)
-        allowed = kcol_ref[w] == krow_ref[w]
-
-        def head_step(h, carry):
-            qo = pl.multiple_of(h * HEAD, HEAD)
-            q_t = qkv_s[pl.ds(qo, HEAD), :]
-            k_t = qkv_s[pl.ds(qo + C, HEAD), :]
-            v_t = qkv_s[pl.ds(qo + 2 * C, HEAD), :]
-            ga_th = ga_s[pl.ds(qo, HEAD), :]
-            q = q_t.T.astype(bf16)
-            scores = jnp.dot(q, k_t.astype(bf16), preferred_element_type=f32) * SCALE
-            weights = jnp.where(allowed, jnp.exp(scores), 0.0)
-            probs = weights / jnp.sum(weights, axis=1, keepdims=True)
-            probs_bf = probs.astype(bf16)
-            att_t = lax.dot_general(v_t.astype(bf16), probs_bf, nt, preferred_element_type=f32)
-            att_t = att_t.astype(bf16)
-            gproj_ref[pl.ds(qo, HEAD), :] += lax.dot_general(
-                att_t, g, nt, preferred_element_type=f32
+def make_window_kernel(first):
+    def window_kernel(*refs):
+        if first:
+            (tok_ref, grd_ref, kcol_ref, krow_ref, gain_ref, wqkvT_ref, wqkv_ref, wp_ref,
+             gs_ref, gqkvT_ref, gproj_ref, ggain_ref, qkv_s, ga_s, drow_s) = refs
+        else:
+            (both_ref, kcol_ref, krow_ref, gain_ref, wqkvT_ref, wqkv_ref, wp_ref,
+             gs0_ref, gqkvT0_ref, gproj0_ref, ggain0_ref,
+             gs_ref, gqkvT_ref, gproj_ref, ggain_ref, qkv_s, ga_s, drow_s) = refs
+        f32 = jnp.float32
+        bf16 = jnp.bfloat16
+        if first:
+            gqkvT_ref[...] = jnp.zeros_like(gqkvT_ref)
+            gproj_ref[...] = jnp.zeros_like(gproj_ref)
+            ggain_ref[...] = jnp.zeros_like(ggain_ref)
+        else:
+            gqkvT_ref[...] = gqkvT0_ref[...]
+            gproj_ref[...] = gproj0_ref[...]
+            ggain_ref[...] = ggain0_ref[...]
+            gs_ref[pl.ds(0, WIN), pl.ds(0, WIN), :] = gs0_ref[...]
+        gain = gain_ref[...]
+        nt = (((1,), (1,)), ((), ()))
+        pair = 2 * C
+        n_pairs = NZ // 2
+
+        def gathered(which, i, j, l):
+            pieces = []
+            for q in range(WIN // 2):
+                p = (WIN // 2 * l + SHIFT // 2 + q) % n_pairs
+                if first:
+                    source = (tok_ref, grd_ref)[which]
+                    block = source[pl.ds(SHIFT, WIN), :, pl.ds(p * pair, pair)].astype(f32)
+                    block = block[:, SHIFT:SHIFT + WIN]
+                else:
+                    block = both_ref[which, pl.ds(i * WIN, WIN), :, pl.ds(p * pair, pair)]
+                    block = block.astype(f32)
+                    block = jnp.where(j == 0, block[:, :WIN], block[:, WIN:])
+                block = block.reshape(WIN * WIN, pair)
+                pieces.append(block[:, :C])
+                pieces.append(block[:, C:])
+            return jnp.concatenate(pieces, axis=0).T
+
+        def scattered(values_t, i, j, l):
+            rows = values_t.T
+            for q in range(WIN // 2):
+                p = (WIN // 2 * l + SHIFT // 2 + q) % n_pairs
+                even = rows[2 * q * WIN * WIN:(2 * q + 1) * WIN * WIN]
+                odd = rows[(2 * q + 1) * WIN * WIN:(2 * q + 2) * WIN * WIN]
+                block = jnp.concatenate([even, odd], axis=1).reshape(WIN, WIN, pair)
+                if first:
+                    gs_ref[:, :, pl.ds(p * pair, pair)] = block
+                else:
+                    gs_ref[
+                        pl.ds(i * WIN, WIN),
+                        pl.ds(pl.multiple_of(j * WIN, WIN), WIN),
+                        pl.ds(p * pair, pair),
+                    ] = block
+
+        def window(ij, l):
+            i = ij // 2
+            j = ij % 2
+            w = ij * 2 + l
+            x = gathered(0, i, j, l)
+            row_mean = jnp.mean(x, axis=0, keepdims=True)
+            centred = x - row_mean
+            inv_std = lax.rsqrt(jnp.mean(centred * centred, axis=0, keepdims=True) + 1e-05)
+            x_hat = centred * inv_std
+            normed = (x_hat * gain).astype(bf16)
+            qkv_t = jnp.dot(wqkvT_ref[...], normed, preferred_element_type=f32)
+            qkv_s[...] = qkv_t.astype(bf16).astype(f32)
+            g = gathered(1, i, j, l).astype(bf16)
+            ga_t = jnp.dot(wp_ref[...], g, preferred_element_type=f32)
+            ga_s[...] = ga_t.astype(bf16).astype(f32)
+            allowed = kcol_ref[w] == krow_ref[w]
+
+            def head_step(h, carry):
+                qo = pl.multiple_of(h * HEAD, HEAD)
+                q_t = qkv_s[pl.ds(qo, HEAD), :]
+                k_t = qkv_s[pl.ds(qo + C, HEAD), :]
+                v_t = qkv_s[pl.ds(qo + 2 * C, HEAD), :]
+                ga_th = ga_s[pl.ds(qo, HEAD), :]
+                q = q_t.T.astype(bf16)
+                scores = jnp.dot(q, k_t.astype(bf16), preferred_element_type=f32) * SCALE
+                weights = jnp.where(allowed, jnp.exp(scores), 0.0)
+                probs = weights / jnp.sum(weights, axis=1, keepdims=True)
+                probs_bf = probs.astype(bf16)
+                att_t = lax.dot_general(v_t.astype(bf16), probs_bf, nt, preferred_element_type=f32)
+                att_t = att_t.astype(bf16)
+                gproj_ref[pl.ds(qo, HEAD), :] += lax.dot_general(
+                    att_t, g, nt, preferred_element_type=f32
+                )
+                ga = ga_th.T.astype(bf16)
+                grad_probs = jnp.dot(ga, v_t.astype(bf16), preferred_element_type=f32)
+                dv_t = jnp.dot(ga_th.astype(bf16), probs_bf, preferred_element_type=f32)
+                row_total = jnp.sum(probs * grad_probs, axis=1, keepdims=True)
+                grad_scores = (probs * (grad_probs - row_total) * SCALE).astype(bf16)
+                dq_t = lax.dot_general(k_t.astype(bf16), grad_scores, nt, preferred_element_type=f32)
+                dk_t = jnp.dot(q_t.astype(bf16), grad_scores, preferred_element_type=f32)
+                drow_s[pl.ds(qo, HEAD), :] = dq_t.astype(bf16).astype(f32)
+                drow_s[pl.ds(qo + C, HEAD), :] = dk_t.astype(bf16).astype(f32)
+                drow_s[pl.ds(qo + 2 * C, HEAD), :] = dv_t.astype(bf16).astype(f32)
+                return carry
+
+            lax.fori_loop(0, HEADS, head_step, 0)
+            rows_t = drow_s[...].astype(bf16)
+            gqkvT_ref[...] += lax.dot_general(rows_t, normed, nt, preferred_element_type=f32)
+            grad_normed = jnp.dot(wqkv_ref[...], rows_t, preferred_element_type=f32)
+            ggain_ref[...] += jnp.sum(grad_normed * x_hat, axis=1, keepdims=True)
+            scaled = grad_normed * gain
+            grad_shifted = inv_std * (
+                scaled
+                - jnp.mean(scaled, axis=0, keepdims=True)
+                - x_hat * jnp.mean(scaled * x_hat, axis=0, keepdims=True)
             )
-            ga = ga_th.T.astype(bf16)
-            grad_probs = jnp.dot(ga, v_t.astype(bf16), preferred_element_type=f32)
-            dv_t = jnp.dot(ga_th.astype(bf16), probs_bf, preferred_element_type=f32)
-            row_total = jnp.sum(probs * grad_probs, axis=1, keepdims=True)
-            grad_scores = (probs * (grad_probs - row_total) * SCALE).astype(bf16)
-            dq_t = lax.dot_general(k_t.astype(bf16), grad_scores, nt, preferred_element_type=f32)
-            dk_t = jnp.dot(q_t.astype(bf16), grad_scores, preferred_element_type=f32)
-            drow_s[pl.ds(qo, HEAD), :] = dq_t.astype(bf16).astype(f32)
-            drow_s[pl.ds(qo + C, HEAD), :] = dk_t.astype(bf16).astype(f32)
-            drow_s[pl.ds(qo + 2 * C, HEAD), :] = dv_t.astype(bf16).astype(f32)
+            scattered(grad_shifted.astype(bf16).astype(f32), i, j, l)
+
+        def block_step(ij, carry):
+            for l in range(2):
+                window(ij, l)
             return carry
 
-        lax.fori_loop(0, HEADS, head_step, 0)
-        rows_t = drow_s[...].astype(bf16)
-        gqkvT_ref[...] += lax.dot_general(rows_t, normed, nt, preferred_element_type=f32)
-        grad_normed = jnp.dot(wqkv_ref[...], rows_t, preferred_element_type=f32)
-        ggain_ref[...] += jnp.sum(grad_normed * x_hat, axis=1, keepdims=True)
-        scaled = grad_normed * gain
-        grad_shifted = inv_std * (
-            scaled
-            - jnp.mean(scaled, axis=0, keepdims=True)
-            - x_hat * jnp.mean(scaled * x_hat, axis=0, keepdims=True)
-        )
-        scattered(grad_shifted.astype(bf16).astype(f32), i, j, l)
-
-    def block_step(ij, carry):
-        for l in range(2):
-            window(ij, l)
-        return carry
-
-    lax.fori_loop(0, 4, block_step, 0)
-
-
-def window_grads(both, kcol, krow, gain_col, wqkv_t, wqkv, wp):
-    extent_a, extent_b, width = both.shape[1:]
+        if first:
+            block_step(0, 0)
+        else:
+            lax.fori_loop(1, 4, block_step, 0)
+
+    return window_kernel
+
+
+def window_grads(first, arrays, kcol, krow, gain_col, wqkv_t, wqkv, wp, partial=()):
+    if first:
+        extent_a, extent_b, width = WIN, WIN, arrays[0].shape[2]
+    else:
+        extent_a, extent_b, width = arrays[0].shape[1:]
     return pl.pallas_call(
-        window_kernel,
+        make_window_kernel(first),
         out_shape=[
             jax.ShapeDtypeStruct((extent_a, extent_b, width), jnp.float32),
             jax.ShapeDtypeStruct((3 * C, C), jnp.float32),
@@ -151,7 +186,7 @@
             pltpu.VMEM((C, CELLS), jnp.float32),
             pltpu.VMEM((3 * C, CELLS), jnp.float32),
         ],
-    )(both, kcol, krow, gain_col, wqkv_t, wqkv, wp)
+    )(*arrays, kcol, krow, gain_col, wqkv_t, wqkv, wp, *partial)
 
 
 SUM_AXES = ("gy", "gx", "gz")
@@ -249,14 +284,17 @@
     )
     mask_key = to_windows_key(labels * 8 + region)
 
-    grad_branch, qkv_grad_t, proj_grad, gain_grad = window_grads(
-        both,
+    constants = (
         mask_key[:, :, None],
         mask_key[:, None, :],
         ln_gain.reshape(channels, 1),
         qkv_weight.T,
         qkv_weight,
         proj_weight,
+    )
+    partial = window_grads(True, (tokens, grads_out), *constants)
+    grad_branch, qkv_grad_t, proj_grad, gain_grad = window_grads(
+        False, (both,), *constants, partial=partial
     )
     qkv_grad_t, proj_grad, gain_grad = summed_everywhere((qkv_grad_t, proj_grad, gain_grad))
     qkv_grad = qkv_grad_t.T

time: 169 us -> 170 us (level)
  waiting for transfers between devices: 35.1 us -> 28.8 us
  Pallas kernels: 79.2 us -> 83.7 us
  local copies, waits for them, and re-layouts: 13.5 us -> 16.4 us
  starting transfers between devices: 23.5 us -> 21.3 us
    ppermute x6, waiting for transfers between devices: 12.9 us -> 7.12 us  [moved(): lax.ppermute(block, ('gx', 'gy', 'gz'), halo_route(distance_a, distance_b))]
    pallas_call x1 -> x2, Pallas kernels: 79.2 us -> 83.7 us  [window_grads(): pl.pallas_call(make_window_kernel(first), out_shape=[jax.ShapeDtypeStruct...]
    add x5, other arithmetic: 0.51 us -> 3.36 us  [summed_everywhere(): values = keep + swapped(send, axis, distance)]
    convert_element_type x1, other arithmetic: 2.25 us -> 0.21 us  [unshifted_sum(): narrow = grad_shifted.astype(jnp.bfloat16)]
  transfers between devices with their start and end apart: 16 -> 16, of which waited for: 13 -> 10; matrix products, arithmetic and copies ran while one was open for 8% -> 7% of each run, Pallas kernels for 0% -> 14%
where the time goes in v6:
time: 170 us; the launch traced here: 168 us
  Pallas kernels  83.7 us (49%)
  waiting for transfers between devices  28.8 us (17%)
  starting transfers between devices  21.3 us (13%)
  other arithmetic  16.7 us (10%)
  local copies, waits for them, and re-layouts  16.4 us (10%)
    pallas_call x2, Pallas kernels, window_grads(): pl.pallas_call(make_window_kernel(first), out_shape=[jax.ShapeDtypeStruct...  83.7 us
    ppermute x10, waiting for transfers between devices, swapped(): lax.ppermute(block, axis, [(i, i ^ distance) for i in range(lax.axis_size...  21.6 us
    ppermute x6, starting transfers between devices, moved(): lax.ppermute(block, ('gx', 'gy', 'gz'), halo_route(distance_a, distance_b))  15.6 us
    ppermute x6, waiting for transfers between devices, moved(): lax.ppermute(block, ('gx', 'gy', 'gz'), halo_route(distance_a, distance_b))  7.12 us
    ppermute x10, starting transfers between devices, swapped(): lax.ppermute(block, axis, [(i, i ^ distance) for i in range(lax.axis_size...  5.65 us
    another operation x4, other arithmetic, per_device(): both = shifted_block(jnp.stack([tokens, grads_out]))  4.87 us
  transfers between devices with their start and end apart: 16, of which 10 were waited for; matrix products, arithmetic and copies ran while one was open for 7% of the time, Pallas kernels for 14%

profile of v6, /device:TPU:5, one launch (start us, length us, event | category | flops | bytes accessed | tf_op | source)
XLA Modules:
  0.0 167.7 jit_solution(11469852852755700029)
XLA Ops:
  0.7 1.5 fusion.2
  2.2 1.3 copy.19
  3.5 3.3 %collective-permute-start.1 = (bf16[2,4,12,3072]{3,1,2,0:T(4,128)(2,1)}, bf16[2,4,12,3072]{3,1,2,0:T(4,128)(2,1)}, u32[]{:S(2)}, u32[]{:S(2)}) collective-permute-start(bf16[2,4,12,3072]{3,1,2,0:T(4,128)(2,1)} %copy.19), channel_id=1, source_target_pairs={{0,24},{1,25},{2,26},{3,27},{4,28},{5,29},{6,30},{7,31},{8,0},{9,1... | collective-permute-start | bytes 1769480 | tf_op jit(solution)/shard_map/ppermute | solution.py:247
  6.8 1.0 fusion.3
  7.8 0.2 collective-permute-start
  8.1 2.0 %collective-permute-start.2 = (bf16[2,4,4,3072]{3,2,1,0:T(4,128)(2,1)S(1)}, bf16[2,4,4,3072]{3,2,1,0:T(4,128)(2,1)S(1)}, u32[]{:S(2)}, u32[]{:S(2)}) collective-permute-start(bf16[2,4,4,3072]{3,2,1,0:T(4,128)(2,1)S(1)} %pad_maximum_fusion.1), channel_id=1, source_target_pairs={{0,31},{1,24},{2,25},{3,26},{4,27},{5,28},{6,29},{7,30},{8,7},{9,0... | collective-permute-start | bytes 589832 | tf_op jit(solution)/shard_map/ppermute | solution.py:247
  10.2 2.3 %fusion.1 = bf16[2,12,12,3072]{3,2,1,0:T(8,128)(2,1)} fusion(bf16[1,16,16,3072]{3,2,1,0:T(8,128)(2,1)S(1)} %bitcast.17, bf16[1,16,16,3072]{3,2,1,0:T(8,128)(2,1)S(1)} %bitcast.13), kind=kLoop, calls=%fused_computation.9 | loop fusion | flops 884736 | bytes 4915200 | tf_op jit(solution)/shard_map/stack | solution.py:274
  12.9 2.0 %broadcast_in_dim_reshape.8.refs_2_.refs_1_ = s32[8,512,1]{2,1,0:T(8,128)} reshape(s32[2,2,2,8,8,8]{5,4,3,2,1,0:T(8,128)S(1)} %bitcast.20) | data formatting | bytes 32768 | tf_op jit(solution)/shard_map/broadcast_in_dim;reshape | solution.py:288
  14.9 0.8 broadcast_in_dim_reshape.7.refs_3_.refs_2_
  15.7 0.9 copy.22
  16.6 0.8 copy.26.refs_4_.refs_3_
  17.4 22.7 %shard_map.93 = (f32[8,8,3072]{2,1,0:T(8,128)}, f32[576,192]{1,0:T(8,128)}, f32[192,192]{1,0:T(8,128)}, f32[192,1]{1,0:T(8,128)}) custom-call(bf16[16,16,3072]{2,1,0:T(8,128)(2,1)} %refs_0_.1, bf16[16,16,3072]{2,1,0:T(8,128)(2,1)} %refs_1_.1, s32[8,512,1]{2,1,0:T(8,128)} %broadcast_in_dim_reshape.8.refs_2_.refs_1_, ...), custom_call_target="tpu_custom_call" | custom-call | tf_op jit(solution)/shard_map/pallas_call | solution.py:176
  40.1 1.3 copy.20
  41.4 3.4 %maximum_maximum_fusion.refs_0_ = bf16[2,16,16,3072]{3,2,1,0:T(8,128)(2,1)} fusion(bf16[2,4,4,3072]{3,2,1,0:T(4,128)(2,1)S(1)} %collective-permute-done.2, bf16[2,4,12,3072]{3,2,1,0:T(8,128)(2,1)S(1)} %copy.20, bf16[2,12,4,3072]{3,2,1,0:T(4,128)(2,1)} %collective-permute-done, bf16[2,12,12,3072]{3,2,1,0:T(8,128)(2,1)S(1)} %copy-done.4), kind=kLoop, calls=%fused_computation.6 | loop fusion | flops 12582912 | bytes 6291456 | tf_op jit(solution)/shard_map/concatenate | solution.py:256
  44.7 61.0 %shard_map.94 = (f32[16,16,3072]{2,1,0:T(8,128)}, f32[576,192]{1,0:T(8,128)}, f32[192,192]{1,0:T(8,128)}, f32[192,1]{1,0:T(8,128)}) custom-call(bf16[2,16,16,3072]{3,2,1,0:T(8,128)(2,1)} %maximum_maximum_fusion.refs_0_, s32[8,512,1]{2,1,0:T(8,128)} %broadcast_in_dim_reshape.8.refs_2_.refs_1_, s32[8,1,512]{2,1,0:T(1,128)} %broadcast_in_dim_reshape.7.refs_3_.refs_2_, ...), custom_call_target="tpu_custom_call" | custom-call | tf_op jit(solution)/shard_map/pallas_call | solution.py:176
  105.7 2.3 %reshape.86 = f32[110592]{0:T(1024)} reshape(f32[576,192]{1,0:T(8,128)} %get-tuple-element.17) | data formatting | bytes 884736 | tf_op jit(solution)/shard_map/reshape | solution.py:203
  108.0 1.0 reshape.87
  109.1 1.0 reduce
  110.1 1.1 pad_maximum_fusion
  111.1 0.8 copy-done.5
  112.1 0.9 collective-permute-start.6
  113.0 1.3 collective-permute-done.6
  114.3 1.2 dynamic-slice_add_fusion
  115.5 0.8 dynamic_slice.33
  116.3 0.8 collective-permute-start.7
  117.1 4.7 %collective-permute-done.7 = f32[36912]{0:T(1024)} collective-permute-done((f32[36912]{0:T(1024)}, f32[36912]{0:T(1024)}, u32[]{:S(2)}, u32[]{:S(2)}) %collective-permute-start.7) | collective-permute-done | bytes 147680 | tf_op jit(solution)/shard_map/ppermute | solution.py:196
  121.8 1.0 dynamic-slice_add_fusion.1
  122.8 0.7 copy-done.7
  123.5 1.4 collective-permute-start.8
  124.9 1.9 %collective-permute-done.8 = f32[18456]{0:T(1024)S(1)} collective-permute-done((f32[18456]{0:T(1024)S(1)}, f32[18456]{0:T(1024)S(1)}, u32[]{:S(2)}, u32[]{:S(2)}) %collective-permute-start.8) | collective-permute-done | bytes 73856 | tf_op jit(solution)/shard_map/ppermute | solution.py:196
  126.9 1.0 dynamic-slice_add_fusion.2
  128.0 3.7 %collective-permute-done.9 = f32[9228]{0:T(1024)S(1)} collective-permute-done((f32[9228]{0:T(1024)S(1)}, f32[9228]{0:T(1024)S(1)}, u32[]{:S(2)}, u32[]{:S(2)}) %collective-permute-start.9) | collective-permute-done | bytes 36944 | tf_op jit(solution)/shard_map/ppermute | solution.py:196
  131.9 0.3 collective-permute-start.10
  132.1 2.7 %collective-permute-done.10 = f32[4614]{0:T(1024)S(1)} collective-permute-done((f32[4614]{0:T(1024)S(1)}, f32[4614]{0:T(1024)S(1)}, u32[]{:S(2)}, u32[]{:S(2)}) %collective-permute-start.10) | collective-permute-done | bytes 18488 | tf_op jit(solution)/shard_map/ppermute | solution.py:196
  135.0 2.6 %collective-permute-done.11 = f32[4614]{0:T(1024)S(1)} collective-permute-done((f32[4614]{0:T(1024)S(1)}, f32[4614]{0:T(1024)S(1)}, u32[]{:S(2)}, u32[]{:S(2)}) %collective-permute-start.11) | collective-permute-done | bytes 18488 | tf_op jit(solution)/shard_map/ppermute | solution.py:196
  137.7 3.7 %collective-permute-done.12 = f32[9228]{0:T(1024)S(1)} collective-permute-done((f32[9228]{0:T(1024)S(1)}, f32[9228]{0:T(1024)S(1)}, u32[]{:S(2)}, u32[]{:S(2)}) %collective-permute-start.12) | collective-permute-done | bytes 36944 | tf_op jit(solution)/shard_map/ppermute | solution.py:196
  141.5 1.4 collective-permute-start.13
  143.8 8.6 %collective-permute-start.3 = (bf16[4,4,3072]{2,1,0:T(4,128)(2,1)S(1)}, bf16[4,4,3072]{2,1,0:T(4,128)(2,1)S(1)}, u32[]{:S(2)}, u32[]{:S(2)}) collective-permute-start(bf16[4,4,3072]{2,1,0:T(4,128)(2,1)S(1)} %slice.55), channel_id=1, source_target_pairs={{0,9},{1,10},{2,11},{3,12},{4,13},{5,14},{6,15},{7,8},{8,17},{9,18... | collective-permute-start | bytes 294920 | tf_op jit(solution)/shard_map/ppermute | solution.py:247
  152.4 1.2 collective-permute-start.5
  153.8 0.8 collective-permute-start.14
  154.5 0.6 collective-permute-done.3
  155.2 6.6 %collective-permute-done.5 = bf16[12,4,3072]{2,1,0:T(4,128)(2,1)S(1)} collective-permute-done((bf16[12,4,3072]{2,1,0:T(4,128)(2,1)S(1)}, bf16[12,4,3072]{2,1,0:T(4,128)(2,1)S(1)}, u32[]{:S(2)}, u32[]{:S(2)}) %collective-permute-start.5) | collective-permute-done | bytes 294944 | tf_op jit(solution)/shard_map/ppermute | solution.py:247
  161.8 1.0 collective-permute-done.14
  163.1 1.8 %fusion = bf16[16,16,3072]{2,1,0:T(8,128)(2,1)} fusion(f32[12,12,3072]{2,1,0:T(8,128)S(1)} %slice.44, f32[12,4,3072]{2,1,0:T(4,128)S(1)} %convert_element_type.28, f32[4,16,3072]{2,1,0:T(8,128)S(1)} %maximum_convert_fusion, bf16[16,16,3072]{2,1,0:T(8,128)(2,1)S(1)} %copy-done.1), kind=kLoop, calls=%fused_computation.8 | loop fusion | flops 3932160 | bytes 6291456 | tf_op jit(solution)/shard_map/convert_element_type | solution.py:267
  164.8 0.2 maximum_select_fusion
  165.1 0.7 slice.60
  165.8 0.6 slice.58
  166.7 1.0 reshape.89
  (56 shorter events, 3.3 us)
Async XLA Ops:
  0.6 6.1 %copy-start.2 = (bf16[16,16,3072]{2,1,0:T(8,128)(2,1)S(1)}, bf16[16,16,3072]{2,1,0:T(8,128)(2,1)}, u32[]{:S(2)}) copy-start(bf16[16,16,3072]{2,1,0:T(8,128)(2,1)} %refs_0_.1) | copy-start | bytes 4718596
  0.6 6.1 %copy-start = (bf16[16,16,3072]{2,1,0:T(8,128)(2,1)S(1)}, bf16[16,16,3072]{2,1,0:T(8,128)(2,1)}, u32[]{:S(2)}) copy-start(bf16[16,16,3072]{2,1,0:T(8,128)(2,1)} %refs_1_.1) | copy-start | bytes 4718596
  3.5 36.6 %collective-permute-start.1 = (bf16[2,4,12,3072]{3,1,2,0:T(4,128)(2,1)}, bf16[2,4,12,3072]{3,1,2,0:T(4,128)(2,1)}, u32[]{:S(2)}, u32[]{:S(2)}) collective-permute-start(bf16[2,4,12,3072]{3,1,2,0:T(4,128)(2,1)} %copy.19), channel_id=1, source_target_pairs={{0,24},{1,25},{2,26},{3,27},{4,28},{5,29},{6,30},{7,31},{8,0},{9,1... | collective-permute-start | bytes 1769480 | tf_op jit(solution)/shard_map/ppermute | solution.py:247
  7.8 33.5 %collective-permute-start = (bf16[2,12,4,3072]{3,2,1,0:T(4,128)(2,1)}, bf16[2,12,4,3072]{3,2,1,0:T(4,128)(2,1)}, u32[]{:S(2)}, u32[]{:S(2)}) collective-permute-start(bf16[2,12,4,3072]{3,2,1,0:T(4,128)(2,1)} %fusion.3), channel_id=1, source_target_pairs={{0,7},{1,0},{2,1},{3,2},{4,3},{5,4},{6,5},{7,6},{8,15},{9,8},{10,9... | collective-permute-start | bytes 1769480 | tf_op jit(solution)/shard_map/ppermute | solution.py:247
  8.1 33.2 %collective-permute-start.2 = (bf16[2,4,4,3072]{3,2,1,0:T(4,128)(2,1)S(1)}, bf16[2,4,4,3072]{3,2,1,0:T(4,128)(2,1)S(1)}, u32[]{:S(2)}, u32[]{:S(2)}) collective-permute-start(bf16[2,4,4,3072]{3,2,1,0:T(4,128)(2,1)S(1)} %pad_maximum_fusion.1), channel_id=1, source_target_pairs={{0,31},{1,24},{2,25},{3,26},{4,27},{5,28},{6,29},{7,30},{8,7},{9,0... | collective-permute-start | bytes 589832 | tf_op jit(solution)/shard_map/ppermute | solution.py:247
  10.1 2.3 %copy-start.8 = (s32[16,16,16]{2,1,0:T(8,128)S(1)}, s32[16,16,16]{2,1,0:T(8,128)}, u32[]{:S(2)}) copy-start(s32[16,16,16]{2,1,0:T(8,128)} %param.8) | copy-start | bytes 49156
  12.5 3.2 %copy-start.6 = (bf16[192,576]{1,0:T(8,128)(2,1)S(1)}, bf16[192,576]{1,0:T(8,128)(2,1)}, u32[]{:S(2)}) copy-start(bf16[192,576]{1,0:T(8,128)(2,1)} %refs_5_.1) | copy-start | bytes 663556
  12.5 4.1 %copy-start.9 = (f32[192]{0:T(256)S(1)}, f32[192]{0:T(256)}, u32[]{:S(2)}) copy-start(f32[192]{0:T(256)} %param.9) | copy-start | bytes 2308
  17.4 24.0 %copy-start.4 = (bf16[2,12,12,3072]{3,2,1,0:T(8,128)(2,1)S(1)}, bf16[2,12,12,3072]{3,2,1,0:T(8,128)(2,1)}, u32[]{:S(2)}) copy-start(bf16[2,12,12,3072]{3,2,1,0:T(8,128)(2,1)} %fusion.1) | copy-start | bytes 5308420
  105.7 37.2 %copy-start.3 = (f32[16,16,3072]{2,1,0:T(8,128)S(1)}, f32[16,16,3072]{2,1,0:T(8,128)}, u32[]{:S(2)}) copy-start(f32[16,16,3072]{2,1,0:T(8,128)} %get-tuple-element.16) | copy-start | bytes 9437188
  111.1 0.8 copy-start.5
  112.1 2.2 %collective-permute-start.6 = (f32[73824]{0:T(1024)S(1)}, f32[73824]{0:T(1024)}, u32[]{:S(2)}, u32[]{:S(2)}) collective-permute-start(f32[73824]{0:T(1024)S(1)} %dynamic_slice.31), channel_id=1, source_target_pairs={{0,2},{2,0},{4,6},{6,4},{1,3},{3,1},{5,7},{7,5},{8,10},{10,8},{12,... | collective-permute-start | bytes 885896 | tf_op jit(solution)/shard_map/ppermute | solution.py:196
  116.3 5.5 %collective-permute-start.7 = (f32[36912]{0:T(1024)}, f32[36912]{0:T(1024)}, u32[]{:S(2)}, u32[]{:S(2)}) collective-permute-start(f32[36912]{0:T(1024)} %dynamic_slice.33), channel_id=1, source_target_pairs={{0,4},{2,6},{4,0},{6,2},{1,5},{3,7},{5,1},{7,3},{8,12},{10,14},{12... | collective-permute-start | bytes 442952 | tf_op jit(solution)/shard_map/ppermute | solution.py:196
  122.8 0.7 copy-start.7
  123.5 3.3 %collective-permute-start.8 = (f32[18456]{0:T(1024)S(1)}, f32[18456]{0:T(1024)S(1)}, u32[]{:S(2)}, u32[]{:S(2)}) collective-permute-start(f32[18456]{0:T(1024)S(1)} %dynamic_slice.35), channel_id=1, source_target_pairs={{0,8},{8,0},{16,24},{24,16},{1,9},{9,1},{17,25},{25,17},{2,10},{10... | collective-permute-start | bytes 221480 | tf_op jit(solution)/shard_map/ppermute | solution.py:196
  127.9 3.8 %collective-permute-start.9 = (f32[9228]{0:T(1024)S(1)}, f32[9228]{0:T(1024)S(1)}, u32[]{:S(2)}, u32[]{:S(2)}) collective-permute-start(f32[9228]{0:T(1024)S(1)} %dynamic_slice.37), channel_id=1, source_target_pairs={{0,16},{8,24},{16,0},{24,8},{1,17},{9,25},{17,1},{25,9},{2,18},{10... | collective-permute-start | bytes 110744 | tf_op jit(solution)/shard_map/ppermute | solution.py:196
  131.9 2.9 %collective-permute-start.10 = (f32[4614]{0:T(1024)S(1)}, f32[4614]{0:T(1024)S(1)}, u32[]{:S(2)}, u32[]{:S(2)}) collective-permute-start(f32[4614]{0:T(1024)S(1)} %dynamic_slice.39), channel_id=1, source_target_pairs={{0,1},{1,0},{2,3},{3,2},{4,5},{5,4},{6,7},{7,6},{8,9},{9,8},{10,11... | collective-permute-start | bytes 55376 | tf_op jit(solution)/shard_map/ppermute | solution.py:196
  134.9 2.6 %collective-permute-start.11 = (f32[4614]{0:T(1024)S(1)}, f32[4614]{0:T(1024)S(1)}, u32[]{:S(2)}, u32[]{:S(2)}) collective-permute-start(f32[4614]{0:T(1024)S(1)} %dynamic-slice_add_fusion.4), channel_id=1, source_target_pairs={{0,1},{1,0},{2,3},{3,2},{4,5},{5,4},{6,7},{7,6},{8,9},{9,8},{10,11... | collective-permute-start | bytes 55376 | tf_op jit(solution)/shard_map/ppermute | solution.py:196
  137.6 3.8 %collective-permute-start.12 = (f32[9228]{0:T(1024)S(1)}, f32[9228]{0:T(1024)S(1)}, u32[]{:S(2)}, u32[]{:S(2)}) collective-permute-start(f32[9228]{0:T(1024)S(1)} %maximum_select_fusion.4), channel_id=1, source_target_pairs={{0,16},{8,24},{16,0},{24,8},{1,17},{9,25},{17,1},{25,9},{2,18},{10... | collective-permute-start | bytes 110744 | tf_op jit(solution)/shard_map/ppermute | solution.py:196
  141.5 12.1 %collective-permute-start.13 = (f32[18456]{0:T(1024)S(1)}, f32[18456]{0:T(1024)S(1)}, u32[]{:S(2)}, u32[]{:S(2)}) collective-permute-start(f32[18456]{0:T(1024)S(1)} %maximum_select_fusion.3), channel_id=1, source_target_pairs={{0,8},{8,0},{16,24},{24,16},{1,9},{9,1},{17,25},{25,17},{2,10},{10... | collective-permute-start | bytes 221480 | tf_op jit(solution)/shard_map/ppermute | solution.py:196
  143.4 19.7 %copy-start.1 = (bf16[16,16,3072]{2,1,0:T(8,128)(2,1)S(1)}, bf16[16,16,3072]{2,1,0:T(8,128)(2,1)}, u32[]{:S(2)}) copy-start(bf16[16,16,3072]{2,1,0:T(8,128)(2,1)} %refs_1_.1) | copy-start | bytes 4718596
  143.6 11.5 %collective-permute-start.4 = (bf16[4,12,3072]{2,1,0:T(8,128)(2,1)S(1)}, bf16[4,12,3072]{2,1,0:T(8,128)(2,1)S(1)}, u32[]{:S(2)}, u32[]{:S(2)}) collective-permute-start(bf16[4,12,3072]{2,1,0:T(8,128)(2,1)S(1)} %slice.56), channel_id=1, source_target_pairs={{0,8},{1,9},{2,10},{3,11},{4,12},{5,13},{6,14},{7,15},{8,16},{9,17... | collective-permute-start | bytes 884744 | tf_op jit(solution)/shard_map/ppermute | solution.py:247
  143.8 11.2 %collective-permute-start.3 = (bf16[4,4,3072]{2,1,0:T(4,128)(2,1)S(1)}, bf16[4,4,3072]{2,1,0:T(4,128)(2,1)S(1)}, u32[]{:S(2)}, u32[]{:S(2)}) collective-permute-start(bf16[4,4,3072]{2,1,0:T(4,128)(2,1)S(1)} %slice.55), channel_id=1, source_target_pairs={{0,9},{1,10},{2,11},{3,12},{4,13},{5,14},{6,15},{7,8},{8,17},{9,18... | collective-permute-start | bytes 294920 | tf_op jit(solution)/shard_map/ppermute | solution.py:247
  152.4 9.4 %collective-permute-start.5 = (bf16[12,4,3072]{2,1,0:T(4,128)(2,1)S(1)}, bf16[12,4,3072]{2,1,0:T(4,128)(2,1)S(1)}, u32[]{:S(2)}, u32[]{:S(2)}) collective-permute-start(bf16[12,4,3072]{2,1,0:T(4,128)(2,1)S(1)} %slice.57), channel_id=1, source_target_pairs={{0,1},{1,2},{2,3},{3,4},{4,5},{5,6},{6,7},{7,0},{8,9},{9,10},{10,1... | collective-permute-start | bytes 884744 | tf_op jit(solution)/shard_map/ppermute | solution.py:247
  153.8 9.0 %collective-permute-start.14 = (f32[36912]{0:T(1024)S(1)}, f32[36912]{0:T(1024)S(1)}, u32[]{:S(2)}, u32[]{:S(2)}) collective-permute-start(f32[36912]{0:T(1024)S(1)} %maximum_select_fusion.2), channel_id=1, source_target_pairs={{0,4},{2,6},{4,0},{6,2},{1,5},{3,7},{5,1},{7,3},{8,12},{10,14},{12... | collective-permute-start | bytes 442952 | tf_op jit(solution)/shard_map/ppermute | solution.py:196
  163.0 1.9 %collective-permute-start.15 = (f32[73824]{0:T(1024)S(1)}, f32[73824]{0:T(1024)S(1)}, u32[]{:S(2)}, u32[]{:S(2)}) collective-permute-start(f32[73824]{0:T(1024)S(1)} %maximum_select_fusion.1), channel_id=1, source_target_pairs={{0,2},{2,0},{4,6},{6,4},{1,3},{3,1},{5,7},{7,5},{8,10},{10,8},{12,... | collective-permute-start | bytes 885896 | tf_op jit(solution)/shard_map/ppermute | solution.py:196

commit v7 on v6

--- a/solution.py
+++ b/solution.py
@@ -13,6 +13,7 @@
 CELLS = WIN**3
 HEAD = C // HEADS
 SCALE = HEAD ** (-0.5)
+ROWS = 128
 
 
 def passed_along(block, axis, distance):
@@ -121,22 +122,37 @@
                 v_t = qkv_s[pl.ds(qo + 2 * C, HEAD), :]
                 ga_th = ga_s[pl.ds(qo, HEAD), :]
                 q = q_t.T.astype(bf16)
-                scores = jnp.dot(q, k_t.astype(bf16), preferred_element_type=f32) * SCALE
-                weights = jnp.where(allowed, jnp.exp(scores), 0.0)
-                probs = weights / jnp.sum(weights, axis=1, keepdims=True)
-                probs_bf = probs.astype(bf16)
-                att_t = lax.dot_general(v_t.astype(bf16), probs_bf, nt, preferred_element_type=f32)
-                att_t = att_t.astype(bf16)
+                ga = ga_th.T.astype(bf16)
+                q_tb = q_t.astype(bf16)
+                k_tb = k_t.astype(bf16)
+                v_tb = v_t.astype(bf16)
+                ga_tb = ga_th.astype(bf16)
+                att_parts = []
+                dq_parts = []
+                dv_t = jnp.zeros((HEAD, CELLS), f32)
+                dk_t = jnp.zeros((HEAD, CELLS), f32)
+                for r in range(CELLS // ROWS):
+                    rows = slice(r * ROWS, (r + 1) * ROWS)
+                    scores = jnp.dot(q[rows], k_tb, preferred_element_type=f32) * SCALE
+                    weights = jnp.where(allowed[rows], jnp.exp(scores), 0.0)
+                    probs = weights / jnp.sum(weights, axis=1, keepdims=True)
+                    probs_bf = probs.astype(bf16)
+                    att_parts.append(
+                        lax.dot_general(v_tb, probs_bf, nt, preferred_element_type=f32)
+                    )
+                    grad_probs = jnp.dot(ga[rows], v_tb, preferred_element_type=f32)
+                    dv_t = dv_t + jnp.dot(ga_tb[:, rows], probs_bf, preferred_element_type=f32)
+                    row_total = jnp.sum(probs * grad_probs, axis=1, keepdims=True)
+                    grad_scores = (probs * (grad_probs - row_total) * SCALE).astype(bf16)
+                    dq_parts.append(
+                        lax.dot_general(k_tb, grad_scores, nt, preferred_element_type=f32)
+                    )
+                    dk_t = dk_t + jnp.dot(q_tb[:, rows], grad_scores, preferred_element_type=f32)
+                att_t = jnp.concatenate(att_parts, axis=1).astype(bf16)
                 gproj_ref[pl.ds(qo, HEAD), :] += lax.dot_general(
                     att_t, g, nt, preferred_element_type=f32
                 )
-                ga = ga_th.T.astype(bf16)
-                grad_probs = jnp.dot(ga, v_t.astype(bf16), preferred_element_type=f32)
-                dv_t = jnp.dot(ga_th.astype(bf16), probs_bf, preferred_element_type=f32)
-                row_total = jnp.sum(probs * grad_probs, axis=1, keepdims=True)
-                grad_scores = (probs * (grad_probs - row_total) * SCALE).astype(bf16)
-                dq_t = lax.dot_general(k_t.astype(bf16), grad_scores, nt, preferred_element_type=f32)
-                dk_t = jnp.dot(q_t.astype(bf16), grad_scores, preferred_element_type=f32)
+                dq_t = jnp.concatenate(dq_parts, axis=1)
                 drow_s[pl.ds(qo, HEAD), :] = dq_t.astype(bf16).astype(f32)
                 drow_s[pl.ds(qo + C, HEAD), :] = dk_t.astype(bf16).astype(f32)
                 drow_s[pl.ds(qo + 2 * C, HEAD), :] = dv_t.astype(bf16).astype(f32)

time: 170 us -> 185 us (1.088)
  Pallas kernels: 83.7 us -> 98.9 us
    pallas_call x2, Pallas kernels: 83.7 us -> 98.9 us  [window_grads(): pl.pallas_call(make_window_kernel(first), out_shape=[jax.ShapeDtypeStruct...]
  transfers between devices with their start and end apart: 16 -> 16, of which waited for: 10 -> 10; matrix products, arithmetic and copies ran while one was open for 7% -> 7% of each run, Pallas kernels for 14% -> 15%
where the time goes in v7:
time: 185 us; the launch traced here: 183 us
  Pallas kernels  98.9 us (53%)
  waiting for transfers between devices  28.6 us (15%)
  starting transfers between devices  21.4 us (12%)
  other arithmetic  16.7 us (9%)
  local copies, waits for them, and re-layouts  16.4 us (9%)
    pallas_call x2, Pallas kernels, window_grads(): pl.pallas_call(make_window_kernel(first), out_shape=[jax.ShapeDtypeStruct...  98.9 us
    ppermute x10, waiting for transfers between devices, swapped(): lax.ppermute(block, axis, [(i, i ^ distance) for i in range(lax.axis_size...  21.5 us
    ppermute x6, starting transfers between devices, moved(): lax.ppermute(block, ('gx', 'gy', 'gz'), halo_route(distance_a, distance_b))  15.7 us
    ppermute x6, waiting for transfers between devices, moved(): lax.ppermute(block, ('gx', 'gy', 'gz'), halo_route(distance_a, distance_b))  7.12 us
    ppermute x10, starting transfers between devices, swapped(): lax.ppermute(block, axis, [(i, i ^ distance) for i in range(lax.axis_size...  5.72 us
    another operation x4, other arithmetic, per_device(): both = shifted_block(jnp.stack([tokens, grads_out]))  4.87 us
  transfers between devices with their start and end apart: 16, of which 10 were waited for; matrix products, arithmetic and copies ran while one was open for 7% of the time, Pallas kernels for 15%

profile of v7, /device:TPU:5, one launch (start us, length us, event | category | flops | bytes accessed | tf_op | source)
XLA Modules:
  0.0 182.8 jit_solution(157143719081079709)
XLA Ops:
  0.7 1.5 fusion.2
  2.2 1.3 copy.19
  3.5 3.3 %collective-permute-start.1 = (bf16[2,4,12,3072]{3,1,2,0:T(4,128)(2,1)}, bf16[2,4,12,3072]{3,1,2,0:T(4,128)(2,1)}, u32[]{:S(2)}, u32[]{:S(2)}) collective-permute-start(bf16[2,4,12,3072]{3,1,2,0:T(4,128)(2,1)} %copy.19), channel_id=1, source_target_pairs={{0,24},{1,25},{2,26},{3,27},{4,28},{5,29},{6,30},{7,31},{8,0},{9,1... | collective-permute-start | bytes 1769480 | tf_op jit(solution)/shard_map/ppermute | solution.py:263
  6.8 1.0 fusion.3
  7.8 0.2 collective-permute-start
  8.1 2.0 %collective-permute-start.2 = (bf16[2,4,4,3072]{3,2,1,0:T(4,128)(2,1)S(1)}, bf16[2,4,4,3072]{3,2,1,0:T(4,128)(2,1)S(1)}, u32[]{:S(2)}, u32[]{:S(2)}) collective-permute-start(bf16[2,4,4,3072]{3,2,1,0:T(4,128)(2,1)S(1)} %pad_maximum_fusion.1), channel_id=1, source_target_pairs={{0,31},{1,24},{2,25},{3,26},{4,27},{5,28},{6,29},{7,30},{8,7},{9,0... | collective-permute-start | bytes 589832 | tf_op jit(solution)/shard_map/ppermute | solution.py:263
  10.2 2.3 %fusion.1 = bf16[2,12,12,3072]{3,2,1,0:T(8,128)(2,1)} fusion(bf16[1,16,16,3072]{3,2,1,0:T(8,128)(2,1)S(1)} %bitcast.17, bf16[1,16,16,3072]{3,2,1,0:T(8,128)(2,1)S(1)} %bitcast.13), kind=kLoop, calls=%fused_computation.9 | loop fusion | flops 884736 | bytes 4915200 | tf_op jit(solution)/shard_map/stack | solution.py:290
  12.9 2.0 %broadcast_in_dim_reshape.8.refs_2_.refs_1_ = s32[8,512,1]{2,1,0:T(8,128)} reshape(s32[2,2,2,8,8,8]{5,4,3,2,1,0:T(8,128)S(1)} %bitcast.20) | data formatting | bytes 32768 | tf_op jit(solution)/shard_map/broadcast_in_dim;reshape | solution.py:304
  14.9 0.8 broadcast_in_dim_reshape.7.refs_3_.refs_2_
  15.7 0.9 copy.22
  16.6 0.8 copy.26.refs_4_.refs_3_
  17.4 26.5 %shard_map.93 = (f32[8,8,3072]{2,1,0:T(8,128)}, f32[576,192]{1,0:T(8,128)}, f32[192,192]{1,0:T(8,128)}, f32[192,1]{1,0:T(8,128)}) custom-call(bf16[16,16,3072]{2,1,0:T(8,128)(2,1)} %refs_0_.1, bf16[16,16,3072]{2,1,0:T(8,128)(2,1)} %refs_1_.1, s32[8,512,1]{2,1,0:T(8,128)} %broadcast_in_dim_reshape.8.refs_2_.refs_1_, ...), custom_call_target="tpu_custom_call" | custom-call | tf_op jit(solution)/shard_map/pallas_call | solution.py:192
  43.9 1.3 copy.20
  45.2 3.4 %maximum_maximum_fusion.refs_0_ = bf16[2,16,16,3072]{3,2,1,0:T(8,128)(2,1)} fusion(bf16[2,4,4,3072]{3,2,1,0:T(4,128)(2,1)S(1)} %collective-permute-done.2, bf16[2,4,12,3072]{3,2,1,0:T(8,128)(2,1)S(1)} %copy.20, bf16[2,12,4,3072]{3,2,1,0:T(4,128)(2,1)} %collective-permute-done, bf16[2,12,12,3072]{3,2,1,0:T(8,128)(2,1)S(1)} %copy-done.4), kind=kLoop, calls=%fused_computation.6 | loop fusion | flops 12582912 | bytes 6291456 | tf_op jit(solution)/shard_map/concatenate | solution.py:272
  48.5 72.4 %shard_map.94 = (f32[16,16,3072]{2,1,0:T(8,128)}, f32[576,192]{1,0:T(8,128)}, f32[192,192]{1,0:T(8,128)}, f32[192,1]{1,0:T(8,128)}) custom-call(bf16[2,16,16,3072]{3,2,1,0:T(8,128)(2,1)} %maximum_maximum_fusion.refs_0_, s32[8,512,1]{2,1,0:T(8,128)} %broadcast_in_dim_reshape.8.refs_2_.refs_1_, s32[8,1,512]{2,1,0:T(1,128)} %broadcast_in_dim_reshape.7.refs_3_.refs_2_, ...), custom_call_target="tpu_custom_call" | custom-call | tf_op jit(solution)/shard_map/pallas_call | solution.py:192
  120.9 2.3 %reshape.86 = f32[110592]{0:T(1024)} reshape(f32[576,192]{1,0:T(8,128)} %get-tuple-element.17) | data formatting | bytes 884736 | tf_op jit(solution)/shard_map/reshape | solution.py:219
  123.2 1.0 reshape.87
  124.2 1.0 reduce
  125.2 1.1 pad_maximum_fusion
  126.3 0.8 copy-done.5
  127.3 0.8 collective-permute-start.6
  128.1 1.3 collective-permute-done.6
  129.5 1.2 dynamic-slice_add_fusion
  130.7 0.8 dynamic_slice.33
  131.4 0.8 collective-permute-start.7
  132.3 4.6 %collective-permute-done.7 = f32[36912]{0:T(1024)} collective-permute-done((f32[36912]{0:T(1024)}, f32[36912]{0:T(1024)}, u32[]{:S(2)}, u32[]{:S(2)}) %collective-permute-start.7) | collective-permute-done | bytes 147680 | tf_op jit(solution)/shard_map/ppermute | solution.py:212
  136.9 1.0 dynamic-slice_add_fusion.1
  137.9 0.7 copy-done.7
  138.7 1.4 collective-permute-start.8
  140.0 1.9 %collective-permute-done.8 = f32[18456]{0:T(1024)S(1)} collective-permute-done((f32[18456]{0:T(1024)S(1)}, f32[18456]{0:T(1024)S(1)}, u32[]{:S(2)}, u32[]{:S(2)}) %collective-permute-start.8) | collective-permute-done | bytes 73856 | tf_op jit(solution)/shard_map/ppermute | solution.py:212
  142.0 1.0 dynamic-slice_add_fusion.2
  143.1 3.7 %collective-permute-done.9 = f32[9228]{0:T(1024)S(1)} collective-permute-done((f32[9228]{0:T(1024)S(1)}, f32[9228]{0:T(1024)S(1)}, u32[]{:S(2)}, u32[]{:S(2)}) %collective-permute-start.9) | collective-permute-done | bytes 36944 | tf_op jit(solution)/shard_map/ppermute | solution.py:212
  147.0 0.3 collective-permute-start.10
  147.4 2.6 %collective-permute-done.10 = f32[4614]{0:T(1024)S(1)} collective-permute-done((f32[4614]{0:T(1024)S(1)}, f32[4614]{0:T(1024)S(1)}, u32[]{:S(2)}, u32[]{:S(2)}) %collective-permute-start.10) | collective-permute-done | bytes 18488 | tf_op jit(solution)/shard_map/ppermute | solution.py:212
  150.2 2.5 %collective-permute-done.11 = f32[4614]{0:T(1024)S(1)} collective-permute-done((f32[4614]{0:T(1024)S(1)}, f32[4614]{0:T(1024)S(1)}, u32[]{:S(2)}, u32[]{:S(2)}) %collective-permute-start.11) | collective-permute-done | bytes 18488 | tf_op jit(solution)/shard_map/ppermute | solution.py:212
  152.8 3.7 %collective-permute-done.12 = f32[9228]{0:T(1024)S(1)} collective-permute-done((f32[9228]{0:T(1024)S(1)}, f32[9228]{0:T(1024)S(1)}, u32[]{:S(2)}, u32[]{:S(2)}) %collective-permute-start.12) | collective-permute-done | bytes 36944 | tf_op jit(solution)/shard_map/ppermute | solution.py:212
  156.7 1.4 collective-permute-start.13
  159.0 8.6 %collective-permute-start.3 = (bf16[4,4,3072]{2,1,0:T(4,128)(2,1)S(1)}, bf16[4,4,3072]{2,1,0:T(4,128)(2,1)S(1)}, u32[]{:S(2)}, u32[]{:S(2)}) collective-permute-start(bf16[4,4,3072]{2,1,0:T(4,128)(2,1)S(1)} %slice.55), channel_id=1, source_target_pairs={{0,9},{1,10},{2,11},{3,12},{4,13},{5,14},{6,15},{7,8},{8,17},{9,18... | collective-permute-start | bytes 294920 | tf_op jit(solution)/shard_map/ppermute | solution.py:263
  167.6 1.2 collective-permute-start.5
  169.0 0.7 collective-permute-start.14
  169.7 0.6 collective-permute-done.3
  170.4 6.5 %collective-permute-done.5 = bf16[12,4,3072]{2,1,0:T(4,128)(2,1)S(1)} collective-permute-done((bf16[12,4,3072]{2,1,0:T(4,128)(2,1)S(1)}, bf16[12,4,3072]{2,1,0:T(4,128)(2,1)S(1)}, u32[]{:S(2)}, u32[]{:S(2)}) %collective-permute-start.5) | collective-permute-done | bytes 294944 | tf_op jit(solution)/shard_map/ppermute | solution.py:263
  177.0 1.0 collective-permute-done.14
  178.2 1.8 fusion
  180.0 0.2 maximum_select_fusion
  180.3 0.7 slice.60
  180.9 0.6 slice.58
  181.9 1.0 reshape.89
  (56 shorter events, 3.4 us)
Async XLA Ops:
  0.6 6.1 %copy-start.2 = (bf16[16,16,3072]{2,1,0:T(8,128)(2,1)S(1)}, bf16[16,16,3072]{2,1,0:T(8,128)(2,1)}, u32[]{:S(2)}) copy-start(bf16[16,16,3072]{2,1,0:T(8,128)(2,1)} %refs_0_.1) | copy-start | bytes 4718596
  0.6 6.1 %copy-start = (bf16[16,16,3072]{2,1,0:T(8,128)(2,1)S(1)}, bf16[16,16,3072]{2,1,0:T(8,128)(2,1)}, u32[]{:S(2)}) copy-start(bf16[16,16,3072]{2,1,0:T(8,128)(2,1)} %refs_1_.1) | copy-start | bytes 4718596
  3.5 40.4 %collective-permute-start.1 = (bf16[2,4,12,3072]{3,1,2,0:T(4,128)(2,1)}, bf16[2,4,12,3072]{3,1,2,0:T(4,128)(2,1)}, u32[]{:S(2)}, u32[]{:S(2)}) collective-permute-start(bf16[2,4,12,3072]{3,1,2,0:T(4,128)(2,1)} %copy.19), channel_id=1, source_target_pairs={{0,24},{1,25},{2,26},{3,27},{4,28},{5,29},{6,30},{7,31},{8,0},{9,1... | collective-permute-start | bytes 1769480 | tf_op jit(solution)/shard_map/ppermute | solution.py:263
  7.8 37.3 %collective-permute-start = (bf16[2,12,4,3072]{3,2,1,0:T(4,128)(2,1)}, bf16[2,12,4,3072]{3,2,1,0:T(4,128)(2,1)}, u32[]{:S(2)}, u32[]{:S(2)}) collective-permute-start(bf16[2,12,4,3072]{3,2,1,0:T(4,128)(2,1)} %fusion.3), channel_id=1, source_target_pairs={{0,7},{1,0},{2,1},{3,2},{4,3},{5,4},{6,5},{7,6},{8,15},{9,8},{10,9... | collective-permute-start | bytes 1769480 | tf_op jit(solution)/shard_map/ppermute | solution.py:263
  8.1 37.0 %collective-permute-start.2 = (bf16[2,4,4,3072]{3,2,1,0:T(4,128)(2,1)S(1)}, bf16[2,4,4,3072]{3,2,1,0:T(4,128)(2,1)S(1)}, u32[]{:S(2)}, u32[]{:S(2)}) collective-permute-start(bf16[2,4,4,3072]{3,2,1,0:T(4,128)(2,1)S(1)} %pad_maximum_fusion.1), channel_id=1, source_target_pairs={{0,31},{1,24},{2,25},{3,26},{4,27},{5,28},{6,29},{7,30},{8,7},{9,0... | collective-permute-start | bytes 589832 | tf_op jit(solution)/shard_map/ppermute | solution.py:263
  10.1 2.3 %copy-start.8 = (s32[16,16,16]{2,1,0:T(8,128)S(1)}, s32[16,16,16]{2,1,0:T(8,128)}, u32[]{:S(2)}) copy-start(s32[16,16,16]{2,1,0:T(8,128)} %param.8) | copy-start | bytes 49156
  12.5 3.2 %copy-start.6 = (bf16[192,576]{1,0:T(8,128)(2,1)S(1)}, bf16[192,576]{1,0:T(8,128)(2,1)}, u32[]{:S(2)}) copy-start(bf16[192,576]{1,0:T(8,128)(2,1)} %refs_5_.1) | copy-start | bytes 663556
  12.5 4.1 %copy-start.9 = (f32[192]{0:T(256)S(1)}, f32[192]{0:T(256)}, u32[]{:S(2)}) copy-start(f32[192]{0:T(256)} %param.9) | copy-start | bytes 2308
  17.4 27.8 %copy-start.4 = (bf16[2,12,12,3072]{3,2,1,0:T(8,128)(2,1)S(1)}, bf16[2,12,12,3072]{3,2,1,0:T(8,128)(2,1)}, u32[]{:S(2)}) copy-start(bf16[2,12,12,3072]{3,2,1,0:T(8,128)(2,1)} %fusion.1) | copy-start | bytes 5308420
  120.9 37.1 %copy-start.3 = (f32[16,16,3072]{2,1,0:T(8,128)S(1)}, f32[16,16,3072]{2,1,0:T(8,128)}, u32[]{:S(2)}) copy-start(f32[16,16,3072]{2,1,0:T(8,128)} %get-tuple-element.16) | copy-start | bytes 9437188
  126.3 0.8 copy-start.5
  127.3 2.2 %collective-permute-start.6 = (f32[73824]{0:T(1024)S(1)}, f32[73824]{0:T(1024)}, u32[]{:S(2)}, u32[]{:S(2)}) collective-permute-start(f32[73824]{0:T(1024)S(1)} %dynamic_slice.31), channel_id=1, source_target_pairs={{0,2},{2,0},{4,6},{6,4},{1,3},{3,1},{5,7},{7,5},{8,10},{10,8},{12,... | collective-permute-start | bytes 885896 | tf_op jit(solution)/shard_map/ppermute | solution.py:212
  131.4 5.5 %collective-permute-start.7 = (f32[36912]{0:T(1024)}, f32[36912]{0:T(1024)}, u32[]{:S(2)}, u32[]{:S(2)}) collective-permute-start(f32[36912]{0:T(1024)} %dynamic_slice.33), channel_id=1, source_target_pairs={{0,4},{2,6},{4,0},{6,2},{1,5},{3,7},{5,1},{7,3},{8,12},{10,14},{12... | collective-permute-start | bytes 442952 | tf_op jit(solution)/shard_map/ppermute | solution.py:212
  137.9 0.7 copy-start.7
  138.7 3.3 %collective-permute-start.8 = (f32[18456]{0:T(1024)S(1)}, f32[18456]{0:T(1024)S(1)}, u32[]{:S(2)}, u32[]{:S(2)}) collective-permute-start(f32[18456]{0:T(1024)S(1)} %dynamic_slice.35), channel_id=1, source_target_pairs={{0,8},{8,0},{16,24},{24,16},{1,9},{9,1},{17,25},{25,17},{2,10},{10... | collective-permute-start | bytes 221480 | tf_op jit(solution)/shard_map/ppermute | solution.py:212
  143.1 3.8 %collective-permute-start.9 = (f32[9228]{0:T(1024)S(1)}, f32[9228]{0:T(1024)S(1)}, u32[]{:S(2)}, u32[]{:S(2)}) collective-permute-start(f32[9228]{0:T(1024)S(1)} %dynamic_slice.37), channel_id=1, source_target_pairs={{0,16},{8,24},{16,0},{24,8},{1,17},{9,25},{17,1},{25,9},{2,18},{10... | collective-permute-start | bytes 110744 | tf_op jit(solution)/shard_map/ppermute | solution.py:212
  147.0 2.9 %collective-permute-start.10 = (f32[4614]{0:T(1024)S(1)}, f32[4614]{0:T(1024)S(1)}, u32[]{:S(2)}, u32[]{:S(2)}) collective-permute-start(f32[4614]{0:T(1024)S(1)} %dynamic_slice.39), channel_id=1, source_target_pairs={{0,1},{1,0},{2,3},{3,2},{4,5},{5,4},{6,7},{7,6},{8,9},{9,8},{10,11... | collective-permute-start | bytes 55376 | tf_op jit(solution)/shard_map/ppermute | solution.py:212
  150.0 2.6 %collective-permute-start.11 = (f32[4614]{0:T(1024)S(1)}, f32[4614]{0:T(1024)S(1)}, u32[]{:S(2)}, u32[]{:S(2)}) collective-permute-start(f32[4614]{0:T(1024)S(1)} %dynamic-slice_add_fusion.4), channel_id=1, source_target_pairs={{0,1},{1,0},{2,3},{3,2},{4,5},{5,4},{6,7},{7,6},{8,9},{9,8},{10,11... | collective-permute-start | bytes 55376 | tf_op jit(solution)/shard_map/ppermute | solution.py:212
  152.8 3.8 %collective-permute-start.12 = (f32[9228]{0:T(1024)S(1)}, f32[9228]{0:T(1024)S(1)}, u32[]{:S(2)}, u32[]{:S(2)}) collective-permute-start(f32[9228]{0:T(1024)S(1)} %maximum_select_fusion.4), channel_id=1, source_target_pairs={{0,16},{8,24},{16,0},{24,8},{1,17},{9,25},{17,1},{25,9},{2,18},{10... | collective-permute-start | bytes 110744 | tf_op jit(solution)/shard_map/ppermute | solution.py:212
  156.7 12.2 %collective-permute-start.13 = (f32[18456]{0:T(1024)S(1)}, f32[18456]{0:T(1024)S(1)}, u32[]{:S(2)}, u32[]{:S(2)}) collective-permute-start(f32[18456]{0:T(1024)S(1)} %maximum_select_fusion.3), channel_id=1, source_target_pairs={{0,8},{8,0},{16,24},{24,16},{1,9},{9,1},{17,25},{25,17},{2,10},{10... | collective-permute-start | bytes 221480 | tf_op jit(solution)/shard_map/ppermute | solution.py:212
  158.5 19.7 %copy-start.1 = (bf16[16,16,3072]{2,1,0:T(8,128)(2,1)S(1)}, bf16[16,16,3072]{2,1,0:T(8,128)(2,1)}, u32[]{:S(2)}) copy-start(bf16[16,16,3072]{2,1,0:T(8,128)(2,1)} %refs_1_.1) | copy-start | bytes 4718596
  158.8 11.5 %collective-permute-start.4 = (bf16[4,12,3072]{2,1,0:T(8,128)(2,1)S(1)}, bf16[4,12,3072]{2,1,0:T(8,128)(2,1)S(1)}, u32[]{:S(2)}, u32[]{:S(2)}) collective-permute-start(bf16[4,12,3072]{2,1,0:T(8,128)(2,1)S(1)} %slice.56), channel_id=1, source_target_pairs={{0,8},{1,9},{2,10},{3,11},{4,12},{5,13},{6,14},{7,15},{8,16},{9,17... | collective-permute-start | bytes 884744 | tf_op jit(solution)/shard_map/ppermute | solution.py:263
  159.0 11.3 %collective-permute-start.3 = (bf16[4,4,3072]{2,1,0:T(4,128)(2,1)S(1)}, bf16[4,4,3072]{2,1,0:T(4,128)(2,1)S(1)}, u32[]{:S(2)}, u32[]{:S(2)}) collective-permute-start(bf16[4,4,3072]{2,1,0:T(4,128)(2,1)S(1)} %slice.55), channel_id=1, source_target_pairs={{0,9},{1,10},{2,11},{3,12},{4,13},{5,14},{6,15},{7,8},{8,17},{9,18... | collective-permute-start | bytes 294920 | tf_op jit(solution)/shard_map/ppermute | solution.py:263
  167.6 9.3 %collective-permute-start.5 = (bf16[12,4,3072]{2,1,0:T(4,128)(2,1)S(1)}, bf16[12,4,3072]{2,1,0:T(4,128)(2,1)S(1)}, u32[]{:S(2)}, u32[]{:S(2)}) collective-permute-start(bf16[12,4,3072]{2,1,0:T(4,128)(2,1)S(1)} %slice.57), channel_id=1, source_target_pairs={{0,1},{1,2},{2,3},{3,4},{4,5},{5,6},{6,7},{7,0},{8,9},{9,10},{10,1... | collective-permute-start | bytes 884744 | tf_op jit(solution)/shard_map/ppermute | solution.py:263
  169.0 9.0 %collective-permute-start.14 = (f32[36912]{0:T(1024)S(1)}, f32[36912]{0:T(1024)S(1)}, u32[]{:S(2)}, u32[]{:S(2)}) collective-permute-start(f32[36912]{0:T(1024)S(1)} %maximum_select_fusion.2), channel_id=1, source_target_pairs={{0,4},{2,6},{4,0},{6,2},{1,5},{3,7},{5,1},{7,3},{8,12},{10,14},{12... | collective-permute-start | bytes 442952 | tf_op jit(solution)/shard_map/ppermute | solution.py:212
  178.1 1.9 %collective-permute-start.15 = (f32[73824]{0:T(1024)S(1)}, f32[73824]{0:T(1024)S(1)}, u32[]{:S(2)}, u32[]{:S(2)}) collective-permute-start(f32[73824]{0:T(1024)S(1)} %maximum_select_fusion.1), channel_id=1, source_target_pairs={{0,2},{2,0},{4,6},{6,4},{1,3},{3,1},{5,7},{7,5},{8,10},{10,8},{12,... | collective-permute-start | bytes 885896 | tf_op jit(solution)/shard_map/ppermute | solution.py:212

commit v8 on v6

--- a/solution.py
+++ b/solution.py
@@ -125,8 +125,8 @@
                 weights = jnp.where(allowed, jnp.exp(scores), 0.0)
                 probs = weights / jnp.sum(weights, axis=1, keepdims=True)
                 probs_bf = probs.astype(bf16)
-                att_t = lax.dot_general(v_t.astype(bf16), probs_bf, nt, preferred_element_type=f32)
-                att_t = att_t.astype(bf16)
+                attended = jnp.dot(probs_bf, v_t.T.astype(bf16), preferred_element_type=f32)
+                att_t = attended.T.astype(bf16)
                 gproj_ref[pl.ds(qo, HEAD), :] += lax.dot_general(
                     att_t, g, nt, preferred_element_type=f32
                 )
@@ -135,7 +135,7 @@
                 dv_t = jnp.dot(ga_th.astype(bf16), probs_bf, preferred_element_type=f32)
                 row_total = jnp.sum(probs * grad_probs, axis=1, keepdims=True)
                 grad_scores = (probs * (grad_probs - row_total) * SCALE).astype(bf16)
-                dq_t = lax.dot_general(k_t.astype(bf16), grad_scores, nt, preferred_element_type=f32)
+                dq_t = jnp.dot(grad_scores, k_t.T.astype(bf16), preferred_element_type=f32).T
                 dk_t = jnp.dot(q_t.astype(bf16), grad_scores, preferred_element_type=f32)
                 drow_s[pl.ds(qo, HEAD), :] = dq_t.astype(bf16).astype(f32)
                 drow_s[pl.ds(qo + C, HEAD), :] = dk_t.astype(bf16).astype(f32)

time: 170 us -> 190 us (1.12)
  Pallas kernels: 83.7 us -> 103 us
    pallas_call x2, Pallas kernels: 83.7 us -> 103 us  [window_grads(): pl.pallas_call(make_window_kernel(first), out_shape=[jax.ShapeDtypeStruct...]
  transfers between devices with their start and end apart: 16 -> 16, of which waited for: 10 -> 10; matrix products, arithmetic and copies ran while one was open for 7% -> 7% of each run, Pallas kernels for 14% -> 15%
where the time goes in v8:
time: 190 us; the launch traced here: 187 us
  Pallas kernels  103 us (54%)
  waiting for transfers between devices  28.6 us (15%)
  starting transfers between devices  21.4 us (11%)
  other arithmetic  16.7 us (9%)
  local copies, waits for them, and re-layouts  16.4 us (9%)
    pallas_call x2, Pallas kernels, window_grads(): pl.pallas_call(make_window_kernel(first), out_shape=[jax.ShapeDtypeStruct...  103 us
    ppermute x10, waiting for transfers between devices, swapped(): lax.ppermute(block, axis, [(i, i ^ distance) for i in range(lax.axis_size...  21.5 us
    ppermute x6, starting transfers between devices, moved(): lax.ppermute(block, ('gx', 'gy', 'gz'), halo_route(distance_a, distance_b))  15.7 us
    ppermute x6, waiting for transfers between devices, moved(): lax.ppermute(block, ('gx', 'gy', 'gz'), halo_route(distance_a, distance_b))  7.12 us
    ppermute x10, starting transfers between devices, swapped(): lax.ppermute(block, axis, [(i, i ^ distance) for i in range(lax.axis_size...  5.72 us
    another operation x4, other arithmetic, per_device(): both = shifted_block(jnp.stack([tokens, grads_out]))  4.87 us
  transfers between devices with their start and end apart: 16, of which 10 were waited for; matrix products, arithmetic and copies ran while one was open for 7% of the time, Pallas kernels for 15%

profile of v8, /device:TPU:5, one launch (start us, length us, event | category | flops | bytes accessed | tf_op | source)
XLA Modules:
  0.0 187.3 jit_solution(9411273277308671525)
XLA Ops:
  0.7 1.5 fusion.2
  2.2 1.3 copy.19
  3.5 3.3 %collective-permute-start.1 = (bf16[2,4,12,3072]{3,1,2,0:T(4,128)(2,1)}, bf16[2,4,12,3072]{3,1,2,0:T(4,128)(2,1)}, u32[]{:S(2)}, u32[]{:S(2)}) collective-permute-start(bf16[2,4,12,3072]{3,1,2,0:T(4,128)(2,1)} %copy.19), channel_id=1, source_target_pairs={{0,24},{1,25},{2,26},{3,27},{4,28},{5,29},{6,30},{7,31},{8,0},{9,1... | collective-permute-start | bytes 1769480 | tf_op jit(solution)/shard_map/ppermute | solution.py:247
  6.8 1.0 fusion.3
  7.8 0.2 collective-permute-start
  8.1 2.0 %collective-permute-start.2 = (bf16[2,4,4,3072]{3,2,1,0:T(4,128)(2,1)S(1)}, bf16[2,4,4,3072]{3,2,1,0:T(4,128)(2,1)S(1)}, u32[]{:S(2)}, u32[]{:S(2)}) collective-permute-start(bf16[2,4,4,3072]{3,2,1,0:T(4,128)(2,1)S(1)} %pad_maximum_fusion.1), channel_id=1, source_target_pairs={{0,31},{1,24},{2,25},{3,26},{4,27},{5,28},{6,29},{7,30},{8,7},{9,0... | collective-permute-start | bytes 589832 | tf_op jit(solution)/shard_map/ppermute | solution.py:247
  10.2 2.3 %fusion.1 = bf16[2,12,12,3072]{3,2,1,0:T(8,128)(2,1)} fusion(bf16[1,16,16,3072]{3,2,1,0:T(8,128)(2,1)S(1)} %bitcast.17, bf16[1,16,16,3072]{3,2,1,0:T(8,128)(2,1)S(1)} %bitcast.13), kind=kLoop, calls=%fused_computation.9 | loop fusion | flops 884736 | bytes 4915200 | tf_op jit(solution)/shard_map/stack | solution.py:274
  12.9 2.0 %broadcast_in_dim_reshape.8.refs_2_.refs_1_ = s32[8,512,1]{2,1,0:T(8,128)} reshape(s32[2,2,2,8,8,8]{5,4,3,2,1,0:T(8,128)S(1)} %bitcast.20) | data formatting | bytes 32768 | tf_op jit(solution)/shard_map/broadcast_in_dim;reshape | solution.py:288
  14.9 0.8 broadcast_in_dim_reshape.7.refs_3_.refs_2_
  15.7 0.9 copy.22
  16.6 0.8 copy.26.refs_4_.refs_3_
  17.4 27.6 %shard_map.93 = (f32[8,8,3072]{2,1,0:T(8,128)}, f32[576,192]{1,0:T(8,128)}, f32[192,192]{1,0:T(8,128)}, f32[192,1]{1,0:T(8,128)}) custom-call(bf16[16,16,3072]{2,1,0:T(8,128)(2,1)} %refs_0_.1, bf16[16,16,3072]{2,1,0:T(8,128)(2,1)} %refs_1_.1, s32[8,512,1]{2,1,0:T(8,128)} %broadcast_in_dim_reshape.8.refs_2_.refs_1_, ...), custom_call_target="tpu_custom_call" | custom-call | tf_op jit(solution)/shard_map/pallas_call | solution.py:176
  45.0 1.3 copy.20
  46.3 3.4 %maximum_maximum_fusion.refs_0_ = bf16[2,16,16,3072]{3,2,1,0:T(8,128)(2,1)} fusion(bf16[2,4,4,3072]{3,2,1,0:T(4,128)(2,1)S(1)} %collective-permute-done.2, bf16[2,4,12,3072]{3,2,1,0:T(8,128)(2,1)S(1)} %copy.20, bf16[2,12,4,3072]{3,2,1,0:T(4,128)(2,1)} %collective-permute-done, bf16[2,12,12,3072]{3,2,1,0:T(8,128)(2,1)S(1)} %copy-done.4), kind=kLoop, calls=%fused_computation.6 | loop fusion | flops 12582912 | bytes 6291456 | tf_op jit(solution)/shard_map/concatenate | solution.py:256
  49.6 75.7 %shard_map.94 = (f32[16,16,3072]{2,1,0:T(8,128)}, f32[576,192]{1,0:T(8,128)}, f32[192,192]{1,0:T(8,128)}, f32[192,1]{1,0:T(8,128)}) custom-call(bf16[2,16,16,3072]{3,2,1,0:T(8,128)(2,1)} %maximum_maximum_fusion.refs_0_, s32[8,512,1]{2,1,0:T(8,128)} %broadcast_in_dim_reshape.8.refs_2_.refs_1_, s32[8,1,512]{2,1,0:T(1,128)} %broadcast_in_dim_reshape.7.refs_3_.refs_2_, ...), custom_call_target="tpu_custom_call" | custom-call | tf_op jit(solution)/shard_map/pallas_call | solution.py:176
  125.4 2.3 %reshape.86 = f32[110592]{0:T(1024)} reshape(f32[576,192]{1,0:T(8,128)} %get-tuple-element.17) | data formatting | bytes 884736 | tf_op jit(solution)/shard_map/reshape | solution.py:203
  127.6 1.0 reshape.87
  128.7 1.0 reduce
  129.7 1.1 pad_maximum_fusion
  130.8 0.8 copy-done.5
  131.7 0.8 collective-permute-start.6
  132.5 1.3 collective-permute-done.6
  133.9 1.2 dynamic-slice_add_fusion
  135.1 0.8 dynamic_slice.33
  135.9 0.8 collective-permute-start.7
  136.7 4.6 %collective-permute-done.7 = f32[36912]{0:T(1024)} collective-permute-done((f32[36912]{0:T(1024)}, f32[36912]{0:T(1024)}, u32[]{:S(2)}, u32[]{:S(2)}) %collective-permute-start.7) | collective-permute-done | bytes 147680 | tf_op jit(solution)/shard_map/ppermute | solution.py:196
  141.3 1.0 dynamic-slice_add_fusion.1
  142.4 0.7 copy-done.7
  143.1 1.4 collective-permute-start.8
  144.5 1.9 %collective-permute-done.8 = f32[18456]{0:T(1024)S(1)} collective-permute-done((f32[18456]{0:T(1024)S(1)}, f32[18456]{0:T(1024)S(1)}, u32[]{:S(2)}, u32[]{:S(2)}) %collective-permute-start.8) | collective-permute-done | bytes 73856 | tf_op jit(solution)/shard_map/ppermute | solution.py:196
  146.4 1.0 dynamic-slice_add_fusion.2
  147.6 3.7 %collective-permute-done.9 = f32[9228]{0:T(1024)S(1)} collective-permute-done((f32[9228]{0:T(1024)S(1)}, f32[9228]{0:T(1024)S(1)}, u32[]{:S(2)}, u32[]{:S(2)}) %collective-permute-start.9) | collective-permute-done | bytes 36944 | tf_op jit(solution)/shard_map/ppermute | solution.py:196
  151.5 0.3 collective-permute-start.10
  151.8 2.6 %collective-permute-done.10 = f32[4614]{0:T(1024)S(1)} collective-permute-done((f32[4614]{0:T(1024)S(1)}, f32[4614]{0:T(1024)S(1)}, u32[]{:S(2)}, u32[]{:S(2)}) %collective-permute-start.10) | collective-permute-done | bytes 18488 | tf_op jit(solution)/shard_map/ppermute | solution.py:196
  154.6 2.5 %collective-permute-done.11 = f32[4614]{0:T(1024)S(1)} collective-permute-done((f32[4614]{0:T(1024)S(1)}, f32[4614]{0:T(1024)S(1)}, u32[]{:S(2)}, u32[]{:S(2)}) %collective-permute-start.11) | collective-permute-done | bytes 18488 | tf_op jit(solution)/shard_map/ppermute | solution.py:196
  157.3 3.7 %collective-permute-done.12 = f32[9228]{0:T(1024)S(1)} collective-permute-done((f32[9228]{0:T(1024)S(1)}, f32[9228]{0:T(1024)S(1)}, u32[]{:S(2)}, u32[]{:S(2)}) %collective-permute-start.12) | collective-permute-done | bytes 36944 | tf_op jit(solution)/shard_map/ppermute | solution.py:196
  161.1 1.4 collective-permute-start.13
  163.4 8.6 %collective-permute-start.3 = (bf16[4,4,3072]{2,1,0:T(4,128)(2,1)S(1)}, bf16[4,4,3072]{2,1,0:T(4,128)(2,1)S(1)}, u32[]{:S(2)}, u32[]{:S(2)}) collective-permute-start(bf16[4,4,3072]{2,1,0:T(4,128)(2,1)S(1)} %slice.55), channel_id=1, source_target_pairs={{0,9},{1,10},{2,11},{3,12},{4,13},{5,14},{6,15},{7,8},{8,17},{9,18... | collective-permute-start | bytes 294920 | tf_op jit(solution)/shard_map/ppermute | solution.py:247
  172.0 1.3 collective-permute-start.5
  173.4 0.7 collective-permute-start.14
  174.1 0.6 collective-permute-done.3
  174.9 6.5 %collective-permute-done.5 = bf16[12,4,3072]{2,1,0:T(4,128)(2,1)S(1)} collective-permute-done((bf16[12,4,3072]{2,1,0:T(4,128)(2,1)S(1)}, bf16[12,4,3072]{2,1,0:T(4,128)(2,1)S(1)}, u32[]{:S(2)}, u32[]{:S(2)}) %collective-permute-start.5) | collective-permute-done | bytes 294944 | tf_op jit(solution)/shard_map/ppermute | solution.py:247
  181.4 1.0 collective-permute-done.14
  182.6 1.8 fusion
  184.4 0.2 maximum_select_fusion
  184.7 0.7 slice.60
  185.4 0.6 slice.58
  186.3 1.0 reshape.89
  (56 shorter events, 3.4 us)
Async XLA Ops:
  0.6 6.1 %copy-start.2 = (bf16[16,16,3072]{2,1,0:T(8,128)(2,1)S(1)}, bf16[16,16,3072]{2,1,0:T(8,128)(2,1)}, u32[]{:S(2)}) copy-start(bf16[16,16,3072]{2,1,0:T(8,128)(2,1)} %refs_0_.1) | copy-start | bytes 4718596
  0.6 6.1 %copy-start = (bf16[16,16,3072]{2,1,0:T(8,128)(2,1)S(1)}, bf16[16,16,3072]{2,1,0:T(8,128)(2,1)}, u32[]{:S(2)}) copy-start(bf16[16,16,3072]{2,1,0:T(8,128)(2,1)} %refs_1_.1) | copy-start | bytes 4718596
  3.5 41.5 %collective-permute-start.1 = (bf16[2,4,12,3072]{3,1,2,0:T(4,128)(2,1)}, bf16[2,4,12,3072]{3,1,2,0:T(4,128)(2,1)}, u32[]{:S(2)}, u32[]{:S(2)}) collective-permute-start(bf16[2,4,12,3072]{3,1,2,0:T(4,128)(2,1)} %copy.19), channel_id=1, source_target_pairs={{0,24},{1,25},{2,26},{3,27},{4,28},{5,29},{6,30},{7,31},{8,0},{9,1... | collective-permute-start | bytes 1769480 | tf_op jit(solution)/shard_map/ppermute | solution.py:247
  7.8 38.4 %collective-permute-start = (bf16[2,12,4,3072]{3,2,1,0:T(4,128)(2,1)}, bf16[2,12,4,3072]{3,2,1,0:T(4,128)(2,1)}, u32[]{:S(2)}, u32[]{:S(2)}) collective-permute-start(bf16[2,12,4,3072]{3,2,1,0:T(4,128)(2,1)} %fusion.3), channel_id=1, source_target_pairs={{0,7},{1,0},{2,1},{3,2},{4,3},{5,4},{6,5},{7,6},{8,15},{9,8},{10,9... | collective-permute-start | bytes 1769480 | tf_op jit(solution)/shard_map/ppermute | solution.py:247
  8.1 38.1 %collective-permute-start.2 = (bf16[2,4,4,3072]{3,2,1,0:T(4,128)(2,1)S(1)}, bf16[2,4,4,3072]{3,2,1,0:T(4,128)(2,1)S(1)}, u32[]{:S(2)}, u32[]{:S(2)}) collective-permute-start(bf16[2,4,4,3072]{3,2,1,0:T(4,128)(2,1)S(1)} %pad_maximum_fusion.1), channel_id=1, source_target_pairs={{0,31},{1,24},{2,25},{3,26},{4,27},{5,28},{6,29},{7,30},{8,7},{9,0... | collective-permute-start | bytes 589832 | tf_op jit(solution)/shard_map/ppermute | solution.py:247
  10.1 2.3 %copy-start.8 = (s32[16,16,16]{2,1,0:T(8,128)S(1)}, s32[16,16,16]{2,1,0:T(8,128)}, u32[]{:S(2)}) copy-start(s32[16,16,16]{2,1,0:T(8,128)} %param.8) | copy-start | bytes 49156
  12.5 3.2 %copy-start.6 = (bf16[192,576]{1,0:T(8,128)(2,1)S(1)}, bf16[192,576]{1,0:T(8,128)(2,1)}, u32[]{:S(2)}) copy-start(bf16[192,576]{1,0:T(8,128)(2,1)} %refs_5_.1) | copy-start | bytes 663556
  12.5 4.1 %copy-start.9 = (f32[192]{0:T(256)S(1)}, f32[192]{0:T(256)}, u32[]{:S(2)}) copy-start(f32[192]{0:T(256)} %param.9) | copy-start | bytes 2308
  17.4 28.9 %copy-start.4 = (bf16[2,12,12,3072]{3,2,1,0:T(8,128)(2,1)S(1)}, bf16[2,12,12,3072]{3,2,1,0:T(8,128)(2,1)}, u32[]{:S(2)}) copy-start(bf16[2,12,12,3072]{3,2,1,0:T(8,128)(2,1)} %fusion.1) | copy-start | bytes 5308420
  125.3 37.1 %copy-start.3 = (f32[16,16,3072]{2,1,0:T(8,128)S(1)}, f32[16,16,3072]{2,1,0:T(8,128)}, u32[]{:S(2)}) copy-start(f32[16,16,3072]{2,1,0:T(8,128)} %get-tuple-element.16) | copy-start | bytes 9437188
  130.8 0.8 copy-start.5
  131.7 2.2 %collective-permute-start.6 = (f32[73824]{0:T(1024)S(1)}, f32[73824]{0:T(1024)}, u32[]{:S(2)}, u32[]{:S(2)}) collective-permute-start(f32[73824]{0:T(1024)S(1)} %dynamic_slice.31), channel_id=1, source_target_pairs={{0,2},{2,0},{4,6},{6,4},{1,3},{3,1},{5,7},{7,5},{8,10},{10,8},{12,... | collective-permute-start | bytes 885896 | tf_op jit(solution)/shard_map/ppermute | solution.py:196
  135.9 5.5 %collective-permute-start.7 = (f32[36912]{0:T(1024)}, f32[36912]{0:T(1024)}, u32[]{:S(2)}, u32[]{:S(2)}) collective-permute-start(f32[36912]{0:T(1024)} %dynamic_slice.33), channel_id=1, source_target_pairs={{0,4},{2,6},{4,0},{6,2},{1,5},{3,7},{5,1},{7,3},{8,12},{10,14},{12... | collective-permute-start | bytes 442952 | tf_op jit(solution)/shard_map/ppermute | solution.py:196
  142.4 0.7 copy-start.7
  143.1 3.3 %collective-permute-start.8 = (f32[18456]{0:T(1024)S(1)}, f32[18456]{0:T(1024)S(1)}, u32[]{:S(2)}, u32[]{:S(2)}) collective-permute-start(f32[18456]{0:T(1024)S(1)} %dynamic_slice.35), channel_id=1, source_target_pairs={{0,8},{8,0},{16,24},{24,16},{1,9},{9,1},{17,25},{25,17},{2,10},{10... | collective-permute-start | bytes 221480 | tf_op jit(solution)/shard_map/ppermute | solution.py:196
  147.5 3.8 %collective-permute-start.9 = (f32[9228]{0:T(1024)S(1)}, f32[9228]{0:T(1024)S(1)}, u32[]{:S(2)}, u32[]{:S(2)}) collective-permute-start(f32[9228]{0:T(1024)S(1)} %dynamic_slice.37), channel_id=1, source_target_pairs={{0,16},{8,24},{16,0},{24,8},{1,17},{9,25},{17,1},{25,9},{2,18},{10... | collective-permute-start | bytes 110744 | tf_op jit(solution)/shard_map/ppermute | solution.py:196
  151.5 2.9 %collective-permute-start.10 = (f32[4614]{0:T(1024)S(1)}, f32[4614]{0:T(1024)S(1)}, u32[]{:S(2)}, u32[]{:S(2)}) collective-permute-start(f32[4614]{0:T(1024)S(1)} %dynamic_slice.39), channel_id=1, source_target_pairs={{0,1},{1,0},{2,3},{3,2},{4,5},{5,4},{6,7},{7,6},{8,9},{9,8},{10,11... | collective-permute-start | bytes 55376 | tf_op jit(solution)/shard_map/ppermute | solution.py:196
  154.5 2.6 %collective-permute-start.11 = (f32[4614]{0:T(1024)S(1)}, f32[4614]{0:T(1024)S(1)}, u32[]{:S(2)}, u32[]{:S(2)}) collective-permute-start(f32[4614]{0:T(1024)S(1)} %dynamic-slice_add_fusion.4), channel_id=1, source_target_pairs={{0,1},{1,0},{2,3},{3,2},{4,5},{5,4},{6,7},{7,6},{8,9},{9,8},{10,11... | collective-permute-start | bytes 55376 | tf_op jit(solution)/shard_map/ppermute | solution.py:196
  157.2 3.8 %collective-permute-start.12 = (f32[9228]{0:T(1024)S(1)}, f32[9228]{0:T(1024)S(1)}, u32[]{:S(2)}, u32[]{:S(2)}) collective-permute-start(f32[9228]{0:T(1024)S(1)} %maximum_select_fusion.4), channel_id=1, source_target_pairs={{0,16},{8,24},{16,0},{24,8},{1,17},{9,25},{17,1},{25,9},{2,18},{10... | collective-permute-start | bytes 110744 | tf_op jit(solution)/shard_map/ppermute | solution.py:196
  161.1 12.2 %collective-permute-start.13 = (f32[18456]{0:T(1024)S(1)}, f32[18456]{0:T(1024)S(1)}, u32[]{:S(2)}, u32[]{:S(2)}) collective-permute-start(f32[18456]{0:T(1024)S(1)} %maximum_select_fusion.3), channel_id=1, source_target_pairs={{0,8},{8,0},{16,24},{24,16},{1,9},{9,1},{17,25},{25,17},{2,10},{10... | collective-permute-start | bytes 221480 | tf_op jit(solution)/shard_map/ppermute | solution.py:196
  163.0 19.7 %copy-start.1 = (bf16[16,16,3072]{2,1,0:T(8,128)(2,1)S(1)}, bf16[16,16,3072]{2,1,0:T(8,128)(2,1)}, u32[]{:S(2)}) copy-start(bf16[16,16,3072]{2,1,0:T(8,128)(2,1)} %refs_1_.1) | copy-start | bytes 4718596
  163.2 11.5 %collective-permute-start.4 = (bf16[4,12,3072]{2,1,0:T(8,128)(2,1)S(1)}, bf16[4,12,3072]{2,1,0:T(8,128)(2,1)S(1)}, u32[]{:S(2)}, u32[]{:S(2)}) collective-permute-start(bf16[4,12,3072]{2,1,0:T(8,128)(2,1)S(1)} %slice.56), channel_id=1, source_target_pairs={{0,8},{1,9},{2,10},{3,11},{4,12},{5,13},{6,14},{7,15},{8,16},{9,17... | collective-permute-start | bytes 884744 | tf_op jit(solution)/shard_map/ppermute | solution.py:247
  163.4 11.3 %collective-permute-start.3 = (bf16[4,4,3072]{2,1,0:T(4,128)(2,1)S(1)}, bf16[4,4,3072]{2,1,0:T(4,128)(2,1)S(1)}, u32[]{:S(2)}, u32[]{:S(2)}) collective-permute-start(bf16[4,4,3072]{2,1,0:T(4,128)(2,1)S(1)} %slice.55), channel_id=1, source_target_pairs={{0,9},{1,10},{2,11},{3,12},{4,13},{5,14},{6,15},{7,8},{8,17},{9,18... | collective-permute-start | bytes 294920 | tf_op jit(solution)/shard_map/ppermute | solution.py:247
  172.0 9.3 %collective-permute-start.5 = (bf16[12,4,3072]{2,1,0:T(4,128)(2,1)S(1)}, bf16[12,4,3072]{2,1,0:T(4,128)(2,1)S(1)}, u32[]{:S(2)}, u32[]{:S(2)}) collective-permute-start(bf16[12,4,3072]{2,1,0:T(4,128)(2,1)S(1)} %slice.57), channel_id=1, source_target_pairs={{0,1},{1,2},{2,3},{3,4},{4,5},{5,6},{6,7},{7,0},{8,9},{9,10},{10,1... | collective-permute-start | bytes 884744 | tf_op jit(solution)/shard_map/ppermute | solution.py:247
  173.4 9.0 %collective-permute-start.14 = (f32[36912]{0:T(1024)S(1)}, f32[36912]{0:T(1024)S(1)}, u32[]{:S(2)}, u32[]{:S(2)}) collective-permute-start(f32[36912]{0:T(1024)S(1)} %maximum_select_fusion.2), channel_id=1, source_target_pairs={{0,4},{2,6},{4,0},{6,2},{1,5},{3,7},{5,1},{7,3},{8,12},{10,14},{12... | collective-permute-start | bytes 442952 | tf_op jit(solution)/shard_map/ppermute | solution.py:196
  182.5 1.9 %collective-permute-start.15 = (f32[73824]{0:T(1024)S(1)}, f32[73824]{0:T(1024)S(1)}, u32[]{:S(2)}, u32[]{:S(2)}) collective-permute-start(f32[73824]{0:T(1024)S(1)} %maximum_select_fusion.1), channel_id=1, source_target_pairs={{0,2},{2,0},{4,6},{6,4},{1,3},{3,1},{5,7},{7,5},{8,10},{10,8},{12,... | collective-permute-start | bytes 885896 | tf_op jit(solution)/shard_map/ppermute | solution.py:196

commit v9 on v6

--- a/solution.py
+++ b/solution.py
@@ -142,7 +142,7 @@
                 drow_s[pl.ds(qo + 2 * C, HEAD), :] = dv_t.astype(bf16).astype(f32)
                 return carry
 
-            lax.fori_loop(0, HEADS, head_step, 0)
+            lax.fori_loop(0, HEADS, head_step, 0, unroll=2)
             rows_t = drow_s[...].astype(bf16)
             gqkvT_ref[...] += lax.dot_general(rows_t, normed, nt, preferred_element_type=f32)
             grad_normed = jnp.dot(wqkv_ref[...], rows_t, preferred_element_type=f32)

time: 170 us -> 166 us (0.976)
  Pallas kernels: 83.7 us -> 79.4 us
    pallas_call x2, Pallas kernels: 83.7 us -> 79.4 us  [window_grads(): pl.pallas_call(make_window_kernel(first), out_shape=[jax.ShapeDtypeStruct...]
  transfers between devices with their start and end apart: 16 -> 16, of which waited for: 10 -> 10; matrix products, arithmetic and copies ran while one was open for 7% -> 8% of each run, Pallas kernels for 14% -> 13%
where the time goes in v9:
time: 166 us; the launch traced here: 163 us
  Pallas kernels  79.4 us (48%)
  waiting for transfers between devices  28.6 us (17%)
  starting transfers between devices  21.4 us (13%)
  other arithmetic  16.7 us (10%)
  local copies, waits for them, and re-layouts  16.4 us (10%)
    pallas_call x2, Pallas kernels, window_grads(): pl.pallas_call(make_window_kernel(first), out_shape=[jax.ShapeDtypeStruct...  79.4 us
    ppermute x10, waiting for transfers between devices, swapped(): lax.ppermute(block, axis, [(i, i ^ distance) for i in range(lax.axis_size...  21.5 us
    ppermute x6, starting transfers between devices, moved(): lax.ppermute(block, ('gx', 'gy', 'gz'), halo_route(distance_a, distance_b))  15.7 us
    ppermute x6, waiting for transfers between devices, moved(): lax.ppermute(block, ('gx', 'gy', 'gz'), halo_route(distance_a, distance_b))  7.12 us
    ppermute x10, starting transfers between devices, swapped(): lax.ppermute(block, axis, [(i, i ^ distance) for i in range(lax.axis_size...  5.72 us
    another operation x4, other arithmetic, per_device(): both = shifted_block(jnp.stack([tokens, grads_out]))  4.87 us
    concatenate x1, other arithmetic, shifted_block(): return jnp.concatenate([upper, lower], axis=1)  3.36 us
    add x5, other arithmetic, summed_everywhere(): values = keep + swapped(send, axis, distance)  3.36 us
  transfers between devices with their start and end apart: 16, of which 10 were waited for; matrix products, arithmetic and copies ran while one was open for 8% of the time, Pallas kernels for 13%

profile of v9, /device:TPU:5, one launch (start us, length us, event | category | flops | bytes accessed | tf_op | source)
XLA Modules:
  0.0 163.3 jit_solution(13022234542192437267)
XLA Ops:
  0.7 1.5 fusion.2
  2.2 1.3 copy.19
  3.5 3.3 %collective-permute-start.1 = (bf16[2,4,12,3072]{3,1,2,0:T(4,128)(2,1)}, bf16[2,4,12,3072]{3,1,2,0:T(4,128)(2,1)}, u32[]{:S(2)}, u32[]{:S(2)}) collective-permute-start(bf16[2,4,12,3072]{3,1,2,0:T(4,128)(2,1)} %copy.19), channel_id=1, source_target_pairs={{0,24},{1,25},{2,26},{3,27},{4,28},{5,29},{6,30},{7,31},{8,0},{9,1... | collective-permute-start | bytes 1769480 | tf_op jit(solution)/shard_map/ppermute | solution.py:247
  6.8 1.0 fusion.3
  7.8 0.2 collective-permute-start
  8.1 2.0 %collective-permute-start.2 = (bf16[2,4,4,3072]{3,2,1,0:T(4,128)(2,1)S(1)}, bf16[2,4,4,3072]{3,2,1,0:T(4,128)(2,1)S(1)}, u32[]{:S(2)}, u32[]{:S(2)}) collective-permute-start(bf16[2,4,4,3072]{3,2,1,0:T(4,128)(2,1)S(1)} %pad_maximum_fusion.1), channel_id=1, source_target_pairs={{0,31},{1,24},{2,25},{3,26},{4,27},{5,28},{6,29},{7,30},{8,7},{9,0... | collective-permute-start | bytes 589832 | tf_op jit(solution)/shard_map/ppermute | solution.py:247
  10.2 2.3 %fusion.1 = bf16[2,12,12,3072]{3,2,1,0:T(8,128)(2,1)} fusion(bf16[1,16,16,3072]{3,2,1,0:T(8,128)(2,1)S(1)} %bitcast.17, bf16[1,16,16,3072]{3,2,1,0:T(8,128)(2,1)S(1)} %bitcast.13), kind=kLoop, calls=%fused_computation.9 | loop fusion | flops 884736 | bytes 4915200 | tf_op jit(solution)/shard_map/stack | solution.py:274
  12.9 2.0 %broadcast_in_dim_reshape.8.refs_2_.refs_1_ = s32[8,512,1]{2,1,0:T(8,128)} reshape(s32[2,2,2,8,8,8]{5,4,3,2,1,0:T(8,128)S(1)} %bitcast.20) | data formatting | bytes 32768 | tf_op jit(solution)/shard_map/broadcast_in_dim;reshape | solution.py:288
  14.9 0.8 broadcast_in_dim_reshape.7.refs_3_.refs_2_
  15.7 0.9 copy.22
  16.6 0.8 copy.26.refs_4_.refs_3_
  17.4 21.5 %shard_map.93 = (f32[8,8,3072]{2,1,0:T(8,128)}, f32[576,192]{1,0:T(8,128)}, f32[192,192]{1,0:T(8,128)}, f32[192,1]{1,0:T(8,128)}) custom-call(bf16[16,16,3072]{2,1,0:T(8,128)(2,1)} %refs_0_.1, bf16[16,16,3072]{2,1,0:T(8,128)(2,1)} %refs_1_.1, s32[8,512,1]{2,1,0:T(8,128)} %broadcast_in_dim_reshape.8.refs_2_.refs_1_, ...), custom_call_target="tpu_custom_call" | custom-call | tf_op jit(solution)/shard_map/pallas_call | solution.py:176
  38.8 1.3 copy.20
  40.1 3.4 %maximum_maximum_fusion.refs_0_ = bf16[2,16,16,3072]{3,2,1,0:T(8,128)(2,1)} fusion(bf16[2,4,4,3072]{3,2,1,0:T(4,128)(2,1)S(1)} %collective-permute-done.2, bf16[2,4,12,3072]{3,2,1,0:T(8,128)(2,1)S(1)} %copy.20, bf16[2,12,4,3072]{3,2,1,0:T(4,128)(2,1)} %collective-permute-done, bf16[2,12,12,3072]{3,2,1,0:T(8,128)(2,1)S(1)} %copy-done.4), kind=kLoop, calls=%fused_computation.6 | loop fusion | flops 12582912 | bytes 6291456 | tf_op jit(solution)/shard_map/concatenate | solution.py:256
  43.5 57.9 %shard_map.94 = (f32[16,16,3072]{2,1,0:T(8,128)}, f32[576,192]{1,0:T(8,128)}, f32[192,192]{1,0:T(8,128)}, f32[192,1]{1,0:T(8,128)}) custom-call(bf16[2,16,16,3072]{3,2,1,0:T(8,128)(2,1)} %maximum_maximum_fusion.refs_0_, s32[8,512,1]{2,1,0:T(8,128)} %broadcast_in_dim_reshape.8.refs_2_.refs_1_, s32[8,1,512]{2,1,0:T(1,128)} %broadcast_in_dim_reshape.7.refs_3_.refs_2_, ...), custom_call_target="tpu_custom_call" | custom-call | tf_op jit(solution)/shard_map/pallas_call | solution.py:176
  101.4 2.3 %reshape.86 = f32[110592]{0:T(1024)} reshape(f32[576,192]{1,0:T(8,128)} %get-tuple-element.17) | data formatting | bytes 884736 | tf_op jit(solution)/shard_map/reshape | solution.py:203
  103.7 1.0 reshape.87
  104.7 1.0 reduce
  105.7 1.1 pad_maximum_fusion
  106.8 0.8 copy-done.5
  107.8 0.8 collective-permute-start.6
  108.6 1.3 collective-permute-done.6
  109.9 1.2 dynamic-slice_add_fusion
  111.2 0.8 dynamic_slice.33
  111.9 0.8 collective-permute-start.7
  112.8 4.6 %collective-permute-done.7 = f32[36912]{0:T(1024)} collective-permute-done((f32[36912]{0:T(1024)}, f32[36912]{0:T(1024)}, u32[]{:S(2)}, u32[]{:S(2)}) %collective-permute-start.7) | collective-permute-done | bytes 147680 | tf_op jit(solution)/shard_map/ppermute | solution.py:196
  117.4 1.0 dynamic-slice_add_fusion.1
  118.4 0.7 copy-done.7
  119.2 1.4 collective-permute-start.8
  120.5 1.9 %collective-permute-done.8 = f32[18456]{0:T(1024)S(1)} collective-permute-done((f32[18456]{0:T(1024)S(1)}, f32[18456]{0:T(1024)S(1)}, u32[]{:S(2)}, u32[]{:S(2)}) %collective-permute-start.8) | collective-permute-done | bytes 73856 | tf_op jit(solution)/shard_map/ppermute | solution.py:196
  122.5 1.0 dynamic-slice_add_fusion.2
  123.6 3.7 %collective-permute-done.9 = f32[9228]{0:T(1024)S(1)} collective-permute-done((f32[9228]{0:T(1024)S(1)}, f32[9228]{0:T(1024)S(1)}, u32[]{:S(2)}, u32[]{:S(2)}) %collective-permute-start.9) | collective-permute-done | bytes 36944 | tf_op jit(solution)/shard_map/ppermute | solution.py:196
  127.5 0.3 collective-permute-start.10
  127.8 2.6 %collective-permute-done.10 = f32[4614]{0:T(1024)S(1)} collective-permute-done((f32[4614]{0:T(1024)S(1)}, f32[4614]{0:T(1024)S(1)}, u32[]{:S(2)}, u32[]{:S(2)}) %collective-permute-start.10) | collective-permute-done | bytes 18488 | tf_op jit(solution)/shard_map/ppermute | solution.py:196
  130.7 2.5 %collective-permute-done.11 = f32[4614]{0:T(1024)S(1)} collective-permute-done((f32[4614]{0:T(1024)S(1)}, f32[4614]{0:T(1024)S(1)}, u32[]{:S(2)}, u32[]{:S(2)}) %collective-permute-start.11) | collective-permute-done | bytes 18488 | tf_op jit(solution)/shard_map/ppermute | solution.py:196
  133.3 3.7 %collective-permute-done.12 = f32[9228]{0:T(1024)S(1)} collective-permute-done((f32[9228]{0:T(1024)S(1)}, f32[9228]{0:T(1024)S(1)}, u32[]{:S(2)}, u32[]{:S(2)}) %collective-permute-start.12) | collective-permute-done | bytes 36944 | tf_op jit(solution)/shard_map/ppermute | solution.py:196
  137.2 1.4 collective-permute-start.13
  139.5 8.6 %collective-permute-start.3 = (bf16[4,4,3072]{2,1,0:T(4,128)(2,1)S(1)}, bf16[4,4,3072]{2,1,0:T(4,128)(2,1)S(1)}, u32[]{:S(2)}, u32[]{:S(2)}) collective-permute-start(bf16[4,4,3072]{2,1,0:T(4,128)(2,1)S(1)} %slice.55), channel_id=1, source_target_pairs={{0,9},{1,10},{2,11},{3,12},{4,13},{5,14},{6,15},{7,8},{8,17},{9,18... | collective-permute-start | bytes 294920 | tf_op jit(solution)/shard_map/ppermute | solution.py:247
  148.1 1.2 collective-permute-start.5
  149.5 0.7 collective-permute-start.14
  150.2 0.6 collective-permute-done.3
  150.9 6.5 %collective-permute-done.5 = bf16[12,4,3072]{2,1,0:T(4,128)(2,1)S(1)} collective-permute-done((bf16[12,4,3072]{2,1,0:T(4,128)(2,1)S(1)}, bf16[12,4,3072]{2,1,0:T(4,128)(2,1)S(1)}, u32[]{:S(2)}, u32[]{:S(2)}) %collective-permute-start.5) | collective-permute-done | bytes 294944 | tf_op jit(solution)/shard_map/ppermute | solution.py:247
  157.5 1.0 collective-permute-done.14
  158.7 1.8 %fusion = bf16[16,16,3072]{2,1,0:T(8,128)(2,1)} fusion(f32[12,12,3072]{2,1,0:T(8,128)S(1)} %slice.44, f32[12,4,3072]{2,1,0:T(4,128)S(1)} %convert_element_type.28, f32[4,16,3072]{2,1,0:T(8,128)S(1)} %maximum_convert_fusion, bf16[16,16,3072]{2,1,0:T(8,128)(2,1)S(1)} %copy-done.1), kind=kLoop, calls=%fused_computation.8 | loop fusion | flops 3932160 | bytes 6291456 | tf_op jit(solution)/shard_map/convert_element_type | solution.py:267
  160.5 0.2 maximum_select_fusion
  160.7 0.7 slice.60
  161.4 0.6 slice.58
  162.4 1.0 reshape.89
  (56 shorter events, 3.4 us)
Async XLA Ops:
  0.6 6.1 %copy-start.2 = (bf16[16,16,3072]{2,1,0:T(8,128)(2,1)S(1)}, bf16[16,16,3072]{2,1,0:T(8,128)(2,1)}, u32[]{:S(2)}) copy-start(bf16[16,16,3072]{2,1,0:T(8,128)(2,1)} %refs_0_.1) | copy-start | bytes 4718596
  0.6 6.1 %copy-start = (bf16[16,16,3072]{2,1,0:T(8,128)(2,1)S(1)}, bf16[16,16,3072]{2,1,0:T(8,128)(2,1)}, u32[]{:S(2)}) copy-start(bf16[16,16,3072]{2,1,0:T(8,128)(2,1)} %refs_1_.1) | copy-start | bytes 4718596
  3.5 35.4 %collective-permute-start.1 = (bf16[2,4,12,3072]{3,1,2,0:T(4,128)(2,1)}, bf16[2,4,12,3072]{3,1,2,0:T(4,128)(2,1)}, u32[]{:S(2)}, u32[]{:S(2)}) collective-permute-start(bf16[2,4,12,3072]{3,1,2,0:T(4,128)(2,1)} %copy.19), channel_id=1, source_target_pairs={{0,24},{1,25},{2,26},{3,27},{4,28},{5,29},{6,30},{7,31},{8,0},{9,1... | collective-permute-start | bytes 1769480 | tf_op jit(solution)/shard_map/ppermute | solution.py:247
  7.8 32.3 %collective-permute-start = (bf16[2,12,4,3072]{3,2,1,0:T(4,128)(2,1)}, bf16[2,12,4,3072]{3,2,1,0:T(4,128)(2,1)}, u32[]{:S(2)}, u32[]{:S(2)}) collective-permute-start(bf16[2,12,4,3072]{3,2,1,0:T(4,128)(2,1)} %fusion.3), channel_id=1, source_target_pairs={{0,7},{1,0},{2,1},{3,2},{4,3},{5,4},{6,5},{7,6},{8,15},{9,8},{10,9... | collective-permute-start | bytes 1769480 | tf_op jit(solution)/shard_map/ppermute | solution.py:247
  8.1 32.0 %collective-permute-start.2 = (bf16[2,4,4,3072]{3,2,1,0:T(4,128)(2,1)S(1)}, bf16[2,4,4,3072]{3,2,1,0:T(4,128)(2,1)S(1)}, u32[]{:S(2)}, u32[]{:S(2)}) collective-permute-start(bf16[2,4,4,3072]{3,2,1,0:T(4,128)(2,1)S(1)} %pad_maximum_fusion.1), channel_id=1, source_target_pairs={{0,31},{1,24},{2,25},{3,26},{4,27},{5,28},{6,29},{7,30},{8,7},{9,0... | collective-permute-start | bytes 589832 | tf_op jit(solution)/shard_map/ppermute | solution.py:247
  10.1 2.3 %copy-start.8 = (s32[16,16,16]{2,1,0:T(8,128)S(1)}, s32[16,16,16]{2,1,0:T(8,128)}, u32[]{:S(2)}) copy-start(s32[16,16,16]{2,1,0:T(8,128)} %param.8) | copy-start | bytes 49156
  12.5 3.2 %copy-start.6 = (bf16[192,576]{1,0:T(8,128)(2,1)S(1)}, bf16[192,576]{1,0:T(8,128)(2,1)}, u32[]{:S(2)}) copy-start(bf16[192,576]{1,0:T(8,128)(2,1)} %refs_5_.1) | copy-start | bytes 663556
  12.5 4.1 %copy-start.9 = (f32[192]{0:T(256)S(1)}, f32[192]{0:T(256)}, u32[]{:S(2)}) copy-start(f32[192]{0:T(256)} %param.9) | copy-start | bytes 2308
  17.4 22.8 %copy-start.4 = (bf16[2,12,12,3072]{3,2,1,0:T(8,128)(2,1)S(1)}, bf16[2,12,12,3072]{3,2,1,0:T(8,128)(2,1)}, u32[]{:S(2)}) copy-start(bf16[2,12,12,3072]{3,2,1,0:T(8,128)(2,1)} %fusion.1) | copy-start | bytes 5308420
  101.4 37.1 %copy-start.3 = (f32[16,16,3072]{2,1,0:T(8,128)S(1)}, f32[16,16,3072]{2,1,0:T(8,128)}, u32[]{:S(2)}) copy-start(f32[16,16,3072]{2,1,0:T(8,128)} %get-tuple-element.16) | copy-start | bytes 9437188
  106.8 0.8 copy-start.5
  107.8 2.2 %collective-permute-start.6 = (f32[73824]{0:T(1024)S(1)}, f32[73824]{0:T(1024)}, u32[]{:S(2)}, u32[]{:S(2)}) collective-permute-start(f32[73824]{0:T(1024)S(1)} %dynamic_slice.31), channel_id=1, source_target_pairs={{0,2},{2,0},{4,6},{6,4},{1,3},{3,1},{5,7},{7,5},{8,10},{10,8},{12,... | collective-permute-start | bytes 885896 | tf_op jit(solution)/shard_map/ppermute | solution.py:196
  111.9 5.5 %collective-permute-start.7 = (f32[36912]{0:T(1024)}, f32[36912]{0:T(1024)}, u32[]{:S(2)}, u32[]{:S(2)}) collective-permute-start(f32[36912]{0:T(1024)} %dynamic_slice.33), channel_id=1, source_target_pairs={{0,4},{2,6},{4,0},{6,2},{1,5},{3,7},{5,1},{7,3},{8,12},{10,14},{12... | collective-permute-start | bytes 442952 | tf_op jit(solution)/shard_map/ppermute | solution.py:196
  118.4 0.7 copy-start.7
  119.2 3.3 %collective-permute-start.8 = (f32[18456]{0:T(1024)S(1)}, f32[18456]{0:T(1024)S(1)}, u32[]{:S(2)}, u32[]{:S(2)}) collective-permute-start(f32[18456]{0:T(1024)S(1)} %dynamic_slice.35), channel_id=1, source_target_pairs={{0,8},{8,0},{16,24},{24,16},{1,9},{9,1},{17,25},{25,17},{2,10},{10... | collective-permute-start | bytes 221480 | tf_op jit(solution)/shard_map/ppermute | solution.py:196
  123.6 3.8 %collective-permute-start.9 = (f32[9228]{0:T(1024)S(1)}, f32[9228]{0:T(1024)S(1)}, u32[]{:S(2)}, u32[]{:S(2)}) collective-permute-start(f32[9228]{0:T(1024)S(1)} %dynamic_slice.37), channel_id=1, source_target_pairs={{0,16},{8,24},{16,0},{24,8},{1,17},{9,25},{17,1},{25,9},{2,18},{10... | collective-permute-start | bytes 110744 | tf_op jit(solution)/shard_map/ppermute | solution.py:196
  127.5 2.9 %collective-permute-start.10 = (f32[4614]{0:T(1024)S(1)}, f32[4614]{0:T(1024)S(1)}, u32[]{:S(2)}, u32[]{:S(2)}) collective-permute-start(f32[4614]{0:T(1024)S(1)} %dynamic_slice.39), channel_id=1, source_target_pairs={{0,1},{1,0},{2,3},{3,2},{4,5},{5,4},{6,7},{7,6},{8,9},{9,8},{10,11... | collective-permute-start | bytes 55376 | tf_op jit(solution)/shard_map/ppermute | solution.py:196
  130.5 2.6 %collective-permute-start.11 = (f32[4614]{0:T(1024)S(1)}, f32[4614]{0:T(1024)S(1)}, u32[]{:S(2)}, u32[]{:S(2)}) collective-permute-start(f32[4614]{0:T(1024)S(1)} %dynamic-slice_add_fusion.4), channel_id=1, source_target_pairs={{0,1},{1,0},{2,3},{3,2},{4,5},{5,4},{6,7},{7,6},{8,9},{9,8},{10,11... | collective-permute-start | bytes 55376 | tf_op jit(solution)/shard_map/ppermute | solution.py:196
  133.3 3.8 %collective-permute-start.12 = (f32[9228]{0:T(1024)S(1)}, f32[9228]{0:T(1024)S(1)}, u32[]{:S(2)}, u32[]{:S(2)}) collective-permute-start(f32[9228]{0:T(1024)S(1)} %maximum_select_fusion.4), channel_id=1, source_target_pairs={{0,16},{8,24},{16,0},{24,8},{1,17},{9,25},{17,1},{25,9},{2,18},{10... | collective-permute-start | bytes 110744 | tf_op jit(solution)/shard_map/ppermute | solution.py:196
  137.2 12.2 %collective-permute-start.13 = (f32[18456]{0:T(1024)S(1)}, f32[18456]{0:T(1024)S(1)}, u32[]{:S(2)}, u32[]{:S(2)}) collective-permute-start(f32[18456]{0:T(1024)S(1)} %maximum_select_fusion.3), channel_id=1, source_target_pairs={{0,8},{8,0},{16,24},{24,16},{1,9},{9,1},{17,25},{25,17},{2,10},{10... | collective-permute-start | bytes 221480 | tf_op jit(solution)/shard_map/ppermute | solution.py:196
  139.0 19.7 %copy-start.1 = (bf16[16,16,3072]{2,1,0:T(8,128)(2,1)S(1)}, bf16[16,16,3072]{2,1,0:T(8,128)(2,1)}, u32[]{:S(2)}) copy-start(bf16[16,16,3072]{2,1,0:T(8,128)(2,1)} %refs_1_.1) | copy-start | bytes 4718596
  139.3 11.5 %collective-permute-start.4 = (bf16[4,12,3072]{2,1,0:T(8,128)(2,1)S(1)}, bf16[4,12,3072]{2,1,0:T(8,128)(2,1)S(1)}, u32[]{:S(2)}, u32[]{:S(2)}) collective-permute-start(bf16[4,12,3072]{2,1,0:T(8,128)(2,1)S(1)} %slice.56), channel_id=1, source_target_pairs={{0,8},{1,9},{2,10},{3,11},{4,12},{5,13},{6,14},{7,15},{8,16},{9,17... | collective-permute-start | bytes 884744 | tf_op jit(solution)/shard_map/ppermute | solution.py:247
  139.5 11.3 %collective-permute-start.3 = (bf16[4,4,3072]{2,1,0:T(4,128)(2,1)S(1)}, bf16[4,4,3072]{2,1,0:T(4,128)(2,1)S(1)}, u32[]{:S(2)}, u32[]{:S(2)}) collective-permute-start(bf16[4,4,3072]{2,1,0:T(4,128)(2,1)S(1)} %slice.55), channel_id=1, source_target_pairs={{0,9},{1,10},{2,11},{3,12},{4,13},{5,14},{6,15},{7,8},{8,17},{9,18... | collective-permute-start | bytes 294920 | tf_op jit(solution)/shard_map/ppermute | solution.py:247
  148.1 9.3 %collective-permute-start.5 = (bf16[12,4,3072]{2,1,0:T(4,128)(2,1)S(1)}, bf16[12,4,3072]{2,1,0:T(4,128)(2,1)S(1)}, u32[]{:S(2)}, u32[]{:S(2)}) collective-permute-start(bf16[12,4,3072]{2,1,0:T(4,128)(2,1)S(1)} %slice.57), channel_id=1, source_target_pairs={{0,1},{1,2},{2,3},{3,4},{4,5},{5,6},{6,7},{7,0},{8,9},{9,10},{10,1... | collective-permute-start | bytes 884744 | tf_op jit(solution)/shard_map/ppermute | solution.py:247
  149.5 9.0 %collective-permute-start.14 = (f32[36912]{0:T(1024)S(1)}, f32[36912]{0:T(1024)S(1)}, u32[]{:S(2)}, u32[]{:S(2)}) collective-permute-start(f32[36912]{0:T(1024)S(1)} %maximum_select_fusion.2), channel_id=1, source_target_pairs={{0,4},{2,6},{4,0},{6,2},{1,5},{3,7},{5,1},{7,3},{8,12},{10,14},{12... | collective-permute-start | bytes 442952 | tf_op jit(solution)/shard_map/ppermute | solution.py:196
  158.6 1.9 %collective-permute-start.15 = (f32[73824]{0:T(1024)S(1)}, f32[73824]{0:T(1024)S(1)}, u32[]{:S(2)}, u32[]{:S(2)}) collective-permute-start(f32[73824]{0:T(1024)S(1)} %maximum_select_fusion.1), channel_id=1, source_target_pairs={{0,2},{2,0},{4,6},{6,4},{1,3},{3,1},{5,7},{7,5},{8,10},{10,8},{12,... | collective-permute-start | bytes 885896 | tf_op jit(solution)/shard_map/ppermute | solution.py:196

commit v10 on v9

--- a/solution.py
+++ b/solution.py
@@ -142,7 +142,7 @@
                 drow_s[pl.ds(qo + 2 * C, HEAD), :] = dv_t.astype(bf16).astype(f32)
                 return carry
 
-            lax.fori_loop(0, HEADS, head_step, 0, unroll=2)
+            lax.fori_loop(0, HEADS, head_step, 0, unroll=3)
             rows_t = drow_s[...].astype(bf16)
             gqkvT_ref[...] += lax.dot_general(rows_t, normed, nt, preferred_element_type=f32)
             grad_normed = jnp.dot(wqkv_ref[...], rows_t, preferred_element_type=f32)

time: 166 us -> 164 us (0.988)
  Pallas kernels: 79.4 us -> 77.7 us
    pallas_call x2, Pallas kernels: 79.4 us -> 77.7 us  [window_grads(): pl.pallas_call(make_window_kernel(first), out_shape=[jax.ShapeDtypeStruct...]
where the time goes in v10:
time: 164 us; the launch traced here: 162 us
  Pallas kernels  77.7 us (47%)
  waiting for transfers between devices  28.6 us (17%)
  starting transfers between devices  21.4 us (13%)
  other arithmetic  16.7 us (10%)
  local copies, waits for them, and re-layouts  16.4 us (10%)
    pallas_call x2, Pallas kernels, window_grads(): pl.pallas_call(make_window_kernel(first), out_shape=[jax.ShapeDtypeStruct...  77.7 us
    ppermute x10, waiting for transfers between devices, swapped(): lax.ppermute(block, axis, [(i, i ^ distance) for i in range(lax.axis_size...  21.5 us
    ppermute x6, starting transfers between devices, moved(): lax.ppermute(block, ('gx', 'gy', 'gz'), halo_route(distance_a, distance_b))  15.7 us
    ppermute x6, waiting for transfers between devices, moved(): lax.ppermute(block, ('gx', 'gy', 'gz'), halo_route(distance_a, distance_b))  7.12 us
    ppermute x10, starting transfers between devices, swapped(): lax.ppermute(block, axis, [(i, i ^ distance) for i in range(lax.axis_size...  5.72 us
    another operation x4, other arithmetic, per_device(): both = shifted_block(jnp.stack([tokens, grads_out]))  4.87 us
    concatenate x1, other arithmetic, shifted_block(): return jnp.concatenate([upper, lower], axis=1)  3.36 us
    add x5, other arithmetic, summed_everywhere(): values = keep + swapped(send, axis, distance)  3.36 us
  transfers between devices with their start and end apart: 16, of which 10 were waited for; matrix products, arithmetic and copies ran while one was open for 8% of the time, Pallas kernels for 13%

profile of v10, /device:TPU:5, one launch (start us, length us, event | category | flops | bytes accessed | tf_op | source)
XLA Modules:
  0.0 161.6 jit_solution(8863600433925545262)
XLA Ops:
  0.7 1.5 fusion.2
  2.2 1.3 copy.19
  3.5 3.3 %collective-permute-start.1 = (bf16[2,4,12,3072]{3,1,2,0:T(4,128)(2,1)}, bf16[2,4,12,3072]{3,1,2,0:T(4,128)(2,1)}, u32[]{:S(2)}, u32[]{:S(2)}) collective-permute-start(bf16[2,4,12,3072]{3,1,2,0:T(4,128)(2,1)} %copy.19), channel_id=1, source_target_pairs={{0,24},{1,25},{2,26},{3,27},{4,28},{5,29},{6,30},{7,31},{8,0},{9,1... | collective-permute-start | bytes 1769480 | tf_op jit(solution)/shard_map/ppermute | solution.py:247
  6.8 1.0 fusion.3
  7.8 0.2 collective-permute-start
  8.1 2.0 %collective-permute-start.2 = (bf16[2,4,4,3072]{3,2,1,0:T(4,128)(2,1)S(1)}, bf16[2,4,4,3072]{3,2,1,0:T(4,128)(2,1)S(1)}, u32[]{:S(2)}, u32[]{:S(2)}) collective-permute-start(bf16[2,4,4,3072]{3,2,1,0:T(4,128)(2,1)S(1)} %pad_maximum_fusion.1), channel_id=1, source_target_pairs={{0,31},{1,24},{2,25},{3,26},{4,27},{5,28},{6,29},{7,30},{8,7},{9,0... | collective-permute-start | bytes 589832 | tf_op jit(solution)/shard_map/ppermute | solution.py:247
  10.2 2.3 %fusion.1 = bf16[2,12,12,3072]{3,2,1,0:T(8,128)(2,1)} fusion(bf16[1,16,16,3072]{3,2,1,0:T(8,128)(2,1)S(1)} %bitcast.17, bf16[1,16,16,3072]{3,2,1,0:T(8,128)(2,1)S(1)} %bitcast.13), kind=kLoop, calls=%fused_computation.9 | loop fusion | flops 884736 | bytes 4915200 | tf_op jit(solution)/shard_map/stack | solution.py:274
  12.9 2.0 %broadcast_in_dim_reshape.8.refs_2_.refs_1_ = s32[8,512,1]{2,1,0:T(8,128)} reshape(s32[2,2,2,8,8,8]{5,4,3,2,1,0:T(8,128)S(1)} %bitcast.20) | data formatting | bytes 32768 | tf_op jit(solution)/shard_map/broadcast_in_dim;reshape | solution.py:288
  14.9 0.8 broadcast_in_dim_reshape.7.refs_3_.refs_2_
  15.7 0.9 copy.22
  16.6 0.8 copy.26.refs_4_.refs_3_
  17.4 21.0 %shard_map.93 = (f32[8,8,3072]{2,1,0:T(8,128)}, f32[576,192]{1,0:T(8,128)}, f32[192,192]{1,0:T(8,128)}, f32[192,1]{1,0:T(8,128)}) custom-call(bf16[16,16,3072]{2,1,0:T(8,128)(2,1)} %refs_0_.1, bf16[16,16,3072]{2,1,0:T(8,128)(2,1)} %refs_1_.1, s32[8,512,1]{2,1,0:T(8,128)} %broadcast_in_dim_reshape.8.refs_2_.refs_1_, ...), custom_call_target="tpu_custom_call" | custom-call | tf_op jit(solution)/shard_map/pallas_call | solution.py:176
  38.4 1.3 copy.20
  39.7 3.4 %maximum_maximum_fusion.refs_0_ = bf16[2,16,16,3072]{3,2,1,0:T(8,128)(2,1)} fusion(bf16[2,4,4,3072]{3,2,1,0:T(4,128)(2,1)S(1)} %collective-permute-done.2, bf16[2,4,12,3072]{3,2,1,0:T(8,128)(2,1)S(1)} %copy.20, bf16[2,12,4,3072]{3,2,1,0:T(4,128)(2,1)} %collective-permute-done, bf16[2,12,12,3072]{3,2,1,0:T(8,128)(2,1)S(1)} %copy-done.4), kind=kLoop, calls=%fused_computation.6 | loop fusion | flops 12582912 | bytes 6291456 | tf_op jit(solution)/shard_map/concatenate | solution.py:256
  43.0 56.6 %shard_map.94 = (f32[16,16,3072]{2,1,0:T(8,128)}, f32[576,192]{1,0:T(8,128)}, f32[192,192]{1,0:T(8,128)}, f32[192,1]{1,0:T(8,128)}) custom-call(bf16[2,16,16,3072]{3,2,1,0:T(8,128)(2,1)} %maximum_maximum_fusion.refs_0_, s32[8,512,1]{2,1,0:T(8,128)} %broadcast_in_dim_reshape.8.refs_2_.refs_1_, s32[8,1,512]{2,1,0:T(1,128)} %broadcast_in_dim_reshape.7.refs_3_.refs_2_, ...), custom_call_target="tpu_custom_call" | custom-call | tf_op jit(solution)/shard_map/pallas_call | solution.py:176
  99.7 2.3 %reshape.86 = f32[110592]{0:T(1024)} reshape(f32[576,192]{1,0:T(8,128)} %get-tuple-element.17) | data formatting | bytes 884736 | tf_op jit(solution)/shard_map/reshape | solution.py:203
  102.0 1.0 reshape.87
  103.0 1.0 reduce
  104.0 1.1 pad_maximum_fusion
  105.1 0.8 copy-done.5
  106.0 0.8 collective-permute-start.6
  106.9 1.3 collective-permute-done.6
  108.2 1.2 dynamic-slice_add_fusion
  109.4 0.8 dynamic_slice.33
  110.2 0.8 collective-permute-start.7
  111.0 4.6 %collective-permute-done.7 = f32[36912]{0:T(1024)} collective-permute-done((f32[36912]{0:T(1024)}, f32[36912]{0:T(1024)}, u32[]{:S(2)}, u32[]{:S(2)}) %collective-permute-start.7) | collective-permute-done | bytes 147680 | tf_op jit(solution)/shard_map/ppermute | solution.py:196
  115.7 1.0 dynamic-slice_add_fusion.1
  116.7 0.7 copy-done.7
  117.4 1.4 collective-permute-start.8
  118.8 1.9 %collective-permute-done.8 = f32[18456]{0:T(1024)S(1)} collective-permute-done((f32[18456]{0:T(1024)S(1)}, f32[18456]{0:T(1024)S(1)}, u32[]{:S(2)}, u32[]{:S(2)}) %collective-permute-start.8) | collective-permute-done | bytes 73856 | tf_op jit(solution)/shard_map/ppermute | solution.py:196
  120.8 1.0 dynamic-slice_add_fusion.2
  121.9 3.7 %collective-permute-done.9 = f32[9228]{0:T(1024)S(1)} collective-permute-done((f32[9228]{0:T(1024)S(1)}, f32[9228]{0:T(1024)S(1)}, u32[]{:S(2)}, u32[]{:S(2)}) %collective-permute-start.9) | collective-permute-done | bytes 36944 | tf_op jit(solution)/shard_map/ppermute | solution.py:196
  125.8 0.3 collective-permute-start.10
  126.1 2.6 %collective-permute-done.10 = f32[4614]{0:T(1024)S(1)} collective-permute-done((f32[4614]{0:T(1024)S(1)}, f32[4614]{0:T(1024)S(1)}, u32[]{:S(2)}, u32[]{:S(2)}) %collective-permute-start.10) | collective-permute-done | bytes 18488 | tf_op jit(solution)/shard_map/ppermute | solution.py:196
  128.9 2.5 %collective-permute-done.11 = f32[4614]{0:T(1024)S(1)} collective-permute-done((f32[4614]{0:T(1024)S(1)}, f32[4614]{0:T(1024)S(1)}, u32[]{:S(2)}, u32[]{:S(2)}) %collective-permute-start.11) | collective-permute-done | bytes 18488 | tf_op jit(solution)/shard_map/ppermute | solution.py:196
  131.6 3.7 %collective-permute-done.12 = f32[9228]{0:T(1024)S(1)} collective-permute-done((f32[9228]{0:T(1024)S(1)}, f32[9228]{0:T(1024)S(1)}, u32[]{:S(2)}, u32[]{:S(2)}) %collective-permute-start.12) | collective-permute-done | bytes 36944 | tf_op jit(solution)/shard_map/ppermute | solution.py:196
  135.4 1.4 collective-permute-start.13
  137.7 8.6 %collective-permute-start.3 = (bf16[4,4,3072]{2,1,0:T(4,128)(2,1)S(1)}, bf16[4,4,3072]{2,1,0:T(4,128)(2,1)S(1)}, u32[]{:S(2)}, u32[]{:S(2)}) collective-permute-start(bf16[4,4,3072]{2,1,0:T(4,128)(2,1)S(1)} %slice.55), channel_id=1, source_target_pairs={{0,9},{1,10},{2,11},{3,12},{4,13},{5,14},{6,15},{7,8},{8,17},{9,18... | collective-permute-start | bytes 294920 | tf_op jit(solution)/shard_map/ppermute | solution.py:247
  146.4 1.2 collective-permute-start.5
  147.7 0.7 collective-permute-start.14
  148.4 0.6 collective-permute-done.3
  149.2 6.5 %collective-permute-done.5 = bf16[12,4,3072]{2,1,0:T(4,128)(2,1)S(1)} collective-permute-done((bf16[12,4,3072]{2,1,0:T(4,128)(2,1)S(1)}, bf16[12,4,3072]{2,1,0:T(4,128)(2,1)S(1)}, u32[]{:S(2)}, u32[]{:S(2)}) %collective-permute-start.5) | collective-permute-done | bytes 294944 | tf_op jit(solution)/shard_map/ppermute | solution.py:247
  155.7 1.0 collective-permute-done.14
  157.0 1.8 %fusion = bf16[16,16,3072]{2,1,0:T(8,128)(2,1)} fusion(f32[12,12,3072]{2,1,0:T(8,128)S(1)} %slice.44, f32[12,4,3072]{2,1,0:T(4,128)S(1)} %convert_element_type.28, f32[4,16,3072]{2,1,0:T(8,128)S(1)} %maximum_convert_fusion, bf16[16,16,3072]{2,1,0:T(8,128)(2,1)S(1)} %copy-done.1), kind=kLoop, calls=%fused_computation.8 | loop fusion | flops 3932160 | bytes 6291456 | tf_op jit(solution)/shard_map/convert_element_type | solution.py:267
  158.8 0.2 maximum_select_fusion
  159.0 0.7 slice.60
  159.7 0.6 slice.58
  160.6 1.0 reshape.89
  (56 shorter events, 3.4 us)
Async XLA Ops:
  0.6 6.1 %copy-start.2 = (bf16[16,16,3072]{2,1,0:T(8,128)(2,1)S(1)}, bf16[16,16,3072]{2,1,0:T(8,128)(2,1)}, u32[]{:S(2)}) copy-start(bf16[16,16,3072]{2,1,0:T(8,128)(2,1)} %refs_0_.1) | copy-start | bytes 4718596
  0.6 6.1 %copy-start = (bf16[16,16,3072]{2,1,0:T(8,128)(2,1)S(1)}, bf16[16,16,3072]{2,1,0:T(8,128)(2,1)}, u32[]{:S(2)}) copy-start(bf16[16,16,3072]{2,1,0:T(8,128)(2,1)} %refs_1_.1) | copy-start | bytes 4718596
  3.5 34.9 %collective-permute-start.1 = (bf16[2,4,12,3072]{3,1,2,0:T(4,128)(2,1)}, bf16[2,4,12,3072]{3,1,2,0:T(4,128)(2,1)}, u32[]{:S(2)}, u32[]{:S(2)}) collective-permute-start(bf16[2,4,12,3072]{3,1,2,0:T(4,128)(2,1)} %copy.19), channel_id=1, source_target_pairs={{0,24},{1,25},{2,26},{3,27},{4,28},{5,29},{6,30},{7,31},{8,0},{9,1... | collective-permute-start | bytes 1769480 | tf_op jit(solution)/shard_map/ppermute | solution.py:247
  7.8 31.8 %collective-permute-start = (bf16[2,12,4,3072]{3,2,1,0:T(4,128)(2,1)}, bf16[2,12,4,3072]{3,2,1,0:T(4,128)(2,1)}, u32[]{:S(2)}, u32[]{:S(2)}) collective-permute-start(bf16[2,12,4,3072]{3,2,1,0:T(4,128)(2,1)} %fusion.3), channel_id=1, source_target_pairs={{0,7},{1,0},{2,1},{3,2},{4,3},{5,4},{6,5},{7,6},{8,15},{9,8},{10,9... | collective-permute-start | bytes 1769480 | tf_op jit(solution)/shard_map/ppermute | solution.py:247
  8.1 31.5 %collective-permute-start.2 = (bf16[2,4,4,3072]{3,2,1,0:T(4,128)(2,1)S(1)}, bf16[2,4,4,3072]{3,2,1,0:T(4,128)(2,1)S(1)}, u32[]{:S(2)}, u32[]{:S(2)}) collective-permute-start(bf16[2,4,4,3072]{3,2,1,0:T(4,128)(2,1)S(1)} %pad_maximum_fusion.1), channel_id=1, source_target_pairs={{0,31},{1,24},{2,25},{3,26},{4,27},{5,28},{6,29},{7,30},{8,7},{9,0... | collective-permute-start | bytes 589832 | tf_op jit(solution)/shard_map/ppermute | solution.py:247
  10.1 2.3 %copy-start.8 = (s32[16,16,16]{2,1,0:T(8,128)S(1)}, s32[16,16,16]{2,1,0:T(8,128)}, u32[]{:S(2)}) copy-start(s32[16,16,16]{2,1,0:T(8,128)} %param.8) | copy-start | bytes 49156
  12.5 3.2 %copy-start.6 = (bf16[192,576]{1,0:T(8,128)(2,1)S(1)}, bf16[192,576]{1,0:T(8,128)(2,1)}, u32[]{:S(2)}) copy-start(bf16[192,576]{1,0:T(8,128)(2,1)} %refs_5_.1) | copy-start | bytes 663556
  12.5 4.1 %copy-start.9 = (f32[192]{0:T(256)S(1)}, f32[192]{0:T(256)}, u32[]{:S(2)}) copy-start(f32[192]{0:T(256)} %param.9) | copy-start | bytes 2308
  17.4 22.3 %copy-start.4 = (bf16[2,12,12,3072]{3,2,1,0:T(8,128)(2,1)S(1)}, bf16[2,12,12,3072]{3,2,1,0:T(8,128)(2,1)}, u32[]{:S(2)}) copy-start(bf16[2,12,12,3072]{3,2,1,0:T(8,128)(2,1)} %fusion.1) | copy-start | bytes 5308420
  99.7 37.1 %copy-start.3 = (f32[16,16,3072]{2,1,0:T(8,128)S(1)}, f32[16,16,3072]{2,1,0:T(8,128)}, u32[]{:S(2)}) copy-start(f32[16,16,3072]{2,1,0:T(8,128)} %get-tuple-element.16) | copy-start | bytes 9437188
  105.1 0.8 copy-start.5
  106.0 2.2 %collective-permute-start.6 = (f32[73824]{0:T(1024)S(1)}, f32[73824]{0:T(1024)}, u32[]{:S(2)}, u32[]{:S(2)}) collective-permute-start(f32[73824]{0:T(1024)S(1)} %dynamic_slice.31), channel_id=1, source_target_pairs={{0,2},{2,0},{4,6},{6,4},{1,3},{3,1},{5,7},{7,5},{8,10},{10,8},{12,... | collective-permute-start | bytes 885896 | tf_op jit(solution)/shard_map/ppermute | solution.py:196
  110.2 5.5 %collective-permute-start.7 = (f32[36912]{0:T(1024)}, f32[36912]{0:T(1024)}, u32[]{:S(2)}, u32[]{:S(2)}) collective-permute-start(f32[36912]{0:T(1024)} %dynamic_slice.33), channel_id=1, source_target_pairs={{0,4},{2,6},{4,0},{6,2},{1,5},{3,7},{5,1},{7,3},{8,12},{10,14},{12... | collective-permute-start | bytes 442952 | tf_op jit(solution)/shard_map/ppermute | solution.py:196
  116.7 0.7 copy-start.7
  117.4 3.3 %collective-permute-start.8 = (f32[18456]{0:T(1024)S(1)}, f32[18456]{0:T(1024)S(1)}, u32[]{:S(2)}, u32[]{:S(2)}) collective-permute-start(f32[18456]{0:T(1024)S(1)} %dynamic_slice.35), channel_id=1, source_target_pairs={{0,8},{8,0},{16,24},{24,16},{1,9},{9,1},{17,25},{25,17},{2,10},{10... | collective-permute-start | bytes 221480 | tf_op jit(solution)/shard_map/ppermute | solution.py:196
  121.8 3.8 %collective-permute-start.9 = (f32[9228]{0:T(1024)S(1)}, f32[9228]{0:T(1024)S(1)}, u32[]{:S(2)}, u32[]{:S(2)}) collective-permute-start(f32[9228]{0:T(1024)S(1)} %dynamic_slice.37), channel_id=1, source_target_pairs={{0,16},{8,24},{16,0},{24,8},{1,17},{9,25},{17,1},{25,9},{2,18},{10... | collective-permute-start | bytes 110744 | tf_op jit(solution)/shard_map/ppermute | solution.py:196
  125.8 2.9 %collective-permute-start.10 = (f32[4614]{0:T(1024)S(1)}, f32[4614]{0:T(1024)S(1)}, u32[]{:S(2)}, u32[]{:S(2)}) collective-permute-start(f32[4614]{0:T(1024)S(1)} %dynamic_slice.39), channel_id=1, source_target_pairs={{0,1},{1,0},{2,3},{3,2},{4,5},{5,4},{6,7},{7,6},{8,9},{9,8},{10,11... | collective-permute-start | bytes 55376 | tf_op jit(solution)/shard_map/ppermute | solution.py:196
  128.8 2.6 %collective-permute-start.11 = (f32[4614]{0:T(1024)S(1)}, f32[4614]{0:T(1024)S(1)}, u32[]{:S(2)}, u32[]{:S(2)}) collective-permute-start(f32[4614]{0:T(1024)S(1)} %dynamic-slice_add_fusion.4), channel_id=1, source_target_pairs={{0,1},{1,0},{2,3},{3,2},{4,5},{5,4},{6,7},{7,6},{8,9},{9,8},{10,11... | collective-permute-start | bytes 55376 | tf_op jit(solution)/shard_map/ppermute | solution.py:196
  131.5 3.8 %collective-permute-start.12 = (f32[9228]{0:T(1024)S(1)}, f32[9228]{0:T(1024)S(1)}, u32[]{:S(2)}, u32[]{:S(2)}) collective-permute-start(f32[9228]{0:T(1024)S(1)} %maximum_select_fusion.4), channel_id=1, source_target_pairs={{0,16},{8,24},{16,0},{24,8},{1,17},{9,25},{17,1},{25,9},{2,18},{10... | collective-permute-start | bytes 110744 | tf_op jit(solution)/shard_map/ppermute | solution.py:196
  135.4 12.2 %collective-permute-start.13 = (f32[18456]{0:T(1024)S(1)}, f32[18456]{0:T(1024)S(1)}, u32[]{:S(2)}, u32[]{:S(2)}) collective-permute-start(f32[18456]{0:T(1024)S(1)} %maximum_select_fusion.3), channel_id=1, source_target_pairs={{0,8},{8,0},{16,24},{24,16},{1,9},{9,1},{17,25},{25,17},{2,10},{10... | collective-permute-start | bytes 221480 | tf_op jit(solution)/shard_map/ppermute | solution.py:196
  137.3 19.7 %copy-start.1 = (bf16[16,16,3072]{2,1,0:T(8,128)(2,1)S(1)}, bf16[16,16,3072]{2,1,0:T(8,128)(2,1)}, u32[]{:S(2)}) copy-start(bf16[16,16,3072]{2,1,0:T(8,128)(2,1)} %refs_1_.1) | copy-start | bytes 4718596
  137.5 11.5 %collective-permute-start.4 = (bf16[4,12,3072]{2,1,0:T(8,128)(2,1)S(1)}, bf16[4,12,3072]{2,1,0:T(8,128)(2,1)S(1)}, u32[]{:S(2)}, u32[]{:S(2)}) collective-permute-start(bf16[4,12,3072]{2,1,0:T(8,128)(2,1)S(1)} %slice.56), channel_id=1, source_target_pairs={{0,8},{1,9},{2,10},{3,11},{4,12},{5,13},{6,14},{7,15},{8,16},{9,17... | collective-permute-start | bytes 884744 | tf_op jit(solution)/shard_map/ppermute | solution.py:247
  137.7 11.3 %collective-permute-start.3 = (bf16[4,4,3072]{2,1,0:T(4,128)(2,1)S(1)}, bf16[4,4,3072]{2,1,0:T(4,128)(2,1)S(1)}, u32[]{:S(2)}, u32[]{:S(2)}) collective-permute-start(bf16[4,4,3072]{2,1,0:T(4,128)(2,1)S(1)} %slice.55), channel_id=1, source_target_pairs={{0,9},{1,10},{2,11},{3,12},{4,13},{5,14},{6,15},{7,8},{8,17},{9,18... | collective-permute-start | bytes 294920 | tf_op jit(solution)/shard_map/ppermute | solution.py:247
  146.4 9.3 %collective-permute-start.5 = (bf16[12,4,3072]{2,1,0:T(4,128)(2,1)S(1)}, bf16[12,4,3072]{2,1,0:T(4,128)(2,1)S(1)}, u32[]{:S(2)}, u32[]{:S(2)}) collective-permute-start(bf16[12,4,3072]{2,1,0:T(4,128)(2,1)S(1)} %slice.57), channel_id=1, source_target_pairs={{0,1},{1,2},{2,3},{3,4},{4,5},{5,6},{6,7},{7,0},{8,9},{9,10},{10,1... | collective-permute-start | bytes 884744 | tf_op jit(solution)/shard_map/ppermute | solution.py:247
  147.7 9.0 %collective-permute-start.14 = (f32[36912]{0:T(1024)S(1)}, f32[36912]{0:T(1024)S(1)}, u32[]{:S(2)}, u32[]{:S(2)}) collective-permute-start(f32[36912]{0:T(1024)S(1)} %maximum_select_fusion.2), channel_id=1, source_target_pairs={{0,4},{2,6},{4,0},{6,2},{1,5},{3,7},{5,1},{7,3},{8,12},{10,14},{12... | collective-permute-start | bytes 442952 | tf_op jit(solution)/shard_map/ppermute | solution.py:196
  156.9 1.9 %collective-permute-start.15 = (f32[73824]{0:T(1024)S(1)}, f32[73824]{0:T(1024)S(1)}, u32[]{:S(2)}, u32[]{:S(2)}) collective-permute-start(f32[73824]{0:T(1024)S(1)} %maximum_select_fusion.1), channel_id=1, source_target_pairs={{0,2},{2,0},{4,6},{6,4},{1,3},{3,1},{5,7},{7,5},{8,10},{10,8},{12,... | collective-permute-start | bytes 885896 | tf_op jit(solution)/shard_map/ppermute | solution.py:196

commit v11 on v10

--- a/solution.py
+++ b/solution.py
@@ -144,7 +144,7 @@
 
             lax.fori_loop(0, HEADS, head_step, 0, unroll=3)
             rows_t = drow_s[...].astype(bf16)
-            gqkvT_ref[...] += lax.dot_general(rows_t, normed, nt, preferred_element_type=f32)
+            gqkvT_ref[...] += lax.dot_general(normed, rows_t, nt, preferred_element_type=f32)
             grad_normed = jnp.dot(wqkv_ref[...], rows_t, preferred_element_type=f32)
             ggain_ref[...] += jnp.sum(grad_normed * x_hat, axis=1, keepdims=True)
             scaled = grad_normed * gain
@@ -177,7 +177,7 @@
         make_window_kernel(first),
         out_shape=[
             jax.ShapeDtypeStruct((extent_a, extent_b, width), jnp.float32),
-            jax.ShapeDtypeStruct((3 * C, C), jnp.float32),
+            jax.ShapeDtypeStruct((C, 3 * C), jnp.float32),
             jax.ShapeDtypeStruct((C, C), jnp.float32),
             jax.ShapeDtypeStruct((C, 1), jnp.float32),
         ],
@@ -196,17 +196,16 @@
     return lax.ppermute(block, axis, [(i, i ^ distance) for i in range(lax.axis_size(axis))])
 
 
-def summed_everywhere(parts):
+def summed_everywhere(matrix):
     sizes = [lax.axis_size(axis) for axis in SUM_AXES]
     if any(size & (size - 1) for size in sizes):
-        return lax.psum(parts, SUM_AXES)
-    flat = jnp.concatenate([part.reshape(-1) for part in parts])
-    total = flat.shape[0]
+        return lax.psum(matrix, SUM_AXES)
     devices = 1
     for size in sizes:
         devices *= size
-    padded = -(-total // devices) * devices
-    values = jnp.pad(flat, (0, padded - total))
+    unit = devices * 8 if devices * 8 <= 2 * matrix.shape[0] else devices
+    padded = -(-matrix.shape[0] // unit) * unit
+    values = jnp.pad(matrix, ((0, padded - matrix.shape[0]), (0, 0)))
     steps = []
     for axis, size in zip(SUM_AXES, sizes):
         distance = 1
@@ -224,12 +223,7 @@
         values = jnp.where(
             bit == 0, jnp.concatenate([values, other]), jnp.concatenate([other, values])
         )
-    out = []
-    start = 0
-    for part in parts:
-        out.append(values[start : start + part.size].reshape(part.shape))
-        start += part.size
-    return tuple(out)
+    return values[: matrix.shape[0]]
 
 
 def halo_route(distance_a, distance_b):
@@ -293,11 +287,17 @@
         proj_weight,
     )
     partial = window_grads(True, (tokens, grads_out), *constants)
-    grad_branch, qkv_grad_t, proj_grad, gain_grad = window_grads(
+    grad_branch, qkv_part, proj_grad, gain_grad = window_grads(
         False, (both,), *constants, partial=partial
     )
-    qkv_grad_t, proj_grad, gain_grad = summed_everywhere((qkv_grad_t, proj_grad, gain_grad))
-    qkv_grad = qkv_grad_t.T
+    width = 4 * channels
+    gain_row = jnp.pad(gain_grad.reshape(1, channels), ((0, 0), (0, width - channels)))
+    summed = summed_everywhere(
+        jnp.concatenate([jnp.concatenate([qkv_part, proj_grad], axis=1), gain_row], axis=0)
+    )
+    qkv_grad = summed[:channels, : 3 * channels]
+    proj_grad = summed[:channels, 3 * channels :]
+    gain_grad = summed[channels, :channels]
     grad_tokens = unshifted_sum(grads_out, grad_branch)
     return (grad_tokens, gain_grad.reshape(-1), qkv_grad.reshape(-1), proj_grad.reshape(-1))
 

time: 164 us -> 165 us (level); the launches traced: 162 us -> 165 us
  other arithmetic: 16.7 us -> 21.2 us
  waiting for transfers between devices: 28.6 us -> 26.2 us
  starting transfers between devices: 21.4 us -> 23.2 us
    ppermute x6, waiting for transfers between devices: 7.12 us -> 0.02 us  [moved(): lax.ppermute(block, ('gx', 'gy', 'gz'), halo_route(distance_a, distance_b))]
    ppermute x10, waiting for transfers between devices: 21.5 us -> 26.2 us  [swapped(): lax.ppermute(block, axis, [(i, i ^ distance) for i in range(lax.axis_size...]
    select_n x5, other arithmetic: 0.64 us -> 3.3 us  [summed_everywhere(): jnp.where(bit == 0, jnp.concatenate([values, other]), jnp.concatenate([ot...]
    reshape x2 -> x1, local copies, waits for them, and re-layouts: 3.33 us -> 0.78 us  [per_device(): proj_grad.reshape(-1)]
    unnamed x21 -> x23, local copies, waits for them, and re-layouts: 2.38 us -> 3.54 us
  transfers between devices with their start and end apart: 16 -> 16, of which waited for: 10 -> 8; matrix products, arithmetic and copies ran while one was open for 8% -> 12% of each run, Pallas kernels for 13% -> 13%
where the time goes in v11:
time: 165 us
  Pallas kernels  76.7 us (46%)
  waiting for transfers between devices  26.2 us (16%)
  starting transfers between devices  23.2 us (14%)
  other arithmetic  21.2 us (13%)
  local copies, waits for them, and re-layouts  16.3 us (10%)
    pallas_call x2, Pallas kernels, window_grads(): pl.pallas_call(make_window_kernel(first), out_shape=[jax.ShapeDtypeStruct...  76.7 us
    ppermute x10, waiting for transfers between devices, swapped(): lax.ppermute(block, axis, [(i, i ^ distance) for i in range(lax.axis_size...  26.2 us
    ppermute x6, starting transfers between devices, moved(): lax.ppermute(block, ('gx', 'gy', 'gz'), halo_route(distance_a, distance_b))  16 us
    ppermute x10, starting transfers between devices, swapped(): lax.ppermute(block, axis, [(i, i ^ distance) for i in range(lax.axis_size...  7.22 us
    another operation x4, other arithmetic, per_device(): both = shifted_block(jnp.stack([tokens, grads_out]))  4.87 us
    unnamed x23, local copies, waits for them, and re-layouts  3.54 us
    concatenate x1, other arithmetic, shifted_block(): return jnp.concatenate([upper, lower], axis=1)  3.36 us
    select_n x5, other arithmetic, summed_everywhere(): jnp.where(bit == 0, jnp.concatenate([values, other]), jnp.concatenate([ot...  3.3 us
  transfers between devices with their start and end apart: 16, of which 8 were waited for; matrix products, arithmetic and copies ran while one was open for 12% of the time, Pallas kernels for 13%

profile of v11, /device:TPU:5, one launch (start us, length us, event | category | flops | bytes accessed | tf_op | source)
XLA Modules:
  0.0 164.5 jit_solution(9672683025704078500)
XLA Ops:
  0.7 1.5 fusion.2
  2.2 1.3 copy.18
  3.5 3.3 %collective-permute-start.1 = (bf16[2,4,12,3072]{3,1,2,0:T(4,128)(2,1)}, bf16[2,4,12,3072]{3,1,2,0:T(4,128)(2,1)}, u32[]{:S(2)}, u32[]{:S(2)}) collective-permute-start(bf16[2,4,12,3072]{3,1,2,0:T(4,128)(2,1)} %copy.18), channel_id=1, source_target_pairs={{0,24},{1,25},{2,26},{3,27},{4,28},{5,29},{6,30},{7,31},{8,0},{9,1... | collective-permute-start | bytes 1769480 | tf_op jit(solution)/shard_map/ppermute | solution.py:241
  6.8 1.0 fusion.3
  8.1 2.0 %collective-permute-start.2 = (bf16[2,4,4,3072]{3,2,1,0:T(4,128)(2,1)S(1)}, bf16[2,4,4,3072]{3,2,1,0:T(4,128)(2,1)S(1)}, u32[]{:S(2)}, u32[]{:S(2)}) collective-permute-start(bf16[2,4,4,3072]{3,2,1,0:T(4,128)(2,1)S(1)} %pad_maximum_fusion), channel_id=1, source_target_pairs={{0,31},{1,24},{2,25},{3,26},{4,27},{5,28},{6,29},{7,30},{8,7},{9,0... | collective-permute-start | bytes 589832 | tf_op jit(solution)/shard_map/ppermute | solution.py:241
  10.2 2.2 %fusion.1 = bf16[2,12,12,3072]{3,2,1,0:T(8,128)(2,1)} fusion(bf16[1,16,16,3072]{3,2,1,0:T(8,128)(2,1)S(1)} %bitcast.18, bf16[1,16,16,3072]{3,2,1,0:T(8,128)(2,1)S(1)} %bitcast.14), kind=kLoop, calls=%fused_computation.9 | loop fusion | flops 884736 | bytes 4915200 | tf_op jit(solution)/shard_map/stack | solution.py:268
  12.9 2.0 %broadcast_in_dim_reshape.8.refs_2_.refs_1_ = s32[8,512,1]{2,1,0:T(8,128)} reshape(s32[2,2,2,8,8,8]{5,4,3,2,1,0:T(8,128)S(1)} %bitcast.21) | data formatting | bytes 32768 | tf_op jit(solution)/shard_map/broadcast_in_dim;reshape | solution.py:282
  14.9 0.8 broadcast_in_dim_reshape.7.refs_3_.refs_2_
  15.7 0.9 copy.21
  16.6 0.8 copy.25.refs_4_.refs_3_
  17.3 20.7 %shard_map.93 = (f32[8,8,3072]{2,1,0:T(8,128)}, f32[192,576]{1,0:T(8,128)}, f32[192,192]{1,0:T(8,128)}, f32[192,1]{1,0:T(8,128)}) custom-call(bf16[16,16,3072]{2,1,0:T(8,128)(2,1)} %refs_0_.1, bf16[16,16,3072]{2,1,0:T(8,128)(2,1)} %refs_1_.1, s32[8,512,1]{2,1,0:T(8,128)} %broadcast_in_dim_reshape.8.refs_2_.refs_1_, ...), custom_call_target="tpu_custom_call" | custom-call | tf_op jit(solution)/shard_map/pallas_call | solution.py:176
  38.0 1.3 copy.19
  39.3 3.4 %maximum_maximum_fusion.refs_0_ = bf16[2,16,16,3072]{3,2,1,0:T(8,128)(2,1)} fusion(bf16[2,4,4,3072]{3,2,1,0:T(4,128)(2,1)S(1)} %collective-permute-done.2, bf16[2,4,12,3072]{3,2,1,0:T(8,128)(2,1)S(1)} %copy.19, bf16[2,12,4,3072]{3,2,1,0:T(4,128)(2,1)} %collective-permute-done, bf16[2,12,12,3072]{3,2,1,0:T(8,128)(2,1)S(1)} %copy-done.4), kind=kLoop, calls=%fused_computation.6 | loop fusion | flops 12582912 | bytes 6291456 | tf_op jit(solution)/shard_map/concatenate | solution.py:250
  42.7 56.0 %shard_map.94 = (f32[16,16,3072]{2,1,0:T(8,128)}, f32[192,576]{1,0:T(8,128)}, f32[192,192]{1,0:T(8,128)}, f32[192,1]{1,0:T(8,128)}) custom-call(bf16[2,16,16,3072]{3,2,1,0:T(8,128)(2,1)} %maximum_maximum_fusion.refs_0_, s32[8,512,1]{2,1,0:T(8,128)} %broadcast_in_dim_reshape.8.refs_2_.refs_1_, s32[8,1,512]{2,1,0:T(1,128)} %broadcast_in_dim_reshape.7.refs_3_.refs_2_, ...), custom_call_target="tpu_custom_call" | custom-call | tf_op jit(solution)/shard_map/pallas_call | solution.py:176
  98.7 1.1 reduce
  99.9 1.3 select_maximum_fusion
  101.1 0.8 copy-done.5
  102.0 0.8 collective-permute-start.6
  102.8 1.5 collective-permute-done.6
  104.3 1.1 fusion.4
  106.1 0.8 collective-permute-start.7
  106.9 5.5 %collective-permute-done.7 = f32[64,768]{1,0:T(8,128)} collective-permute-done((f32[64,768]{1,0:T(8,128)}, f32[64,768]{1,0:T(8,128)}, u32[]{:S(2)}, u32[]{:S(2)}) %collective-permute-start.7) | collective-permute-done | bytes 196640 | tf_op jit(solution)/shard_map/ppermute | solution.py:196
  112.5 0.9 dynamic-slice_add_fusion
  114.1 1.4 collective-permute-start.8
  115.5 2.2 %collective-permute-done.8 = f32[32,768]{1,0:T(8,128)S(1)} collective-permute-done((f32[32,768]{1,0:T(8,128)S(1)}, f32[32,768]{1,0:T(8,128)S(1)}, u32[]{:S(2)}, u32[]{:S(2)}) %collective-permute-start.8) | collective-permute-done | bytes 98336 | tf_op jit(solution)/shard_map/ppermute | solution.py:196
  117.7 0.9 dynamic-slice_add_fusion.1
  118.7 3.8 %collective-permute-done.9 = f32[16,768]{1,0:T(8,128)S(1)} collective-permute-done((f32[16,768]{1,0:T(8,128)S(1)}, f32[16,768]{1,0:T(8,128)S(1)}, u32[]{:S(2)}, u32[]{:S(2)}) %collective-permute-start.9) | collective-permute-done | bytes 49184 | tf_op jit(solution)/shard_map/ppermute | solution.py:196
  122.9 2.7 %collective-permute-done.10 = f32[8,768]{1,0:T(8,128)S(1)} collective-permute-done((f32[8,768]{1,0:T(8,128)S(1)}, f32[8,768]{1,0:T(8,128)S(1)}, u32[]{:S(2)}, u32[]{:S(2)}) %collective-permute-start.10) | collective-permute-done | bytes 24608 | tf_op jit(solution)/shard_map/ppermute | solution.py:196
  126.0 1.1 copy-done.6
  127.2 0.9 slice.56
  128.0 6.4 %collective-permute-start.5 = (bf16[12,4,3072]{2,1,0:T(4,128)(2,1)}, bf16[12,4,3072]{2,1,0:T(4,128)(2,1)}, u32[]{:S(2)}, u32[]{:S(2)}) collective-permute-start(bf16[12,4,3072]{2,1,0:T(4,128)(2,1)} %slice.56), channel_id=1, source_target_pairs={{0,1},{1,2},{2,3},{3,4},{4,5},{5,6},{6,7},{7,0},{8,9},{9,10},{10,1... | collective-permute-start | bytes 884744 | tf_op jit(solution)/shard_map/ppermute | solution.py:241
  135.0 1.0 slice.55
  136.1 1.5 collective-permute-start.4
  137.5 2.3 %collective-permute-done.12 = f32[16,768]{1,0:T(8,128)} collective-permute-done((f32[16,768]{1,0:T(8,128)}, f32[16,768]{1,0:T(8,128)}, u32[]{:S(2)}, u32[]{:S(2)}) %collective-permute-start.12) | collective-permute-done | bytes 49184 | tf_op jit(solution)/shard_map/ppermute | solution.py:196
  139.8 1.5 maximum_select_fusion.3
  141.3 1.3 collective-permute-start.13
  142.6 1.0 slice.54
  143.9 2.5 %collective-permute-start.3 = (bf16[4,4,3072]{2,1,0:T(4,128)(2,1)S(1)}, bf16[4,4,3072]{2,1,0:T(4,128)(2,1)S(1)}, u32[]{:S(2)}, u32[]{:S(2)}) collective-permute-start(bf16[4,4,3072]{2,1,0:T(4,128)(2,1)S(1)} %slice.54), channel_id=1, source_target_pairs={{0,9},{1,10},{2,11},{3,12},{4,13},{5,14},{6,15},{7,8},{8,17},{9,18... | collective-permute-start | bytes 294920 | tf_op jit(solution)/shard_map/ppermute | solution.py:241
  146.4 1.0 convert_element_type.32
  147.4 4.2 %collective-permute-done.13 = f32[32,768]{1,0:T(8,128)} collective-permute-done((f32[32,768]{1,0:T(8,128)}, f32[32,768]{1,0:T(8,128)}, u32[]{:S(2)}, u32[]{:S(2)}) %collective-permute-start.13) | collective-permute-done | bytes 98336 | tf_op jit(solution)/shard_map/ppermute | solution.py:196
  151.6 1.1 maximum_select_fusion.2
  152.7 0.7 collective-permute-start.14
  153.4 1.1 maximum_convert_fusion
  154.6 4.1 %collective-permute-done.14 = f32[64,768]{1,0:T(8,128)S(1)} collective-permute-done((f32[64,768]{1,0:T(8,128)S(1)}, f32[64,768]{1,0:T(8,128)S(1)}, u32[]{:S(2)}, u32[]{:S(2)}) %collective-permute-start.14) | collective-permute-done | bytes 196640 | tf_op jit(solution)/shard_map/ppermute | solution.py:196
  158.7 1.5 collective-permute-start.15
  160.2 1.8 %fusion = bf16[16,16,3072]{2,1,0:T(8,128)(2,1)} fusion(f32[12,12,3072]{2,1,0:T(8,128)S(1)} %slice.44, f32[12,4,3072]{2,1,0:T(4,128)S(1)} %convert_element_type.32, f32[4,16,3072]{2,1,0:T(8,128)S(1)} %maximum_convert_fusion, bf16[16,16,3072]{2,1,0:T(8,128)(2,1)S(1)} %copy-done.1), kind=kLoop, calls=%fused_computation.8 | loop fusion | flops 3932160 | bytes 6291456 | tf_op jit(solution)/shard_map/convert_element_type | solution.py:261
  162.8 1.0 reshape.77
  163.7 0.8 reshape.78
  (55 shorter events, 4.9 us)
Async XLA Ops:
  0.6 6.2 %copy-start.2 = (bf16[16,16,3072]{2,1,0:T(8,128)(2,1)S(1)}, bf16[16,16,3072]{2,1,0:T(8,128)(2,1)}, u32[]{:S(2)}) copy-start(bf16[16,16,3072]{2,1,0:T(8,128)(2,1)} %refs_0_.1) | copy-start | bytes 4718596
  0.6 6.1 %copy-start = (bf16[16,16,3072]{2,1,0:T(8,128)(2,1)S(1)}, bf16[16,16,3072]{2,1,0:T(8,128)(2,1)}, u32[]{:S(2)}) copy-start(bf16[16,16,3072]{2,1,0:T(8,128)(2,1)} %refs_1_.1) | copy-start | bytes 4718596
  3.5 34.6 %collective-permute-start.1 = (bf16[2,4,12,3072]{3,1,2,0:T(4,128)(2,1)}, bf16[2,4,12,3072]{3,1,2,0:T(4,128)(2,1)}, u32[]{:S(2)}, u32[]{:S(2)}) collective-permute-start(bf16[2,4,12,3072]{3,1,2,0:T(4,128)(2,1)} %copy.18), channel_id=1, source_target_pairs={{0,24},{1,25},{2,26},{3,27},{4,28},{5,29},{6,30},{7,31},{8,0},{9,1... | collective-permute-start | bytes 1769480 | tf_op jit(solution)/shard_map/ppermute | solution.py:241
  7.8 31.5 %collective-permute-start = (bf16[2,12,4,3072]{3,2,1,0:T(4,128)(2,1)}, bf16[2,12,4,3072]{3,2,1,0:T(4,128)(2,1)}, u32[]{:S(2)}, u32[]{:S(2)}) collective-permute-start(bf16[2,12,4,3072]{3,2,1,0:T(4,128)(2,1)} %fusion.3), channel_id=1, source_target_pairs={{0,7},{1,0},{2,1},{3,2},{4,3},{5,4},{6,5},{7,6},{8,15},{9,8},{10,9... | collective-permute-start | bytes 1769480 | tf_op jit(solution)/shard_map/ppermute | solution.py:241
  8.1 31.2 %collective-permute-start.2 = (bf16[2,4,4,3072]{3,2,1,0:T(4,128)(2,1)S(1)}, bf16[2,4,4,3072]{3,2,1,0:T(4,128)(2,1)S(1)}, u32[]{:S(2)}, u32[]{:S(2)}) collective-permute-start(bf16[2,4,4,3072]{3,2,1,0:T(4,128)(2,1)S(1)} %pad_maximum_fusion), channel_id=1, source_target_pairs={{0,31},{1,24},{2,25},{3,26},{4,27},{5,28},{6,29},{7,30},{8,7},{9,0... | collective-permute-start | bytes 589832 | tf_op jit(solution)/shard_map/ppermute | solution.py:241
  10.1 2.3 %copy-start.9 = (s32[16,16,16]{2,1,0:T(8,128)S(1)}, s32[16,16,16]{2,1,0:T(8,128)}, u32[]{:S(2)}) copy-start(s32[16,16,16]{2,1,0:T(8,128)} %param.8) | copy-start | bytes 49156
  12.5 3.2 %copy-start.7 = (bf16[192,576]{1,0:T(8,128)(2,1)S(1)}, bf16[192,576]{1,0:T(8,128)(2,1)}, u32[]{:S(2)}) copy-start(bf16[192,576]{1,0:T(8,128)(2,1)} %refs_5_.1) | copy-start | bytes 663556
  12.5 4.1 %copy-start.10 = (f32[192]{0:T(256)S(1)}, f32[192]{0:T(256)}, u32[]{:S(2)}) copy-start(f32[192]{0:T(256)} %param.9) | copy-start | bytes 2308
  17.3 22.0 %copy-start.4 = (bf16[2,12,12,3072]{3,2,1,0:T(8,128)(2,1)S(1)}, bf16[2,12,12,3072]{3,2,1,0:T(8,128)(2,1)}, u32[]{:S(2)}) copy-start(bf16[2,12,12,3072]{3,2,1,0:T(8,128)(2,1)} %fusion.1) | copy-start | bytes 5308420
  98.7 27.1 %copy-start.3 = (f32[16,16,3072]{2,1,0:T(8,128)S(1)}, f32[16,16,3072]{2,1,0:T(8,128)}, u32[]{:S(2)}) copy-start(f32[16,16,3072]{2,1,0:T(8,128)} %get-tuple-element.16) | copy-start | bytes 9437188
  101.1 0.8 copy-start.5
  102.0 2.3 %collective-permute-start.6 = (f32[128,768]{1,0:T(8,128)S(1)}, f32[128,768]{1,0:T(8,128)}, u32[]{:S(2)}, u32[]{:S(2)}) collective-permute-start(f32[128,768]{1,0:T(8,128)S(1)} %pad_dynamic-slice_fusion), channel_id=1, source_target_pairs={{0,2},{2,0},{4,6},{6,4},{1,3},{3,1},{5,7},{7,5},{8,10},{10,8},{12,... | collective-permute-start | bytes 1179656 | tf_op jit(solution)/shard_map/ppermute | solution.py:196
  106.1 6.4 %collective-permute-start.7 = (f32[64,768]{1,0:T(8,128)}, f32[64,768]{1,0:T(8,128)}, u32[]{:S(2)}, u32[]{:S(2)}) collective-permute-start(f32[64,768]{1,0:T(8,128)} %constant_dynamic-slice_fusion.3), channel_id=1, source_target_pairs={{0,4},{2,6},{4,0},{6,2},{1,5},{3,7},{5,1},{7,3},{8,12},{10,14},{12... | collective-permute-start | bytes 589832 | tf_op jit(solution)/shard_map/ppermute | solution.py:196
  113.4 0.7 copy-start.8
  114.1 3.5 %collective-permute-start.8 = (f32[32,768]{1,0:T(8,128)S(1)}, f32[32,768]{1,0:T(8,128)S(1)}, u32[]{:S(2)}, u32[]{:S(2)}) collective-permute-start(f32[32,768]{1,0:T(8,128)S(1)} %constant_dynamic-slice_fusion.2), channel_id=1, source_target_pairs={{0,8},{8,0},{16,24},{24,16},{1,9},{9,1},{17,25},{25,17},{2,10},{10... | collective-permute-start | bytes 294920 | tf_op jit(solution)/shard_map/ppermute | solution.py:196
  118.6 3.9 %collective-permute-start.9 = (f32[16,768]{1,0:T(8,128)S(1)}, f32[16,768]{1,0:T(8,128)S(1)}, u32[]{:S(2)}, u32[]{:S(2)}) collective-permute-start(f32[16,768]{1,0:T(8,128)S(1)} %constant_dynamic-slice_fusion.1), channel_id=1, source_target_pairs={{0,16},{8,24},{16,0},{24,8},{1,17},{9,25},{17,1},{25,9},{2,18},{10... | collective-permute-start | bytes 147464 | tf_op jit(solution)/shard_map/ppermute | solution.py:196
  122.5 3.0 %collective-permute-start.10 = (f32[8,768]{1,0:T(8,128)S(1)}, f32[8,768]{1,0:T(8,128)S(1)}, u32[]{:S(2)}, u32[]{:S(2)}) collective-permute-start(f32[8,768]{1,0:T(8,128)S(1)} %constant_dynamic-slice_fusion), channel_id=1, source_target_pairs={{0,1},{1,0},{2,3},{3,2},{4,5},{5,4},{6,7},{7,6},{8,9},{9,8},{10,11... | collective-permute-start | bytes 73736 | tf_op jit(solution)/shard_map/ppermute | solution.py:196
  125.6 8.8 %collective-permute-start.11 = (f32[8,768]{1,0:T(8,128)S(1)}, f32[8,768]{1,0:T(8,128)S(1)}, u32[]{:S(2)}, u32[]{:S(2)}) collective-permute-start(f32[8,768]{1,0:T(8,128)S(1)} %dynamic-slice_add_fusion.3), channel_id=1, source_target_pairs={{0,1},{1,0},{2,3},{3,2},{4,5},{5,4},{6,7},{7,6},{8,9},{9,8},{10,11... | collective-permute-start | bytes 73736 | tf_op jit(solution)/shard_map/ppermute | solution.py:196
  126.0 1.1 copy-start.6
  128.0 18.4 %collective-permute-start.5 = (bf16[12,4,3072]{2,1,0:T(4,128)(2,1)}, bf16[12,4,3072]{2,1,0:T(4,128)(2,1)}, u32[]{:S(2)}, u32[]{:S(2)}) collective-permute-start(bf16[12,4,3072]{2,1,0:T(4,128)(2,1)} %slice.56), channel_id=1, source_target_pairs={{0,1},{1,2},{2,3},{3,4},{4,5},{5,6},{6,7},{7,0},{8,9},{9,10},{10,1... | collective-permute-start | bytes 884744 | tf_op jit(solution)/shard_map/ppermute | solution.py:241
  135.0 4.8 %collective-permute-start.12 = (f32[16,768]{1,0:T(8,128)}, f32[16,768]{1,0:T(8,128)}, u32[]{:S(2)}, u32[]{:S(2)}) collective-permute-start(f32[16,768]{1,0:T(8,128)} %maximum_select_fusion.4), channel_id=1, source_target_pairs={{0,16},{8,24},{16,0},{24,8},{1,17},{9,25},{17,1},{25,9},{2,18},{10... | collective-permute-start | bytes 147464 | tf_op jit(solution)/shard_map/ppermute | solution.py:196
  136.1 17.4 %collective-permute-start.4 = (bf16[4,12,3072]{2,1,0:T(8,128)(2,1)S(1)}, bf16[4,12,3072]{2,1,0:T(8,128)(2,1)}, u32[]{:S(2)}, u32[]{:S(2)}) collective-permute-start(bf16[4,12,3072]{2,1,0:T(8,128)(2,1)S(1)} %slice.55), channel_id=1, source_target_pairs={{0,8},{1,9},{2,10},{3,11},{4,12},{5,13},{6,14},{7,15},{8,16},{9,17... | collective-permute-start | bytes 884744 | tf_op jit(solution)/shard_map/ppermute | solution.py:241
  141.3 10.3 %collective-permute-start.13 = (f32[32,768]{1,0:T(8,128)}, f32[32,768]{1,0:T(8,128)}, u32[]{:S(2)}, u32[]{:S(2)}) collective-permute-start(f32[32,768]{1,0:T(8,128)} %maximum_select_fusion.3), channel_id=1, source_target_pairs={{0,8},{8,0},{16,24},{24,16},{1,9},{9,1},{17,25},{25,17},{2,10},{10... | collective-permute-start | bytes 294920 | tf_op jit(solution)/shard_map/ppermute | solution.py:196
  143.6 16.6 %copy-start.1 = (bf16[16,16,3072]{2,1,0:T(8,128)(2,1)S(1)}, bf16[16,16,3072]{2,1,0:T(8,128)(2,1)}, u32[]{:S(2)}) copy-start(bf16[16,16,3072]{2,1,0:T(8,128)(2,1)} %refs_1_.1) | copy-start | bytes 4718596
  143.9 9.6 %collective-permute-start.3 = (bf16[4,4,3072]{2,1,0:T(4,128)(2,1)S(1)}, bf16[4,4,3072]{2,1,0:T(4,128)(2,1)S(1)}, u32[]{:S(2)}, u32[]{:S(2)}) collective-permute-start(bf16[4,4,3072]{2,1,0:T(4,128)(2,1)S(1)} %slice.54), channel_id=1, source_target_pairs={{0,9},{1,10},{2,11},{3,12},{4,13},{5,14},{6,15},{7,8},{8,17},{9,18... | collective-permute-start | bytes 294920 | tf_op jit(solution)/shard_map/ppermute | solution.py:241
  152.7 5.9 %collective-permute-start.14 = (f32[64,768]{1,0:T(8,128)S(1)}, f32[64,768]{1,0:T(8,128)S(1)}, u32[]{:S(2)}, u32[]{:S(2)}) collective-permute-start(f32[64,768]{1,0:T(8,128)S(1)} %maximum_select_fusion.2), channel_id=1, source_target_pairs={{0,4},{2,6},{4,0},{6,2},{1,5},{3,7},{5,1},{7,3},{8,12},{10,14},{12... | collective-permute-start | bytes 589832 | tf_op jit(solution)/shard_map/ppermute | solution.py:196
  158.7 3.3 %collective-permute-start.15 = (f32[128,768]{1,0:T(8,128)S(1)}, f32[128,768]{1,0:T(8,128)S(1)}, u32[]{:S(2)}, u32[]{:S(2)}) collective-permute-start(f32[128,768]{1,0:T(8,128)S(1)} %maximum_select_fusion.1), channel_id=1, source_target_pairs={{0,2},{2,0},{4,6},{6,4},{1,3},{3,1},{5,7},{7,5},{8,10},{10,8},{12,... | collective-permute-start | bytes 1179656 | tf_op jit(solution)/shard_map/ppermute | solution.py:196

commit v12 on v11

--- a/solution.py
+++ b/solution.py
@@ -42,10 +42,10 @@
 def make_window_kernel(first):
     def window_kernel(*refs):
         if first:
-            (tok_ref, grd_ref, kcol_ref, krow_ref, gain_ref, wqkvT_ref, wqkv_ref, wp_ref,
+            (tok_ref, grd_ref, krow_ref, gain_ref, wqkv_ref, wp_ref,
              gs_ref, gqkvT_ref, gproj_ref, ggain_ref, qkv_s, ga_s, drow_s) = refs
         else:
-            (both_ref, kcol_ref, krow_ref, gain_ref, wqkvT_ref, wqkv_ref, wp_ref,
+            (both_ref, krow_ref, gain_ref, wqkv_ref, wp_ref,
              gs0_ref, gqkvT0_ref, gproj0_ref, ggain0_ref,
              gs_ref, gqkvT_ref, gproj_ref, ggain_ref, qkv_s, ga_s, drow_s) = refs
         f32 = jnp.float32
@@ -59,7 +59,8 @@
             gproj_ref[...] = gproj0_ref[...]
             ggain_ref[...] = ggain0_ref[...]
             gs_ref[pl.ds(0, WIN), pl.ds(0, WIN), :] = gs0_ref[...]
-        gain = gain_ref[...]
+        gain = jnp.broadcast_to(gain_ref[...], (8, C)).T[:, 0:1]
+        wqkv_t = wqkv_ref[...].astype(f32).T.astype(bf16)
         nt = (((1,), (1,)), ((), ()))
         pair = 2 * C
         n_pairs = NZ // 2
@@ -107,12 +108,14 @@
             inv_std = lax.rsqrt(jnp.mean(centred * centred, axis=0, keepdims=True) + 1e-05)
             x_hat = centred * inv_std
             normed = (x_hat * gain).astype(bf16)
-            qkv_t = jnp.dot(wqkvT_ref[...], normed, preferred_element_type=f32)
+            qkv_t = jnp.dot(wqkv_t, normed, preferred_element_type=f32)
             qkv_s[...] = qkv_t.astype(bf16).astype(f32)
             g = gathered(1, i, j, l).astype(bf16)
             ga_t = jnp.dot(wp_ref[...], g, preferred_element_type=f32)
             ga_s[...] = ga_t.astype(bf16).astype(f32)
-            allowed = kcol_ref[w] == krow_ref[w]
+            key_row = krow_ref[w].astype(f32)
+            key_col = jnp.broadcast_to(key_row, (8, CELLS)).T[:, 0:1]
+            allowed = key_col == key_row
 
             def head_step(h, carry):
                 qo = pl.multiple_of(h * HEAD, HEAD)
@@ -168,7 +171,7 @@
     return window_kernel
 
 
-def window_grads(first, arrays, kcol, krow, gain_col, wqkv_t, wqkv, wp, partial=()):
+def window_grads(first, arrays, krow, gain_row, wqkv, wp, partial=()):
     if first:
         extent_a, extent_b, width = WIN, WIN, arrays[0].shape[2]
     else:
@@ -186,7 +189,7 @@
             pltpu.VMEM((C, CELLS), jnp.float32),
             pltpu.VMEM((3 * C, CELLS), jnp.float32),
         ],
-    )(*arrays, kcol, krow, gain_col, wqkv_t, wqkv, wp, *partial)
+    )(*arrays, krow, gain_row, wqkv, wp, *partial)
 
 
 SUM_AXES = ("gy", "gx", "gz")
@@ -279,10 +282,8 @@
     mask_key = to_windows_key(labels * 8 + region)
 
     constants = (
-        mask_key[:, :, None],
         mask_key[:, None, :],
-        ln_gain.reshape(channels, 1),
-        qkv_weight.T,
+        ln_gain.reshape(1, channels),
         qkv_weight,
         proj_weight,
     )

time: 165 us -> 160 us (0.970)
  local copies, waits for them, and re-layouts: 16.3 us -> 12.6 us
    another operation x1 -> x0, local copies, waits for them, and re-layouts: 1.99 us -> none  [per_device(): mask_key[:, :, None]]
    unnamed x23 -> x18, local copies, waits for them, and re-layouts: 3.54 us -> 2.66 us
  transfers between devices with their start and end apart: 16 -> 16, of which waited for: 8 -> 8; matrix products, arithmetic and copies ran while one was open for 12% -> 10% of each run, Pallas kernels for 13% -> 13%
where the time goes in v12:
time: 160 us
  Pallas kernels  75.8 us (47%)
  waiting for transfers between devices  26.2 us (16%)
  starting transfers between devices  23.2 us (14%)
  other arithmetic  21.2 us (13%)
  local copies, waits for them, and re-layouts  12.6 us (8%)
    pallas_call x2, Pallas kernels, window_grads(): pl.pallas_call(make_window_kernel(first), out_shape=[jax.ShapeDtypeStruct...  75.8 us
    ppermute x10, waiting for transfers between devices, swapped(): lax.ppermute(block, axis, [(i, i ^ distance) for i in range(lax.axis_size...  26.2 us
    ppermute x6, starting transfers between devices, moved(): lax.ppermute(block, ('gx', 'gy', 'gz'), halo_route(distance_a, distance_b))  16 us
    ppermute x10, starting transfers between devices, swapped(): lax.ppermute(block, axis, [(i, i ^ distance) for i in range(lax.axis_size...  7.24 us
    another operation x4, other arithmetic, per_device(): both = shifted_block(jnp.stack([tokens, grads_out]))  4.85 us
    concatenate x1, other arithmetic, shifted_block(): return jnp.concatenate([upper, lower], axis=1)  3.35 us
    select_n x5, other arithmetic, summed_everywhere(): jnp.where(bit == 0, jnp.concatenate([values, other]), jnp.concatenate([ot...  3.3 us
  transfers between devices with their start and end apart: 16, of which 8 were waited for; matrix products, arithmetic and copies ran while one was open for 10% of the time, Pallas kernels for 13%

profile of v12, /device:TPU:5, one launch (start us, length us, event | category | flops | bytes accessed | tf_op | source)
XLA Modules:
  0.0 159.9 jit_solution(4074948668432911190)
XLA Ops:
  0.7 1.5 fusion.2
  2.2 1.3 copy.12
  3.5 3.3 %collective-permute-start.1 = (bf16[2,4,12,3072]{3,1,2,0:T(4,128)(2,1)}, bf16[2,4,12,3072]{3,1,2,0:T(4,128)(2,1)}, u32[]{:S(2)}, u32[]{:S(2)}) collective-permute-start(bf16[2,4,12,3072]{3,1,2,0:T(4,128)(2,1)} %copy.12), channel_id=1, source_target_pairs={{0,24},{1,25},{2,26},{3,27},{4,28},{5,29},{6,30},{7,31},{8,0},{9,1... | collective-permute-start | bytes 1769480 | tf_op jit(solution)/shard_map/ppermute | solution.py:244
  6.8 1.0 fusion.3
  8.1 2.0 %collective-permute-start.2 = (bf16[2,4,4,3072]{3,2,1,0:T(4,128)(2,1)S(1)}, bf16[2,4,4,3072]{3,2,1,0:T(4,128)(2,1)S(1)}, u32[]{:S(2)}, u32[]{:S(2)}) collective-permute-start(bf16[2,4,4,3072]{3,2,1,0:T(4,128)(2,1)S(1)} %pad_maximum_fusion), channel_id=1, source_target_pairs={{0,31},{1,24},{2,25},{3,26},{4,27},{5,28},{6,29},{7,30},{8,7},{9,0... | collective-permute-start | bytes 589832 | tf_op jit(solution)/shard_map/ppermute | solution.py:244
  10.2 2.2 %fusion.1 = bf16[2,12,12,3072]{3,2,1,0:T(8,128)(2,1)} fusion(bf16[1,16,16,3072]{3,2,1,0:T(8,128)(2,1)S(1)} %bitcast.15, bf16[1,16,16,3072]{3,2,1,0:T(8,128)(2,1)S(1)} %bitcast.11), kind=kLoop, calls=%fused_computation.9 | loop fusion | flops 884736 | bytes 4915200 | tf_op jit(solution)/shard_map/stack | solution.py:271
  12.9 0.8 broadcast_in_dim_reshape.3.refs_2_.refs_1_
  13.7 20.0 %shard_map.93 = (f32[8,8,3072]{2,1,0:T(8,128)}, f32[192,576]{1,0:T(8,128)}, f32[192,192]{1,0:T(8,128)}, f32[192,1]{1,0:T(8,128)}) custom-call(bf16[16,16,3072]{2,1,0:T(8,128)(2,1)} %refs_0_.1, bf16[16,16,3072]{2,1,0:T(8,128)(2,1)} %refs_1_.1, s32[8,1,512]{2,1,0:T(1,128)} %broadcast_in_dim_reshape.3.refs_2_.refs_1_, f32[1,192]{1,0:T(1,128)} %bitcast.18, ...), custom_call_target="tpu_custom_call" | custom-call | tf_op jit(solution)/shard_map/pallas_call | solution.py:179
  33.7 1.3 copy.13
  35.0 3.3 %maximum_maximum_fusion.refs_0_ = bf16[2,16,16,3072]{3,2,1,0:T(8,128)(2,1)} fusion(bf16[2,4,4,3072]{3,2,1,0:T(4,128)(2,1)S(1)} %collective-permute-done.2, bf16[2,4,12,3072]{3,2,1,0:T(8,128)(2,1)S(1)} %copy.13, bf16[2,12,4,3072]{3,2,1,0:T(4,128)(2,1)} %collective-permute-done, bf16[2,12,12,3072]{3,2,1,0:T(8,128)(2,1)S(1)} %copy-done.4), kind=kLoop, calls=%fused_computation.6 | loop fusion | flops 12582912 | bytes 6291456 | tf_op jit(solution)/shard_map/concatenate | solution.py:253
  38.4 55.7 %shard_map.94 = (f32[16,16,3072]{2,1,0:T(8,128)}, f32[192,576]{1,0:T(8,128)}, f32[192,192]{1,0:T(8,128)}, f32[192,1]{1,0:T(8,128)}) custom-call(bf16[2,16,16,3072]{3,2,1,0:T(8,128)(2,1)} %maximum_maximum_fusion.refs_0_, s32[8,1,512]{2,1,0:T(1,128)} %broadcast_in_dim_reshape.3.refs_2_.refs_1_, f32[1,192]{1,0:T(1,128)} %bitcast.19, bf16[192,576]{1,0:T(8,128)(2,1)} %refs_3_.1, ...), custom_call_target="tpu_custom_call" | custom-call | tf_op jit(solution)/shard_map/pallas_call | solution.py:179
  94.1 1.1 reduce
  95.3 1.3 select_maximum_fusion
  96.5 0.8 copy-done.5
  97.4 0.8 collective-permute-start.6
  98.2 1.5 collective-permute-done.6
  99.7 1.1 fusion.4
  100.8 0.7 constant_dynamic-slice_fusion.3
  101.5 0.8 collective-permute-start.7
  102.3 5.5 %collective-permute-done.7 = f32[64,768]{1,0:T(8,128)} collective-permute-done((f32[64,768]{1,0:T(8,128)}, f32[64,768]{1,0:T(8,128)}, u32[]{:S(2)}, u32[]{:S(2)}) %collective-permute-start.7) | collective-permute-done | bytes 196640 | tf_op jit(solution)/shard_map/ppermute | solution.py:199
  107.9 0.9 dynamic-slice_add_fusion
  108.8 0.7 copy-done.7
  109.5 1.4 collective-permute-start.8
  110.9 2.2 %collective-permute-done.8 = f32[32,768]{1,0:T(8,128)S(1)} collective-permute-done((f32[32,768]{1,0:T(8,128)S(1)}, f32[32,768]{1,0:T(8,128)S(1)}, u32[]{:S(2)}, u32[]{:S(2)}) %collective-permute-start.8) | collective-permute-done | bytes 98336 | tf_op jit(solution)/shard_map/ppermute | solution.py:199
  113.0 0.9 dynamic-slice_add_fusion.1
  114.1 3.8 %collective-permute-done.9 = f32[16,768]{1,0:T(8,128)S(1)} collective-permute-done((f32[16,768]{1,0:T(8,128)S(1)}, f32[16,768]{1,0:T(8,128)S(1)}, u32[]{:S(2)}, u32[]{:S(2)}) %collective-permute-start.9) | collective-permute-done | bytes 49184 | tf_op jit(solution)/shard_map/ppermute | solution.py:199
  118.3 2.7 %collective-permute-done.10 = f32[8,768]{1,0:T(8,128)S(1)} collective-permute-done((f32[8,768]{1,0:T(8,128)S(1)}, f32[8,768]{1,0:T(8,128)S(1)}, u32[]{:S(2)}, u32[]{:S(2)}) %collective-permute-start.10) | collective-permute-done | bytes 24608 | tf_op jit(solution)/shard_map/ppermute | solution.py:199
  121.4 1.1 copy-done.6
  122.5 0.9 slice.56
  123.4 6.4 %collective-permute-start.5 = (bf16[12,4,3072]{2,1,0:T(4,128)(2,1)}, bf16[12,4,3072]{2,1,0:T(4,128)(2,1)}, u32[]{:S(2)}, u32[]{:S(2)}) collective-permute-start(bf16[12,4,3072]{2,1,0:T(4,128)(2,1)} %slice.56), channel_id=1, source_target_pairs={{0,1},{1,2},{2,3},{3,4},{4,5},{5,6},{6,7},{7,0},{8,9},{9,10},{10,1... | collective-permute-start | bytes 884744 | tf_op jit(solution)/shard_map/ppermute | solution.py:244
  129.8 0.6 maximum_select_fusion.4
  130.4 1.0 slice.55
  131.4 1.5 collective-permute-start.4
  132.9 2.3 %collective-permute-done.12 = f32[16,768]{1,0:T(8,128)} collective-permute-done((f32[16,768]{1,0:T(8,128)}, f32[16,768]{1,0:T(8,128)}, u32[]{:S(2)}, u32[]{:S(2)}) %collective-permute-start.12) | collective-permute-done | bytes 49184 | tf_op jit(solution)/shard_map/ppermute | solution.py:199
  135.2 1.5 maximum_select_fusion.3
  136.7 1.3 collective-permute-start.13
  138.0 1.0 slice.54
  139.2 2.5 %collective-permute-start.3 = (bf16[4,4,3072]{2,1,0:T(4,128)(2,1)S(1)}, bf16[4,4,3072]{2,1,0:T(4,128)(2,1)S(1)}, u32[]{:S(2)}, u32[]{:S(2)}) collective-permute-start(bf16[4,4,3072]{2,1,0:T(4,128)(2,1)S(1)} %slice.54), channel_id=1, source_target_pairs={{0,9},{1,10},{2,11},{3,12},{4,13},{5,14},{6,15},{7,8},{8,17},{9,18... | collective-permute-start | bytes 294920 | tf_op jit(solution)/shard_map/ppermute | solution.py:244
  141.8 1.0 convert_element_type.32
  142.8 4.2 %collective-permute-done.13 = f32[32,768]{1,0:T(8,128)} collective-permute-done((f32[32,768]{1,0:T(8,128)}, f32[32,768]{1,0:T(8,128)}, u32[]{:S(2)}, u32[]{:S(2)}) %collective-permute-start.13) | collective-permute-done | bytes 98336 | tf_op jit(solution)/shard_map/ppermute | solution.py:199
  147.0 1.1 maximum_select_fusion.2
  148.1 0.7 collective-permute-start.14
  148.8 1.1 maximum_convert_fusion
  149.9 4.1 %collective-permute-done.14 = f32[64,768]{1,0:T(8,128)S(1)} collective-permute-done((f32[64,768]{1,0:T(8,128)S(1)}, f32[64,768]{1,0:T(8,128)S(1)}, u32[]{:S(2)}, u32[]{:S(2)}) %collective-permute-start.14) | collective-permute-done | bytes 196640 | tf_op jit(solution)/shard_map/ppermute | solution.py:199
  154.0 1.5 collective-permute-start.15
  155.6 1.8 %fusion = bf16[16,16,3072]{2,1,0:T(8,128)(2,1)} fusion(f32[12,12,3072]{2,1,0:T(8,128)S(1)} %slice.44, f32[12,4,3072]{2,1,0:T(4,128)S(1)} %convert_element_type.32, f32[4,16,3072]{2,1,0:T(8,128)S(1)} %maximum_convert_fusion, bf16[16,16,3072]{2,1,0:T(8,128)(2,1)S(1)} %copy-done.1), kind=kLoop, calls=%fused_computation.8 | loop fusion | flops 3932160 | bytes 6291456 | tf_op jit(solution)/shard_map/convert_element_type | solution.py:264
  158.1 1.0 reshape.77
  159.1 0.8 reshape.78
  (48 shorter events, 2.9 us)
Async XLA Ops:
  0.6 6.1 %copy-start.2 = (bf16[16,16,3072]{2,1,0:T(8,128)(2,1)S(1)}, bf16[16,16,3072]{2,1,0:T(8,128)(2,1)}, u32[]{:S(2)}) copy-start(bf16[16,16,3072]{2,1,0:T(8,128)(2,1)} %refs_0_.1) | copy-start | bytes 4718596
  0.6 6.1 %copy-start = (bf16[16,16,3072]{2,1,0:T(8,128)(2,1)S(1)}, bf16[16,16,3072]{2,1,0:T(8,128)(2,1)}, u32[]{:S(2)}) copy-start(bf16[16,16,3072]{2,1,0:T(8,128)(2,1)} %refs_1_.1) | copy-start | bytes 4718596
  3.5 30.3 %collective-permute-start.1 = (bf16[2,4,12,3072]{3,1,2,0:T(4,128)(2,1)}, bf16[2,4,12,3072]{3,1,2,0:T(4,128)(2,1)}, u32[]{:S(2)}, u32[]{:S(2)}) collective-permute-start(bf16[2,4,12,3072]{3,1,2,0:T(4,128)(2,1)} %copy.12), channel_id=1, source_target_pairs={{0,24},{1,25},{2,26},{3,27},{4,28},{5,29},{6,30},{7,31},{8,0},{9,1... | collective-permute-start | bytes 1769480 | tf_op jit(solution)/shard_map/ppermute | solution.py:244
  7.8 27.2 %collective-permute-start = (bf16[2,12,4,3072]{3,2,1,0:T(4,128)(2,1)}, bf16[2,12,4,3072]{3,2,1,0:T(4,128)(2,1)}, u32[]{:S(2)}, u32[]{:S(2)}) collective-permute-start(bf16[2,12,4,3072]{3,2,1,0:T(4,128)(2,1)} %fusion.3), channel_id=1, source_target_pairs={{0,7},{1,0},{2,1},{3,2},{4,3},{5,4},{6,5},{7,6},{8,15},{9,8},{10,9... | collective-permute-start | bytes 1769480 | tf_op jit(solution)/shard_map/ppermute | solution.py:244
  8.1 26.9 %collective-permute-start.2 = (bf16[2,4,4,3072]{3,2,1,0:T(4,128)(2,1)S(1)}, bf16[2,4,4,3072]{3,2,1,0:T(4,128)(2,1)S(1)}, u32[]{:S(2)}, u32[]{:S(2)}) collective-permute-start(bf16[2,4,4,3072]{3,2,1,0:T(4,128)(2,1)S(1)} %pad_maximum_fusion), channel_id=1, source_target_pairs={{0,31},{1,24},{2,25},{3,26},{4,27},{5,28},{6,29},{7,30},{8,7},{9,0... | collective-permute-start | bytes 589832 | tf_op jit(solution)/shard_map/ppermute | solution.py:244
  10.1 2.3 %copy-start.8 = (s32[16,16,16]{2,1,0:T(8,128)S(1)}, s32[16,16,16]{2,1,0:T(8,128)}, u32[]{:S(2)}) copy-start(s32[16,16,16]{2,1,0:T(8,128)} %param.8) | copy-start | bytes 49156
  12.5 22.6 %copy-start.4 = (bf16[2,12,12,3072]{3,2,1,0:T(8,128)(2,1)S(1)}, bf16[2,12,12,3072]{3,2,1,0:T(8,128)(2,1)}, u32[]{:S(2)}) copy-start(bf16[2,12,12,3072]{3,2,1,0:T(8,128)(2,1)} %fusion.1) | copy-start | bytes 5308420
  94.1 27.1 %copy-start.3 = (f32[16,16,3072]{2,1,0:T(8,128)S(1)}, f32[16,16,3072]{2,1,0:T(8,128)}, u32[]{:S(2)}) copy-start(f32[16,16,3072]{2,1,0:T(8,128)} %get-tuple-element.16) | copy-start | bytes 9437188
  96.5 0.8 copy-start.5
  97.4 2.3 %collective-permute-start.6 = (f32[128,768]{1,0:T(8,128)S(1)}, f32[128,768]{1,0:T(8,128)}, u32[]{:S(2)}, u32[]{:S(2)}) collective-permute-start(f32[128,768]{1,0:T(8,128)S(1)} %pad_dynamic-slice_fusion), channel_id=1, source_target_pairs={{0,2},{2,0},{4,6},{6,4},{1,3},{3,1},{5,7},{7,5},{8,10},{10,8},{12,... | collective-permute-start | bytes 1179656 | tf_op jit(solution)/shard_map/ppermute | solution.py:199
  101.5 6.4 %collective-permute-start.7 = (f32[64,768]{1,0:T(8,128)}, f32[64,768]{1,0:T(8,128)}, u32[]{:S(2)}, u32[]{:S(2)}) collective-permute-start(f32[64,768]{1,0:T(8,128)} %constant_dynamic-slice_fusion.3), channel_id=1, source_target_pairs={{0,4},{2,6},{4,0},{6,2},{1,5},{3,7},{5,1},{7,3},{8,12},{10,14},{12... | collective-permute-start | bytes 589832 | tf_op jit(solution)/shard_map/ppermute | solution.py:199
  108.8 0.7 copy-start.7
  109.5 3.5 %collective-permute-start.8 = (f32[32,768]{1,0:T(8,128)S(1)}, f32[32,768]{1,0:T(8,128)S(1)}, u32[]{:S(2)}, u32[]{:S(2)}) collective-permute-start(f32[32,768]{1,0:T(8,128)S(1)} %constant_dynamic-slice_fusion.2), channel_id=1, source_target_pairs={{0,8},{8,0},{16,24},{24,16},{1,9},{9,1},{17,25},{25,17},{2,10},{10... | collective-permute-start | bytes 294920 | tf_op jit(solution)/shard_map/ppermute | solution.py:199
  114.0 3.9 %collective-permute-start.9 = (f32[16,768]{1,0:T(8,128)S(1)}, f32[16,768]{1,0:T(8,128)S(1)}, u32[]{:S(2)}, u32[]{:S(2)}) collective-permute-start(f32[16,768]{1,0:T(8,128)S(1)} %constant_dynamic-slice_fusion.1), channel_id=1, source_target_pairs={{0,16},{8,24},{16,0},{24,8},{1,17},{9,25},{17,1},{25,9},{2,18},{10... | collective-permute-start | bytes 147464 | tf_op jit(solution)/shard_map/ppermute | solution.py:199
  117.9 3.0 %collective-permute-start.10 = (f32[8,768]{1,0:T(8,128)S(1)}, f32[8,768]{1,0:T(8,128)S(1)}, u32[]{:S(2)}, u32[]{:S(2)}) collective-permute-start(f32[8,768]{1,0:T(8,128)S(1)} %constant_dynamic-slice_fusion), channel_id=1, source_target_pairs={{0,1},{1,0},{2,3},{3,2},{4,5},{5,4},{6,7},{7,6},{8,9},{9,8},{10,11... | collective-permute-start | bytes 73736 | tf_op jit(solution)/shard_map/ppermute | solution.py:199
  120.9 8.8 %collective-permute-start.11 = (f32[8,768]{1,0:T(8,128)S(1)}, f32[8,768]{1,0:T(8,128)S(1)}, u32[]{:S(2)}, u32[]{:S(2)}) collective-permute-start(f32[8,768]{1,0:T(8,128)S(1)} %dynamic-slice_add_fusion.3), channel_id=1, source_target_pairs={{0,1},{1,0},{2,3},{3,2},{4,5},{5,4},{6,7},{7,6},{8,9},{9,8},{10,11... | collective-permute-start | bytes 73736 | tf_op jit(solution)/shard_map/ppermute | solution.py:199
  121.4 1.1 copy-start.6
  123.4 18.4 %collective-permute-start.5 = (bf16[12,4,3072]{2,1,0:T(4,128)(2,1)}, bf16[12,4,3072]{2,1,0:T(4,128)(2,1)}, u32[]{:S(2)}, u32[]{:S(2)}) collective-permute-start(bf16[12,4,3072]{2,1,0:T(4,128)(2,1)} %slice.56), channel_id=1, source_target_pairs={{0,1},{1,2},{2,3},{3,4},{4,5},{5,6},{6,7},{7,0},{8,9},{9,10},{10,1... | collective-permute-start | bytes 884744 | tf_op jit(solution)/shard_map/ppermute | solution.py:244
  130.4 4.8 %collective-permute-start.12 = (f32[16,768]{1,0:T(8,128)}, f32[16,768]{1,0:T(8,128)}, u32[]{:S(2)}, u32[]{:S(2)}) collective-permute-start(f32[16,768]{1,0:T(8,128)} %maximum_select_fusion.4), channel_id=1, source_target_pairs={{0,16},{8,24},{16,0},{24,8},{1,17},{9,25},{17,1},{25,9},{2,18},{10... | collective-permute-start | bytes 147464 | tf_op jit(solution)/shard_map/ppermute | solution.py:199
  131.4 17.4 %collective-permute-start.4 = (bf16[4,12,3072]{2,1,0:T(8,128)(2,1)S(1)}, bf16[4,12,3072]{2,1,0:T(8,128)(2,1)}, u32[]{:S(2)}, u32[]{:S(2)}) collective-permute-start(bf16[4,12,3072]{2,1,0:T(8,128)(2,1)S(1)} %slice.55), channel_id=1, source_target_pairs={{0,8},{1,9},{2,10},{3,11},{4,12},{5,13},{6,14},{7,15},{8,16},{9,17... | collective-permute-start | bytes 884744 | tf_op jit(solution)/shard_map/ppermute | solution.py:244
  136.7 10.3 %collective-permute-start.13 = (f32[32,768]{1,0:T(8,128)}, f32[32,768]{1,0:T(8,128)}, u32[]{:S(2)}, u32[]{:S(2)}) collective-permute-start(f32[32,768]{1,0:T(8,128)} %maximum_select_fusion.3), channel_id=1, source_target_pairs={{0,8},{8,0},{16,24},{24,16},{1,9},{9,1},{17,25},{25,17},{2,10},{10... | collective-permute-start | bytes 294920 | tf_op jit(solution)/shard_map/ppermute | solution.py:199
  139.0 16.6 %copy-start.1 = (bf16[16,16,3072]{2,1,0:T(8,128)(2,1)S(1)}, bf16[16,16,3072]{2,1,0:T(8,128)(2,1)}, u32[]{:S(2)}) copy-start(bf16[16,16,3072]{2,1,0:T(8,128)(2,1)} %refs_1_.1) | copy-start | bytes 4718596
  139.2 9.6 %collective-permute-start.3 = (bf16[4,4,3072]{2,1,0:T(4,128)(2,1)S(1)}, bf16[4,4,3072]{2,1,0:T(4,128)(2,1)S(1)}, u32[]{:S(2)}, u32[]{:S(2)}) collective-permute-start(bf16[4,4,3072]{2,1,0:T(4,128)(2,1)S(1)} %slice.54), channel_id=1, source_target_pairs={{0,9},{1,10},{2,11},{3,12},{4,13},{5,14},{6,15},{7,8},{8,17},{9,18... | collective-permute-start | bytes 294920 | tf_op jit(solution)/shard_map/ppermute | solution.py:244
  148.1 5.9 %collective-permute-start.14 = (f32[64,768]{1,0:T(8,128)S(1)}, f32[64,768]{1,0:T(8,128)S(1)}, u32[]{:S(2)}, u32[]{:S(2)}) collective-permute-start(f32[64,768]{1,0:T(8,128)S(1)} %maximum_select_fusion.2), channel_id=1, source_target_pairs={{0,4},{2,6},{4,0},{6,2},{1,5},{3,7},{5,1},{7,3},{8,12},{10,14},{12... | collective-permute-start | bytes 589832 | tf_op jit(solution)/shard_map/ppermute | solution.py:199
  154.0 3.3 %collective-permute-start.15 = (f32[128,768]{1,0:T(8,128)S(1)}, f32[128,768]{1,0:T(8,128)S(1)}, u32[]{:S(2)}, u32[]{:S(2)}) collective-permute-start(f32[128,768]{1,0:T(8,128)S(1)} %maximum_select_fusion.1), channel_id=1, source_target_pairs={{0,2},{2,0},{4,6},{6,4},{1,3},{3,1},{5,7},{7,5},{8,10},{10,8},{12,... | collective-permute-start | bytes 1179656 | tf_op jit(solution)/shard_map/ppermute | solution.py:199

commit v13 on v12

--- a/solution.py
+++ b/solution.py
@@ -13,6 +13,7 @@
 CELLS = WIN**3
 HEAD = C // HEADS
 SCALE = HEAD ** (-0.5)
+EXP2_SCALE = SCALE * 1.4426950408889634
 
 
 def passed_along(block, axis, distance):
@@ -124,8 +125,8 @@
                 v_t = qkv_s[pl.ds(qo + 2 * C, HEAD), :]
                 ga_th = ga_s[pl.ds(qo, HEAD), :]
                 q = q_t.T.astype(bf16)
-                scores = jnp.dot(q, k_t.astype(bf16), preferred_element_type=f32) * SCALE
-                weights = jnp.where(allowed, jnp.exp(scores), 0.0)
+                scores = jnp.dot(q, k_t.astype(bf16), preferred_element_type=f32)
+                weights = jnp.where(allowed, jnp.exp2(scores * EXP2_SCALE), 0.0)
                 probs = weights / jnp.sum(weights, axis=1, keepdims=True)
                 probs_bf = probs.astype(bf16)
                 att_t = lax.dot_general(v_t.astype(bf16), probs_bf, nt, preferred_element_type=f32)

time: 160 us -> 159 us (level)
  transfers between devices with their start and end apart: 16 -> 16, of which waited for: 8 -> 8; matrix products, arithmetic and copies ran while one was open for 10% -> 10% of each run, Pallas kernels for 13% -> 12%
where the time goes in v13:
time: 159 us
  Pallas kernels  74.8 us (47%)
  waiting for transfers between devices  26.2 us (16%)
  starting transfers between devices  23.2 us (15%)
  other arithmetic  21.2 us (13%)
  local copies, waits for them, and re-layouts  12.6 us (8%)
    pallas_call x2, Pallas kernels, window_grads(): pl.pallas_call(make_window_kernel(first), out_shape=[jax.ShapeDtypeStruct...  74.8 us
    ppermute x10, waiting for transfers between devices, swapped(): lax.ppermute(block, axis, [(i, i ^ distance) for i in range(lax.axis_size...  26.2 us
    ppermute x6, starting transfers between devices, moved(): lax.ppermute(block, ('gx', 'gy', 'gz'), halo_route(distance_a, distance_b))  16 us
    ppermute x10, starting transfers between devices, swapped(): lax.ppermute(block, axis, [(i, i ^ distance) for i in range(lax.axis_size...  7.26 us
    another operation x4, other arithmetic, per_device(): both = shifted_block(jnp.stack([tokens, grads_out]))  4.85 us
    concatenate x1, other arithmetic, shifted_block(): return jnp.concatenate([upper, lower], axis=1)  3.35 us
    select_n x5, other arithmetic, summed_everywhere(): jnp.where(bit == 0, jnp.concatenate([values, other]), jnp.concatenate([ot...  3.3 us
  transfers between devices with their start and end apart: 16, of which 8 were waited for; matrix products, arithmetic and copies ran while one was open for 10% of the time, Pallas kernels for 12%

profile of v13, /device:TPU:5, one launch (start us, length us, event | category | flops | bytes accessed | tf_op | source)
XLA Modules:
  0.0 159.0 jit_solution(5474729265703040168)
XLA Ops:
  0.7 1.5 fusion.2
  2.2 1.3 copy.12
  3.5 3.3 %collective-permute-start.1 = (bf16[2,4,12,3072]{3,1,2,0:T(4,128)(2,1)}, bf16[2,4,12,3072]{3,1,2,0:T(4,128)(2,1)}, u32[]{:S(2)}, u32[]{:S(2)}) collective-permute-start(bf16[2,4,12,3072]{3,1,2,0:T(4,128)(2,1)} %copy.12), channel_id=1, source_target_pairs={{0,24},{1,25},{2,26},{3,27},{4,28},{5,29},{6,30},{7,31},{8,0},{9,1... | collective-permute-start | bytes 1769480 | tf_op jit(solution)/shard_map/ppermute | solution.py:245
  6.8 1.0 fusion.3
  8.1 2.0 %collective-permute-start.2 = (bf16[2,4,4,3072]{3,2,1,0:T(4,128)(2,1)S(1)}, bf16[2,4,4,3072]{3,2,1,0:T(4,128)(2,1)S(1)}, u32[]{:S(2)}, u32[]{:S(2)}) collective-permute-start(bf16[2,4,4,3072]{3,2,1,0:T(4,128)(2,1)S(1)} %pad_maximum_fusion), channel_id=1, source_target_pairs={{0,31},{1,24},{2,25},{3,26},{4,27},{5,28},{6,29},{7,30},{8,7},{9,0... | collective-permute-start | bytes 589832 | tf_op jit(solution)/shard_map/ppermute | solution.py:245
  10.2 2.2 %fusion.1 = bf16[2,12,12,3072]{3,2,1,0:T(8,128)(2,1)} fusion(bf16[1,16,16,3072]{3,2,1,0:T(8,128)(2,1)S(1)} %bitcast.15, bf16[1,16,16,3072]{3,2,1,0:T(8,128)(2,1)S(1)} %bitcast.11), kind=kLoop, calls=%fused_computation.9 | loop fusion | flops 884736 | bytes 4915200 | tf_op jit(solution)/shard_map/stack | solution.py:272
  12.9 0.8 broadcast_in_dim_reshape.3.refs_2_.refs_1_
  13.7 19.8 %shard_map.93 = (f32[8,8,3072]{2,1,0:T(8,128)}, f32[192,576]{1,0:T(8,128)}, f32[192,192]{1,0:T(8,128)}, f32[192,1]{1,0:T(8,128)}) custom-call(bf16[16,16,3072]{2,1,0:T(8,128)(2,1)} %refs_0_.1, bf16[16,16,3072]{2,1,0:T(8,128)(2,1)} %refs_1_.1, s32[8,1,512]{2,1,0:T(1,128)} %broadcast_in_dim_reshape.3.refs_2_.refs_1_, f32[1,192]{1,0:T(1,128)} %bitcast.18, ...), custom_call_target="tpu_custom_call" | custom-call | tf_op jit(solution)/shard_map/pallas_call | solution.py:180
  33.5 1.3 copy.13
  34.8 3.3 %maximum_maximum_fusion.refs_0_ = bf16[2,16,16,3072]{3,2,1,0:T(8,128)(2,1)} fusion(bf16[2,4,4,3072]{3,2,1,0:T(4,128)(2,1)S(1)} %collective-permute-done.2, bf16[2,4,12,3072]{3,2,1,0:T(8,128)(2,1)S(1)} %copy.13, bf16[2,12,4,3072]{3,2,1,0:T(4,128)(2,1)} %collective-permute-done, bf16[2,12,12,3072]{3,2,1,0:T(8,128)(2,1)S(1)} %copy-done.4), kind=kLoop, calls=%fused_computation.6 | loop fusion | flops 12582912 | bytes 6291456 | tf_op jit(solution)/shard_map/concatenate | solution.py:254
  38.1 55.0 %shard_map.94 = (f32[16,16,3072]{2,1,0:T(8,128)}, f32[192,576]{1,0:T(8,128)}, f32[192,192]{1,0:T(8,128)}, f32[192,1]{1,0:T(8,128)}) custom-call(bf16[2,16,16,3072]{3,2,1,0:T(8,128)(2,1)} %maximum_maximum_fusion.refs_0_, s32[8,1,512]{2,1,0:T(1,128)} %broadcast_in_dim_reshape.3.refs_2_.refs_1_, f32[1,192]{1,0:T(1,128)} %bitcast.19, bf16[192,576]{1,0:T(8,128)(2,1)} %refs_3_.1, ...), custom_call_target="tpu_custom_call" | custom-call | tf_op jit(solution)/shard_map/pallas_call | solution.py:180
  93.2 1.1 reduce
  94.3 1.3 select_maximum_fusion
  95.6 0.8 copy-done.5
  96.5 0.8 collective-permute-start.6
  97.3 1.5 collective-permute-done.6
  98.8 1.1 fusion.4
  99.9 0.7 constant_dynamic-slice_fusion.3
  100.6 0.8 collective-permute-start.7
  101.4 5.5 %collective-permute-done.7 = f32[64,768]{1,0:T(8,128)} collective-permute-done((f32[64,768]{1,0:T(8,128)}, f32[64,768]{1,0:T(8,128)}, u32[]{:S(2)}, u32[]{:S(2)}) %collective-permute-start.7) | collective-permute-done | bytes 196640 | tf_op jit(solution)/shard_map/ppermute | solution.py:200
  106.9 0.9 dynamic-slice_add_fusion
  107.9 0.7 copy-done.7
  108.6 1.4 collective-permute-start.8
  109.9 2.2 %collective-permute-done.8 = f32[32,768]{1,0:T(8,128)S(1)} collective-permute-done((f32[32,768]{1,0:T(8,128)S(1)}, f32[32,768]{1,0:T(8,128)S(1)}, u32[]{:S(2)}, u32[]{:S(2)}) %collective-permute-start.8) | collective-permute-done | bytes 98336 | tf_op jit(solution)/shard_map/ppermute | solution.py:200
  112.1 0.9 dynamic-slice_add_fusion.1
  113.1 3.8 %collective-permute-done.9 = f32[16,768]{1,0:T(8,128)S(1)} collective-permute-done((f32[16,768]{1,0:T(8,128)S(1)}, f32[16,768]{1,0:T(8,128)S(1)}, u32[]{:S(2)}, u32[]{:S(2)}) %collective-permute-start.9) | collective-permute-done | bytes 49184 | tf_op jit(solution)/shard_map/ppermute | solution.py:200
  117.4 2.6 %collective-permute-done.10 = f32[8,768]{1,0:T(8,128)S(1)} collective-permute-done((f32[8,768]{1,0:T(8,128)S(1)}, f32[8,768]{1,0:T(8,128)S(1)}, u32[]{:S(2)}, u32[]{:S(2)}) %collective-permute-start.10) | collective-permute-done | bytes 24608 | tf_op jit(solution)/shard_map/ppermute | solution.py:200
  120.5 1.1 copy-done.6
  121.6 0.9 slice.56
  122.5 6.4 %collective-permute-start.5 = (bf16[12,4,3072]{2,1,0:T(4,128)(2,1)}, bf16[12,4,3072]{2,1,0:T(4,128)(2,1)}, u32[]{:S(2)}, u32[]{:S(2)}) collective-permute-start(bf16[12,4,3072]{2,1,0:T(4,128)(2,1)} %slice.56), channel_id=1, source_target_pairs={{0,1},{1,2},{2,3},{3,4},{4,5},{5,6},{6,7},{7,0},{8,9},{9,10},{10,1... | collective-permute-start | bytes 884744 | tf_op jit(solution)/shard_map/ppermute | solution.py:245
  128.8 0.6 maximum_select_fusion.4
  129.5 1.0 slice.55
  130.5 1.5 collective-permute-start.4
  132.0 2.3 %collective-permute-done.12 = f32[16,768]{1,0:T(8,128)} collective-permute-done((f32[16,768]{1,0:T(8,128)}, f32[16,768]{1,0:T(8,128)}, u32[]{:S(2)}, u32[]{:S(2)}) %collective-permute-start.12) | collective-permute-done | bytes 49184 | tf_op jit(solution)/shard_map/ppermute | solution.py:200
  134.2 1.5 maximum_select_fusion.3
  135.8 1.3 collective-permute-start.13
  137.1 1.0 slice.54
  138.3 2.5 %collective-permute-start.3 = (bf16[4,4,3072]{2,1,0:T(4,128)(2,1)S(1)}, bf16[4,4,3072]{2,1,0:T(4,128)(2,1)S(1)}, u32[]{:S(2)}, u32[]{:S(2)}) collective-permute-start(bf16[4,4,3072]{2,1,0:T(4,128)(2,1)S(1)} %slice.54), channel_id=1, source_target_pairs={{0,9},{1,10},{2,11},{3,12},{4,13},{5,14},{6,15},{7,8},{8,17},{9,18... | collective-permute-start | bytes 294920 | tf_op jit(solution)/shard_map/ppermute | solution.py:245
  140.8 1.0 convert_element_type.32
  141.9 4.2 %collective-permute-done.13 = f32[32,768]{1,0:T(8,128)} collective-permute-done((f32[32,768]{1,0:T(8,128)}, f32[32,768]{1,0:T(8,128)}, u32[]{:S(2)}, u32[]{:S(2)}) %collective-permute-start.13) | collective-permute-done | bytes 98336 | tf_op jit(solution)/shard_map/ppermute | solution.py:200
  146.1 1.1 maximum_select_fusion.2
  147.1 0.7 collective-permute-start.14
  147.9 1.1 maximum_convert_fusion
  149.0 4.1 %collective-permute-done.14 = f32[64,768]{1,0:T(8,128)S(1)} collective-permute-done((f32[64,768]{1,0:T(8,128)S(1)}, f32[64,768]{1,0:T(8,128)S(1)}, u32[]{:S(2)}, u32[]{:S(2)}) %collective-permute-start.14) | collective-permute-done | bytes 196640 | tf_op jit(solution)/shard_map/ppermute | solution.py:200
  153.1 1.5 collective-permute-start.15
  154.6 1.8 %fusion = bf16[16,16,3072]{2,1,0:T(8,128)(2,1)} fusion(f32[12,12,3072]{2,1,0:T(8,128)S(1)} %slice.44, f32[12,4,3072]{2,1,0:T(4,128)S(1)} %convert_element_type.32, f32[4,16,3072]{2,1,0:T(8,128)S(1)} %maximum_convert_fusion, bf16[16,16,3072]{2,1,0:T(8,128)(2,1)S(1)} %copy-done.1), kind=kLoop, calls=%fused_computation.8 | loop fusion | flops 3932160 | bytes 6291456 | tf_op jit(solution)/shard_map/convert_element_type | solution.py:265
  157.2 1.0 reshape.77
  158.2 0.8 reshape.78
  (48 shorter events, 2.9 us)
Async XLA Ops:
  0.6 6.1 %copy-start.2 = (bf16[16,16,3072]{2,1,0:T(8,128)(2,1)S(1)}, bf16[16,16,3072]{2,1,0:T(8,128)(2,1)}, u32[]{:S(2)}) copy-start(bf16[16,16,3072]{2,1,0:T(8,128)(2,1)} %refs_0_.1) | copy-start | bytes 4718596
  0.6 6.1 %copy-start = (bf16[16,16,3072]{2,1,0:T(8,128)(2,1)S(1)}, bf16[16,16,3072]{2,1,0:T(8,128)(2,1)}, u32[]{:S(2)}) copy-start(bf16[16,16,3072]{2,1,0:T(8,128)(2,1)} %refs_1_.1) | copy-start | bytes 4718596
  3.5 30.0 %collective-permute-start.1 = (bf16[2,4,12,3072]{3,1,2,0:T(4,128)(2,1)}, bf16[2,4,12,3072]{3,1,2,0:T(4,128)(2,1)}, u32[]{:S(2)}, u32[]{:S(2)}) collective-permute-start(bf16[2,4,12,3072]{3,1,2,0:T(4,128)(2,1)} %copy.12), channel_id=1, source_target_pairs={{0,24},{1,25},{2,26},{3,27},{4,28},{5,29},{6,30},{7,31},{8,0},{9,1... | collective-permute-start | bytes 1769480 | tf_op jit(solution)/shard_map/ppermute | solution.py:245
  7.8 26.9 %collective-permute-start = (bf16[2,12,4,3072]{3,2,1,0:T(4,128)(2,1)}, bf16[2,12,4,3072]{3,2,1,0:T(4,128)(2,1)}, u32[]{:S(2)}, u32[]{:S(2)}) collective-permute-start(bf16[2,12,4,3072]{3,2,1,0:T(4,128)(2,1)} %fusion.3), channel_id=1, source_target_pairs={{0,7},{1,0},{2,1},{3,2},{4,3},{5,4},{6,5},{7,6},{8,15},{9,8},{10,9... | collective-permute-start | bytes 1769480 | tf_op jit(solution)/shard_map/ppermute | solution.py:245
  8.1 26.7 %collective-permute-start.2 = (bf16[2,4,4,3072]{3,2,1,0:T(4,128)(2,1)S(1)}, bf16[2,4,4,3072]{3,2,1,0:T(4,128)(2,1)S(1)}, u32[]{:S(2)}, u32[]{:S(2)}) collective-permute-start(bf16[2,4,4,3072]{3,2,1,0:T(4,128)(2,1)S(1)} %pad_maximum_fusion), channel_id=1, source_target_pairs={{0,31},{1,24},{2,25},{3,26},{4,27},{5,28},{6,29},{7,30},{8,7},{9,0... | collective-permute-start | bytes 589832 | tf_op jit(solution)/shard_map/ppermute | solution.py:245
  10.1 2.3 %copy-start.8 = (s32[16,16,16]{2,1,0:T(8,128)S(1)}, s32[16,16,16]{2,1,0:T(8,128)}, u32[]{:S(2)}) copy-start(s32[16,16,16]{2,1,0:T(8,128)} %param.8) | copy-start | bytes 49156
  12.5 22.3 %copy-start.4 = (bf16[2,12,12,3072]{3,2,1,0:T(8,128)(2,1)S(1)}, bf16[2,12,12,3072]{3,2,1,0:T(8,128)(2,1)}, u32[]{:S(2)}) copy-start(bf16[2,12,12,3072]{3,2,1,0:T(8,128)(2,1)} %fusion.1) | copy-start | bytes 5308420
  93.2 27.1 %copy-start.3 = (f32[16,16,3072]{2,1,0:T(8,128)S(1)}, f32[16,16,3072]{2,1,0:T(8,128)}, u32[]{:S(2)}) copy-start(f32[16,16,3072]{2,1,0:T(8,128)} %get-tuple-element.16) | copy-start | bytes 9437188
  95.6 0.8 copy-start.5
  96.5 2.3 %collective-permute-start.6 = (f32[128,768]{1,0:T(8,128)S(1)}, f32[128,768]{1,0:T(8,128)}, u32[]{:S(2)}, u32[]{:S(2)}) collective-permute-start(f32[128,768]{1,0:T(8,128)S(1)} %pad_dynamic-slice_fusion), channel_id=1, source_target_pairs={{0,2},{2,0},{4,6},{6,4},{1,3},{3,1},{5,7},{7,5},{8,10},{10,8},{12,... | collective-permute-start | bytes 1179656 | tf_op jit(solution)/shard_map/ppermute | solution.py:200
  100.6 6.4 %collective-permute-start.7 = (f32[64,768]{1,0:T(8,128)}, f32[64,768]{1,0:T(8,128)}, u32[]{:S(2)}, u32[]{:S(2)}) collective-permute-start(f32[64,768]{1,0:T(8,128)} %constant_dynamic-slice_fusion.3), channel_id=1, source_target_pairs={{0,4},{2,6},{4,0},{6,2},{1,5},{3,7},{5,1},{7,3},{8,12},{10,14},{12... | collective-permute-start | bytes 589832 | tf_op jit(solution)/shard_map/ppermute | solution.py:200
  107.9 0.7 copy-start.7
  108.6 3.5 %collective-permute-start.8 = (f32[32,768]{1,0:T(8,128)S(1)}, f32[32,768]{1,0:T(8,128)S(1)}, u32[]{:S(2)}, u32[]{:S(2)}) collective-permute-start(f32[32,768]{1,0:T(8,128)S(1)} %constant_dynamic-slice_fusion.2), channel_id=1, source_target_pairs={{0,8},{8,0},{16,24},{24,16},{1,9},{9,1},{17,25},{25,17},{2,10},{10... | collective-permute-start | bytes 294920 | tf_op jit(solution)/shard_map/ppermute | solution.py:200
  113.0 3.9 %collective-permute-start.9 = (f32[16,768]{1,0:T(8,128)S(1)}, f32[16,768]{1,0:T(8,128)S(1)}, u32[]{:S(2)}, u32[]{:S(2)}) collective-permute-start(f32[16,768]{1,0:T(8,128)S(1)} %constant_dynamic-slice_fusion.1), channel_id=1, source_target_pairs={{0,16},{8,24},{16,0},{24,8},{1,17},{9,25},{17,1},{25,9},{2,18},{10... | collective-permute-start | bytes 147464 | tf_op jit(solution)/shard_map/ppermute | solution.py:200
  117.0 3.0 %collective-permute-start.10 = (f32[8,768]{1,0:T(8,128)S(1)}, f32[8,768]{1,0:T(8,128)S(1)}, u32[]{:S(2)}, u32[]{:S(2)}) collective-permute-start(f32[8,768]{1,0:T(8,128)S(1)} %constant_dynamic-slice_fusion), channel_id=1, source_target_pairs={{0,1},{1,0},{2,3},{3,2},{4,5},{5,4},{6,7},{7,6},{8,9},{9,8},{10,11... | collective-permute-start | bytes 73736 | tf_op jit(solution)/shard_map/ppermute | solution.py:200
  120.0 8.8 %collective-permute-start.11 = (f32[8,768]{1,0:T(8,128)S(1)}, f32[8,768]{1,0:T(8,128)S(1)}, u32[]{:S(2)}, u32[]{:S(2)}) collective-permute-start(f32[8,768]{1,0:T(8,128)S(1)} %dynamic-slice_add_fusion.3), channel_id=1, source_target_pairs={{0,1},{1,0},{2,3},{3,2},{4,5},{5,4},{6,7},{7,6},{8,9},{9,8},{10,11... | collective-permute-start | bytes 73736 | tf_op jit(solution)/shard_map/ppermute | solution.py:200
  120.5 1.1 copy-start.6
  122.5 18.4 %collective-permute-start.5 = (bf16[12,4,3072]{2,1,0:T(4,128)(2,1)}, bf16[12,4,3072]{2,1,0:T(4,128)(2,1)}, u32[]{:S(2)}, u32[]{:S(2)}) collective-permute-start(bf16[12,4,3072]{2,1,0:T(4,128)(2,1)} %slice.56), channel_id=1, source_target_pairs={{0,1},{1,2},{2,3},{3,4},{4,5},{5,6},{6,7},{7,0},{8,9},{9,10},{10,1... | collective-permute-start | bytes 884744 | tf_op jit(solution)/shard_map/ppermute | solution.py:245
  129.5 4.8 %collective-permute-start.12 = (f32[16,768]{1,0:T(8,128)}, f32[16,768]{1,0:T(8,128)}, u32[]{:S(2)}, u32[]{:S(2)}) collective-permute-start(f32[16,768]{1,0:T(8,128)} %maximum_select_fusion.4), channel_id=1, source_target_pairs={{0,16},{8,24},{16,0},{24,8},{1,17},{9,25},{17,1},{25,9},{2,18},{10... | collective-permute-start | bytes 147464 | tf_op jit(solution)/shard_map/ppermute | solution.py:200
  130.5 17.4 %collective-permute-start.4 = (bf16[4,12,3072]{2,1,0:T(8,128)(2,1)S(1)}, bf16[4,12,3072]{2,1,0:T(8,128)(2,1)}, u32[]{:S(2)}, u32[]{:S(2)}) collective-permute-start(bf16[4,12,3072]{2,1,0:T(8,128)(2,1)S(1)} %slice.55), channel_id=1, source_target_pairs={{0,8},{1,9},{2,10},{3,11},{4,12},{5,13},{6,14},{7,15},{8,16},{9,17... | collective-permute-start | bytes 884744 | tf_op jit(solution)/shard_map/ppermute | solution.py:245
  135.8 10.3 %collective-permute-start.13 = (f32[32,768]{1,0:T(8,128)}, f32[32,768]{1,0:T(8,128)}, u32[]{:S(2)}, u32[]{:S(2)}) collective-permute-start(f32[32,768]{1,0:T(8,128)} %maximum_select_fusion.3), channel_id=1, source_target_pairs={{0,8},{8,0},{16,24},{24,16},{1,9},{9,1},{17,25},{25,17},{2,10},{10... | collective-permute-start | bytes 294920 | tf_op jit(solution)/shard_map/ppermute | solution.py:200
  138.0 16.6 %copy-start.1 = (bf16[16,16,3072]{2,1,0:T(8,128)(2,1)S(1)}, bf16[16,16,3072]{2,1,0:T(8,128)(2,1)}, u32[]{:S(2)}) copy-start(bf16[16,16,3072]{2,1,0:T(8,128)(2,1)} %refs_1_.1) | copy-start | bytes 4718596
  138.3 9.6 %collective-permute-start.3 = (bf16[4,4,3072]{2,1,0:T(4,128)(2,1)S(1)}, bf16[4,4,3072]{2,1,0:T(4,128)(2,1)S(1)}, u32[]{:S(2)}, u32[]{:S(2)}) collective-permute-start(bf16[4,4,3072]{2,1,0:T(4,128)(2,1)S(1)} %slice.54), channel_id=1, source_target_pairs={{0,9},{1,10},{2,11},{3,12},{4,13},{5,14},{6,15},{7,8},{8,17},{9,18... | collective-permute-start | bytes 294920 | tf_op jit(solution)/shard_map/ppermute | solution.py:245
  147.1 5.9 %collective-permute-start.14 = (f32[64,768]{1,0:T(8,128)S(1)}, f32[64,768]{1,0:T(8,128)S(1)}, u32[]{:S(2)}, u32[]{:S(2)}) collective-permute-start(f32[64,768]{1,0:T(8,128)S(1)} %maximum_select_fusion.2), channel_id=1, source_target_pairs={{0,4},{2,6},{4,0},{6,2},{1,5},{3,7},{5,1},{7,3},{8,12},{10,14},{12... | collective-permute-start | bytes 589832 | tf_op jit(solution)/shard_map/ppermute | solution.py:200
  153.1 3.3 %collective-permute-start.15 = (f32[128,768]{1,0:T(8,128)S(1)}, f32[128,768]{1,0:T(8,128)S(1)}, u32[]{:S(2)}, u32[]{:S(2)}) collective-permute-start(f32[128,768]{1,0:T(8,128)S(1)} %maximum_select_fusion.1), channel_id=1, source_target_pairs={{0,2},{2,0},{4,6},{6,4},{1,3},{3,1},{5,7},{7,5},{8,10},{10,8},{12,... | collective-permute-start | bytes 1179656 | tf_op jit(solution)/shard_map/ppermute | solution.py:200

commit v14 on v13

--- a/solution.py
+++ b/solution.py
@@ -224,9 +224,10 @@
     for axis, distance in reversed(steps):
         bit = (lax.axis_index(axis) // distance) % 2
         other = swapped(values, axis, distance)
-        values = jnp.where(
-            bit == 0, jnp.concatenate([values, other]), jnp.concatenate([other, values])
-        )
+        half = values.shape[0]
+        joined = jnp.zeros((2 * half,) + values.shape[1:], values.dtype)
+        joined = lax.dynamic_update_slice_in_dim(joined, values, bit * half, 0)
+        values = lax.dynamic_update_slice_in_dim(joined, other, (1 - bit) * half, 0)
     return values[: matrix.shape[0]]
 
 

time: 159 us -> 156 us (0.981)
  other arithmetic: 21.2 us -> 15.9 us
  waiting for transfers between devices: 26.2 us -> 30.4 us
  local copies, waits for them, and re-layouts: 12.6 us -> 9.13 us
    ppermute x10, waiting for transfers between devices: 26.2 us -> 30.4 us  [swapped(): lax.ppermute(block, axis, [(i, i ^ distance) for i in range(lax.axis_size...]
    select_n x5 -> x0, other arithmetic: 3.3 us -> none  [summed_everywhere(): jnp.where(bit == 0, jnp.concatenate([values, other]), jnp.concatenate([ot...]
    ppermute x10, starting transfers between devices: 7.26 us -> 9.78 us  [swapped(): lax.ppermute(block, axis, [(i, i ^ distance) for i in range(lax.axis_size...]
    ppermute x6, starting transfers between devices: 16 us -> 13.9 us  [moved(): lax.ppermute(block, ('gx', 'gy', 'gz'), halo_route(distance_a, distance_b))]
  transfers between devices with their start and end apart: 16 -> 16, of which waited for: 8 -> 8; matrix products, arithmetic and copies ran while one was open for 10% -> 6% of each run, Pallas kernels for 12% -> 13%
where the time goes in v14:
time: 156 us; the launch traced here: 155 us
  Pallas kernels  74.8 us (48%)
  waiting for transfers between devices  30.4 us (19%)
  starting transfers between devices  23.6 us (15%)
  other arithmetic  15.9 us (10%)
  local copies, waits for them, and re-layouts  9.13 us (6%)
    pallas_call x2, Pallas kernels, window_grads(): pl.pallas_call(make_window_kernel(first), out_shape=[jax.ShapeDtypeStruct...  74.8 us
    ppermute x10, waiting for transfers between devices, swapped(): lax.ppermute(block, axis, [(i, i ^ distance) for i in range(lax.axis_size...  30.4 us
    ppermute x6, starting transfers between devices, moved(): lax.ppermute(block, ('gx', 'gy', 'gz'), halo_route(distance_a, distance_b))  13.9 us
    ppermute x10, starting transfers between devices, swapped(): lax.ppermute(block, axis, [(i, i ^ distance) for i in range(lax.axis_size...  9.78 us
    another operation x4, other arithmetic, per_device(): both = shifted_block(jnp.stack([tokens, grads_out]))  4.85 us
    concatenate x1, other arithmetic, shifted_block(): return jnp.concatenate([upper, lower], axis=1)  3.35 us
  transfers between devices with their start and end apart: 16, of which 8 were waited for; matrix products, arithmetic and copies ran while one was open for 6% of the time, Pallas kernels for 13%

profile of v14, /device:TPU:5, one launch (start us, length us, event | category | flops | bytes accessed | tf_op | source)
XLA Modules:
  0.0 154.9 jit_solution(848032766450730994)
XLA Ops:
  0.7 1.5 fusion.2
  2.2 1.3 copy.12
  3.5 3.3 %collective-permute-start.1 = (bf16[2,4,12,3072]{3,1,2,0:T(4,128)(2,1)}, bf16[2,4,12,3072]{3,1,2,0:T(4,128)(2,1)}, u32[]{:S(2)}, u32[]{:S(2)}) collective-permute-start(bf16[2,4,12,3072]{3,1,2,0:T(4,128)(2,1)} %copy.12), channel_id=1, source_target_pairs={{0,24},{1,25},{2,26},{3,27},{4,28},{5,29},{6,30},{7,31},{8,0},{9,1... | collective-permute-start | bytes 1769480 | tf_op jit(solution)/shard_map/ppermute | solution.py:246
  6.8 1.0 fusion.3
  7.8 0.2 collective-permute-start
  8.1 2.0 %collective-permute-start.2 = (bf16[2,4,4,3072]{3,2,1,0:T(4,128)(2,1)S(1)}, bf16[2,4,4,3072]{3,2,1,0:T(4,128)(2,1)S(1)}, u32[]{:S(2)}, u32[]{:S(2)}) collective-permute-start(bf16[2,4,4,3072]{3,2,1,0:T(4,128)(2,1)S(1)} %pad_maximum_fusion), channel_id=1, source_target_pairs={{0,31},{1,24},{2,25},{3,26},{4,27},{5,28},{6,29},{7,30},{8,7},{9,0... | collective-permute-start | bytes 589832 | tf_op jit(solution)/shard_map/ppermute | solution.py:246
  10.2 2.2 %fusion.1 = bf16[2,12,12,3072]{3,2,1,0:T(8,128)(2,1)} fusion(bf16[1,16,16,3072]{3,2,1,0:T(8,128)(2,1)S(1)} %bitcast.15, bf16[1,16,16,3072]{3,2,1,0:T(8,128)(2,1)S(1)} %bitcast.11), kind=kLoop, calls=%fused_computation.9 | loop fusion | flops 884736 | bytes 4915200 | tf_op jit(solution)/shard_map/stack | solution.py:273
  12.6 0.2 reshape.74
  12.8 0.2 copy.14
  12.9 0.8 broadcast_in_dim_reshape.3.refs_2_.refs_1_
  13.7 19.8 %shard_map.93 = (f32[8,8,3072]{2,1,0:T(8,128)}, f32[192,576]{1,0:T(8,128)}, f32[192,192]{1,0:T(8,128)}, f32[192,1]{1,0:T(8,128)}) custom-call(bf16[16,16,3072]{2,1,0:T(8,128)(2,1)} %refs_0_.1, bf16[16,16,3072]{2,1,0:T(8,128)(2,1)} %refs_1_.1, s32[8,1,512]{2,1,0:T(1,128)} %broadcast_in_dim_reshape.3.refs_2_.refs_1_, f32[1,192]{1,0:T(1,128)} %bitcast.18, ...), custom_call_target="tpu_custom_call" | custom-call | tf_op jit(solution)/shard_map/pallas_call | solution.py:180
  33.5 1.3 copy.13
  34.8 3.3 %maximum_maximum_fusion.refs_0_ = bf16[2,16,16,3072]{3,2,1,0:T(8,128)(2,1)} fusion(bf16[2,4,4,3072]{3,2,1,0:T(4,128)(2,1)S(1)} %collective-permute-done.2, bf16[2,4,12,3072]{3,2,1,0:T(8,128)(2,1)S(1)} %copy.13, bf16[2,12,4,3072]{3,2,1,0:T(4,128)(2,1)} %collective-permute-done, bf16[2,12,12,3072]{3,2,1,0:T(8,128)(2,1)S(1)} %copy-done.4), kind=kLoop, calls=%fused_computation.6 | loop fusion | flops 12582912 | bytes 6291456 | tf_op jit(solution)/shard_map/concatenate | solution.py:255
  38.1 55.0 %shard_map.94 = (f32[16,16,3072]{2,1,0:T(8,128)}, f32[192,576]{1,0:T(8,128)}, f32[192,192]{1,0:T(8,128)}, f32[192,1]{1,0:T(8,128)}) custom-call(bf16[2,16,16,3072]{3,2,1,0:T(8,128)(2,1)} %maximum_maximum_fusion.refs_0_, s32[8,1,512]{2,1,0:T(1,128)} %broadcast_in_dim_reshape.3.refs_2_.refs_1_, f32[1,192]{1,0:T(1,128)} %bitcast.19, bf16[192,576]{1,0:T(8,128)(2,1)} %refs_3_.1, ...), custom_call_target="tpu_custom_call" | custom-call | tf_op jit(solution)/shard_map/pallas_call | solution.py:180
  93.2 1.1 reduce
  94.3 1.3 select_maximum_fusion
  95.6 0.8 copy-done.5
  96.5 0.8 collective-permute-start.6
  97.3 1.5 collective-permute-done.6
  98.8 1.1 fusion.4
  99.9 0.7 constant_dynamic-slice_fusion.3
  100.6 0.8 collective-permute-start.7
  101.4 5.5 %collective-permute-done.7 = f32[64,768]{1,0:T(8,128)} collective-permute-done((f32[64,768]{1,0:T(8,128)}, f32[64,768]{1,0:T(8,128)}, u32[]{:S(2)}, u32[]{:S(2)}) %collective-permute-start.7) | collective-permute-done | bytes 196640 | tf_op jit(solution)/shard_map/ppermute | solution.py:200
  106.9 0.9 dynamic-slice_add_fusion
  107.9 0.7 copy-done.6
  108.6 1.4 collective-permute-start.8
  109.9 2.2 %collective-permute-done.8 = f32[32,768]{1,0:T(8,128)S(1)} collective-permute-done((f32[32,768]{1,0:T(8,128)S(1)}, f32[32,768]{1,0:T(8,128)S(1)}, u32[]{:S(2)}, u32[]{:S(2)}) %collective-permute-start.8) | collective-permute-done | bytes 98336 | tf_op jit(solution)/shard_map/ppermute | solution.py:200
  112.1 0.9 dynamic-slice_add_fusion.1
  113.1 3.8 %collective-permute-done.9 = f32[16,768]{1,0:T(8,128)S(1)} collective-permute-done((f32[16,768]{1,0:T(8,128)S(1)}, f32[16,768]{1,0:T(8,128)S(1)}, u32[]{:S(2)}, u32[]{:S(2)}) %collective-permute-start.9) | collective-permute-done | bytes 49184 | tf_op jit(solution)/shard_map/ppermute | solution.py:200
  117.0 0.4 collective-permute-start.10
  117.4 2.6 %collective-permute-done.10 = f32[8,768]{1,0:T(8,128)S(1)} collective-permute-done((f32[8,768]{1,0:T(8,128)S(1)}, f32[8,768]{1,0:T(8,128)S(1)}, u32[]{:S(2)}, u32[]{:S(2)}) %collective-permute-start.10) | collective-permute-done | bytes 24608 | tf_op jit(solution)/shard_map/ppermute | solution.py:200
  120.0 0.3 collective-permute-start.11
  120.3 0.2 convert_element_type.31
  120.6 0.2 slice.56
  120.8 0.2 slice.44
  121.0 1.3 collective-permute-start.4
  122.4 6.2 %collective-permute-start.3 = (bf16[4,4,3072]{2,1,0:T(4,128)(2,1)S(1)}, bf16[4,4,3072]{2,1,0:T(4,128)(2,1)S(1)}, u32[]{:S(2)}, u32[]{:S(2)}) collective-permute-start(bf16[4,4,3072]{2,1,0:T(4,128)(2,1)S(1)} %slice.54), channel_id=1, source_target_pairs={{0,9},{1,10},{2,11},{3,12},{4,13},{5,14},{6,15},{7,8},{8,17},{9,18... | collective-permute-start | bytes 294920 | tf_op jit(solution)/shard_map/ppermute | solution.py:246
  128.6 0.8 collective-permute-start.5
  129.3 2.5 %collective-permute-start.12 = (f32[16,768]{1,0:T(8,128)S(1)}, f32[16,768]{1,0:T(8,128)S(1)}, u32[]{:S(2)}, u32[]{:S(2)}) collective-permute-start(f32[16,768]{1,0:T(8,128)S(1)} %constant_dynamic-update-slice_fusion.8), channel_id=1, source_target_pairs={{0,16},{8,24},{16,0},{24,8},{1,17},{9,25},{17,1},{25,9},{2,18},{10... | collective-permute-start | bytes 147464 | tf_op jit(solution)/shard_map/ppermute | solution.py:200
  131.8 7.2 %collective-permute-done.12 = f32[16,768]{1,0:T(8,128)S(1)} collective-permute-done((f32[16,768]{1,0:T(8,128)S(1)}, f32[16,768]{1,0:T(8,128)S(1)}, u32[]{:S(2)}, u32[]{:S(2)}) %collective-permute-start.12) | collective-permute-done | bytes 49184 | tf_op jit(solution)/shard_map/ppermute | solution.py:200
  139.1 3.9 %collective-permute-done.13 = f32[32,768]{1,0:T(8,128)S(1)} collective-permute-done((f32[32,768]{1,0:T(8,128)S(1)}, f32[32,768]{1,0:T(8,128)S(1)}, u32[]{:S(2)}, u32[]{:S(2)}) %collective-permute-start.13) | collective-permute-done | bytes 98336 | tf_op jit(solution)/shard_map/ppermute | solution.py:200
  143.0 1.3 collective-permute-start.14
  144.6 3.6 %collective-permute-done.14 = f32[64,768]{1,0:T(8,128)S(1)} collective-permute-done((f32[64,768]{1,0:T(8,128)S(1)}, f32[64,768]{1,0:T(8,128)S(1)}, u32[]{:S(2)}, u32[]{:S(2)}) %collective-permute-start.14) | collective-permute-done | bytes 196640 | tf_op jit(solution)/shard_map/ppermute | solution.py:200
  148.3 2.2 %collective-permute-start.15 = (f32[128,768]{1,0:T(8,128)S(1)}, f32[128,768]{1,0:T(8,128)S(1)}, u32[]{:S(2)}, u32[]{:S(2)}) collective-permute-start(f32[128,768]{1,0:T(8,128)S(1)} %constant_dynamic-update-slice_fusion.2), channel_id=1, source_target_pairs={{0,2},{2,0},{4,6},{6,4},{1,3},{3,1},{5,7},{7,5},{8,10},{10,8},{12,... | collective-permute-start | bytes 1179656 | tf_op jit(solution)/shard_map/ppermute | solution.py:200
  150.5 1.8 %fusion = bf16[16,16,3072]{2,1,0:T(8,128)(2,1)} fusion(f32[12,12,3072]{2,1,0:T(8,128)S(1)} %slice.44, f32[12,4,3072]{2,1,0:T(4,128)S(1)} %convert_element_type.32, f32[4,16,3072]{2,1,0:T(8,128)S(1)} %maximum_convert_fusion, bf16[16,16,3072]{2,1,0:T(8,128)(2,1)S(1)} %copy-done.1), kind=kLoop, calls=%fused_computation.8 | loop fusion | flops 3932160 | bytes 6291456 | tf_op jit(solution)/shard_map/convert_element_type | solution.py:266
  152.6 0.6 slice.57
  153.2 1.0 reshape.77
  154.1 0.8 reshape.78
  (55 shorter events, 1.1 us)
Async XLA Ops:
  0.6 6.1 %copy-start.2 = (bf16[16,16,3072]{2,1,0:T(8,128)(2,1)S(1)}, bf16[16,16,3072]{2,1,0:T(8,128)(2,1)}, u32[]{:S(2)}) copy-start(bf16[16,16,3072]{2,1,0:T(8,128)(2,1)} %refs_0_.1) | copy-start | bytes 4718596
  0.6 6.1 %copy-start = (bf16[16,16,3072]{2,1,0:T(8,128)(2,1)S(1)}, bf16[16,16,3072]{2,1,0:T(8,128)(2,1)}, u32[]{:S(2)}) copy-start(bf16[16,16,3072]{2,1,0:T(8,128)(2,1)} %refs_1_.1) | copy-start | bytes 4718596
  3.5 30.0 %collective-permute-start.1 = (bf16[2,4,12,3072]{3,1,2,0:T(4,128)(2,1)}, bf16[2,4,12,3072]{3,1,2,0:T(4,128)(2,1)}, u32[]{:S(2)}, u32[]{:S(2)}) collective-permute-start(bf16[2,4,12,3072]{3,1,2,0:T(4,128)(2,1)} %copy.12), channel_id=1, source_target_pairs={{0,24},{1,25},{2,26},{3,27},{4,28},{5,29},{6,30},{7,31},{8,0},{9,1... | collective-permute-start | bytes 1769480 | tf_op jit(solution)/shard_map/ppermute | solution.py:246
  7.8 26.9 %collective-permute-start = (bf16[2,12,4,3072]{3,2,1,0:T(4,128)(2,1)}, bf16[2,12,4,3072]{3,2,1,0:T(4,128)(2,1)}, u32[]{:S(2)}, u32[]{:S(2)}) collective-permute-start(bf16[2,12,4,3072]{3,2,1,0:T(4,128)(2,1)} %fusion.3), channel_id=1, source_target_pairs={{0,7},{1,0},{2,1},{3,2},{4,3},{5,4},{6,5},{7,6},{8,15},{9,8},{10,9... | collective-permute-start | bytes 1769480 | tf_op jit(solution)/shard_map/ppermute | solution.py:246
  8.1 26.7 %collective-permute-start.2 = (bf16[2,4,4,3072]{3,2,1,0:T(4,128)(2,1)S(1)}, bf16[2,4,4,3072]{3,2,1,0:T(4,128)(2,1)S(1)}, u32[]{:S(2)}, u32[]{:S(2)}) collective-permute-start(bf16[2,4,4,3072]{3,2,1,0:T(4,128)(2,1)S(1)} %pad_maximum_fusion), channel_id=1, source_target_pairs={{0,31},{1,24},{2,25},{3,26},{4,27},{5,28},{6,29},{7,30},{8,7},{9,0... | collective-permute-start | bytes 589832 | tf_op jit(solution)/shard_map/ppermute | solution.py:246
  10.1 2.3 %copy-start.7 = (s32[16,16,16]{2,1,0:T(8,128)S(1)}, s32[16,16,16]{2,1,0:T(8,128)}, u32[]{:S(2)}) copy-start(s32[16,16,16]{2,1,0:T(8,128)} %param.8) | copy-start | bytes 49156
  12.5 22.3 %copy-start.4 = (bf16[2,12,12,3072]{3,2,1,0:T(8,128)(2,1)S(1)}, bf16[2,12,12,3072]{3,2,1,0:T(8,128)(2,1)}, u32[]{:S(2)}) copy-start(bf16[2,12,12,3072]{3,2,1,0:T(8,128)(2,1)} %fusion.1) | copy-start | bytes 5308420
  93.2 27.2 %copy-start.3 = (f32[16,16,3072]{2,1,0:T(8,128)S(1)}, f32[16,16,3072]{2,1,0:T(8,128)}, u32[]{:S(2)}) copy-start(f32[16,16,3072]{2,1,0:T(8,128)} %get-tuple-element.16) | copy-start | bytes 9437188
  95.6 0.8 copy-start.5
  96.5 2.3 %collective-permute-start.6 = (f32[128,768]{1,0:T(8,128)S(1)}, f32[128,768]{1,0:T(8,128)}, u32[]{:S(2)}, u32[]{:S(2)}) collective-permute-start(f32[128,768]{1,0:T(8,128)S(1)} %pad_dynamic-slice_fusion), channel_id=1, source_target_pairs={{0,2},{2,0},{4,6},{6,4},{1,3},{3,1},{5,7},{7,5},{8,10},{10,8},{12,... | collective-permute-start | bytes 1179656 | tf_op jit(solution)/shard_map/ppermute | solution.py:200
  100.6 6.4 %collective-permute-start.7 = (f32[64,768]{1,0:T(8,128)}, f32[64,768]{1,0:T(8,128)}, u32[]{:S(2)}, u32[]{:S(2)}) collective-permute-start(f32[64,768]{1,0:T(8,128)} %constant_dynamic-slice_fusion.3), channel_id=1, source_target_pairs={{0,4},{2,6},{4,0},{6,2},{1,5},{3,7},{5,1},{7,3},{8,12},{10,14},{12... | collective-permute-start | bytes 589832 | tf_op jit(solution)/shard_map/ppermute | solution.py:200
  107.9 0.7 copy-start.6
  108.6 3.5 %collective-permute-start.8 = (f32[32,768]{1,0:T(8,128)S(1)}, f32[32,768]{1,0:T(8,128)S(1)}, u32[]{:S(2)}, u32[]{:S(2)}) collective-permute-start(f32[32,768]{1,0:T(8,128)S(1)} %constant_dynamic-slice_fusion.2), channel_id=1, source_target_pairs={{0,8},{8,0},{16,24},{24,16},{1,9},{9,1},{17,25},{25,17},{2,10},{10... | collective-permute-start | bytes 294920 | tf_op jit(solution)/shard_map/ppermute | solution.py:200
  113.0 3.9 %collective-permute-start.9 = (f32[16,768]{1,0:T(8,128)S(1)}, f32[16,768]{1,0:T(8,128)S(1)}, u32[]{:S(2)}, u32[]{:S(2)}) collective-permute-start(f32[16,768]{1,0:T(8,128)S(1)} %constant_dynamic-slice_fusion.1), channel_id=1, source_target_pairs={{0,16},{8,24},{16,0},{24,8},{1,17},{9,25},{17,1},{25,9},{2,18},{10... | collective-permute-start | bytes 147464 | tf_op jit(solution)/shard_map/ppermute | solution.py:200
  117.0 3.0 %collective-permute-start.10 = (f32[8,768]{1,0:T(8,128)S(1)}, f32[8,768]{1,0:T(8,128)S(1)}, u32[]{:S(2)}, u32[]{:S(2)}) collective-permute-start(f32[8,768]{1,0:T(8,128)S(1)} %constant_dynamic-slice_fusion), channel_id=1, source_target_pairs={{0,1},{1,0},{2,3},{3,2},{4,5},{5,4},{6,7},{7,6},{8,9},{9,8},{10,11... | collective-permute-start | bytes 73736 | tf_op jit(solution)/shard_map/ppermute | solution.py:200
  120.0 9.3 %collective-permute-start.11 = (f32[8,768]{1,0:T(8,128)S(1)}, f32[8,768]{1,0:T(8,128)S(1)}, u32[]{:S(2)}, u32[]{:S(2)}) collective-permute-start(f32[8,768]{1,0:T(8,128)S(1)} %get-tuple-element.21), channel_id=1, source_target_pairs={{0,1},{1,0},{2,3},{3,2},{4,5},{5,4},{6,7},{7,6},{8,9},{9,8},{10,11... | collective-permute-start | bytes 73736 | tf_op jit(solution)/shard_map/ppermute | solution.py:200
  121.0 29.5 %copy-start.1 = (bf16[16,16,3072]{2,1,0:T(8,128)(2,1)S(1)}, bf16[16,16,3072]{2,1,0:T(8,128)(2,1)}, u32[]{:S(2)}) copy-start(bf16[16,16,3072]{2,1,0:T(8,128)(2,1)} %refs_1_.1) | copy-start | bytes 4718596
  121.0 23.3 %collective-permute-start.4 = (bf16[4,12,3072]{2,1,0:T(8,128)(2,1)S(1)}, bf16[4,12,3072]{2,1,0:T(8,128)(2,1)S(1)}, u32[]{:S(2)}, u32[]{:S(2)}) collective-permute-start(bf16[4,12,3072]{2,1,0:T(8,128)(2,1)S(1)} %slice.55), channel_id=1, source_target_pairs={{0,8},{1,9},{2,10},{3,11},{4,12},{5,13},{6,14},{7,15},{8,16},{9,17... | collective-permute-start | bytes 884744 | tf_op jit(solution)/shard_map/ppermute | solution.py:246
  122.4 22.0 %collective-permute-start.3 = (bf16[4,4,3072]{2,1,0:T(4,128)(2,1)S(1)}, bf16[4,4,3072]{2,1,0:T(4,128)(2,1)S(1)}, u32[]{:S(2)}, u32[]{:S(2)}) collective-permute-start(bf16[4,4,3072]{2,1,0:T(4,128)(2,1)S(1)} %slice.54), channel_id=1, source_target_pairs={{0,9},{1,10},{2,11},{3,12},{4,13},{5,14},{6,15},{7,8},{8,17},{9,18... | collective-permute-start | bytes 294920 | tf_op jit(solution)/shard_map/ppermute | solution.py:246
  128.6 16.0 %collective-permute-start.5 = (bf16[12,4,3072]{2,1,0:T(4,128)(2,1)S(1)}, bf16[12,4,3072]{2,1,0:T(4,128)(2,1)S(1)}, u32[]{:S(2)}, u32[]{:S(2)}) collective-permute-start(bf16[12,4,3072]{2,1,0:T(4,128)(2,1)S(1)} %slice.56), channel_id=1, source_target_pairs={{0,1},{1,2},{2,3},{3,4},{4,5},{5,6},{6,7},{7,0},{8,9},{9,10},{10,1... | collective-permute-start | bytes 884744 | tf_op jit(solution)/shard_map/ppermute | solution.py:246
  129.3 9.7 %collective-permute-start.12 = (f32[16,768]{1,0:T(8,128)S(1)}, f32[16,768]{1,0:T(8,128)S(1)}, u32[]{:S(2)}, u32[]{:S(2)}) collective-permute-start(f32[16,768]{1,0:T(8,128)S(1)} %constant_dynamic-update-slice_fusion.8), channel_id=1, source_target_pairs={{0,16},{8,24},{16,0},{24,8},{1,17},{9,25},{17,1},{25,9},{2,18},{10... | collective-permute-start | bytes 147464 | tf_op jit(solution)/shard_map/ppermute | solution.py:200
  139.0 4.0 %collective-permute-start.13 = (f32[32,768]{1,0:T(8,128)S(1)}, f32[32,768]{1,0:T(8,128)S(1)}, u32[]{:S(2)}, u32[]{:S(2)}) collective-permute-start(f32[32,768]{1,0:T(8,128)S(1)} %constant_dynamic-update-slice_fusion.6), channel_id=1, source_target_pairs={{0,8},{8,0},{16,24},{24,16},{1,9},{9,1},{17,25},{25,17},{2,10},{10... | collective-permute-start | bytes 294920 | tf_op jit(solution)/shard_map/ppermute | solution.py:200
  143.0 5.2 %collective-permute-start.14 = (f32[64,768]{1,0:T(8,128)S(1)}, f32[64,768]{1,0:T(8,128)S(1)}, u32[]{:S(2)}, u32[]{:S(2)}) collective-permute-start(f32[64,768]{1,0:T(8,128)S(1)} %constant_dynamic-update-slice_fusion.4), channel_id=1, source_target_pairs={{0,4},{2,6},{4,0},{6,2},{1,5},{3,7},{5,1},{7,3},{8,12},{10,14},{12... | collective-permute-start | bytes 589832 | tf_op jit(solution)/shard_map/ppermute | solution.py:200
  148.3 4.1 %collective-permute-start.15 = (f32[128,768]{1,0:T(8,128)S(1)}, f32[128,768]{1,0:T(8,128)S(1)}, u32[]{:S(2)}, u32[]{:S(2)}) collective-permute-start(f32[128,768]{1,0:T(8,128)S(1)} %constant_dynamic-update-slice_fusion.2), channel_id=1, source_target_pairs={{0,2},{2,0},{4,6},{6,4},{1,3},{3,1},{5,7},{7,5},{8,10},{10,8},{12,... | collective-permute-start | bytes 1179656 | tf_op jit(solution)/shard_map/ppermute | solution.py:200

commit v15 on v14

--- a/solution.py
+++ b/solution.py
@@ -44,11 +44,11 @@
     def window_kernel(*refs):
         if first:
             (tok_ref, grd_ref, krow_ref, gain_ref, wqkv_ref, wp_ref,
-             gs_ref, gqkvT_ref, gproj_ref, ggain_ref, qkv_s, ga_s, drow_s) = refs
+             gs_ref, gqkvT_ref, gproj_ref, ggain_ref, qkv_s, ga_s, drow_s, bias_s) = refs
         else:
             (both_ref, krow_ref, gain_ref, wqkv_ref, wp_ref,
              gs0_ref, gqkvT0_ref, gproj0_ref, ggain0_ref,
-             gs_ref, gqkvT_ref, gproj_ref, ggain_ref, qkv_s, ga_s, drow_s) = refs
+             gs_ref, gqkvT_ref, gproj_ref, ggain_ref, qkv_s, ga_s, drow_s, bias_s) = refs
         f32 = jnp.float32
         bf16 = jnp.bfloat16
         if first:
@@ -116,7 +116,7 @@
             ga_s[...] = ga_t.astype(bf16).astype(f32)
             key_row = krow_ref[w].astype(f32)
             key_col = jnp.broadcast_to(key_row, (8, CELLS)).T[:, 0:1]
-            allowed = key_col == key_row
+            bias_s[...] = jnp.where(key_col == key_row, 0.0, -jnp.inf)
 
             def head_step(h, carry):
                 qo = pl.multiple_of(h * HEAD, HEAD)
@@ -126,7 +126,7 @@
                 ga_th = ga_s[pl.ds(qo, HEAD), :]
                 q = q_t.T.astype(bf16)
                 scores = jnp.dot(q, k_t.astype(bf16), preferred_element_type=f32)
-                weights = jnp.where(allowed, jnp.exp2(scores * EXP2_SCALE), 0.0)
+                weights = jnp.exp2(scores * EXP2_SCALE + bias_s[...])
                 probs = weights / jnp.sum(weights, axis=1, keepdims=True)
                 probs_bf = probs.astype(bf16)
                 att_t = lax.dot_general(v_t.astype(bf16), probs_bf, nt, preferred_element_type=f32)
@@ -189,6 +189,7 @@
             pltpu.VMEM((3 * C, CELLS), jnp.float32),
             pltpu.VMEM((C, CELLS), jnp.float32),
             pltpu.VMEM((3 * C, CELLS), jnp.float32),
+            pltpu.VMEM((CELLS, CELLS), jnp.float32),
         ],
     )(*arrays, krow, gain_row, wqkv, wp, *partial)
 

time: 156 us -> 156 us (level)
  no operation moved by 1% of the time
where the time goes in v15:
time: 156 us; the launch traced here: 154 us
  Pallas kernels  74.2 us (48%)
  waiting for transfers between devices  30.4 us (19%)
  starting transfers between devices  23.6 us (15%)
  other arithmetic  15.9 us (10%)
  local copies, waits for them, and re-layouts  9.13 us (6%)
    pallas_call x2, Pallas kernels, window_grads(): pl.pallas_call(make_window_kernel(first), out_shape=[jax.ShapeDtypeStruct...  74.2 us
    ppermute x10, waiting for transfers between devices, swapped(): lax.ppermute(block, axis, [(i, i ^ distance) for i in range(lax.axis_size...  30.4 us
    ppermute x6, starting transfers between devices, moved(): lax.ppermute(block, ('gx', 'gy', 'gz'), halo_route(distance_a, distance_b))  13.9 us
    ppermute x10, starting transfers between devices, swapped(): lax.ppermute(block, axis, [(i, i ^ distance) for i in range(lax.axis_size...  9.77 us
    another operation x4, other arithmetic, per_device(): both = shifted_block(jnp.stack([tokens, grads_out]))  4.85 us
    concatenate x1, other arithmetic, shifted_block(): return jnp.concatenate([upper, lower], axis=1)  3.35 us
  transfers between devices with their start and end apart: 16, of which 8 were waited for; matrix products, arithmetic and copies ran while one was open for 6% of the time, Pallas kernels for 13%

profile of v15, /device:TPU:5, one launch (start us, length us, event | category | flops | bytes accessed | tf_op | source)
XLA Modules:
  0.0 154.3 jit_solution(3637050202865550733)
XLA Ops:
  0.7 1.5 fusion.2
  2.2 1.3 copy.12
  3.5 3.3 %collective-permute-start.1 = (bf16[2,4,12,3072]{3,1,2,0:T(4,128)(2,1)}, bf16[2,4,12,3072]{3,1,2,0:T(4,128)(2,1)}, u32[]{:S(2)}, u32[]{:S(2)}) collective-permute-start(bf16[2,4,12,3072]{3,1,2,0:T(4,128)(2,1)} %copy.12), channel_id=1, source_target_pairs={{0,24},{1,25},{2,26},{3,27},{4,28},{5,29},{6,30},{7,31},{8,0},{9,1... | collective-permute-start | bytes 1769480 | tf_op jit(solution)/shard_map/ppermute | solution.py:247
  6.8 1.0 fusion.3
  7.8 0.2 collective-permute-start
  8.1 2.0 %collective-permute-start.2 = (bf16[2,4,4,3072]{3,2,1,0:T(4,128)(2,1)S(1)}, bf16[2,4,4,3072]{3,2,1,0:T(4,128)(2,1)S(1)}, u32[]{:S(2)}, u32[]{:S(2)}) collective-permute-start(bf16[2,4,4,3072]{3,2,1,0:T(4,128)(2,1)S(1)} %pad_maximum_fusion), channel_id=1, source_target_pairs={{0,31},{1,24},{2,25},{3,26},{4,27},{5,28},{6,29},{7,30},{8,7},{9,0... | collective-permute-start | bytes 589832 | tf_op jit(solution)/shard_map/ppermute | solution.py:247
  10.2 2.2 %fusion.1 = bf16[2,12,12,3072]{3,2,1,0:T(8,128)(2,1)} fusion(bf16[1,16,16,3072]{3,2,1,0:T(8,128)(2,1)S(1)} %bitcast.15, bf16[1,16,16,3072]{3,2,1,0:T(8,128)(2,1)S(1)} %bitcast.11), kind=kLoop, calls=%fused_computation.9 | loop fusion | flops 884736 | bytes 4915200 | tf_op jit(solution)/shard_map/stack | solution.py:274
  12.6 0.2 reshape.74
  12.8 0.2 copy.14
  12.9 0.8 broadcast_in_dim_reshape.3.refs_2_.refs_1_
  13.7 19.6 %shard_map.93 = (f32[8,8,3072]{2,1,0:T(8,128)}, f32[192,576]{1,0:T(8,128)}, f32[192,192]{1,0:T(8,128)}, f32[192,1]{1,0:T(8,128)}) custom-call(bf16[16,16,3072]{2,1,0:T(8,128)(2,1)} %refs_0_.1, bf16[16,16,3072]{2,1,0:T(8,128)(2,1)} %refs_1_.1, s32[8,1,512]{2,1,0:T(1,128)} %broadcast_in_dim_reshape.3.refs_2_.refs_1_, f32[1,192]{1,0:T(1,128)} %bitcast.18, ...), custom_call_target="tpu_custom_call" | custom-call | tf_op jit(solution)/shard_map/pallas_call | solution.py:180
  33.3 1.3 copy.13
  34.6 3.3 %maximum_maximum_fusion.refs_0_ = bf16[2,16,16,3072]{3,2,1,0:T(8,128)(2,1)} fusion(bf16[2,4,4,3072]{3,2,1,0:T(4,128)(2,1)S(1)} %collective-permute-done.2, bf16[2,4,12,3072]{3,2,1,0:T(8,128)(2,1)S(1)} %copy.13, bf16[2,12,4,3072]{3,2,1,0:T(4,128)(2,1)} %collective-permute-done, bf16[2,12,12,3072]{3,2,1,0:T(8,128)(2,1)S(1)} %copy-done.4), kind=kLoop, calls=%fused_computation.6 | loop fusion | flops 12582912 | bytes 6291456 | tf_op jit(solution)/shard_map/concatenate | solution.py:256
  38.0 54.5 %shard_map.94 = (f32[16,16,3072]{2,1,0:T(8,128)}, f32[192,576]{1,0:T(8,128)}, f32[192,192]{1,0:T(8,128)}, f32[192,1]{1,0:T(8,128)}) custom-call(bf16[2,16,16,3072]{3,2,1,0:T(8,128)(2,1)} %maximum_maximum_fusion.refs_0_, s32[8,1,512]{2,1,0:T(1,128)} %broadcast_in_dim_reshape.3.refs_2_.refs_1_, f32[1,192]{1,0:T(1,128)} %bitcast.19, bf16[192,576]{1,0:T(8,128)(2,1)} %refs_3_.1, ...), custom_call_target="tpu_custom_call" | custom-call | tf_op jit(solution)/shard_map/pallas_call | solution.py:180
  92.5 1.1 reduce
  93.7 1.3 select_maximum_fusion
  94.9 0.8 copy-done.5
  95.8 0.8 collective-permute-start.6
  96.6 1.5 collective-permute-done.6
  98.1 1.1 fusion.4
  99.2 0.7 constant_dynamic-slice_fusion.3
  99.9 0.8 collective-permute-start.7
  100.7 5.5 %collective-permute-done.7 = f32[64,768]{1,0:T(8,128)} collective-permute-done((f32[64,768]{1,0:T(8,128)}, f32[64,768]{1,0:T(8,128)}, u32[]{:S(2)}, u32[]{:S(2)}) %collective-permute-start.7) | collective-permute-done | bytes 196640 | tf_op jit(solution)/shard_map/ppermute | solution.py:201
  106.3 0.9 dynamic-slice_add_fusion
  107.2 0.7 copy-done.6
  107.9 1.4 collective-permute-start.8
  109.3 2.2 %collective-permute-done.8 = f32[32,768]{1,0:T(8,128)S(1)} collective-permute-done((f32[32,768]{1,0:T(8,128)S(1)}, f32[32,768]{1,0:T(8,128)S(1)}, u32[]{:S(2)}, u32[]{:S(2)}) %collective-permute-start.8) | collective-permute-done | bytes 98336 | tf_op jit(solution)/shard_map/ppermute | solution.py:201
  111.4 0.9 dynamic-slice_add_fusion.1
  112.5 3.8 %collective-permute-done.9 = f32[16,768]{1,0:T(8,128)S(1)} collective-permute-done((f32[16,768]{1,0:T(8,128)S(1)}, f32[16,768]{1,0:T(8,128)S(1)}, u32[]{:S(2)}, u32[]{:S(2)}) %collective-permute-start.9) | collective-permute-done | bytes 49184 | tf_op jit(solution)/shard_map/ppermute | solution.py:201
  116.3 0.4 collective-permute-start.10
  116.7 2.7 %collective-permute-done.10 = f32[8,768]{1,0:T(8,128)S(1)} collective-permute-done((f32[8,768]{1,0:T(8,128)S(1)}, f32[8,768]{1,0:T(8,128)S(1)}, u32[]{:S(2)}, u32[]{:S(2)}) %collective-permute-start.10) | collective-permute-done | bytes 24608 | tf_op jit(solution)/shard_map/ppermute | solution.py:201
  119.4 0.3 collective-permute-start.11
  119.7 0.2 convert_element_type.31
  120.0 0.2 slice.56
  120.1 0.2 slice.44
  120.4 1.4 collective-permute-start.4
  121.7 6.2 %collective-permute-start.3 = (bf16[4,4,3072]{2,1,0:T(4,128)(2,1)S(1)}, bf16[4,4,3072]{2,1,0:T(4,128)(2,1)S(1)}, u32[]{:S(2)}, u32[]{:S(2)}) collective-permute-start(bf16[4,4,3072]{2,1,0:T(4,128)(2,1)S(1)} %slice.54), channel_id=1, source_target_pairs={{0,9},{1,10},{2,11},{3,12},{4,13},{5,14},{6,15},{7,8},{8,17},{9,18... | collective-permute-start | bytes 294920 | tf_op jit(solution)/shard_map/ppermute | solution.py:247
  127.9 0.8 collective-permute-start.5
  128.7 2.5 %collective-permute-start.12 = (f32[16,768]{1,0:T(8,128)S(1)}, f32[16,768]{1,0:T(8,128)S(1)}, u32[]{:S(2)}, u32[]{:S(2)}) collective-permute-start(f32[16,768]{1,0:T(8,128)S(1)} %constant_dynamic-update-slice_fusion.8), channel_id=1, source_target_pairs={{0,16},{8,24},{16,0},{24,8},{1,17},{9,25},{17,1},{25,9},{2,18},{10... | collective-permute-start | bytes 147464 | tf_op jit(solution)/shard_map/ppermute | solution.py:201
  131.2 7.2 %collective-permute-done.12 = f32[16,768]{1,0:T(8,128)S(1)} collective-permute-done((f32[16,768]{1,0:T(8,128)S(1)}, f32[16,768]{1,0:T(8,128)S(1)}, u32[]{:S(2)}, u32[]{:S(2)}) %collective-permute-start.12) | collective-permute-done | bytes 49184 | tf_op jit(solution)/shard_map/ppermute | solution.py:201
  138.4 3.9 %collective-permute-done.13 = f32[32,768]{1,0:T(8,128)S(1)} collective-permute-done((f32[32,768]{1,0:T(8,128)S(1)}, f32[32,768]{1,0:T(8,128)S(1)}, u32[]{:S(2)}, u32[]{:S(2)}) %collective-permute-start.13) | collective-permute-done | bytes 98336 | tf_op jit(solution)/shard_map/ppermute | solution.py:201
  142.4 1.3 collective-permute-start.14
  144.0 3.6 %collective-permute-done.14 = f32[64,768]{1,0:T(8,128)S(1)} collective-permute-done((f32[64,768]{1,0:T(8,128)S(1)}, f32[64,768]{1,0:T(8,128)S(1)}, u32[]{:S(2)}, u32[]{:S(2)}) %collective-permute-start.14) | collective-permute-done | bytes 196640 | tf_op jit(solution)/shard_map/ppermute | solution.py:201
  147.6 2.2 %collective-permute-start.15 = (f32[128,768]{1,0:T(8,128)S(1)}, f32[128,768]{1,0:T(8,128)S(1)}, u32[]{:S(2)}, u32[]{:S(2)}) collective-permute-start(f32[128,768]{1,0:T(8,128)S(1)} %constant_dynamic-update-slice_fusion.2), channel_id=1, source_target_pairs={{0,2},{2,0},{4,6},{6,4},{1,3},{3,1},{5,7},{7,5},{8,10},{10,8},{12,... | collective-permute-start | bytes 1179656 | tf_op jit(solution)/shard_map/ppermute | solution.py:201
  149.8 1.8 %fusion = bf16[16,16,3072]{2,1,0:T(8,128)(2,1)} fusion(f32[12,12,3072]{2,1,0:T(8,128)S(1)} %slice.44, f32[12,4,3072]{2,1,0:T(4,128)S(1)} %convert_element_type.32, f32[4,16,3072]{2,1,0:T(8,128)S(1)} %maximum_convert_fusion, bf16[16,16,3072]{2,1,0:T(8,128)(2,1)S(1)} %copy-done.1), kind=kLoop, calls=%fused_computation.8 | loop fusion | flops 3932160 | bytes 6291456 | tf_op jit(solution)/shard_map/convert_element_type | solution.py:267
  151.9 0.6 slice.57
  152.5 1.0 reshape.77
  153.5 0.8 reshape.78
  (55 shorter events, 1.1 us)
Async XLA Ops:
  0.6 6.1 %copy-start.2 = (bf16[16,16,3072]{2,1,0:T(8,128)(2,1)S(1)}, bf16[16,16,3072]{2,1,0:T(8,128)(2,1)}, u32[]{:S(2)}) copy-start(bf16[16,16,3072]{2,1,0:T(8,128)(2,1)} %refs_0_.1) | copy-start | bytes 4718596
  0.6 6.1 %copy-start = (bf16[16,16,3072]{2,1,0:T(8,128)(2,1)S(1)}, bf16[16,16,3072]{2,1,0:T(8,128)(2,1)}, u32[]{:S(2)}) copy-start(bf16[16,16,3072]{2,1,0:T(8,128)(2,1)} %refs_1_.1) | copy-start | bytes 4718596
  3.5 29.9 %collective-permute-start.1 = (bf16[2,4,12,3072]{3,1,2,0:T(4,128)(2,1)}, bf16[2,4,12,3072]{3,1,2,0:T(4,128)(2,1)}, u32[]{:S(2)}, u32[]{:S(2)}) collective-permute-start(bf16[2,4,12,3072]{3,1,2,0:T(4,128)(2,1)} %copy.12), channel_id=1, source_target_pairs={{0,24},{1,25},{2,26},{3,27},{4,28},{5,29},{6,30},{7,31},{8,0},{9,1... | collective-permute-start | bytes 1769480 | tf_op jit(solution)/shard_map/ppermute | solution.py:247
  7.8 26.8 %collective-permute-start = (bf16[2,12,4,3072]{3,2,1,0:T(4,128)(2,1)}, bf16[2,12,4,3072]{3,2,1,0:T(4,128)(2,1)}, u32[]{:S(2)}, u32[]{:S(2)}) collective-permute-start(bf16[2,12,4,3072]{3,2,1,0:T(4,128)(2,1)} %fusion.3), channel_id=1, source_target_pairs={{0,7},{1,0},{2,1},{3,2},{4,3},{5,4},{6,5},{7,6},{8,15},{9,8},{10,9... | collective-permute-start | bytes 1769480 | tf_op jit(solution)/shard_map/ppermute | solution.py:247
  8.1 26.5 %collective-permute-start.2 = (bf16[2,4,4,3072]{3,2,1,0:T(4,128)(2,1)S(1)}, bf16[2,4,4,3072]{3,2,1,0:T(4,128)(2,1)S(1)}, u32[]{:S(2)}, u32[]{:S(2)}) collective-permute-start(bf16[2,4,4,3072]{3,2,1,0:T(4,128)(2,1)S(1)} %pad_maximum_fusion), channel_id=1, source_target_pairs={{0,31},{1,24},{2,25},{3,26},{4,27},{5,28},{6,29},{7,30},{8,7},{9,0... | collective-permute-start | bytes 589832 | tf_op jit(solution)/shard_map/ppermute | solution.py:247
  10.1 2.3 %copy-start.7 = (s32[16,16,16]{2,1,0:T(8,128)S(1)}, s32[16,16,16]{2,1,0:T(8,128)}, u32[]{:S(2)}) copy-start(s32[16,16,16]{2,1,0:T(8,128)} %param.8) | copy-start | bytes 49156
  12.5 22.2 %copy-start.4 = (bf16[2,12,12,3072]{3,2,1,0:T(8,128)(2,1)S(1)}, bf16[2,12,12,3072]{3,2,1,0:T(8,128)(2,1)}, u32[]{:S(2)}) copy-start(bf16[2,12,12,3072]{3,2,1,0:T(8,128)(2,1)} %fusion.1) | copy-start | bytes 5308420
  92.5 27.1 %copy-start.3 = (f32[16,16,3072]{2,1,0:T(8,128)S(1)}, f32[16,16,3072]{2,1,0:T(8,128)}, u32[]{:S(2)}) copy-start(f32[16,16,3072]{2,1,0:T(8,128)} %get-tuple-element.16) | copy-start | bytes 9437188
  94.9 0.8 copy-start.5
  95.8 2.3 %collective-permute-start.6 = (f32[128,768]{1,0:T(8,128)S(1)}, f32[128,768]{1,0:T(8,128)}, u32[]{:S(2)}, u32[]{:S(2)}) collective-permute-start(f32[128,768]{1,0:T(8,128)S(1)} %pad_dynamic-slice_fusion), channel_id=1, source_target_pairs={{0,2},{2,0},{4,6},{6,4},{1,3},{3,1},{5,7},{7,5},{8,10},{10,8},{12,... | collective-permute-start | bytes 1179656 | tf_op jit(solution)/shard_map/ppermute | solution.py:201
  99.9 6.4 %collective-permute-start.7 = (f32[64,768]{1,0:T(8,128)}, f32[64,768]{1,0:T(8,128)}, u32[]{:S(2)}, u32[]{:S(2)}) collective-permute-start(f32[64,768]{1,0:T(8,128)} %constant_dynamic-slice_fusion.3), channel_id=1, source_target_pairs={{0,4},{2,6},{4,0},{6,2},{1,5},{3,7},{5,1},{7,3},{8,12},{10,14},{12... | collective-permute-start | bytes 589832 | tf_op jit(solution)/shard_map/ppermute | solution.py:201
  107.2 0.7 copy-start.6
  107.9 3.5 %collective-permute-start.8 = (f32[32,768]{1,0:T(8,128)S(1)}, f32[32,768]{1,0:T(8,128)S(1)}, u32[]{:S(2)}, u32[]{:S(2)}) collective-permute-start(f32[32,768]{1,0:T(8,128)S(1)} %constant_dynamic-slice_fusion.2), channel_id=1, source_target_pairs={{0,8},{8,0},{16,24},{24,16},{1,9},{9,1},{17,25},{25,17},{2,10},{10... | collective-permute-start | bytes 294920 | tf_op jit(solution)/shard_map/ppermute | solution.py:201
  112.4 3.9 %collective-permute-start.9 = (f32[16,768]{1,0:T(8,128)S(1)}, f32[16,768]{1,0:T(8,128)S(1)}, u32[]{:S(2)}, u32[]{:S(2)}) collective-permute-start(f32[16,768]{1,0:T(8,128)S(1)} %constant_dynamic-slice_fusion.1), channel_id=1, source_target_pairs={{0,16},{8,24},{16,0},{24,8},{1,17},{9,25},{17,1},{25,9},{2,18},{10... | collective-permute-start | bytes 147464 | tf_op jit(solution)/shard_map/ppermute | solution.py:201
  116.3 3.0 %collective-permute-start.10 = (f32[8,768]{1,0:T(8,128)S(1)}, f32[8,768]{1,0:T(8,128)S(1)}, u32[]{:S(2)}, u32[]{:S(2)}) collective-permute-start(f32[8,768]{1,0:T(8,128)S(1)} %constant_dynamic-slice_fusion), channel_id=1, source_target_pairs={{0,1},{1,0},{2,3},{3,2},{4,5},{5,4},{6,7},{7,6},{8,9},{9,8},{10,11... | collective-permute-start | bytes 73736 | tf_op jit(solution)/shard_map/ppermute | solution.py:201
  119.4 9.3 %collective-permute-start.11 = (f32[8,768]{1,0:T(8,128)S(1)}, f32[8,768]{1,0:T(8,128)S(1)}, u32[]{:S(2)}, u32[]{:S(2)}) collective-permute-start(f32[8,768]{1,0:T(8,128)S(1)} %get-tuple-element.21), channel_id=1, source_target_pairs={{0,1},{1,0},{2,3},{3,2},{4,5},{5,4},{6,7},{7,6},{8,9},{9,8},{10,11... | collective-permute-start | bytes 73736 | tf_op jit(solution)/shard_map/ppermute | solution.py:201
  120.4 29.5 %copy-start.1 = (bf16[16,16,3072]{2,1,0:T(8,128)(2,1)S(1)}, bf16[16,16,3072]{2,1,0:T(8,128)(2,1)}, u32[]{:S(2)}) copy-start(bf16[16,16,3072]{2,1,0:T(8,128)(2,1)} %refs_1_.1) | copy-start | bytes 4718596
  120.4 23.3 %collective-permute-start.4 = (bf16[4,12,3072]{2,1,0:T(8,128)(2,1)S(1)}, bf16[4,12,3072]{2,1,0:T(8,128)(2,1)S(1)}, u32[]{:S(2)}, u32[]{:S(2)}) collective-permute-start(bf16[4,12,3072]{2,1,0:T(8,128)(2,1)S(1)} %slice.55), channel_id=1, source_target_pairs={{0,8},{1,9},{2,10},{3,11},{4,12},{5,13},{6,14},{7,15},{8,16},{9,17... | collective-permute-start | bytes 884744 | tf_op jit(solution)/shard_map/ppermute | solution.py:247
  121.7 22.0 %collective-permute-start.3 = (bf16[4,4,3072]{2,1,0:T(4,128)(2,1)S(1)}, bf16[4,4,3072]{2,1,0:T(4,128)(2,1)S(1)}, u32[]{:S(2)}, u32[]{:S(2)}) collective-permute-start(bf16[4,4,3072]{2,1,0:T(4,128)(2,1)S(1)} %slice.54), channel_id=1, source_target_pairs={{0,9},{1,10},{2,11},{3,12},{4,13},{5,14},{6,15},{7,8},{8,17},{9,18... | collective-permute-start | bytes 294920 | tf_op jit(solution)/shard_map/ppermute | solution.py:247
  127.9 16.0 %collective-permute-start.5 = (bf16[12,4,3072]{2,1,0:T(4,128)(2,1)S(1)}, bf16[12,4,3072]{2,1,0:T(4,128)(2,1)S(1)}, u32[]{:S(2)}, u32[]{:S(2)}) collective-permute-start(bf16[12,4,3072]{2,1,0:T(4,128)(2,1)S(1)} %slice.56), channel_id=1, source_target_pairs={{0,1},{1,2},{2,3},{3,4},{4,5},{5,6},{6,7},{7,0},{8,9},{9,10},{10,1... | collective-permute-start | bytes 884744 | tf_op jit(solution)/shard_map/ppermute | solution.py:247
  128.7 9.7 %collective-permute-start.12 = (f32[16,768]{1,0:T(8,128)S(1)}, f32[16,768]{1,0:T(8,128)S(1)}, u32[]{:S(2)}, u32[]{:S(2)}) collective-permute-start(f32[16,768]{1,0:T(8,128)S(1)} %constant_dynamic-update-slice_fusion.8), channel_id=1, source_target_pairs={{0,16},{8,24},{16,0},{24,8},{1,17},{9,25},{17,1},{25,9},{2,18},{10... | collective-permute-start | bytes 147464 | tf_op jit(solution)/shard_map/ppermute | solution.py:201
  138.4 4.0 %collective-permute-start.13 = (f32[32,768]{1,0:T(8,128)S(1)}, f32[32,768]{1,0:T(8,128)S(1)}, u32[]{:S(2)}, u32[]{:S(2)}) collective-permute-start(f32[32,768]{1,0:T(8,128)S(1)} %constant_dynamic-update-slice_fusion.6), channel_id=1, source_target_pairs={{0,8},{8,0},{16,24},{24,16},{1,9},{9,1},{17,25},{25,17},{2,10},{10... | collective-permute-start | bytes 294920 | tf_op jit(solution)/shard_map/ppermute | solution.py:201
  142.4 5.2 %collective-permute-start.14 = (f32[64,768]{1,0:T(8,128)S(1)}, f32[64,768]{1,0:T(8,128)S(1)}, u32[]{:S(2)}, u32[]{:S(2)}) collective-permute-start(f32[64,768]{1,0:T(8,128)S(1)} %constant_dynamic-update-slice_fusion.4), channel_id=1, source_target_pairs={{0,4},{2,6},{4,0},{6,2},{1,5},{3,7},{5,1},{7,3},{8,12},{10,14},{12... | collective-permute-start | bytes 589832 | tf_op jit(solution)/shard_map/ppermute | solution.py:201
  147.6 4.1 %collective-permute-start.15 = (f32[128,768]{1,0:T(8,128)S(1)}, f32[128,768]{1,0:T(8,128)S(1)}, u32[]{:S(2)}, u32[]{:S(2)}) collective-permute-start(f32[128,768]{1,0:T(8,128)S(1)} %constant_dynamic-update-slice_fusion.2), channel_id=1, source_target_pairs={{0,2},{2,0},{4,6},{6,4},{1,3},{3,1},{5,7},{7,5},{8,10},{10,8},{12,... | collective-permute-start | bytes 1179656 | tf_op jit(solution)/shard_map/ppermute | solution.py:201

commit v16 on v15

--- a/solution.py
+++ b/solution.py
@@ -14,6 +14,7 @@
 HEAD = C // HEADS
 SCALE = HEAD ** (-0.5)
 EXP2_SCALE = SCALE * 1.4426950408889634
+PACKED_ROWS = 256
 
 
 def passed_along(block, axis, distance):
@@ -48,7 +49,7 @@
         else:
             (both_ref, krow_ref, gain_ref, wqkv_ref, wp_ref,
              gs0_ref, gqkvT0_ref, gproj0_ref, ggain0_ref,
-             gs_ref, gqkvT_ref, gproj_ref, ggain_ref, qkv_s, ga_s, drow_s, bias_s) = refs
+             gs_ref, gqkvT_ref, gproj_ref, ggain_ref, packed_ref, qkv_s, ga_s, drow_s, bias_s) = refs
         f32 = jnp.float32
         bf16 = jnp.bfloat16
         if first:
@@ -168,6 +169,13 @@
             block_step(0, 0)
         else:
             lax.fori_loop(1, 4, block_step, 0)
+            packed_ref[pl.ds(0, C), :] = jnp.concatenate([gqkvT_ref[...], gproj_ref[...]], axis=1)
+            gain_row = jnp.broadcast_to(ggain_ref[...], (C, 128)).T[0:1]
+            tail = jnp.zeros((packed_ref.shape[0] - C, packed_ref.shape[1]), f32)
+            tail = jnp.concatenate(
+                [jnp.concatenate([gain_row, jnp.zeros((1, 3 * C), f32)], axis=1), tail[1:]], axis=0
+            )
+            packed_ref[pl.ds(C, packed_ref.shape[0] - C), :] = tail
 
     return window_kernel
 
@@ -184,7 +192,8 @@
             jax.ShapeDtypeStruct((C, 3 * C), jnp.float32),
             jax.ShapeDtypeStruct((C, C), jnp.float32),
             jax.ShapeDtypeStruct((C, 1), jnp.float32),
-        ],
+        ]
+        + ([] if first else [jax.ShapeDtypeStruct((PACKED_ROWS, 4 * C), jnp.float32)]),
         scratch_shapes=[
             pltpu.VMEM((3 * C, CELLS), jnp.float32),
             pltpu.VMEM((C, CELLS), jnp.float32),
@@ -291,14 +300,8 @@
         proj_weight,
     )
     partial = window_grads(True, (tokens, grads_out), *constants)
-    grad_branch, qkv_part, proj_grad, gain_grad = window_grads(
-        False, (both,), *constants, partial=partial
-    )
-    width = 4 * channels
-    gain_row = jnp.pad(gain_grad.reshape(1, channels), ((0, 0), (0, width - channels)))
-    summed = summed_everywhere(
-        jnp.concatenate([jnp.concatenate([qkv_part, proj_grad], axis=1), gain_row], axis=0)
-    )
+    grad_branch, _, _, _, packed = window_grads(False, (both,), *constants, partial=partial)
+    summed = summed_everywhere(packed)
     qkv_grad = summed[:channels, : 3 * channels]
     proj_grad = summed[:channels, 3 * channels :]
     gain_grad = summed[channels, :channels]

time: 156 us -> 157 us (level); the launches traced: 154 us -> 157 us
  waiting for transfers between devices: 30.4 us -> 35.6 us
  other arithmetic: 15.9 us -> 13.5 us
    ppermute x10, waiting for transfers between devices: 30.4 us -> 35.5 us  [swapped(): lax.ppermute(block, axis, [(i, i ^ distance) for i in range(lax.axis_size...]
  transfers between devices with their start and end apart: 16 -> 16, of which waited for: 8 -> 8; matrix products, arithmetic and copies ran while one was open for 6% -> 6% of each run, Pallas kernels for 13% -> 12%
where the time goes in v16:
time: 157 us
  Pallas kernels  74.5 us (47%)
  waiting for transfers between devices  35.6 us (23%)
  starting transfers between devices  23.2 us (15%)
  other arithmetic  13.5 us (9%)
  local copies, waits for them, and re-layouts  9.44 us (6%)
    pallas_call x2, Pallas kernels, window_grads(): pl.pallas_call(make_window_kernel(first), out_shape=[jax.ShapeDtypeStruct...  74.5 us
    ppermute x10, waiting for transfers between devices, swapped(): lax.ppermute(block, axis, [(i, i ^ distance) for i in range(lax.axis_size...  35.5 us
    ppermute x6, starting transfers between devices, moved(): lax.ppermute(block, ('gx', 'gy', 'gz'), halo_route(distance_a, distance_b))  13.1 us
    ppermute x10, starting transfers between devices, swapped(): lax.ppermute(block, axis, [(i, i ^ distance) for i in range(lax.axis_size...  10.1 us
    another operation x4, other arithmetic, per_device(): both = shifted_block(jnp.stack([tokens, grads_out]))  4.78 us
    concatenate x1, other arithmetic, shifted_block(): return jnp.concatenate([upper, lower], axis=1)  3.36 us
  transfers between devices with their start and end apart: 16, of which 8 were waited for; matrix products, arithmetic and copies ran while one was open for 6% of the time, Pallas kernels for 12%

profile of v16, /device:TPU:5, one launch (start us, length us, event | category | flops | bytes accessed | tf_op | source)
XLA Modules:
  0.0 157.2 jit_solution(3871240447112408413)
XLA Ops:
  0.7 1.2 pad_maximum_fusion
  1.9 3.3 %collective-permute-start.2 = (bf16[2,4,4,3072]{3,2,1,0:T(4,128)(2,1)S(1)}, bf16[2,4,4,3072]{3,2,1,0:T(4,128)(2,1)S(1)}, u32[]{:S(2)}, u32[]{:S(2)}) collective-permute-start(bf16[2,4,4,3072]{3,2,1,0:T(4,128)(2,1)S(1)} %pad_maximum_fusion), channel_id=1, source_target_pairs={{0,31},{1,24},{2,25},{3,26},{4,27},{5,28},{6,29},{7,30},{8,7},{9,0... | collective-permute-start | bytes 589832 | tf_op jit(solution)/shard_map/ppermute | solution.py:256
  5.2 0.3 fusion.2
  5.5 1.3 copy.11
  6.8 0.8 collective-permute-start.1
  7.6 1.0 fusion.3
  8.6 1.2 collective-permute-start
  9.8 2.3 %fusion.1 = bf16[2,12,12,3072]{3,2,1,0:T(8,128)(2,1)} fusion(bf16[1,16,16,3072]{3,2,1,0:T(8,128)(2,1)S(1)} %bitcast.14, bf16[1,16,16,3072]{3,2,1,0:T(8,128)(2,1)S(1)} %bitcast.10), kind=kLoop, calls=%fused_computation.9 | loop fusion | flops 884736 | bytes 4915200 | tf_op jit(solution)/shard_map/stack | solution.py:283
  12.2 0.2 reshape.71
  12.4 0.2 copy.13
  12.6 0.8 broadcast_in_dim_reshape.3.refs_2_.refs_1_
  13.3 19.6 %shard_map.93 = (f32[8,8,3072]{2,1,0:T(8,128)}, f32[192,576]{1,0:T(8,128)}, f32[192,192]{1,0:T(8,128)}, f32[192,1]{1,0:T(8,128)}) custom-call(bf16[16,16,3072]{2,1,0:T(8,128)(2,1)} %refs_0_.1, bf16[16,16,3072]{2,1,0:T(8,128)(2,1)} %refs_1_.1, s32[8,1,512]{2,1,0:T(1,128)} %broadcast_in_dim_reshape.3.refs_2_.refs_1_, f32[1,192]{1,0:T(1,128)} %bitcast.16, ...), custom_call_target="tpu_custom_call" | custom-call | tf_op jit(solution)/shard_map/pallas_call | solution.py:188
  33.0 1.3 copy.12
  34.3 3.4 %maximum_maximum_fusion.refs_0_ = bf16[2,16,16,3072]{3,2,1,0:T(8,128)(2,1)} fusion(bf16[2,4,4,3072]{3,2,1,0:T(4,128)(2,1)S(1)} %collective-permute-done.2, bf16[2,4,12,3072]{3,2,1,0:T(8,128)(2,1)S(1)} %copy.12, bf16[2,12,4,3072]{3,2,1,0:T(4,128)(2,1)} %collective-permute-done, bf16[2,12,12,3072]{3,2,1,0:T(8,128)(2,1)S(1)} %copy-done.4), kind=kLoop, calls=%fused_computation.6 | loop fusion | flops 12582912 | bytes 6291456 | tf_op jit(solution)/shard_map/concatenate | solution.py:265
  37.6 54.8 %shard_map.94 = (f32[16,16,3072]{2,1,0:T(8,128)}, f32[192,576]{1,0:T(8,128)}, f32[192,192]{1,0:T(8,128)}, f32[192,1]{1,0:T(8,128)}, f32[256,768]{1,0:T(8,128)}) custom-call(bf16[2,16,16,3072]{3,2,1,0:T(8,128)(2,1)} %maximum_maximum_fusion.refs_0_, s32[8,1,512]{2,1,0:T(1,128)} %broadcast_in_dim_reshape.3.refs_2_.refs_1_, f32[1,192]{1,0:T(1,128)} %bitcast.17, ...), custom_call_target="tpu_custom_call" | custom-call | tf_op jit(solution)/shard_map/pallas_call | solution.py:188
  92.5 1.2 constant_dynamic-slice_fusion.4
  93.6 1.4 collective-permute-start.6
  95.0 1.5 collective-permute-done.6
  96.5 1.2 dynamic-slice_add_fusion
  97.7 0.7 constant_dynamic-slice_fusion.3
  98.4 0.3 collective-permute-start.7
  98.6 6.2 %collective-permute-done.7 = f32[64,768]{1,0:T(8,128)} collective-permute-done((f32[64,768]{1,0:T(8,128)}, f32[64,768]{1,0:T(8,128)}, u32[]{:S(2)}, u32[]{:S(2)}) %collective-permute-start.7) | collective-permute-done | bytes 196640 | tf_op jit(solution)/shard_map/ppermute | solution.py:210
  104.8 0.9 dynamic-slice_add_fusion.1
  105.8 0.7 copy-done.5
  106.4 1.4 collective-permute-start.8
  107.8 2.2 %collective-permute-done.8 = f32[32,768]{1,0:T(8,128)S(1)} collective-permute-done((f32[32,768]{1,0:T(8,128)S(1)}, f32[32,768]{1,0:T(8,128)S(1)}, u32[]{:S(2)}, u32[]{:S(2)}) %collective-permute-start.8) | collective-permute-done | bytes 98336 | tf_op jit(solution)/shard_map/ppermute | solution.py:210
  110.0 0.9 dynamic-slice_add_fusion.2
  111.0 3.8 %collective-permute-done.9 = f32[16,768]{1,0:T(8,128)S(1)} collective-permute-done((f32[16,768]{1,0:T(8,128)S(1)}, f32[16,768]{1,0:T(8,128)S(1)}, u32[]{:S(2)}, u32[]{:S(2)}) %collective-permute-start.9) | collective-permute-done | bytes 49184 | tf_op jit(solution)/shard_map/ppermute | solution.py:210
  114.8 0.4 collective-permute-start.10
  115.2 2.7 %collective-permute-done.10 = f32[8,768]{1,0:T(8,128)S(1)} collective-permute-done((f32[8,768]{1,0:T(8,128)S(1)}, f32[8,768]{1,0:T(8,128)S(1)}, u32[]{:S(2)}, u32[]{:S(2)}) %collective-permute-start.10) | collective-permute-done | bytes 24608 | tf_op jit(solution)/shard_map/ppermute | solution.py:210
  117.9 0.4 collective-permute-start.11
  118.3 0.2 slice.40
  118.5 0.2 convert_element_type.27
  118.7 0.2 slice.52
  119.0 5.7 %collective-permute-start.5 = (bf16[12,4,3072]{2,1,0:T(4,128)(2,1)S(1)}, bf16[12,4,3072]{2,1,0:T(4,128)(2,1)S(1)}, u32[]{:S(2)}, u32[]{:S(2)}) collective-permute-start(bf16[12,4,3072]{2,1,0:T(4,128)(2,1)S(1)} %slice.52), channel_id=1, source_target_pairs={{0,1},{1,2},{2,3},{3,4},{4,5},{5,6},{6,7},{7,0},{8,9},{9,10},{10,1... | collective-permute-start | bytes 884744 | tf_op jit(solution)/shard_map/ppermute | solution.py:256
  124.7 1.3 collective-permute-start.4
  126.0 0.8 collective-permute-start.3
  126.8 2.9 %collective-permute-start.12 = (f32[16,768]{1,0:T(8,128)S(1)}, f32[16,768]{1,0:T(8,128)S(1)}, u32[]{:S(2)}, u32[]{:S(2)}) collective-permute-start(f32[16,768]{1,0:T(8,128)S(1)} %constant_dynamic-update-slice_fusion.8), channel_id=1, source_target_pairs={{0,16},{8,24},{16,0},{24,8},{1,17},{9,25},{17,1},{25,9},{2,18},{10... | collective-permute-start | bytes 147464 | tf_op jit(solution)/shard_map/ppermute | solution.py:210
  129.7 11.6 %collective-permute-done.12 = f32[16,768]{1,0:T(8,128)S(1)} collective-permute-done((f32[16,768]{1,0:T(8,128)S(1)}, f32[16,768]{1,0:T(8,128)S(1)}, u32[]{:S(2)}, u32[]{:S(2)}) %collective-permute-start.12) | collective-permute-done | bytes 49184 | tf_op jit(solution)/shard_map/ppermute | solution.py:210
  141.4 3.9 %collective-permute-done.13 = f32[32,768]{1,0:T(8,128)S(1)} collective-permute-done((f32[32,768]{1,0:T(8,128)S(1)}, f32[32,768]{1,0:T(8,128)S(1)}, u32[]{:S(2)}, u32[]{:S(2)}) %collective-permute-start.13) | collective-permute-done | bytes 98336 | tf_op jit(solution)/shard_map/ppermute | solution.py:210
  145.3 1.2 collective-permute-start.14
  146.5 0.1 maximum_convert_fusion
  146.8 3.8 %collective-permute-done.14 = f32[64,768]{1,0:T(8,128)S(1)} collective-permute-done((f32[64,768]{1,0:T(8,128)S(1)}, f32[64,768]{1,0:T(8,128)S(1)}, u32[]{:S(2)}, u32[]{:S(2)}) %collective-permute-start.14) | collective-permute-done | bytes 196640 | tf_op jit(solution)/shard_map/ppermute | solution.py:210
  150.6 2.2 %collective-permute-start.15 = (f32[128,768]{1,0:T(8,128)S(1)}, f32[128,768]{1,0:T(8,128)S(1)}, u32[]{:S(2)}, u32[]{:S(2)}) collective-permute-start(f32[128,768]{1,0:T(8,128)S(1)} %constant_dynamic-update-slice_fusion.2), channel_id=1, source_target_pairs={{0,2},{2,0},{4,6},{6,4},{1,3},{3,1},{5,7},{7,5},{8,10},{10,8},{12,... | collective-permute-start | bytes 1179656 | tf_op jit(solution)/shard_map/ppermute | solution.py:210
  152.8 1.8 %fusion = bf16[16,16,3072]{2,1,0:T(8,128)(2,1)} fusion(f32[12,12,3072]{2,1,0:T(8,128)S(1)} %slice.40, f32[12,4,3072]{2,1,0:T(4,128)S(1)} %convert_element_type.28, f32[4,16,3072]{2,1,0:T(8,128)S(1)} %maximum_convert_fusion, bf16[16,16,3072]{2,1,0:T(8,128)(2,1)S(1)} %copy-done.1), kind=kLoop, calls=%fused_computation.8 | loop fusion | flops 3932160 | bytes 6291456 | tf_op jit(solution)/shard_map/convert_element_type | solution.py:276
  154.7 0.6 slice.53
  155.4 1.0 reshape.73
  156.4 0.8 reshape.74
  (51 shorter events, 0.9 us)
Async XLA Ops:
  0.6 4.6 %copy-start = (bf16[16,16,3072]{2,1,0:T(8,128)(2,1)S(1)}, bf16[16,16,3072]{2,1,0:T(8,128)(2,1)}, u32[]{:S(2)}) copy-start(bf16[16,16,3072]{2,1,0:T(8,128)(2,1)} %refs_1_.1) | copy-start | bytes 4718596
  0.6 4.6 %copy-start.2 = (bf16[16,16,3072]{2,1,0:T(8,128)(2,1)S(1)}, bf16[16,16,3072]{2,1,0:T(8,128)(2,1)}, u32[]{:S(2)}) copy-start(bf16[16,16,3072]{2,1,0:T(8,128)(2,1)} %refs_0_.1) | copy-start | bytes 4718596
  1.9 32.4 %collective-permute-start.2 = (bf16[2,4,4,3072]{3,2,1,0:T(4,128)(2,1)S(1)}, bf16[2,4,4,3072]{3,2,1,0:T(4,128)(2,1)S(1)}, u32[]{:S(2)}, u32[]{:S(2)}) collective-permute-start(bf16[2,4,4,3072]{3,2,1,0:T(4,128)(2,1)S(1)} %pad_maximum_fusion), channel_id=1, source_target_pairs={{0,31},{1,24},{2,25},{3,26},{4,27},{5,28},{6,29},{7,30},{8,7},{9,0... | collective-permute-start | bytes 589832 | tf_op jit(solution)/shard_map/ppermute | solution.py:256
  6.8 26.2 %collective-permute-start.1 = (bf16[2,4,12,3072]{3,1,2,0:T(4,128)(2,1)}, bf16[2,4,12,3072]{3,1,2,0:T(4,128)(2,1)}, u32[]{:S(2)}, u32[]{:S(2)}) collective-permute-start(bf16[2,4,12,3072]{3,1,2,0:T(4,128)(2,1)} %copy.11), channel_id=1, source_target_pairs={{0,24},{1,25},{2,26},{3,27},{4,28},{5,29},{6,30},{7,31},{8,0},{9,1... | collective-permute-start | bytes 1769480 | tf_op jit(solution)/shard_map/ppermute | solution.py:256
  8.6 25.7 %collective-permute-start = (bf16[2,12,4,3072]{3,2,1,0:T(4,128)(2,1)}, bf16[2,12,4,3072]{3,2,1,0:T(4,128)(2,1)}, u32[]{:S(2)}, u32[]{:S(2)}) collective-permute-start(bf16[2,12,4,3072]{3,2,1,0:T(4,128)(2,1)} %fusion.3), channel_id=1, source_target_pairs={{0,7},{1,0},{2,1},{3,2},{4,3},{5,4},{6,5},{7,6},{8,15},{9,8},{10,9... | collective-permute-start | bytes 1769480 | tf_op jit(solution)/shard_map/ppermute | solution.py:256
  9.8 2.3 %copy-start.6 = (s32[16,16,16]{2,1,0:T(8,128)S(1)}, s32[16,16,16]{2,1,0:T(8,128)}, u32[]{:S(2)}) copy-start(s32[16,16,16]{2,1,0:T(8,128)} %param.8) | copy-start | bytes 49156
  12.1 22.2 %copy-start.4 = (bf16[2,12,12,3072]{3,2,1,0:T(8,128)(2,1)S(1)}, bf16[2,12,12,3072]{3,2,1,0:T(8,128)(2,1)}, u32[]{:S(2)}) copy-start(bf16[2,12,12,3072]{3,2,1,0:T(8,128)(2,1)} %fusion.1) | copy-start | bytes 5308420
  92.5 25.8 %copy-start.3 = (f32[16,16,3072]{2,1,0:T(8,128)S(1)}, f32[16,16,3072]{2,1,0:T(8,128)}, u32[]{:S(2)}) copy-start(f32[16,16,3072]{2,1,0:T(8,128)} %get-tuple-element.14) | copy-start | bytes 9437188
  93.6 2.9 %collective-permute-start.6 = (f32[128,768]{1,0:T(8,128)S(1)}, f32[128,768]{1,0:T(8,128)}, u32[]{:S(2)}, u32[]{:S(2)}) collective-permute-start(f32[128,768]{1,0:T(8,128)S(1)} %constant_dynamic-slice_fusion.4), channel_id=1, source_target_pairs={{0,2},{2,0},{4,6},{6,4},{1,3},{3,1},{5,7},{7,5},{8,10},{10,8},{12,... | collective-permute-start | bytes 1179656 | tf_op jit(solution)/shard_map/ppermute | solution.py:210
  98.4 6.4 %collective-permute-start.7 = (f32[64,768]{1,0:T(8,128)}, f32[64,768]{1,0:T(8,128)}, u32[]{:S(2)}, u32[]{:S(2)}) collective-permute-start(f32[64,768]{1,0:T(8,128)} %constant_dynamic-slice_fusion.3), channel_id=1, source_target_pairs={{0,4},{2,6},{4,0},{6,2},{1,5},{3,7},{5,1},{7,3},{8,12},{10,14},{12... | collective-permute-start | bytes 589832 | tf_op jit(solution)/shard_map/ppermute | solution.py:210
  105.8 0.7 copy-start.5
  106.4 3.5 %collective-permute-start.8 = (f32[32,768]{1,0:T(8,128)S(1)}, f32[32,768]{1,0:T(8,128)S(1)}, u32[]{:S(2)}, u32[]{:S(2)}) collective-permute-start(f32[32,768]{1,0:T(8,128)S(1)} %constant_dynamic-slice_fusion.2), channel_id=1, source_target_pairs={{0,8},{8,0},{16,24},{24,16},{1,9},{9,1},{17,25},{25,17},{2,10},{10... | collective-permute-start | bytes 294920 | tf_op jit(solution)/shard_map/ppermute | solution.py:210
  110.9 3.9 %collective-permute-start.9 = (f32[16,768]{1,0:T(8,128)S(1)}, f32[16,768]{1,0:T(8,128)S(1)}, u32[]{:S(2)}, u32[]{:S(2)}) collective-permute-start(f32[16,768]{1,0:T(8,128)S(1)} %constant_dynamic-slice_fusion.1), channel_id=1, source_target_pairs={{0,16},{8,24},{16,0},{24,8},{1,17},{9,25},{17,1},{25,9},{2,18},{10... | collective-permute-start | bytes 147464 | tf_op jit(solution)/shard_map/ppermute | solution.py:210
  114.8 3.0 %collective-permute-start.10 = (f32[8,768]{1,0:T(8,128)S(1)}, f32[8,768]{1,0:T(8,128)S(1)}, u32[]{:S(2)}, u32[]{:S(2)}) collective-permute-start(f32[8,768]{1,0:T(8,128)S(1)} %constant_dynamic-slice_fusion), channel_id=1, source_target_pairs={{0,1},{1,0},{2,3},{3,2},{4,5},{5,4},{6,7},{7,6},{8,9},{9,8},{10,11... | collective-permute-start | bytes 73736 | tf_op jit(solution)/shard_map/ppermute | solution.py:210
  117.9 8.9 %collective-permute-start.11 = (f32[8,768]{1,0:T(8,128)S(1)}, f32[8,768]{1,0:T(8,128)S(1)}, u32[]{:S(2)}, u32[]{:S(2)}) collective-permute-start(f32[8,768]{1,0:T(8,128)S(1)} %get-tuple-element.17), channel_id=1, source_target_pairs={{0,1},{1,0},{2,3},{3,2},{4,5},{5,4},{6,7},{7,6},{8,9},{9,8},{10,11... | collective-permute-start | bytes 73736 | tf_op jit(solution)/shard_map/ppermute | solution.py:210
  118.7 34.0 %copy-start.1 = (bf16[16,16,3072]{2,1,0:T(8,128)(2,1)S(1)}, bf16[16,16,3072]{2,1,0:T(8,128)(2,1)}, u32[]{:S(2)}) copy-start(bf16[16,16,3072]{2,1,0:T(8,128)(2,1)} %refs_1_.1) | copy-start | bytes 4718596
  119.0 27.6 %collective-permute-start.5 = (bf16[12,4,3072]{2,1,0:T(4,128)(2,1)S(1)}, bf16[12,4,3072]{2,1,0:T(4,128)(2,1)S(1)}, u32[]{:S(2)}, u32[]{:S(2)}) collective-permute-start(bf16[12,4,3072]{2,1,0:T(4,128)(2,1)S(1)} %slice.52), channel_id=1, source_target_pairs={{0,1},{1,2},{2,3},{3,4},{4,5},{5,6},{6,7},{7,0},{8,9},{9,10},{10,1... | collective-permute-start | bytes 884744 | tf_op jit(solution)/shard_map/ppermute | solution.py:256
  124.7 21.8 %collective-permute-start.4 = (bf16[4,12,3072]{2,1,0:T(8,128)(2,1)S(1)}, bf16[4,12,3072]{2,1,0:T(8,128)(2,1)S(1)}, u32[]{:S(2)}, u32[]{:S(2)}) collective-permute-start(bf16[4,12,3072]{2,1,0:T(8,128)(2,1)S(1)} %slice.51), channel_id=1, source_target_pairs={{0,8},{1,9},{2,10},{3,11},{4,12},{5,13},{6,14},{7,15},{8,16},{9,17... | collective-permute-start | bytes 884744 | tf_op jit(solution)/shard_map/ppermute | solution.py:256
  126.0 20.5 %collective-permute-start.3 = (bf16[4,4,3072]{2,1,0:T(4,128)(2,1)S(1)}, bf16[4,4,3072]{2,1,0:T(4,128)(2,1)S(1)}, u32[]{:S(2)}, u32[]{:S(2)}) collective-permute-start(bf16[4,4,3072]{2,1,0:T(4,128)(2,1)S(1)} %slice.50), channel_id=1, source_target_pairs={{0,9},{1,10},{2,11},{3,12},{4,13},{5,14},{6,15},{7,8},{8,17},{9,18... | collective-permute-start | bytes 294920 | tf_op jit(solution)/shard_map/ppermute | solution.py:256
  126.8 14.5 %collective-permute-start.12 = (f32[16,768]{1,0:T(8,128)S(1)}, f32[16,768]{1,0:T(8,128)S(1)}, u32[]{:S(2)}, u32[]{:S(2)}) collective-permute-start(f32[16,768]{1,0:T(8,128)S(1)} %constant_dynamic-update-slice_fusion.8), channel_id=1, source_target_pairs={{0,16},{8,24},{16,0},{24,8},{1,17},{9,25},{17,1},{25,9},{2,18},{10... | collective-permute-start | bytes 147464 | tf_op jit(solution)/shard_map/ppermute | solution.py:210
  141.3 4.0 %collective-permute-start.13 = (f32[32,768]{1,0:T(8,128)S(1)}, f32[32,768]{1,0:T(8,128)S(1)}, u32[]{:S(2)}, u32[]{:S(2)}) collective-permute-start(f32[32,768]{1,0:T(8,128)S(1)} %constant_dynamic-update-slice_fusion.6), channel_id=1, source_target_pairs={{0,8},{8,0},{16,24},{24,16},{1,9},{9,1},{17,25},{25,17},{2,10},{10... | collective-permute-start | bytes 294920 | tf_op jit(solution)/shard_map/ppermute | solution.py:210
  145.3 5.2 %collective-permute-start.14 = (f32[64,768]{1,0:T(8,128)S(1)}, f32[64,768]{1,0:T(8,128)S(1)}, u32[]{:S(2)}, u32[]{:S(2)}) collective-permute-start(f32[64,768]{1,0:T(8,128)S(1)} %constant_dynamic-update-slice_fusion.4), channel_id=1, source_target_pairs={{0,4},{2,6},{4,0},{6,2},{1,5},{3,7},{5,1},{7,3},{8,12},{10,14},{12... | collective-permute-start | bytes 589832 | tf_op jit(solution)/shard_map/ppermute | solution.py:210
  150.6 4.1 %collective-permute-start.15 = (f32[128,768]{1,0:T(8,128)S(1)}, f32[128,768]{1,0:T(8,128)S(1)}, u32[]{:S(2)}, u32[]{:S(2)}) collective-permute-start(f32[128,768]{1,0:T(8,128)S(1)} %constant_dynamic-update-slice_fusion.2), channel_id=1, source_target_pairs={{0,2},{2,0},{4,6},{6,4},{1,3},{3,1},{5,7},{7,5},{8,10},{10,8},{12,... | collective-permute-start | bytes 1179656 | tf_op jit(solution)/shard_map/ppermute | solution.py:210

commit v17 on v15

--- a/solution.py
+++ b/solution.py
@@ -194,7 +194,7 @@
     )(*arrays, krow, gain_row, wqkv, wp, *partial)
 
 
-SUM_AXES = ("gy", "gx", "gz")
+SUM_AXES = ("gy", "gz", "gx")
 
 
 def swapped(block, axis, distance):

time: 156 us -> 154 us (0.987)
    ppermute x10, starting transfers between devices: 9.77 us -> 7.91 us  [swapped(): lax.ppermute(block, axis, [(i, i ^ distance) for i in range(lax.axis_size...]
    ppermute x6, starting transfers between devices: 13.9 us -> 15.6 us  [moved(): lax.ppermute(block, ('gx', 'gy', 'gz'), halo_route(distance_a, distance_b))]
where the time goes in v17:
time: 154 us; the launch traced here: 153 us
  Pallas kernels  74.2 us (48%)
  waiting for transfers between devices  29.3 us (19%)
  starting transfers between devices  23.5 us (15%)
  other arithmetic  15.9 us (10%)
  local copies, waits for them, and re-layouts  9.13 us (6%)
    pallas_call x2, Pallas kernels, window_grads(): pl.pallas_call(make_window_kernel(first), out_shape=[jax.ShapeDtypeStruct...  74.2 us
    ppermute x10, waiting for transfers between devices, swapped(): lax.ppermute(block, axis, [(i, i ^ distance) for i in range(lax.axis_size...  29.3 us
    ppermute x6, starting transfers between devices, moved(): lax.ppermute(block, ('gx', 'gy', 'gz'), halo_route(distance_a, distance_b))  15.6 us
    ppermute x10, starting transfers between devices, swapped(): lax.ppermute(block, axis, [(i, i ^ distance) for i in range(lax.axis_size...  7.91 us
    another operation x4, other arithmetic, per_device(): both = shifted_block(jnp.stack([tokens, grads_out]))  4.85 us
    concatenate x1, other arithmetic, shifted_block(): return jnp.concatenate([upper, lower], axis=1)  3.35 us
  transfers between devices with their start and end apart: 16, of which 8 were waited for; matrix products, arithmetic and copies ran while one was open for 6% of the time, Pallas kernels for 13%

profile of v17, /device:TPU:5, one launch (start us, length us, event | category | flops | bytes accessed | tf_op | source)
XLA Modules:
  0.0 153.0 jit_solution(1685865608108492545)
XLA Ops:
  0.7 1.5 fusion.2
  2.2 1.3 copy.12
  3.5 3.3 %collective-permute-start.1 = (bf16[2,4,12,3072]{3,1,2,0:T(4,128)(2,1)}, bf16[2,4,12,3072]{3,1,2,0:T(4,128)(2,1)}, u32[]{:S(2)}, u32[]{:S(2)}) collective-permute-start(bf16[2,4,12,3072]{3,1,2,0:T(4,128)(2,1)} %copy.12), channel_id=1, source_target_pairs={{0,24},{1,25},{2,26},{3,27},{4,28},{5,29},{6,30},{7,31},{8,0},{9,1... | collective-permute-start | bytes 1769480 | tf_op jit(solution)/shard_map/ppermute | solution.py:247
  6.8 1.0 fusion.3
  7.8 0.2 collective-permute-start
  8.1 2.0 %collective-permute-start.2 = (bf16[2,4,4,3072]{3,2,1,0:T(4,128)(2,1)S(1)}, bf16[2,4,4,3072]{3,2,1,0:T(4,128)(2,1)S(1)}, u32[]{:S(2)}, u32[]{:S(2)}) collective-permute-start(bf16[2,4,4,3072]{3,2,1,0:T(4,128)(2,1)S(1)} %pad_maximum_fusion), channel_id=1, source_target_pairs={{0,31},{1,24},{2,25},{3,26},{4,27},{5,28},{6,29},{7,30},{8,7},{9,0... | collective-permute-start | bytes 589832 | tf_op jit(solution)/shard_map/ppermute | solution.py:247
  10.2 2.2 %fusion.1 = bf16[2,12,12,3072]{3,2,1,0:T(8,128)(2,1)} fusion(bf16[1,16,16,3072]{3,2,1,0:T(8,128)(2,1)S(1)} %bitcast.15, bf16[1,16,16,3072]{3,2,1,0:T(8,128)(2,1)S(1)} %bitcast.11), kind=kLoop, calls=%fused_computation.9 | loop fusion | flops 884736 | bytes 4915200 | tf_op jit(solution)/shard_map/stack | solution.py:274
  12.6 0.2 reshape.74
  12.8 0.2 copy.14
  12.9 0.8 broadcast_in_dim_reshape.3.refs_2_.refs_1_
  13.7 19.6 %shard_map.93 = (f32[8,8,3072]{2,1,0:T(8,128)}, f32[192,576]{1,0:T(8,128)}, f32[192,192]{1,0:T(8,128)}, f32[192,1]{1,0:T(8,128)}) custom-call(bf16[16,16,3072]{2,1,0:T(8,128)(2,1)} %refs_0_.1, bf16[16,16,3072]{2,1,0:T(8,128)(2,1)} %refs_1_.1, s32[8,1,512]{2,1,0:T(1,128)} %broadcast_in_dim_reshape.3.refs_2_.refs_1_, f32[1,192]{1,0:T(1,128)} %bitcast.18, ...), custom_call_target="tpu_custom_call" | custom-call | tf_op jit(solution)/shard_map/pallas_call | solution.py:180
  33.3 1.3 copy.13
  34.6 3.3 %maximum_maximum_fusion.refs_0_ = bf16[2,16,16,3072]{3,2,1,0:T(8,128)(2,1)} fusion(bf16[2,4,4,3072]{3,2,1,0:T(4,128)(2,1)S(1)} %collective-permute-done.2, bf16[2,4,12,3072]{3,2,1,0:T(8,128)(2,1)S(1)} %copy.13, bf16[2,12,4,3072]{3,2,1,0:T(4,128)(2,1)} %collective-permute-done, bf16[2,12,12,3072]{3,2,1,0:T(8,128)(2,1)S(1)} %copy-done.4), kind=kLoop, calls=%fused_computation.6 | loop fusion | flops 12582912 | bytes 6291456 | tf_op jit(solution)/shard_map/concatenate | solution.py:256
  38.0 54.5 %shard_map.94 = (f32[16,16,3072]{2,1,0:T(8,128)}, f32[192,576]{1,0:T(8,128)}, f32[192,192]{1,0:T(8,128)}, f32[192,1]{1,0:T(8,128)}) custom-call(bf16[2,16,16,3072]{3,2,1,0:T(8,128)(2,1)} %maximum_maximum_fusion.refs_0_, s32[8,1,512]{2,1,0:T(1,128)} %broadcast_in_dim_reshape.3.refs_2_.refs_1_, f32[1,192]{1,0:T(1,128)} %bitcast.19, bf16[192,576]{1,0:T(8,128)(2,1)} %refs_3_.1, ...), custom_call_target="tpu_custom_call" | custom-call | tf_op jit(solution)/shard_map/pallas_call | solution.py:180
  92.5 1.1 reduce
  93.7 1.3 select_maximum_fusion
  94.9 0.8 copy-done.5
  95.8 0.8 collective-permute-start.6
  96.6 1.5 collective-permute-done.6
  98.1 1.1 fusion.4
  99.2 0.7 constant_dynamic-slice_fusion.3
  99.9 0.8 collective-permute-start.7
  100.7 5.5 %collective-permute-done.7 = f32[64,768]{1,0:T(8,128)} collective-permute-done((f32[64,768]{1,0:T(8,128)}, f32[64,768]{1,0:T(8,128)}, u32[]{:S(2)}, u32[]{:S(2)}) %collective-permute-start.7) | collective-permute-done | bytes 196640 | tf_op jit(solution)/shard_map/ppermute | solution.py:201
  106.3 0.9 dynamic-slice_add_fusion
  107.2 0.7 copy-done.6
  107.9 0.4 collective-permute-start.8
  108.3 3.1 %collective-permute-done.8 = f32[32,768]{1,0:T(8,128)S(1)} collective-permute-done((f32[32,768]{1,0:T(8,128)S(1)}, f32[32,768]{1,0:T(8,128)S(1)}, u32[]{:S(2)}, u32[]{:S(2)}) %collective-permute-start.8) | collective-permute-done | bytes 98336 | tf_op jit(solution)/shard_map/ppermute | solution.py:201
  111.4 0.9 dynamic-slice_add_fusion.1
  112.4 1.4 collective-permute-start.9
  113.7 1.6 %collective-permute-done.9 = f32[16,768]{1,0:T(8,128)S(1)} collective-permute-done((f32[16,768]{1,0:T(8,128)S(1)}, f32[16,768]{1,0:T(8,128)S(1)}, u32[]{:S(2)}, u32[]{:S(2)}) %collective-permute-start.9) | collective-permute-done | bytes 49184 | tf_op jit(solution)/shard_map/ppermute | solution.py:201
  115.5 3.6 %collective-permute-done.10 = f32[8,768]{1,0:T(8,128)S(1)} collective-permute-done((f32[8,768]{1,0:T(8,128)S(1)}, f32[8,768]{1,0:T(8,128)S(1)}, u32[]{:S(2)}, u32[]{:S(2)}) %collective-permute-start.10) | collective-permute-done | bytes 24608 | tf_op jit(solution)/shard_map/ppermute | solution.py:201
  119.1 0.2 convert_element_type.31
  119.5 0.2 slice.56
  119.6 0.2 slice.44
  119.9 1.5 collective-permute-start.4
  121.4 7.3 %collective-permute-start.3 = (bf16[4,4,3072]{2,1,0:T(4,128)(2,1)S(1)}, bf16[4,4,3072]{2,1,0:T(4,128)(2,1)S(1)}, u32[]{:S(2)}, u32[]{:S(2)}) collective-permute-start(bf16[4,4,3072]{2,1,0:T(4,128)(2,1)S(1)} %slice.54), channel_id=1, source_target_pairs={{0,9},{1,10},{2,11},{3,12},{4,13},{5,14},{6,15},{7,8},{8,17},{9,18... | collective-permute-start | bytes 294920 | tf_op jit(solution)/shard_map/ppermute | solution.py:247
  128.6 1.2 collective-permute-start.5
  129.9 1.3 collective-permute-start.12
  131.2 6.0 %collective-permute-done.12 = f32[16,768]{1,0:T(8,128)S(1)} collective-permute-done((f32[16,768]{1,0:T(8,128)S(1)}, f32[16,768]{1,0:T(8,128)S(1)}, u32[]{:S(2)}, u32[]{:S(2)}) %collective-permute-start.12) | collective-permute-done | bytes 49184 | tf_op jit(solution)/shard_map/ppermute | solution.py:201
  137.2 3.9 %collective-permute-done.13 = f32[32,768]{1,0:T(8,128)S(1)} collective-permute-done((f32[32,768]{1,0:T(8,128)S(1)}, f32[32,768]{1,0:T(8,128)S(1)}, u32[]{:S(2)}, u32[]{:S(2)}) %collective-permute-start.13) | collective-permute-done | bytes 98336 | tf_op jit(solution)/shard_map/ppermute | solution.py:201
  141.1 0.8 collective-permute-start.14
  142.0 0.1 maximum_convert_fusion
  142.2 4.1 %collective-permute-done.14 = f32[64,768]{1,0:T(8,128)S(1)} collective-permute-done((f32[64,768]{1,0:T(8,128)S(1)}, f32[64,768]{1,0:T(8,128)S(1)}, u32[]{:S(2)}, u32[]{:S(2)}) %collective-permute-start.14) | collective-permute-done | bytes 196640 | tf_op jit(solution)/shard_map/ppermute | solution.py:201
  146.4 2.2 %collective-permute-start.15 = (f32[128,768]{1,0:T(8,128)S(1)}, f32[128,768]{1,0:T(8,128)S(1)}, u32[]{:S(2)}, u32[]{:S(2)}) collective-permute-start(f32[128,768]{1,0:T(8,128)S(1)} %constant_dynamic-update-slice_fusion.2), channel_id=1, source_target_pairs={{0,2},{2,0},{4,6},{6,4},{1,3},{3,1},{5,7},{7,5},{8,10},{10,8},{12,... | collective-permute-start | bytes 1179656 | tf_op jit(solution)/shard_map/ppermute | solution.py:201
  148.6 1.8 %fusion = bf16[16,16,3072]{2,1,0:T(8,128)(2,1)} fusion(f32[12,12,3072]{2,1,0:T(8,128)S(1)} %slice.44, f32[12,4,3072]{2,1,0:T(4,128)S(1)} %convert_element_type.32, f32[4,16,3072]{2,1,0:T(8,128)S(1)} %maximum_convert_fusion, bf16[16,16,3072]{2,1,0:T(8,128)(2,1)S(1)} %copy-done.1), kind=kLoop, calls=%fused_computation.8 | loop fusion | flops 3932160 | bytes 6291456 | tf_op jit(solution)/shard_map/convert_element_type | solution.py:267
  150.7 0.6 slice.57
  151.3 1.0 reshape.77
  152.3 0.8 reshape.78
  (55 shorter events, 1.1 us)
Async XLA Ops:
  0.6 6.1 %copy-start.2 = (bf16[16,16,3072]{2,1,0:T(8,128)(2,1)S(1)}, bf16[16,16,3072]{2,1,0:T(8,128)(2,1)}, u32[]{:S(2)}) copy-start(bf16[16,16,3072]{2,1,0:T(8,128)(2,1)} %refs_0_.1) | copy-start | bytes 4718596
  0.6 6.1 %copy-start = (bf16[16,16,3072]{2,1,0:T(8,128)(2,1)S(1)}, bf16[16,16,3072]{2,1,0:T(8,128)(2,1)}, u32[]{:S(2)}) copy-start(bf16[16,16,3072]{2,1,0:T(8,128)(2,1)} %refs_1_.1) | copy-start | bytes 4718596
  3.5 29.9 %collective-permute-start.1 = (bf16[2,4,12,3072]{3,1,2,0:T(4,128)(2,1)}, bf16[2,4,12,3072]{3,1,2,0:T(4,128)(2,1)}, u32[]{:S(2)}, u32[]{:S(2)}) collective-permute-start(bf16[2,4,12,3072]{3,1,2,0:T(4,128)(2,1)} %copy.12), channel_id=1, source_target_pairs={{0,24},{1,25},{2,26},{3,27},{4,28},{5,29},{6,30},{7,31},{8,0},{9,1... | collective-permute-start | bytes 1769480 | tf_op jit(solution)/shard_map/ppermute | solution.py:247
  7.8 26.8 %collective-permute-start = (bf16[2,12,4,3072]{3,2,1,0:T(4,128)(2,1)}, bf16[2,12,4,3072]{3,2,1,0:T(4,128)(2,1)}, u32[]{:S(2)}, u32[]{:S(2)}) collective-permute-start(bf16[2,12,4,3072]{3,2,1,0:T(4,128)(2,1)} %fusion.3), channel_id=1, source_target_pairs={{0,7},{1,0},{2,1},{3,2},{4,3},{5,4},{6,5},{7,6},{8,15},{9,8},{10,9... | collective-permute-start | bytes 1769480 | tf_op jit(solution)/shard_map/ppermute | solution.py:247
  8.1 26.5 %collective-permute-start.2 = (bf16[2,4,4,3072]{3,2,1,0:T(4,128)(2,1)S(1)}, bf16[2,4,4,3072]{3,2,1,0:T(4,128)(2,1)S(1)}, u32[]{:S(2)}, u32[]{:S(2)}) collective-permute-start(bf16[2,4,4,3072]{3,2,1,0:T(4,128)(2,1)S(1)} %pad_maximum_fusion), channel_id=1, source_target_pairs={{0,31},{1,24},{2,25},{3,26},{4,27},{5,28},{6,29},{7,30},{8,7},{9,0... | collective-permute-start | bytes 589832 | tf_op jit(solution)/shard_map/ppermute | solution.py:247
  10.1 2.3 %copy-start.7 = (s32[16,16,16]{2,1,0:T(8,128)S(1)}, s32[16,16,16]{2,1,0:T(8,128)}, u32[]{:S(2)}) copy-start(s32[16,16,16]{2,1,0:T(8,128)} %param.8) | copy-start | bytes 49156
  12.5 22.2 %copy-start.4 = (bf16[2,12,12,3072]{3,2,1,0:T(8,128)(2,1)S(1)}, bf16[2,12,12,3072]{3,2,1,0:T(8,128)(2,1)}, u32[]{:S(2)}) copy-start(bf16[2,12,12,3072]{3,2,1,0:T(8,128)(2,1)} %fusion.1) | copy-start | bytes 5308420
  92.5 26.6 %copy-start.3 = (f32[16,16,3072]{2,1,0:T(8,128)S(1)}, f32[16,16,3072]{2,1,0:T(8,128)}, u32[]{:S(2)}) copy-start(f32[16,16,3072]{2,1,0:T(8,128)} %get-tuple-element.16) | copy-start | bytes 9437188
  94.9 0.8 copy-start.5
  95.8 2.3 %collective-permute-start.6 = (f32[128,768]{1,0:T(8,128)S(1)}, f32[128,768]{1,0:T(8,128)}, u32[]{:S(2)}, u32[]{:S(2)}) collective-permute-start(f32[128,768]{1,0:T(8,128)S(1)} %pad_dynamic-slice_fusion), channel_id=1, source_target_pairs={{0,2},{2,0},{4,6},{6,4},{1,3},{3,1},{5,7},{7,5},{8,10},{10,8},{12,... | collective-permute-start | bytes 1179656 | tf_op jit(solution)/shard_map/ppermute | solution.py:201
  99.9 6.4 %collective-permute-start.7 = (f32[64,768]{1,0:T(8,128)}, f32[64,768]{1,0:T(8,128)}, u32[]{:S(2)}, u32[]{:S(2)}) collective-permute-start(f32[64,768]{1,0:T(8,128)} %constant_dynamic-slice_fusion.3), channel_id=1, source_target_pairs={{0,4},{2,6},{4,0},{6,2},{1,5},{3,7},{5,1},{7,3},{8,12},{10,14},{12... | collective-permute-start | bytes 589832 | tf_op jit(solution)/shard_map/ppermute | solution.py:201
  107.2 0.7 copy-start.6
  107.9 3.5 %collective-permute-start.8 = (f32[32,768]{1,0:T(8,128)S(1)}, f32[32,768]{1,0:T(8,128)S(1)}, u32[]{:S(2)}, u32[]{:S(2)}) collective-permute-start(f32[32,768]{1,0:T(8,128)S(1)} %constant_dynamic-slice_fusion.2), channel_id=1, source_target_pairs={{0,1},{1,0},{2,3},{3,2},{4,5},{5,4},{6,7},{7,6},{8,9},{9,8},{10,11... | collective-permute-start | bytes 294920 | tf_op jit(solution)/shard_map/ppermute | solution.py:201
  112.4 3.0 %collective-permute-start.9 = (f32[16,768]{1,0:T(8,128)S(1)}, f32[16,768]{1,0:T(8,128)S(1)}, u32[]{:S(2)}, u32[]{:S(2)}) collective-permute-start(f32[16,768]{1,0:T(8,128)S(1)} %constant_dynamic-slice_fusion.1), channel_id=1, source_target_pairs={{0,8},{8,0},{16,24},{24,16},{1,9},{9,1},{17,25},{25,17},{2,10},{10... | collective-permute-start | bytes 147464 | tf_op jit(solution)/shard_map/ppermute | solution.py:201
  115.4 3.6 %collective-permute-start.10 = (f32[8,768]{1,0:T(8,128)S(1)}, f32[8,768]{1,0:T(8,128)S(1)}, u32[]{:S(2)}, u32[]{:S(2)}) collective-permute-start(f32[8,768]{1,0:T(8,128)S(1)} %constant_dynamic-slice_fusion), channel_id=1, source_target_pairs={{0,16},{8,24},{16,0},{24,8},{1,17},{9,25},{17,1},{25,9},{2,18},{10... | collective-permute-start | bytes 73736 | tf_op jit(solution)/shard_map/ppermute | solution.py:201
  119.1 10.8 %collective-permute-start.11 = (f32[8,768]{1,0:T(8,128)S(1)}, f32[8,768]{1,0:T(8,128)S(1)}, u32[]{:S(2)}, u32[]{:S(2)}) collective-permute-start(f32[8,768]{1,0:T(8,128)S(1)} %get-tuple-element.21), channel_id=1, source_target_pairs={{0,16},{8,24},{16,0},{24,8},{1,17},{9,25},{17,1},{25,9},{2,18},{10... | collective-permute-start | bytes 73736 | tf_op jit(solution)/shard_map/ppermute | solution.py:201
  119.9 28.8 %copy-start.1 = (bf16[16,16,3072]{2,1,0:T(8,128)(2,1)S(1)}, bf16[16,16,3072]{2,1,0:T(8,128)(2,1)}, u32[]{:S(2)}) copy-start(bf16[16,16,3072]{2,1,0:T(8,128)(2,1)} %refs_1_.1) | copy-start | bytes 4718596
  119.9 22.1 %collective-permute-start.4 = (bf16[4,12,3072]{2,1,0:T(8,128)(2,1)S(1)}, bf16[4,12,3072]{2,1,0:T(8,128)(2,1)S(1)}, u32[]{:S(2)}, u32[]{:S(2)}) collective-permute-start(bf16[4,12,3072]{2,1,0:T(8,128)(2,1)S(1)} %slice.55), channel_id=1, source_target_pairs={{0,8},{1,9},{2,10},{3,11},{4,12},{5,13},{6,14},{7,15},{8,16},{9,17... | collective-permute-start | bytes 884744 | tf_op jit(solution)/shard_map/ppermute | solution.py:247
  121.4 20.6 %collective-permute-start.3 = (bf16[4,4,3072]{2,1,0:T(4,128)(2,1)S(1)}, bf16[4,4,3072]{2,1,0:T(4,128)(2,1)S(1)}, u32[]{:S(2)}, u32[]{:S(2)}) collective-permute-start(bf16[4,4,3072]{2,1,0:T(4,128)(2,1)S(1)} %slice.54), channel_id=1, source_target_pairs={{0,9},{1,10},{2,11},{3,12},{4,13},{5,14},{6,15},{7,8},{8,17},{9,18... | collective-permute-start | bytes 294920 | tf_op jit(solution)/shard_map/ppermute | solution.py:247
  128.6 13.5 %collective-permute-start.5 = (bf16[12,4,3072]{2,1,0:T(4,128)(2,1)S(1)}, bf16[12,4,3072]{2,1,0:T(4,128)(2,1)S(1)}, u32[]{:S(2)}, u32[]{:S(2)}) collective-permute-start(bf16[12,4,3072]{2,1,0:T(4,128)(2,1)S(1)} %slice.56), channel_id=1, source_target_pairs={{0,1},{1,2},{2,3},{3,4},{4,5},{5,6},{6,7},{7,0},{8,9},{9,10},{10,1... | collective-permute-start | bytes 884744 | tf_op jit(solution)/shard_map/ppermute | solution.py:247
  129.9 7.3 %collective-permute-start.12 = (f32[16,768]{1,0:T(8,128)S(1)}, f32[16,768]{1,0:T(8,128)S(1)}, u32[]{:S(2)}, u32[]{:S(2)}) collective-permute-start(f32[16,768]{1,0:T(8,128)S(1)} %constant_dynamic-update-slice_fusion.8), channel_id=1, source_target_pairs={{0,8},{8,0},{16,24},{24,16},{1,9},{9,1},{17,25},{25,17},{2,10},{10... | collective-permute-start | bytes 147464 | tf_op jit(solution)/shard_map/ppermute | solution.py:201
  137.2 4.0 %collective-permute-start.13 = (f32[32,768]{1,0:T(8,128)S(1)}, f32[32,768]{1,0:T(8,128)S(1)}, u32[]{:S(2)}, u32[]{:S(2)}) collective-permute-start(f32[32,768]{1,0:T(8,128)S(1)} %constant_dynamic-update-slice_fusion.6), channel_id=1, source_target_pairs={{0,1},{1,0},{2,3},{3,2},{4,5},{5,4},{6,7},{7,6},{8,9},{9,8},{10,11... | collective-permute-start | bytes 294920 | tf_op jit(solution)/shard_map/ppermute | solution.py:201
  141.1 5.2 %collective-permute-start.14 = (f32[64,768]{1,0:T(8,128)S(1)}, f32[64,768]{1,0:T(8,128)S(1)}, u32[]{:S(2)}, u32[]{:S(2)}) collective-permute-start(f32[64,768]{1,0:T(8,128)S(1)} %constant_dynamic-update-slice_fusion.4), channel_id=1, source_target_pairs={{0,4},{2,6},{4,0},{6,2},{1,5},{3,7},{5,1},{7,3},{8,12},{10,14},{12... | collective-permute-start | bytes 589832 | tf_op jit(solution)/shard_map/ppermute | solution.py:201
  146.4 4.1 %collective-permute-start.15 = (f32[128,768]{1,0:T(8,128)S(1)}, f32[128,768]{1,0:T(8,128)S(1)}, u32[]{:S(2)}, u32[]{:S(2)}) collective-permute-start(f32[128,768]{1,0:T(8,128)S(1)} %constant_dynamic-update-slice_fusion.2), channel_id=1, source_target_pairs={{0,2},{2,0},{4,6},{6,4},{1,3},{3,1},{5,7},{7,5},{8,10},{10,8},{12,... | collective-permute-start | bytes 1179656 | tf_op jit(solution)/shard_map/ppermute | solution.py:201

commit v18 on v17

--- a/solution.py
+++ b/solution.py
@@ -194,7 +194,7 @@
     )(*arrays, krow, gain_row, wqkv, wp, *partial)
 
 
-SUM_AXES = ("gy", "gz", "gx")
+SUM_AXES = ("gz", "gy", "gx")
 
 
 def swapped(block, axis, distance):

time: 154 us -> 163 us (1.058)
  waiting for transfers between devices: 29.3 us -> 35.9 us
    ppermute x10, waiting for transfers between devices: 29.3 us -> 35.9 us  [swapped(): lax.ppermute(block, axis, [(i, i ^ distance) for i in range(lax.axis_size...]
    ppermute x10, starting transfers between devices: 7.91 us -> 10.8 us  [swapped(): lax.ppermute(block, axis, [(i, i ^ distance) for i in range(lax.axis_size...]
  transfers between devices with their start and end apart: 16 -> 16, of which waited for: 8 -> 9; matrix products, arithmetic and copies ran while one was open for 6% -> 5% of each run, Pallas kernels for 13% -> 12%
where the time goes in v18:
time: 163 us; the launch traced here: 161 us
  Pallas kernels  74.2 us (46%)
  waiting for transfers between devices  35.9 us (22%)
  starting transfers between devices  25.1 us (15%)
  other arithmetic  15.9 us (10%)
  local copies, waits for them, and re-layouts  9.13 us (6%)
    pallas_call x2, Pallas kernels, window_grads(): pl.pallas_call(make_window_kernel(first), out_shape=[jax.ShapeDtypeStruct...  74.2 us
    ppermute x10, waiting for transfers between devices, swapped(): lax.ppermute(block, axis, [(i, i ^ distance) for i in range(lax.axis_size...  35.9 us
    ppermute x6, starting transfers between devices, moved(): lax.ppermute(block, ('gx', 'gy', 'gz'), halo_route(distance_a, distance_b))  14.3 us
    ppermute x10, starting transfers between devices, swapped(): lax.ppermute(block, axis, [(i, i ^ distance) for i in range(lax.axis_size...  10.8 us
    another operation x4, other arithmetic, per_device(): both = shifted_block(jnp.stack([tokens, grads_out]))  4.85 us
    concatenate x1, other arithmetic, shifted_block(): return jnp.concatenate([upper, lower], axis=1)  3.35 us
  transfers between devices with their start and end apart: 16, of which 9 were waited for; matrix products, arithmetic and copies ran while one was open for 5% of the time, Pallas kernels for 12%

profile of v18, /device:TPU:5, one launch (start us, length us, event | category | flops | bytes accessed | tf_op | source)
XLA Modules:
  0.0 161.2 jit_solution(11199822790506771895)
XLA Ops:
  0.7 1.5 fusion.2
  2.2 1.3 copy.12
  3.5 3.3 %collective-permute-start.1 = (bf16[2,4,12,3072]{3,1,2,0:T(4,128)(2,1)}, bf16[2,4,12,3072]{3,1,2,0:T(4,128)(2,1)}, u32[]{:S(2)}, u32[]{:S(2)}) collective-permute-start(bf16[2,4,12,3072]{3,1,2,0:T(4,128)(2,1)} %copy.12), channel_id=1, source_target_pairs={{0,24},{1,25},{2,26},{3,27},{4,28},{5,29},{6,30},{7,31},{8,0},{9,1... | collective-permute-start | bytes 1769480 | tf_op jit(solution)/shard_map/ppermute | solution.py:247
  6.8 1.0 fusion.3
  7.8 0.2 collective-permute-start
  8.1 2.0 %collective-permute-start.2 = (bf16[2,4,4,3072]{3,2,1,0:T(4,128)(2,1)S(1)}, bf16[2,4,4,3072]{3,2,1,0:T(4,128)(2,1)S(1)}, u32[]{:S(2)}, u32[]{:S(2)}) collective-permute-start(bf16[2,4,4,3072]{3,2,1,0:T(4,128)(2,1)S(1)} %pad_maximum_fusion), channel_id=1, source_target_pairs={{0,31},{1,24},{2,25},{3,26},{4,27},{5,28},{6,29},{7,30},{8,7},{9,0... | collective-permute-start | bytes 589832 | tf_op jit(solution)/shard_map/ppermute | solution.py:247
  10.2 2.2 %fusion.1 = bf16[2,12,12,3072]{3,2,1,0:T(8,128)(2,1)} fusion(bf16[1,16,16,3072]{3,2,1,0:T(8,128)(2,1)S(1)} %bitcast.15, bf16[1,16,16,3072]{3,2,1,0:T(8,128)(2,1)S(1)} %bitcast.11), kind=kLoop, calls=%fused_computation.9 | loop fusion | flops 884736 | bytes 4915200 | tf_op jit(solution)/shard_map/stack | solution.py:274
  12.6 0.2 reshape.74
  12.9 0.8 broadcast_in_dim_reshape.3.refs_2_.refs_1_
  13.7 19.6 %shard_map.93 = (f32[8,8,3072]{2,1,0:T(8,128)}, f32[192,576]{1,0:T(8,128)}, f32[192,192]{1,0:T(8,128)}, f32[192,1]{1,0:T(8,128)}) custom-call(bf16[16,16,3072]{2,1,0:T(8,128)(2,1)} %refs_0_.1, bf16[16,16,3072]{2,1,0:T(8,128)(2,1)} %refs_1_.1, s32[8,1,512]{2,1,0:T(1,128)} %broadcast_in_dim_reshape.3.refs_2_.refs_1_, f32[1,192]{1,0:T(1,128)} %bitcast.18, ...), custom_call_target="tpu_custom_call" | custom-call | tf_op jit(solution)/shard_map/pallas_call | solution.py:180
  33.3 1.3 copy.13
  34.6 3.3 %maximum_maximum_fusion.refs_0_ = bf16[2,16,16,3072]{3,2,1,0:T(8,128)(2,1)} fusion(bf16[2,4,4,3072]{3,2,1,0:T(4,128)(2,1)S(1)} %collective-permute-done.2, bf16[2,4,12,3072]{3,2,1,0:T(8,128)(2,1)S(1)} %copy.13, bf16[2,12,4,3072]{3,2,1,0:T(4,128)(2,1)} %collective-permute-done, bf16[2,12,12,3072]{3,2,1,0:T(8,128)(2,1)S(1)} %copy-done.4), kind=kLoop, calls=%fused_computation.6 | loop fusion | flops 12582912 | bytes 6291456 | tf_op jit(solution)/shard_map/concatenate | solution.py:256
  38.0 54.5 %shard_map.94 = (f32[16,16,3072]{2,1,0:T(8,128)}, f32[192,576]{1,0:T(8,128)}, f32[192,192]{1,0:T(8,128)}, f32[192,1]{1,0:T(8,128)}) custom-call(bf16[2,16,16,3072]{3,2,1,0:T(8,128)(2,1)} %maximum_maximum_fusion.refs_0_, s32[8,1,512]{2,1,0:T(1,128)} %broadcast_in_dim_reshape.3.refs_2_.refs_1_, f32[1,192]{1,0:T(1,128)} %bitcast.19, bf16[192,576]{1,0:T(8,128)(2,1)} %refs_3_.1, ...), custom_call_target="tpu_custom_call" | custom-call | tf_op jit(solution)/shard_map/pallas_call | solution.py:180
  92.5 1.1 reduce
  93.7 1.3 select_maximum_fusion
  94.9 0.8 copy-done.5
  95.8 0.6 collective-permute-start.6
  96.4 9.5 %collective-permute-done.6 = f32[128,768]{1,0:T(8,128)} collective-permute-done((f32[128,768]{1,0:T(8,128)S(1)}, f32[128,768]{1,0:T(8,128)}, u32[]{:S(2)}, u32[]{:S(2)}) %collective-permute-start.6) | collective-permute-done | bytes 393248 | tf_op jit(solution)/shard_map/ppermute | solution.py:201
  105.9 1.1 fusion.4
  107.0 0.7 constant_dynamic-slice_fusion.3
  107.7 1.6 %collective-permute-start.7 = (f32[64,768]{1,0:T(8,128)}, f32[64,768]{1,0:T(8,128)}, u32[]{:S(2)}, u32[]{:S(2)}) collective-permute-start(f32[64,768]{1,0:T(8,128)} %constant_dynamic-slice_fusion.3), channel_id=1, source_target_pairs={{0,2},{2,0},{4,6},{6,4},{1,3},{3,1},{5,7},{7,5},{8,10},{10,8},{12,... | collective-permute-start | bytes 589832 | tf_op jit(solution)/shard_map/ppermute | solution.py:201
  109.3 1.4 collective-permute-done.7
  110.7 0.9 dynamic-slice_add_fusion
  111.7 0.7 copy-done.6
  112.4 1.3 collective-permute-start.8
  113.6 2.8 %collective-permute-done.8 = f32[32,768]{1,0:T(8,128)S(1)} collective-permute-done((f32[32,768]{1,0:T(8,128)S(1)}, f32[32,768]{1,0:T(8,128)S(1)}, u32[]{:S(2)}, u32[]{:S(2)}) %collective-permute-start.8) | collective-permute-done | bytes 98336 | tf_op jit(solution)/shard_map/ppermute | solution.py:201
  116.4 0.9 dynamic-slice_add_fusion.1
  117.4 1.4 collective-permute-start.9
  118.7 1.6 %collective-permute-done.9 = f32[16,768]{1,0:T(8,128)S(1)} collective-permute-done((f32[16,768]{1,0:T(8,128)S(1)}, f32[16,768]{1,0:T(8,128)S(1)}, u32[]{:S(2)}, u32[]{:S(2)}) %collective-permute-start.9) | collective-permute-done | bytes 49184 | tf_op jit(solution)/shard_map/ppermute | solution.py:201
  120.5 3.6 %collective-permute-done.10 = f32[8,768]{1,0:T(8,128)S(1)} collective-permute-done((f32[8,768]{1,0:T(8,128)S(1)}, f32[8,768]{1,0:T(8,128)S(1)}, u32[]{:S(2)}, u32[]{:S(2)}) %collective-permute-start.10) | collective-permute-done | bytes 24608 | tf_op jit(solution)/shard_map/ppermute | solution.py:201
  124.0 0.3 collective-permute-start.11
  124.4 0.2 convert_element_type.31
  124.9 0.2 slice.44
  125.1 1.3 collective-permute-start.4
  126.4 5.7 %collective-permute-start.3 = (bf16[4,4,3072]{2,1,0:T(4,128)(2,1)S(1)}, bf16[4,4,3072]{2,1,0:T(4,128)(2,1)S(1)}, u32[]{:S(2)}, u32[]{:S(2)}) collective-permute-start(bf16[4,4,3072]{2,1,0:T(4,128)(2,1)S(1)} %slice.54), channel_id=1, source_target_pairs={{0,9},{1,10},{2,11},{3,12},{4,13},{5,14},{6,15},{7,8},{8,17},{9,18... | collective-permute-start | bytes 294920 | tf_op jit(solution)/shard_map/ppermute | solution.py:247
  132.1 1.8 %collective-permute-start.5 = (bf16[12,4,3072]{2,1,0:T(4,128)(2,1)S(1)}, bf16[12,4,3072]{2,1,0:T(4,128)(2,1)S(1)}, u32[]{:S(2)}, u32[]{:S(2)}) collective-permute-start(bf16[12,4,3072]{2,1,0:T(4,128)(2,1)S(1)} %slice.56), channel_id=1, source_target_pairs={{0,1},{1,2},{2,3},{3,4},{4,5},{5,6},{6,7},{7,0},{8,9},{9,10},{10,1... | collective-permute-start | bytes 884744 | tf_op jit(solution)/shard_map/ppermute | solution.py:247
  133.9 1.6 collective-permute-start.12
  135.5 5.8 %collective-permute-done.12 = f32[16,768]{1,0:T(8,128)S(1)} collective-permute-done((f32[16,768]{1,0:T(8,128)S(1)}, f32[16,768]{1,0:T(8,128)S(1)}, u32[]{:S(2)}, u32[]{:S(2)}) %collective-permute-start.12) | collective-permute-done | bytes 49184 | tf_op jit(solution)/shard_map/ppermute | solution.py:201
  141.3 1.2 collective-permute-start.13
  142.5 2.2 %collective-permute-done.13 = f32[32,768]{1,0:T(8,128)S(1)} collective-permute-done((f32[32,768]{1,0:T(8,128)S(1)}, f32[32,768]{1,0:T(8,128)S(1)}, u32[]{:S(2)}, u32[]{:S(2)}) %collective-permute-start.13) | collective-permute-done | bytes 98336 | tf_op jit(solution)/shard_map/ppermute | solution.py:201
  144.7 2.4 %collective-permute-start.14 = (f32[64,768]{1,0:T(8,128)S(1)}, f32[64,768]{1,0:T(8,128)S(1)}, u32[]{:S(2)}, u32[]{:S(2)}) collective-permute-start(f32[64,768]{1,0:T(8,128)S(1)} %constant_dynamic-update-slice_fusion.4), channel_id=1, source_target_pairs={{0,2},{2,0},{4,6},{6,4},{1,3},{3,1},{5,7},{7,5},{8,10},{10,8},{12,... | collective-permute-start | bytes 589832 | tf_op jit(solution)/shard_map/ppermute | solution.py:201
  147.5 0.8 collective-permute-done.14
  148.3 0.3 collective-permute-start.15
  148.6 1.8 %fusion = bf16[16,16,3072]{2,1,0:T(8,128)(2,1)} fusion(f32[12,12,3072]{2,1,0:T(8,128)S(1)} %slice.44, f32[12,4,3072]{2,1,0:T(4,128)S(1)} %convert_element_type.32, f32[4,16,3072]{2,1,0:T(8,128)S(1)} %maximum_convert_fusion, bf16[16,16,3072]{2,1,0:T(8,128)(2,1)S(1)} %copy-done.1), kind=kLoop, calls=%fused_computation.8 | loop fusion | flops 3932160 | bytes 6291456 | tf_op jit(solution)/shard_map/convert_element_type | solution.py:267
  150.5 8.2 %collective-permute-done.15 = f32[128,768]{1,0:T(8,128)S(1)} collective-permute-done((f32[128,768]{1,0:T(8,128)S(1)}, f32[128,768]{1,0:T(8,128)S(1)}, u32[]{:S(2)}, u32[]{:S(2)}) %collective-permute-start.15) | collective-permute-done | bytes 393248 | tf_op jit(solution)/shard_map/ppermute | solution.py:201
  158.9 0.6 slice.57
  159.4 1.0 reshape.77
  160.4 0.8 reshape.78
  (55 shorter events, 1.4 us)
Async XLA Ops:
  0.6 6.1 %copy-start.2 = (bf16[16,16,3072]{2,1,0:T(8,128)(2,1)S(1)}, bf16[16,16,3072]{2,1,0:T(8,128)(2,1)}, u32[]{:S(2)}) copy-start(bf16[16,16,3072]{2,1,0:T(8,128)(2,1)} %refs_0_.1) | copy-start | bytes 4718596
  0.6 6.1 %copy-start = (bf16[16,16,3072]{2,1,0:T(8,128)(2,1)S(1)}, bf16[16,16,3072]{2,1,0:T(8,128)(2,1)}, u32[]{:S(2)}) copy-start(bf16[16,16,3072]{2,1,0:T(8,128)(2,1)} %refs_1_.1) | copy-start | bytes 4718596
  3.5 29.9 %collective-permute-start.1 = (bf16[2,4,12,3072]{3,1,2,0:T(4,128)(2,1)}, bf16[2,4,12,3072]{3,1,2,0:T(4,128)(2,1)}, u32[]{:S(2)}, u32[]{:S(2)}) collective-permute-start(bf16[2,4,12,3072]{3,1,2,0:T(4,128)(2,1)} %copy.12), channel_id=1, source_target_pairs={{0,24},{1,25},{2,26},{3,27},{4,28},{5,29},{6,30},{7,31},{8,0},{9,1... | collective-permute-start | bytes 1769480 | tf_op jit(solution)/shard_map/ppermute | solution.py:247
  7.8 26.8 %collective-permute-start = (bf16[2,12,4,3072]{3,2,1,0:T(4,128)(2,1)}, bf16[2,12,4,3072]{3,2,1,0:T(4,128)(2,1)}, u32[]{:S(2)}, u32[]{:S(2)}) collective-permute-start(bf16[2,12,4,3072]{3,2,1,0:T(4,128)(2,1)} %fusion.3), channel_id=1, source_target_pairs={{0,7},{1,0},{2,1},{3,2},{4,3},{5,4},{6,5},{7,6},{8,15},{9,8},{10,9... | collective-permute-start | bytes 1769480 | tf_op jit(solution)/shard_map/ppermute | solution.py:247
  8.1 26.5 %collective-permute-start.2 = (bf16[2,4,4,3072]{3,2,1,0:T(4,128)(2,1)S(1)}, bf16[2,4,4,3072]{3,2,1,0:T(4,128)(2,1)S(1)}, u32[]{:S(2)}, u32[]{:S(2)}) collective-permute-start(bf16[2,4,4,3072]{3,2,1,0:T(4,128)(2,1)S(1)} %pad_maximum_fusion), channel_id=1, source_target_pairs={{0,31},{1,24},{2,25},{3,26},{4,27},{5,28},{6,29},{7,30},{8,7},{9,0... | collective-permute-start | bytes 589832 | tf_op jit(solution)/shard_map/ppermute | solution.py:247
  10.1 2.3 %copy-start.7 = (s32[16,16,16]{2,1,0:T(8,128)S(1)}, s32[16,16,16]{2,1,0:T(8,128)}, u32[]{:S(2)}) copy-start(s32[16,16,16]{2,1,0:T(8,128)} %param.8) | copy-start | bytes 49156
  12.5 22.2 %copy-start.4 = (bf16[2,12,12,3072]{3,2,1,0:T(8,128)(2,1)S(1)}, bf16[2,12,12,3072]{3,2,1,0:T(8,128)(2,1)}, u32[]{:S(2)}) copy-start(bf16[2,12,12,3072]{3,2,1,0:T(8,128)(2,1)} %fusion.1) | copy-start | bytes 5308420
  92.5 31.9 %copy-start.3 = (f32[16,16,3072]{2,1,0:T(8,128)S(1)}, f32[16,16,3072]{2,1,0:T(8,128)}, u32[]{:S(2)}) copy-start(f32[16,16,3072]{2,1,0:T(8,128)} %get-tuple-element.16) | copy-start | bytes 9437188
  94.9 0.8 copy-start.5
  95.8 10.1 %collective-permute-start.6 = (f32[128,768]{1,0:T(8,128)S(1)}, f32[128,768]{1,0:T(8,128)}, u32[]{:S(2)}, u32[]{:S(2)}) collective-permute-start(f32[128,768]{1,0:T(8,128)S(1)} %pad_dynamic-slice_fusion), channel_id=1, source_target_pairs={{0,1},{1,0},{2,3},{3,2},{4,5},{5,4},{6,7},{7,6},{8,9},{9,8},{10,11... | collective-permute-start | bytes 1179656 | tf_op jit(solution)/shard_map/ppermute | solution.py:201
  107.7 3.1 %collective-permute-start.7 = (f32[64,768]{1,0:T(8,128)}, f32[64,768]{1,0:T(8,128)}, u32[]{:S(2)}, u32[]{:S(2)}) collective-permute-start(f32[64,768]{1,0:T(8,128)} %constant_dynamic-slice_fusion.3), channel_id=1, source_target_pairs={{0,2},{2,0},{4,6},{6,4},{1,3},{3,1},{5,7},{7,5},{8,10},{10,8},{12,... | collective-permute-start | bytes 589832 | tf_op jit(solution)/shard_map/ppermute | solution.py:201
  111.7 0.7 copy-start.6
  112.4 4.1 %collective-permute-start.8 = (f32[32,768]{1,0:T(8,128)S(1)}, f32[32,768]{1,0:T(8,128)S(1)}, u32[]{:S(2)}, u32[]{:S(2)}) collective-permute-start(f32[32,768]{1,0:T(8,128)S(1)} %constant_dynamic-slice_fusion.2), channel_id=1, source_target_pairs={{0,4},{2,6},{4,0},{6,2},{1,5},{3,7},{5,1},{7,3},{8,12},{10,14},{12... | collective-permute-start | bytes 294920 | tf_op jit(solution)/shard_map/ppermute | solution.py:201
  117.4 3.0 %collective-permute-start.9 = (f32[16,768]{1,0:T(8,128)S(1)}, f32[16,768]{1,0:T(8,128)S(1)}, u32[]{:S(2)}, u32[]{:S(2)}) collective-permute-start(f32[16,768]{1,0:T(8,128)S(1)} %constant_dynamic-slice_fusion.1), channel_id=1, source_target_pairs={{0,8},{8,0},{16,24},{24,16},{1,9},{9,1},{17,25},{25,17},{2,10},{10... | collective-permute-start | bytes 147464 | tf_op jit(solution)/shard_map/ppermute | solution.py:201
  120.4 3.6 %collective-permute-start.10 = (f32[8,768]{1,0:T(8,128)S(1)}, f32[8,768]{1,0:T(8,128)S(1)}, u32[]{:S(2)}, u32[]{:S(2)}) collective-permute-start(f32[8,768]{1,0:T(8,128)S(1)} %constant_dynamic-slice_fusion), channel_id=1, source_target_pairs={{0,16},{8,24},{16,0},{24,8},{1,17},{9,25},{17,1},{25,9},{2,18},{10... | collective-permute-start | bytes 73736 | tf_op jit(solution)/shard_map/ppermute | solution.py:201
  124.0 9.8 %collective-permute-start.11 = (f32[8,768]{1,0:T(8,128)S(1)}, f32[8,768]{1,0:T(8,128)S(1)}, u32[]{:S(2)}, u32[]{:S(2)}) collective-permute-start(f32[8,768]{1,0:T(8,128)S(1)} %get-tuple-element.21), channel_id=1, source_target_pairs={{0,16},{8,24},{16,0},{24,8},{1,17},{9,25},{17,1},{25,9},{2,18},{10... | collective-permute-start | bytes 73736 | tf_op jit(solution)/shard_map/ppermute | solution.py:201
  125.1 23.5 %copy-start.1 = (bf16[16,16,3072]{2,1,0:T(8,128)(2,1)S(1)}, bf16[16,16,3072]{2,1,0:T(8,128)(2,1)}, u32[]{:S(2)}) copy-start(bf16[16,16,3072]{2,1,0:T(8,128)(2,1)} %refs_1_.1) | copy-start | bytes 4718596
  125.1 22.1 %collective-permute-start.4 = (bf16[4,12,3072]{2,1,0:T(8,128)(2,1)S(1)}, bf16[4,12,3072]{2,1,0:T(8,128)(2,1)S(1)}, u32[]{:S(2)}, u32[]{:S(2)}) collective-permute-start(bf16[4,12,3072]{2,1,0:T(8,128)(2,1)S(1)} %slice.55), channel_id=1, source_target_pairs={{0,8},{1,9},{2,10},{3,11},{4,12},{5,13},{6,14},{7,15},{8,16},{9,17... | collective-permute-start | bytes 884744 | tf_op jit(solution)/shard_map/ppermute | solution.py:247
  126.4 20.8 %collective-permute-start.3 = (bf16[4,4,3072]{2,1,0:T(4,128)(2,1)S(1)}, bf16[4,4,3072]{2,1,0:T(4,128)(2,1)S(1)}, u32[]{:S(2)}, u32[]{:S(2)}) collective-permute-start(bf16[4,4,3072]{2,1,0:T(4,128)(2,1)S(1)} %slice.54), channel_id=1, source_target_pairs={{0,9},{1,10},{2,11},{3,12},{4,13},{5,14},{6,15},{7,8},{8,17},{9,18... | collective-permute-start | bytes 294920 | tf_op jit(solution)/shard_map/ppermute | solution.py:247
  132.1 15.2 %collective-permute-start.5 = (bf16[12,4,3072]{2,1,0:T(4,128)(2,1)S(1)}, bf16[12,4,3072]{2,1,0:T(4,128)(2,1)S(1)}, u32[]{:S(2)}, u32[]{:S(2)}) collective-permute-start(bf16[12,4,3072]{2,1,0:T(4,128)(2,1)S(1)} %slice.56), channel_id=1, source_target_pairs={{0,1},{1,2},{2,3},{3,4},{4,5},{5,6},{6,7},{7,0},{8,9},{9,10},{10,1... | collective-permute-start | bytes 884744 | tf_op jit(solution)/shard_map/ppermute | solution.py:247
  133.9 7.4 %collective-permute-start.12 = (f32[16,768]{1,0:T(8,128)S(1)}, f32[16,768]{1,0:T(8,128)S(1)}, u32[]{:S(2)}, u32[]{:S(2)}) collective-permute-start(f32[16,768]{1,0:T(8,128)S(1)} %constant_dynamic-update-slice_fusion.8), channel_id=1, source_target_pairs={{0,8},{8,0},{16,24},{24,16},{1,9},{9,1},{17,25},{25,17},{2,10},{10... | collective-permute-start | bytes 147464 | tf_op jit(solution)/shard_map/ppermute | solution.py:201
  141.3 3.5 %collective-permute-start.13 = (f32[32,768]{1,0:T(8,128)S(1)}, f32[32,768]{1,0:T(8,128)S(1)}, u32[]{:S(2)}, u32[]{:S(2)}) collective-permute-start(f32[32,768]{1,0:T(8,128)S(1)} %constant_dynamic-update-slice_fusion.6), channel_id=1, source_target_pairs={{0,4},{2,6},{4,0},{6,2},{1,5},{3,7},{5,1},{7,3},{8,12},{10,14},{12... | collective-permute-start | bytes 294920 | tf_op jit(solution)/shard_map/ppermute | solution.py:201
  144.7 3.5 %collective-permute-start.14 = (f32[64,768]{1,0:T(8,128)S(1)}, f32[64,768]{1,0:T(8,128)S(1)}, u32[]{:S(2)}, u32[]{:S(2)}) collective-permute-start(f32[64,768]{1,0:T(8,128)S(1)} %constant_dynamic-update-slice_fusion.4), channel_id=1, source_target_pairs={{0,2},{2,0},{4,6},{6,4},{1,3},{3,1},{5,7},{7,5},{8,10},{10,8},{12,... | collective-permute-start | bytes 589832 | tf_op jit(solution)/shard_map/ppermute | solution.py:201
  148.3 10.4 %collective-permute-start.15 = (f32[128,768]{1,0:T(8,128)S(1)}, f32[128,768]{1,0:T(8,128)S(1)}, u32[]{:S(2)}, u32[]{:S(2)}) collective-permute-start(f32[128,768]{1,0:T(8,128)S(1)} %constant_dynamic-update-slice_fusion.2), channel_id=1, source_target_pairs={{0,1},{1,0},{2,3},{3,2},{4,5},{5,4},{6,7},{7,6},{8,9},{9,8},{10,11... | collective-permute-start | bytes 1179656 | tf_op jit(solution)/shard_map/ppermute | solution.py:201

commit v19 on v17

--- a/solution.py
+++ b/solution.py
@@ -211,17 +211,21 @@
     unit = devices * 8 if devices * 8 <= 2 * matrix.shape[0] else devices
     padded = -(-matrix.shape[0] // unit) * unit
     values = jnp.pad(matrix, ((0, padded - matrix.shape[0]), (0, 0)))
-    steps = []
+    order = []
     for axis, size in zip(SUM_AXES, sizes):
         distance = 1
         while distance < size:
-            bit = (lax.axis_index(axis) // distance) % 2
-            half = values.shape[0] // 2
-            keep = lax.dynamic_slice_in_dim(values, bit * half, half)
-            send = lax.dynamic_slice_in_dim(values, (1 - bit) * half, half)
-            values = keep + swapped(send, axis, distance)
-            steps.append((axis, distance))
+            order.append((axis, distance))
             distance *= 2
+    order.sort(key=lambda step: (step[0] != SUM_AXES[0] or step[1] != 1, step[1] > 1))
+    steps = []
+    for axis, distance in order:
+        bit = (lax.axis_index(axis) // distance) % 2
+        half = values.shape[0] // 2
+        keep = lax.dynamic_slice_in_dim(values, bit * half, half)
+        send = lax.dynamic_slice_in_dim(values, (1 - bit) * half, half)
+        values = keep + swapped(send, axis, distance)
+        steps.append((axis, distance))
     for axis, distance in reversed(steps):
         bit = (lax.axis_index(axis) // distance) % 2
         other = swapped(values, axis, distance)

time: 154 us -> 156 us (1.013)
  no operation moved by 1% of the time
where the time goes in v19:
time: 156 us; the launch traced here: 154 us
  Pallas kernels  74.2 us (48%)
  waiting for transfers between devices  28.6 us (18%)
  starting transfers between devices  24.8 us (16%)
  other arithmetic  15.9 us (10%)
  local copies, waits for them, and re-layouts  9.13 us (6%)
    pallas_call x2, Pallas kernels, window_grads(): pl.pallas_call(make_window_kernel(first), out_shape=[jax.ShapeDtypeStruct...  74.2 us
    ppermute x10, waiting for transfers between devices, swapped(): lax.ppermute(block, axis, [(i, i ^ distance) for i in range(lax.axis_size...  28.6 us
    ppermute x6, starting transfers between devices, moved(): lax.ppermute(block, ('gx', 'gy', 'gz'), halo_route(distance_a, distance_b))  15.6 us
    ppermute x10, starting transfers between devices, swapped(): lax.ppermute(block, axis, [(i, i ^ distance) for i in range(lax.axis_size...  9.22 us
    another operation x4, other arithmetic, per_device(): both = shifted_block(jnp.stack([tokens, grads_out]))  4.85 us
    concatenate x1, other arithmetic, shifted_block(): return jnp.concatenate([upper, lower], axis=1)  3.35 us
  transfers between devices with their start and end apart: 16, of which 8 were waited for; matrix products, arithmetic and copies ran while one was open for 6% of the time, Pallas kernels for 13%

profile of v19, /device:TPU:5, one launch (start us, length us, event | category | flops | bytes accessed | tf_op | source)
XLA Modules:
  0.0 153.6 jit_solution(11974068423473565177)
XLA Ops:
  0.7 1.5 fusion.2
  2.2 1.3 copy.12
  3.5 3.3 %collective-permute-start.1 = (bf16[2,4,12,3072]{3,1,2,0:T(4,128)(2,1)}, bf16[2,4,12,3072]{3,1,2,0:T(4,128)(2,1)}, u32[]{:S(2)}, u32[]{:S(2)}) collective-permute-start(bf16[2,4,12,3072]{3,1,2,0:T(4,128)(2,1)} %copy.12), channel_id=1, source_target_pairs={{0,24},{1,25},{2,26},{3,27},{4,28},{5,29},{6,30},{7,31},{8,0},{9,1... | collective-permute-start | bytes 1769480 | tf_op jit(solution)/shard_map/ppermute | solution.py:251
  6.8 1.0 fusion.3
  7.8 0.2 collective-permute-start
  8.1 2.0 %collective-permute-start.2 = (bf16[2,4,4,3072]{3,2,1,0:T(4,128)(2,1)S(1)}, bf16[2,4,4,3072]{3,2,1,0:T(4,128)(2,1)S(1)}, u32[]{:S(2)}, u32[]{:S(2)}) collective-permute-start(bf16[2,4,4,3072]{3,2,1,0:T(4,128)(2,1)S(1)} %pad_maximum_fusion), channel_id=1, source_target_pairs={{0,31},{1,24},{2,25},{3,26},{4,27},{5,28},{6,29},{7,30},{8,7},{9,0... | collective-permute-start | bytes 589832 | tf_op jit(solution)/shard_map/ppermute | solution.py:251
  10.2 2.2 %fusion.1 = bf16[2,12,12,3072]{3,2,1,0:T(8,128)(2,1)} fusion(bf16[1,16,16,3072]{3,2,1,0:T(8,128)(2,1)S(1)} %bitcast.15, bf16[1,16,16,3072]{3,2,1,0:T(8,128)(2,1)S(1)} %bitcast.11), kind=kLoop, calls=%fused_computation.9 | loop fusion | flops 884736 | bytes 4915200 | tf_op jit(solution)/shard_map/stack | solution.py:278
  12.6 0.2 reshape.74
  12.8 0.2 copy.14
  12.9 0.8 broadcast_in_dim_reshape.3.refs_2_.refs_1_
  13.7 19.6 %shard_map.93 = (f32[8,8,3072]{2,1,0:T(8,128)}, f32[192,576]{1,0:T(8,128)}, f32[192,192]{1,0:T(8,128)}, f32[192,1]{1,0:T(8,128)}) custom-call(bf16[16,16,3072]{2,1,0:T(8,128)(2,1)} %refs_0_.1, bf16[16,16,3072]{2,1,0:T(8,128)(2,1)} %refs_1_.1, s32[8,1,512]{2,1,0:T(1,128)} %broadcast_in_dim_reshape.3.refs_2_.refs_1_, f32[1,192]{1,0:T(1,128)} %bitcast.18, ...), custom_call_target="tpu_custom_call" | custom-call | tf_op jit(solution)/shard_map/pallas_call | solution.py:180
  33.3 1.3 copy.13
  34.6 3.3 %maximum_maximum_fusion.refs_0_ = bf16[2,16,16,3072]{3,2,1,0:T(8,128)(2,1)} fusion(bf16[2,4,4,3072]{3,2,1,0:T(4,128)(2,1)S(1)} %collective-permute-done.2, bf16[2,4,12,3072]{3,2,1,0:T(8,128)(2,1)S(1)} %copy.13, bf16[2,12,4,3072]{3,2,1,0:T(4,128)(2,1)} %collective-permute-done, bf16[2,12,12,3072]{3,2,1,0:T(8,128)(2,1)S(1)} %copy-done.4), kind=kLoop, calls=%fused_computation.6 | loop fusion | flops 12582912 | bytes 6291456 | tf_op jit(solution)/shard_map/concatenate | solution.py:260
  38.0 54.5 %shard_map.94 = (f32[16,16,3072]{2,1,0:T(8,128)}, f32[192,576]{1,0:T(8,128)}, f32[192,192]{1,0:T(8,128)}, f32[192,1]{1,0:T(8,128)}) custom-call(bf16[2,16,16,3072]{3,2,1,0:T(8,128)(2,1)} %maximum_maximum_fusion.refs_0_, s32[8,1,512]{2,1,0:T(1,128)} %broadcast_in_dim_reshape.3.refs_2_.refs_1_, f32[1,192]{1,0:T(1,128)} %bitcast.19, bf16[192,576]{1,0:T(8,128)(2,1)} %refs_3_.1, ...), custom_call_target="tpu_custom_call" | custom-call | tf_op jit(solution)/shard_map/pallas_call | solution.py:180
  92.5 1.1 reduce
  93.7 1.3 select_maximum_fusion
  94.9 0.8 copy-done.5
  95.8 0.8 collective-permute-start.6
  96.6 1.5 collective-permute-done.6
  98.1 1.1 fusion.4
  99.2 0.7 constant_dynamic-slice_fusion.3
  99.9 0.1 collective-permute-start.7
  100.0 6.2 %collective-permute-done.7 = f32[64,768]{1,0:T(8,128)} collective-permute-done((f32[64,768]{1,0:T(8,128)}, f32[64,768]{1,0:T(8,128)}, u32[]{:S(2)}, u32[]{:S(2)}) %collective-permute-start.7) | collective-permute-done | bytes 196640 | tf_op jit(solution)/shard_map/ppermute | solution.py:201
  106.3 0.9 dynamic-slice_add_fusion
  107.2 0.7 copy-done.6
  107.9 1.4 collective-permute-start.8
  109.3 2.2 %collective-permute-done.8 = f32[32,768]{1,0:T(8,128)S(1)} collective-permute-done((f32[32,768]{1,0:T(8,128)S(1)}, f32[32,768]{1,0:T(8,128)S(1)}, u32[]{:S(2)}, u32[]{:S(2)}) %collective-permute-start.8) | collective-permute-done | bytes 98336 | tf_op jit(solution)/shard_map/ppermute | solution.py:201
  111.4 0.9 dynamic-slice_add_fusion.1
  112.4 1.2 collective-permute-start.9
  113.5 1.8 %collective-permute-done.9 = f32[16,768]{1,0:T(8,128)S(1)} collective-permute-done((f32[16,768]{1,0:T(8,128)S(1)}, f32[16,768]{1,0:T(8,128)S(1)}, u32[]{:S(2)}, u32[]{:S(2)}) %collective-permute-start.9) | collective-permute-done | bytes 49184 | tf_op jit(solution)/shard_map/ppermute | solution.py:201
  115.5 3.6 %collective-permute-done.10 = f32[8,768]{1,0:T(8,128)S(1)} collective-permute-done((f32[8,768]{1,0:T(8,128)S(1)}, f32[8,768]{1,0:T(8,128)S(1)}, u32[]{:S(2)}, u32[]{:S(2)}) %collective-permute-start.10) | collective-permute-done | bytes 24608 | tf_op jit(solution)/shard_map/ppermute | solution.py:201
  119.1 0.2 convert_element_type.31
  119.5 0.2 slice.56
  119.6 0.2 slice.44
  119.9 1.5 collective-permute-start.4
  121.4 7.3 %collective-permute-start.3 = (bf16[4,4,3072]{2,1,0:T(4,128)(2,1)S(1)}, bf16[4,4,3072]{2,1,0:T(4,128)(2,1)S(1)}, u32[]{:S(2)}, u32[]{:S(2)}) collective-permute-start(bf16[4,4,3072]{2,1,0:T(4,128)(2,1)S(1)} %slice.54), channel_id=1, source_target_pairs={{0,9},{1,10},{2,11},{3,12},{4,13},{5,14},{6,15},{7,8},{8,17},{9,18... | collective-permute-start | bytes 294920 | tf_op jit(solution)/shard_map/ppermute | solution.py:251
  128.6 1.2 collective-permute-start.5
  129.9 0.5 collective-permute-start.12
  130.4 6.7 %collective-permute-done.12 = f32[16,768]{1,0:T(8,128)S(1)} collective-permute-done((f32[16,768]{1,0:T(8,128)S(1)}, f32[16,768]{1,0:T(8,128)S(1)}, u32[]{:S(2)}, u32[]{:S(2)}) %collective-permute-start.12) | collective-permute-done | bytes 49184 | tf_op jit(solution)/shard_map/ppermute | solution.py:201
  137.2 1.1 collective-permute-start.13
  138.3 2.3 %collective-permute-done.13 = f32[32,768]{1,0:T(8,128)S(1)} collective-permute-done((f32[32,768]{1,0:T(8,128)S(1)}, f32[32,768]{1,0:T(8,128)S(1)}, u32[]{:S(2)}, u32[]{:S(2)}) %collective-permute-start.13) | collective-permute-done | bytes 98336 | tf_op jit(solution)/shard_map/ppermute | solution.py:201
  140.7 0.1 maximum_convert_fusion
  141.0 4.2 %collective-permute-done.14 = f32[64,768]{1,0:T(8,128)S(1)} collective-permute-done((f32[64,768]{1,0:T(8,128)S(1)}, f32[64,768]{1,0:T(8,128)S(1)}, u32[]{:S(2)}, u32[]{:S(2)}) %collective-permute-start.14) | collective-permute-done | bytes 196640 | tf_op jit(solution)/shard_map/ppermute | solution.py:201
  145.2 3.9 %collective-permute-start.15 = (f32[128,768]{1,0:T(8,128)S(1)}, f32[128,768]{1,0:T(8,128)S(1)}, u32[]{:S(2)}, u32[]{:S(2)}) collective-permute-start(f32[128,768]{1,0:T(8,128)S(1)} %constant_dynamic-update-slice_fusion.2), channel_id=1, source_target_pairs={{0,2},{2,0},{4,6},{6,4},{1,3},{3,1},{5,7},{7,5},{8,10},{10,8},{12,... | collective-permute-start | bytes 1179656 | tf_op jit(solution)/shard_map/ppermute | solution.py:201
  149.2 1.8 %fusion = bf16[16,16,3072]{2,1,0:T(8,128)(2,1)} fusion(f32[12,12,3072]{2,1,0:T(8,128)S(1)} %slice.44, f32[12,4,3072]{2,1,0:T(4,128)S(1)} %convert_element_type.32, f32[4,16,3072]{2,1,0:T(8,128)S(1)} %maximum_convert_fusion, bf16[16,16,3072]{2,1,0:T(8,128)(2,1)S(1)} %copy-done.1), kind=kLoop, calls=%fused_computation.8 | loop fusion | flops 3932160 | bytes 6291456 | tf_op jit(solution)/shard_map/convert_element_type | solution.py:271
  151.2 0.6 slice.57
  151.8 1.0 reshape.77
  152.8 0.8 reshape.78
  (55 shorter events, 1.1 us)
Async XLA Ops:
  0.6 6.1 %copy-start.2 = (bf16[16,16,3072]{2,1,0:T(8,128)(2,1)S(1)}, bf16[16,16,3072]{2,1,0:T(8,128)(2,1)}, u32[]{:S(2)}) copy-start(bf16[16,16,3072]{2,1,0:T(8,128)(2,1)} %refs_0_.1) | copy-start | bytes 4718596
  0.6 6.1 %copy-start = (bf16[16,16,3072]{2,1,0:T(8,128)(2,1)S(1)}, bf16[16,16,3072]{2,1,0:T(8,128)(2,1)}, u32[]{:S(2)}) copy-start(bf16[16,16,3072]{2,1,0:T(8,128)(2,1)} %refs_1_.1) | copy-start | bytes 4718596
  3.5 29.9 %collective-permute-start.1 = (bf16[2,4,12,3072]{3,1,2,0:T(4,128)(2,1)}, bf16[2,4,12,3072]{3,1,2,0:T(4,128)(2,1)}, u32[]{:S(2)}, u32[]{:S(2)}) collective-permute-start(bf16[2,4,12,3072]{3,1,2,0:T(4,128)(2,1)} %copy.12), channel_id=1, source_target_pairs={{0,24},{1,25},{2,26},{3,27},{4,28},{5,29},{6,30},{7,31},{8,0},{9,1... | collective-permute-start | bytes 1769480 | tf_op jit(solution)/shard_map/ppermute | solution.py:251
  7.8 26.8 %collective-permute-start = (bf16[2,12,4,3072]{3,2,1,0:T(4,128)(2,1)}, bf16[2,12,4,3072]{3,2,1,0:T(4,128)(2,1)}, u32[]{:S(2)}, u32[]{:S(2)}) collective-permute-start(bf16[2,12,4,3072]{3,2,1,0:T(4,128)(2,1)} %fusion.3), channel_id=1, source_target_pairs={{0,7},{1,0},{2,1},{3,2},{4,3},{5,4},{6,5},{7,6},{8,15},{9,8},{10,9... | collective-permute-start | bytes 1769480 | tf_op jit(solution)/shard_map/ppermute | solution.py:251
  8.1 26.5 %collective-permute-start.2 = (bf16[2,4,4,3072]{3,2,1,0:T(4,128)(2,1)S(1)}, bf16[2,4,4,3072]{3,2,1,0:T(4,128)(2,1)S(1)}, u32[]{:S(2)}, u32[]{:S(2)}) collective-permute-start(bf16[2,4,4,3072]{3,2,1,0:T(4,128)(2,1)S(1)} %pad_maximum_fusion), channel_id=1, source_target_pairs={{0,31},{1,24},{2,25},{3,26},{4,27},{5,28},{6,29},{7,30},{8,7},{9,0... | collective-permute-start | bytes 589832 | tf_op jit(solution)/shard_map/ppermute | solution.py:251
  10.1 2.3 %copy-start.7 = (s32[16,16,16]{2,1,0:T(8,128)S(1)}, s32[16,16,16]{2,1,0:T(8,128)}, u32[]{:S(2)}) copy-start(s32[16,16,16]{2,1,0:T(8,128)} %param.8) | copy-start | bytes 49156
  12.5 22.2 %copy-start.4 = (bf16[2,12,12,3072]{3,2,1,0:T(8,128)(2,1)S(1)}, bf16[2,12,12,3072]{3,2,1,0:T(8,128)(2,1)}, u32[]{:S(2)}) copy-start(bf16[2,12,12,3072]{3,2,1,0:T(8,128)(2,1)} %fusion.1) | copy-start | bytes 5308420
  92.5 26.6 %copy-start.3 = (f32[16,16,3072]{2,1,0:T(8,128)S(1)}, f32[16,16,3072]{2,1,0:T(8,128)}, u32[]{:S(2)}) copy-start(f32[16,16,3072]{2,1,0:T(8,128)} %get-tuple-element.16) | copy-start | bytes 9437188
  94.9 0.8 copy-start.5
  95.8 2.3 %collective-permute-start.6 = (f32[128,768]{1,0:T(8,128)S(1)}, f32[128,768]{1,0:T(8,128)}, u32[]{:S(2)}, u32[]{:S(2)}) collective-permute-start(f32[128,768]{1,0:T(8,128)S(1)} %pad_dynamic-slice_fusion), channel_id=1, source_target_pairs={{0,2},{2,0},{4,6},{6,4},{1,3},{3,1},{5,7},{7,5},{8,10},{10,8},{12,... | collective-permute-start | bytes 1179656 | tf_op jit(solution)/shard_map/ppermute | solution.py:201
  99.9 6.4 %collective-permute-start.7 = (f32[64,768]{1,0:T(8,128)}, f32[64,768]{1,0:T(8,128)}, u32[]{:S(2)}, u32[]{:S(2)}) collective-permute-start(f32[64,768]{1,0:T(8,128)} %constant_dynamic-slice_fusion.3), channel_id=1, source_target_pairs={{0,1},{1,0},{2,3},{3,2},{4,5},{5,4},{6,7},{7,6},{8,9},{9,8},{10,11... | collective-permute-start | bytes 589832 | tf_op jit(solution)/shard_map/ppermute | solution.py:201
  107.2 0.7 copy-start.6
  107.9 3.5 %collective-permute-start.8 = (f32[32,768]{1,0:T(8,128)S(1)}, f32[32,768]{1,0:T(8,128)S(1)}, u32[]{:S(2)}, u32[]{:S(2)}) collective-permute-start(f32[32,768]{1,0:T(8,128)S(1)} %constant_dynamic-slice_fusion.2), channel_id=1, source_target_pairs={{0,8},{8,0},{16,24},{24,16},{1,9},{9,1},{17,25},{25,17},{2,10},{10... | collective-permute-start | bytes 294920 | tf_op jit(solution)/shard_map/ppermute | solution.py:201
  112.4 3.0 %collective-permute-start.9 = (f32[16,768]{1,0:T(8,128)S(1)}, f32[16,768]{1,0:T(8,128)S(1)}, u32[]{:S(2)}, u32[]{:S(2)}) collective-permute-start(f32[16,768]{1,0:T(8,128)S(1)} %constant_dynamic-slice_fusion.1), channel_id=1, source_target_pairs={{0,4},{2,6},{4,0},{6,2},{1,5},{3,7},{5,1},{7,3},{8,12},{10,14},{12... | collective-permute-start | bytes 147464 | tf_op jit(solution)/shard_map/ppermute | solution.py:201
  115.4 3.6 %collective-permute-start.10 = (f32[8,768]{1,0:T(8,128)S(1)}, f32[8,768]{1,0:T(8,128)S(1)}, u32[]{:S(2)}, u32[]{:S(2)}) collective-permute-start(f32[8,768]{1,0:T(8,128)S(1)} %constant_dynamic-slice_fusion), channel_id=1, source_target_pairs={{0,16},{8,24},{16,0},{24,8},{1,17},{9,25},{17,1},{25,9},{2,18},{10... | collective-permute-start | bytes 73736 | tf_op jit(solution)/shard_map/ppermute | solution.py:201
  119.1 10.8 %collective-permute-start.11 = (f32[8,768]{1,0:T(8,128)S(1)}, f32[8,768]{1,0:T(8,128)S(1)}, u32[]{:S(2)}, u32[]{:S(2)}) collective-permute-start(f32[8,768]{1,0:T(8,128)S(1)} %get-tuple-element.21), channel_id=1, source_target_pairs={{0,16},{8,24},{16,0},{24,8},{1,17},{9,25},{17,1},{25,9},{2,18},{10... | collective-permute-start | bytes 73736 | tf_op jit(solution)/shard_map/ppermute | solution.py:201
  119.9 29.3 %copy-start.1 = (bf16[16,16,3072]{2,1,0:T(8,128)(2,1)S(1)}, bf16[16,16,3072]{2,1,0:T(8,128)(2,1)}, u32[]{:S(2)}) copy-start(bf16[16,16,3072]{2,1,0:T(8,128)(2,1)} %refs_1_.1) | copy-start | bytes 4718596
  119.9 20.8 %collective-permute-start.4 = (bf16[4,12,3072]{2,1,0:T(8,128)(2,1)S(1)}, bf16[4,12,3072]{2,1,0:T(8,128)(2,1)S(1)}, u32[]{:S(2)}, u32[]{:S(2)}) collective-permute-start(bf16[4,12,3072]{2,1,0:T(8,128)(2,1)S(1)} %slice.55), channel_id=1, source_target_pairs={{0,8},{1,9},{2,10},{3,11},{4,12},{5,13},{6,14},{7,15},{8,16},{9,17... | collective-permute-start | bytes 884744 | tf_op jit(solution)/shard_map/ppermute | solution.py:251
  121.4 19.4 %collective-permute-start.3 = (bf16[4,4,3072]{2,1,0:T(4,128)(2,1)S(1)}, bf16[4,4,3072]{2,1,0:T(4,128)(2,1)S(1)}, u32[]{:S(2)}, u32[]{:S(2)}) collective-permute-start(bf16[4,4,3072]{2,1,0:T(4,128)(2,1)S(1)} %slice.54), channel_id=1, source_target_pairs={{0,9},{1,10},{2,11},{3,12},{4,13},{5,14},{6,15},{7,8},{8,17},{9,18... | collective-permute-start | bytes 294920 | tf_op jit(solution)/shard_map/ppermute | solution.py:251
  128.6 12.2 %collective-permute-start.5 = (bf16[12,4,3072]{2,1,0:T(4,128)(2,1)S(1)}, bf16[12,4,3072]{2,1,0:T(4,128)(2,1)S(1)}, u32[]{:S(2)}, u32[]{:S(2)}) collective-permute-start(bf16[12,4,3072]{2,1,0:T(4,128)(2,1)S(1)} %slice.56), channel_id=1, source_target_pairs={{0,1},{1,2},{2,3},{3,4},{4,5},{5,6},{6,7},{7,0},{8,9},{9,10},{10,1... | collective-permute-start | bytes 884744 | tf_op jit(solution)/shard_map/ppermute | solution.py:251
  129.9 7.3 %collective-permute-start.12 = (f32[16,768]{1,0:T(8,128)S(1)}, f32[16,768]{1,0:T(8,128)S(1)}, u32[]{:S(2)}, u32[]{:S(2)}) collective-permute-start(f32[16,768]{1,0:T(8,128)S(1)} %constant_dynamic-update-slice_fusion.8), channel_id=1, source_target_pairs={{0,4},{2,6},{4,0},{6,2},{1,5},{3,7},{5,1},{7,3},{8,12},{10,14},{12... | collective-permute-start | bytes 147464 | tf_op jit(solution)/shard_map/ppermute | solution.py:201
  137.2 3.5 %collective-permute-start.13 = (f32[32,768]{1,0:T(8,128)S(1)}, f32[32,768]{1,0:T(8,128)S(1)}, u32[]{:S(2)}, u32[]{:S(2)}) collective-permute-start(f32[32,768]{1,0:T(8,128)S(1)} %constant_dynamic-update-slice_fusion.6), channel_id=1, source_target_pairs={{0,8},{8,0},{16,24},{24,16},{1,9},{9,1},{17,25},{25,17},{2,10},{10... | collective-permute-start | bytes 294920 | tf_op jit(solution)/shard_map/ppermute | solution.py:201
  140.6 4.6 %collective-permute-start.14 = (f32[64,768]{1,0:T(8,128)S(1)}, f32[64,768]{1,0:T(8,128)S(1)}, u32[]{:S(2)}, u32[]{:S(2)}) collective-permute-start(f32[64,768]{1,0:T(8,128)S(1)} %constant_dynamic-update-slice_fusion.4), channel_id=1, source_target_pairs={{0,1},{1,0},{2,3},{3,2},{4,5},{5,4},{6,7},{7,6},{8,9},{9,8},{10,11... | collective-permute-start | bytes 589832 | tf_op jit(solution)/shard_map/ppermute | solution.py:201
  145.2 5.8 %collective-permute-start.15 = (f32[128,768]{1,0:T(8,128)S(1)}, f32[128,768]{1,0:T(8,128)S(1)}, u32[]{:S(2)}, u32[]{:S(2)}) collective-permute-start(f32[128,768]{1,0:T(8,128)S(1)} %constant_dynamic-update-slice_fusion.2), channel_id=1, source_target_pairs={{0,2},{2,0},{4,6},{6,4},{1,3},{3,1},{5,7},{7,5},{8,10},{10,8},{12,... | collective-permute-start | bytes 1179656 | tf_op jit(solution)/shard_map/ppermute | solution.py:201

commit v20 on v17

--- a/solution.py
+++ b/solution.py
@@ -146,7 +146,7 @@
                 drow_s[pl.ds(qo + 2 * C, HEAD), :] = dv_t.astype(bf16).astype(f32)
                 return carry
 
-            lax.fori_loop(0, HEADS, head_step, 0, unroll=3)
+            lax.fori_loop(0, HEADS, head_step, 0, unroll=2)
             rows_t = drow_s[...].astype(bf16)
             gqkvT_ref[...] += lax.dot_general(normed, rows_t, nt, preferred_element_type=f32)
             grad_normed = jnp.dot(wqkv_ref[...], rows_t, preferred_element_type=f32)

time: 154 us -> 156 us (1.013)
  no operation moved by 1% of the time
where the time goes in v20:
time: 156 us; the launch traced here: 154 us
  Pallas kernels  75.4 us (48%)
  waiting for transfers between devices  29.3 us (19%)
  starting transfers between devices  23.5 us (15%)
  other arithmetic  15.9 us (10%)
  local copies, waits for them, and re-layouts  9.13 us (6%)
    pallas_call x2, Pallas kernels, window_grads(): pl.pallas_call(make_window_kernel(first), out_shape=[jax.ShapeDtypeStruct...  75.4 us
    ppermute x10, waiting for transfers between devices, swapped(): lax.ppermute(block, axis, [(i, i ^ distance) for i in range(lax.axis_size...  29.3 us
    ppermute x6, starting transfers between devices, moved(): lax.ppermute(block, ('gx', 'gy', 'gz'), halo_route(distance_a, distance_b))  15.6 us
    ppermute x10, starting transfers between devices, swapped(): lax.ppermute(block, axis, [(i, i ^ distance) for i in range(lax.axis_size...  7.91 us
    another operation x4, other arithmetic, per_device(): both = shifted_block(jnp.stack([tokens, grads_out]))  4.85 us
    concatenate x1, other arithmetic, shifted_block(): return jnp.concatenate([upper, lower], axis=1)  3.35 us
  transfers between devices with their start and end apart: 16, of which 8 were waited for; matrix products, arithmetic and copies ran while one was open for 6% of the time, Pallas kernels for 13%

profile of v20, /device:TPU:5, one launch (start us, length us, event | category | flops | bytes accessed | tf_op | source)
XLA Modules:
  0.0 154.3 jit_solution(4865639262204325927)
XLA Ops:
  0.7 1.5 fusion.2
  2.2 1.3 copy.12
  3.5 3.3 %collective-permute-start.1 = (bf16[2,4,12,3072]{3,1,2,0:T(4,128)(2,1)}, bf16[2,4,12,3072]{3,1,2,0:T(4,128)(2,1)}, u32[]{:S(2)}, u32[]{:S(2)}) collective-permute-start(bf16[2,4,12,3072]{3,1,2,0:T(4,128)(2,1)} %copy.12), channel_id=1, source_target_pairs={{0,24},{1,25},{2,26},{3,27},{4,28},{5,29},{6,30},{7,31},{8,0},{9,1... | collective-permute-start | bytes 1769480 | tf_op jit(solution)/shard_map/ppermute | solution.py:247
  6.8 1.0 fusion.3
  7.8 0.2 collective-permute-start
  8.1 2.0 %collective-permute-start.2 = (bf16[2,4,4,3072]{3,2,1,0:T(4,128)(2,1)S(1)}, bf16[2,4,4,3072]{3,2,1,0:T(4,128)(2,1)S(1)}, u32[]{:S(2)}, u32[]{:S(2)}) collective-permute-start(bf16[2,4,4,3072]{3,2,1,0:T(4,128)(2,1)S(1)} %pad_maximum_fusion), channel_id=1, source_target_pairs={{0,31},{1,24},{2,25},{3,26},{4,27},{5,28},{6,29},{7,30},{8,7},{9,0... | collective-permute-start | bytes 589832 | tf_op jit(solution)/shard_map/ppermute | solution.py:247
  10.2 2.2 %fusion.1 = bf16[2,12,12,3072]{3,2,1,0:T(8,128)(2,1)} fusion(bf16[1,16,16,3072]{3,2,1,0:T(8,128)(2,1)S(1)} %bitcast.15, bf16[1,16,16,3072]{3,2,1,0:T(8,128)(2,1)S(1)} %bitcast.11), kind=kLoop, calls=%fused_computation.9 | loop fusion | flops 884736 | bytes 4915200 | tf_op jit(solution)/shard_map/stack | solution.py:274
  12.6 0.2 reshape.74
  12.8 0.2 copy.14
  12.9 0.8 broadcast_in_dim_reshape.3.refs_2_.refs_1_
  13.7 20.0 %shard_map.93 = (f32[8,8,3072]{2,1,0:T(8,128)}, f32[192,576]{1,0:T(8,128)}, f32[192,192]{1,0:T(8,128)}, f32[192,1]{1,0:T(8,128)}) custom-call(bf16[16,16,3072]{2,1,0:T(8,128)(2,1)} %refs_0_.1, bf16[16,16,3072]{2,1,0:T(8,128)(2,1)} %refs_1_.1, s32[8,1,512]{2,1,0:T(1,128)} %broadcast_in_dim_reshape.3.refs_2_.refs_1_, f32[1,192]{1,0:T(1,128)} %bitcast.18, ...), custom_call_target="tpu_custom_call" | custom-call | tf_op jit(solution)/shard_map/pallas_call | solution.py:180
  33.6 1.3 copy.13
  34.9 3.3 %maximum_maximum_fusion.refs_0_ = bf16[2,16,16,3072]{3,2,1,0:T(8,128)(2,1)} fusion(bf16[2,4,4,3072]{3,2,1,0:T(4,128)(2,1)S(1)} %collective-permute-done.2, bf16[2,4,12,3072]{3,2,1,0:T(8,128)(2,1)S(1)} %copy.13, bf16[2,12,4,3072]{3,2,1,0:T(4,128)(2,1)} %collective-permute-done, bf16[2,12,12,3072]{3,2,1,0:T(8,128)(2,1)S(1)} %copy-done.4), kind=kLoop, calls=%fused_computation.6 | loop fusion | flops 12582912 | bytes 6291456 | tf_op jit(solution)/shard_map/concatenate | solution.py:256
  38.3 55.5 %shard_map.94 = (f32[16,16,3072]{2,1,0:T(8,128)}, f32[192,576]{1,0:T(8,128)}, f32[192,192]{1,0:T(8,128)}, f32[192,1]{1,0:T(8,128)}) custom-call(bf16[2,16,16,3072]{3,2,1,0:T(8,128)(2,1)} %maximum_maximum_fusion.refs_0_, s32[8,1,512]{2,1,0:T(1,128)} %broadcast_in_dim_reshape.3.refs_2_.refs_1_, f32[1,192]{1,0:T(1,128)} %bitcast.19, bf16[192,576]{1,0:T(8,128)(2,1)} %refs_3_.1, ...), custom_call_target="tpu_custom_call" | custom-call | tf_op jit(solution)/shard_map/pallas_call | solution.py:180
  93.8 1.1 reduce
  94.9 1.3 select_maximum_fusion
  96.2 0.8 copy-done.5
  97.1 0.8 collective-permute-start.6
  97.9 1.5 collective-permute-done.6
  99.4 1.1 fusion.4
  100.5 0.7 constant_dynamic-slice_fusion.3
  101.2 0.8 collective-permute-start.7
  102.0 5.5 %collective-permute-done.7 = f32[64,768]{1,0:T(8,128)} collective-permute-done((f32[64,768]{1,0:T(8,128)}, f32[64,768]{1,0:T(8,128)}, u32[]{:S(2)}, u32[]{:S(2)}) %collective-permute-start.7) | collective-permute-done | bytes 196640 | tf_op jit(solution)/shard_map/ppermute | solution.py:201
  107.5 0.9 dynamic-slice_add_fusion
  108.5 0.7 copy-done.6
  109.2 0.4 collective-permute-start.8
  109.5 3.1 %collective-permute-done.8 = f32[32,768]{1,0:T(8,128)S(1)} collective-permute-done((f32[32,768]{1,0:T(8,128)S(1)}, f32[32,768]{1,0:T(8,128)S(1)}, u32[]{:S(2)}, u32[]{:S(2)}) %collective-permute-start.8) | collective-permute-done | bytes 98336 | tf_op jit(solution)/shard_map/ppermute | solution.py:201
  112.7 0.9 dynamic-slice_add_fusion.1
  113.6 1.4 collective-permute-start.9
  115.0 1.6 %collective-permute-done.9 = f32[16,768]{1,0:T(8,128)S(1)} collective-permute-done((f32[16,768]{1,0:T(8,128)S(1)}, f32[16,768]{1,0:T(8,128)S(1)}, u32[]{:S(2)}, u32[]{:S(2)}) %collective-permute-start.9) | collective-permute-done | bytes 49184 | tf_op jit(solution)/shard_map/ppermute | solution.py:201
  116.7 3.6 %collective-permute-done.10 = f32[8,768]{1,0:T(8,128)S(1)} collective-permute-done((f32[8,768]{1,0:T(8,128)S(1)}, f32[8,768]{1,0:T(8,128)S(1)}, u32[]{:S(2)}, u32[]{:S(2)}) %collective-permute-start.10) | collective-permute-done | bytes 24608 | tf_op jit(solution)/shard_map/ppermute | solution.py:201
  120.4 0.2 convert_element_type.31
  120.7 0.2 slice.56
  120.9 0.2 slice.44
  121.1 1.5 collective-permute-start.4
  122.6 7.3 %collective-permute-start.3 = (bf16[4,4,3072]{2,1,0:T(4,128)(2,1)S(1)}, bf16[4,4,3072]{2,1,0:T(4,128)(2,1)S(1)}, u32[]{:S(2)}, u32[]{:S(2)}) collective-permute-start(bf16[4,4,3072]{2,1,0:T(4,128)(2,1)S(1)} %slice.54), channel_id=1, source_target_pairs={{0,9},{1,10},{2,11},{3,12},{4,13},{5,14},{6,15},{7,8},{8,17},{9,18... | collective-permute-start | bytes 294920 | tf_op jit(solution)/shard_map/ppermute | solution.py:247
  129.9 1.2 collective-permute-start.5
  131.2 1.3 collective-permute-start.12
  132.5 6.0 %collective-permute-done.12 = f32[16,768]{1,0:T(8,128)S(1)} collective-permute-done((f32[16,768]{1,0:T(8,128)S(1)}, f32[16,768]{1,0:T(8,128)S(1)}, u32[]{:S(2)}, u32[]{:S(2)}) %collective-permute-start.12) | collective-permute-done | bytes 49184 | tf_op jit(solution)/shard_map/ppermute | solution.py:201
  138.5 3.9 %collective-permute-done.13 = f32[32,768]{1,0:T(8,128)S(1)} collective-permute-done((f32[32,768]{1,0:T(8,128)S(1)}, f32[32,768]{1,0:T(8,128)S(1)}, u32[]{:S(2)}, u32[]{:S(2)}) %collective-permute-start.13) | collective-permute-done | bytes 98336 | tf_op jit(solution)/shard_map/ppermute | solution.py:201
  142.4 0.8 collective-permute-start.14
  143.2 0.1 maximum_convert_fusion
  143.5 4.1 %collective-permute-done.14 = f32[64,768]{1,0:T(8,128)S(1)} collective-permute-done((f32[64,768]{1,0:T(8,128)S(1)}, f32[64,768]{1,0:T(8,128)S(1)}, u32[]{:S(2)}, u32[]{:S(2)}) %collective-permute-start.14) | collective-permute-done | bytes 196640 | tf_op jit(solution)/shard_map/ppermute | solution.py:201
  147.6 2.2 %collective-permute-start.15 = (f32[128,768]{1,0:T(8,128)S(1)}, f32[128,768]{1,0:T(8,128)S(1)}, u32[]{:S(2)}, u32[]{:S(2)}) collective-permute-start(f32[128,768]{1,0:T(8,128)S(1)} %constant_dynamic-update-slice_fusion.2), channel_id=1, source_target_pairs={{0,2},{2,0},{4,6},{6,4},{1,3},{3,1},{5,7},{7,5},{8,10},{10,8},{12,... | collective-permute-start | bytes 1179656 | tf_op jit(solution)/shard_map/ppermute | solution.py:201
  149.9 1.8 %fusion = bf16[16,16,3072]{2,1,0:T(8,128)(2,1)} fusion(f32[12,12,3072]{2,1,0:T(8,128)S(1)} %slice.44, f32[12,4,3072]{2,1,0:T(4,128)S(1)} %convert_element_type.32, f32[4,16,3072]{2,1,0:T(8,128)S(1)} %maximum_convert_fusion, bf16[16,16,3072]{2,1,0:T(8,128)(2,1)S(1)} %copy-done.1), kind=kLoop, calls=%fused_computation.8 | loop fusion | flops 3932160 | bytes 6291456 | tf_op jit(solution)/shard_map/convert_element_type | solution.py:267
  152.0 0.6 slice.57
  152.5 1.0 reshape.77
  153.5 0.8 reshape.78
  (55 shorter events, 1.1 us)
Async XLA Ops:
  0.6 6.1 %copy-start.2 = (bf16[16,16,3072]{2,1,0:T(8,128)(2,1)S(1)}, bf16[16,16,3072]{2,1,0:T(8,128)(2,1)}, u32[]{:S(2)}) copy-start(bf16[16,16,3072]{2,1,0:T(8,128)(2,1)} %refs_0_.1) | copy-start | bytes 4718596
  0.6 6.1 %copy-start = (bf16[16,16,3072]{2,1,0:T(8,128)(2,1)S(1)}, bf16[16,16,3072]{2,1,0:T(8,128)(2,1)}, u32[]{:S(2)}) copy-start(bf16[16,16,3072]{2,1,0:T(8,128)(2,1)} %refs_1_.1) | copy-start | bytes 4718596
  3.5 30.2 %collective-permute-start.1 = (bf16[2,4,12,3072]{3,1,2,0:T(4,128)(2,1)}, bf16[2,4,12,3072]{3,1,2,0:T(4,128)(2,1)}, u32[]{:S(2)}, u32[]{:S(2)}) collective-permute-start(bf16[2,4,12,3072]{3,1,2,0:T(4,128)(2,1)} %copy.12), channel_id=1, source_target_pairs={{0,24},{1,25},{2,26},{3,27},{4,28},{5,29},{6,30},{7,31},{8,0},{9,1... | collective-permute-start | bytes 1769480 | tf_op jit(solution)/shard_map/ppermute | solution.py:247
  7.8 27.1 %collective-permute-start = (bf16[2,12,4,3072]{3,2,1,0:T(4,128)(2,1)}, bf16[2,12,4,3072]{3,2,1,0:T(4,128)(2,1)}, u32[]{:S(2)}, u32[]{:S(2)}) collective-permute-start(bf16[2,12,4,3072]{3,2,1,0:T(4,128)(2,1)} %fusion.3), channel_id=1, source_target_pairs={{0,7},{1,0},{2,1},{3,2},{4,3},{5,4},{6,5},{7,6},{8,15},{9,8},{10,9... | collective-permute-start | bytes 1769480 | tf_op jit(solution)/shard_map/ppermute | solution.py:247
  8.1 26.8 %collective-permute-start.2 = (bf16[2,4,4,3072]{3,2,1,0:T(4,128)(2,1)S(1)}, bf16[2,4,4,3072]{3,2,1,0:T(4,128)(2,1)S(1)}, u32[]{:S(2)}, u32[]{:S(2)}) collective-permute-start(bf16[2,4,4,3072]{3,2,1,0:T(4,128)(2,1)S(1)} %pad_maximum_fusion), channel_id=1, source_target_pairs={{0,31},{1,24},{2,25},{3,26},{4,27},{5,28},{6,29},{7,30},{8,7},{9,0... | collective-permute-start | bytes 589832 | tf_op jit(solution)/shard_map/ppermute | solution.py:247
  10.1 2.3 %copy-start.7 = (s32[16,16,16]{2,1,0:T(8,128)S(1)}, s32[16,16,16]{2,1,0:T(8,128)}, u32[]{:S(2)}) copy-start(s32[16,16,16]{2,1,0:T(8,128)} %param.8) | copy-start | bytes 49156
  12.5 22.5 %copy-start.4 = (bf16[2,12,12,3072]{3,2,1,0:T(8,128)(2,1)S(1)}, bf16[2,12,12,3072]{3,2,1,0:T(8,128)(2,1)}, u32[]{:S(2)}) copy-start(bf16[2,12,12,3072]{3,2,1,0:T(8,128)(2,1)} %fusion.1) | copy-start | bytes 5308420
  93.8 26.6 %copy-start.3 = (f32[16,16,3072]{2,1,0:T(8,128)S(1)}, f32[16,16,3072]{2,1,0:T(8,128)}, u32[]{:S(2)}) copy-start(f32[16,16,3072]{2,1,0:T(8,128)} %get-tuple-element.16) | copy-start | bytes 9437188
  96.2 0.8 copy-start.5
  97.1 2.3 %collective-permute-start.6 = (f32[128,768]{1,0:T(8,128)S(1)}, f32[128,768]{1,0:T(8,128)}, u32[]{:S(2)}, u32[]{:S(2)}) collective-permute-start(f32[128,768]{1,0:T(8,128)S(1)} %pad_dynamic-slice_fusion), channel_id=1, source_target_pairs={{0,2},{2,0},{4,6},{6,4},{1,3},{3,1},{5,7},{7,5},{8,10},{10,8},{12,... | collective-permute-start | bytes 1179656 | tf_op jit(solution)/shard_map/ppermute | solution.py:201
  101.2 6.4 %collective-permute-start.7 = (f32[64,768]{1,0:T(8,128)}, f32[64,768]{1,0:T(8,128)}, u32[]{:S(2)}, u32[]{:S(2)}) collective-permute-start(f32[64,768]{1,0:T(8,128)} %constant_dynamic-slice_fusion.3), channel_id=1, source_target_pairs={{0,4},{2,6},{4,0},{6,2},{1,5},{3,7},{5,1},{7,3},{8,12},{10,14},{12... | collective-permute-start | bytes 589832 | tf_op jit(solution)/shard_map/ppermute | solution.py:201
  108.5 0.7 copy-start.6
  109.2 3.5 %collective-permute-start.8 = (f32[32,768]{1,0:T(8,128)S(1)}, f32[32,768]{1,0:T(8,128)S(1)}, u32[]{:S(2)}, u32[]{:S(2)}) collective-permute-start(f32[32,768]{1,0:T(8,128)S(1)} %constant_dynamic-slice_fusion.2), channel_id=1, source_target_pairs={{0,1},{1,0},{2,3},{3,2},{4,5},{5,4},{6,7},{7,6},{8,9},{9,8},{10,11... | collective-permute-start | bytes 294920 | tf_op jit(solution)/shard_map/ppermute | solution.py:201
  113.6 3.0 %collective-permute-start.9 = (f32[16,768]{1,0:T(8,128)S(1)}, f32[16,768]{1,0:T(8,128)S(1)}, u32[]{:S(2)}, u32[]{:S(2)}) collective-permute-start(f32[16,768]{1,0:T(8,128)S(1)} %constant_dynamic-slice_fusion.1), channel_id=1, source_target_pairs={{0,8},{8,0},{16,24},{24,16},{1,9},{9,1},{17,25},{25,17},{2,10},{10... | collective-permute-start | bytes 147464 | tf_op jit(solution)/shard_map/ppermute | solution.py:201
  116.7 3.6 %collective-permute-start.10 = (f32[8,768]{1,0:T(8,128)S(1)}, f32[8,768]{1,0:T(8,128)S(1)}, u32[]{:S(2)}, u32[]{:S(2)}) collective-permute-start(f32[8,768]{1,0:T(8,128)S(1)} %constant_dynamic-slice_fusion), channel_id=1, source_target_pairs={{0,16},{8,24},{16,0},{24,8},{1,17},{9,25},{17,1},{25,9},{2,18},{10... | collective-permute-start | bytes 73736 | tf_op jit(solution)/shard_map/ppermute | solution.py:201
  120.3 10.8 %collective-permute-start.11 = (f32[8,768]{1,0:T(8,128)S(1)}, f32[8,768]{1,0:T(8,128)S(1)}, u32[]{:S(2)}, u32[]{:S(2)}) collective-permute-start(f32[8,768]{1,0:T(8,128)S(1)} %get-tuple-element.21), channel_id=1, source_target_pairs={{0,16},{8,24},{16,0},{24,8},{1,17},{9,25},{17,1},{25,9},{2,18},{10... | collective-permute-start | bytes 73736 | tf_op jit(solution)/shard_map/ppermute | solution.py:201
  121.1 28.8 %copy-start.1 = (bf16[16,16,3072]{2,1,0:T(8,128)(2,1)S(1)}, bf16[16,16,3072]{2,1,0:T(8,128)(2,1)}, u32[]{:S(2)}) copy-start(bf16[16,16,3072]{2,1,0:T(8,128)(2,1)} %refs_1_.1) | copy-start | bytes 4718596
  121.1 22.1 %collective-permute-start.4 = (bf16[4,12,3072]{2,1,0:T(8,128)(2,1)S(1)}, bf16[4,12,3072]{2,1,0:T(8,128)(2,1)S(1)}, u32[]{:S(2)}, u32[]{:S(2)}) collective-permute-start(bf16[4,12,3072]{2,1,0:T(8,128)(2,1)S(1)} %slice.55), channel_id=1, source_target_pairs={{0,8},{1,9},{2,10},{3,11},{4,12},{5,13},{6,14},{7,15},{8,16},{9,17... | collective-permute-start | bytes 884744 | tf_op jit(solution)/shard_map/ppermute | solution.py:247
  122.6 20.6 %collective-permute-start.3 = (bf16[4,4,3072]{2,1,0:T(4,128)(2,1)S(1)}, bf16[4,4,3072]{2,1,0:T(4,128)(2,1)S(1)}, u32[]{:S(2)}, u32[]{:S(2)}) collective-permute-start(bf16[4,4,3072]{2,1,0:T(4,128)(2,1)S(1)} %slice.54), channel_id=1, source_target_pairs={{0,9},{1,10},{2,11},{3,12},{4,13},{5,14},{6,15},{7,8},{8,17},{9,18... | collective-permute-start | bytes 294920 | tf_op jit(solution)/shard_map/ppermute | solution.py:247
  129.9 13.5 %collective-permute-start.5 = (bf16[12,4,3072]{2,1,0:T(4,128)(2,1)S(1)}, bf16[12,4,3072]{2,1,0:T(4,128)(2,1)S(1)}, u32[]{:S(2)}, u32[]{:S(2)}) collective-permute-start(bf16[12,4,3072]{2,1,0:T(4,128)(2,1)S(1)} %slice.56), channel_id=1, source_target_pairs={{0,1},{1,2},{2,3},{3,4},{4,5},{5,6},{6,7},{7,0},{8,9},{9,10},{10,1... | collective-permute-start | bytes 884744 | tf_op jit(solution)/shard_map/ppermute | solution.py:247
  131.2 7.3 %collective-permute-start.12 = (f32[16,768]{1,0:T(8,128)S(1)}, f32[16,768]{1,0:T(8,128)S(1)}, u32[]{:S(2)}, u32[]{:S(2)}) collective-permute-start(f32[16,768]{1,0:T(8,128)S(1)} %constant_dynamic-update-slice_fusion.8), channel_id=1, source_target_pairs={{0,8},{8,0},{16,24},{24,16},{1,9},{9,1},{17,25},{25,17},{2,10},{10... | collective-permute-start | bytes 147464 | tf_op jit(solution)/shard_map/ppermute | solution.py:201
  138.4 4.0 %collective-permute-start.13 = (f32[32,768]{1,0:T(8,128)S(1)}, f32[32,768]{1,0:T(8,128)S(1)}, u32[]{:S(2)}, u32[]{:S(2)}) collective-permute-start(f32[32,768]{1,0:T(8,128)S(1)} %constant_dynamic-update-slice_fusion.6), channel_id=1, source_target_pairs={{0,1},{1,0},{2,3},{3,2},{4,5},{5,4},{6,7},{7,6},{8,9},{9,8},{10,11... | collective-permute-start | bytes 294920 | tf_op jit(solution)/shard_map/ppermute | solution.py:201
  142.4 5.2 %collective-permute-start.14 = (f32[64,768]{1,0:T(8,128)S(1)}, f32[64,768]{1,0:T(8,128)S(1)}, u32[]{:S(2)}, u32[]{:S(2)}) collective-permute-start(f32[64,768]{1,0:T(8,128)S(1)} %constant_dynamic-update-slice_fusion.4), channel_id=1, source_target_pairs={{0,4},{2,6},{4,0},{6,2},{1,5},{3,7},{5,1},{7,3},{8,12},{10,14},{12... | collective-permute-start | bytes 589832 | tf_op jit(solution)/shard_map/ppermute | solution.py:201
  147.6 4.1 %collective-permute-start.15 = (f32[128,768]{1,0:T(8,128)S(1)}, f32[128,768]{1,0:T(8,128)S(1)}, u32[]{:S(2)}, u32[]{:S(2)}) collective-permute-start(f32[128,768]{1,0:T(8,128)S(1)} %constant_dynamic-update-slice_fusion.2), channel_id=1, source_target_pairs={{0,2},{2,0},{4,6},{6,4},{1,3},{3,1},{5,7},{7,5},{8,10},{10,8},{12,... | collective-permute-start | bytes 1179656 | tf_op jit(solution)/shard_map/ppermute | solution.py:201
